TPU v7x, 32 devices: a whole 2x2x4 slice. The times are simulated.
32 devices in a mesh: lat: 4 (over x, core), lon: 2 (over y), lev: 4 (over z).
Axes of the slice: x: 2, y: 2, z: 4, core: 2. Of those that a mesh axis runs over, the one named last changes fastest.
Arguments:
- fields: float32 [2, 60, 128, 256], P(None, 'lev', 'lat', 'lon'), may hold values from -6 to 6
- diffusivity: float32 [60, 128, 256], P('lev', 'lat', 'lon'), may hold values from 0.02 to 0.24
- cloudy_index: int32 [4, 2048], P('lat', 'lon'), may hold values from 0 to 4095, as said below
- owners: int32 [4, 2048, 1], P('lat', 'lon'), may hold values from 0 to 1; in each aligned block of 256 rows (0 to 255, 256 to 511, ..., all dimensions but the last counted through in order) at most 256 rows name the same one
- w_in: bfloat16 [2, 120, 1024], P('lon'), may hold values from -0.5 to 0.5
- w_mid: bfloat16 [2, 2, 1024, 1024], P('lon'), may hold values from -0.1875 to 0.1875
- w_out: bfloat16 [2, 1024, 120], P('lon'), may hold values from -0.1875 to 0.1875
Outputs:
- fields_next: float32 [2, 60, 128, 256], P(None, 'lev', 'lat', 'lon')
Inputs may be any that keep to these rules, and one draw needn't show every extreme that they name: `cloudy_index`: in row i, entries j * 1024 to (j + 1) * 1024 - 1 are distinct column numbers a * 128 + b of the dycore block (i, j). `owners`: in each aligned block of 256 rows (one level slice of one dycore block), no regime is named by more than 256 rows.
All inputs are finite; a program needn't handle non-finite values.
Results may differ from a plain program's by a relative error of at most 0.00062.
Values may be sent and summed in bfloat16 or wider, within the bound.
No kernel may reach another device: no remote copies, remote signals or barrier semaphores. Data moves between devices by JAX's collectives and lax.ppermute only.
A program may use at most 64 MiB of HBM per device.

v0:
```python
import jax
import jax.numpy as jnp
from jax import lax
from jax.sharding import PartitionSpec as P

LEVELS = 60
STEPS = 3


def padded_2(cells, sides, width):
    for axis, dim in sides:
        count = lax.axis_size(axis)
        head = lax.slice_in_dim(cells, 0, width, axis=dim)
        tail = lax.slice_in_dim(cells, cells.shape[dim] - width, cells.shape[dim], axis=dim)
        cells = jnp.concatenate(
            [
                lax.ppermute(tail, axis, [(i, (i + 1) % count) for i in range(count)]),
                cells,
                lax.ppermute(head, axis, [((i + 1) % count, i) for i in range(count)]),
            ],
            axis=dim,
        )
    return cells


def substep(values, coefficients):
    centre = values[..., 1:-1, 1:-1]
    middle = coefficients[:, 1:-1, 1:-1]
    updated = centre
    for lat_cut, lon_cut in (
        (slice(0, -2), slice(1, -1)),
        (slice(2, None), slice(1, -1)),
        (slice(1, -1), slice(0, -2)),
        (slice(1, -1), slice(2, None)),
    ):
        neighbour = values[..., lat_cut, lon_cut]
        face_coef = 0.5 * (middle + coefficients[:, lat_cut, lon_cut])
        updated = updated + face_coef * (neighbour - centre)
    return updated


def clear_outside(values, rim_width, lat_rows):
    lat_pos = (
        lax.axis_index("lat") * lat_rows - rim_width + jnp.arange(values.shape[-2], dtype=jnp.int32)
    )
    inside = (lat_pos >= 0) & (lat_pos < lat_rows * lax.axis_size("lat"))
    return jnp.where(inside[:, None], values, 0.0)


def network(features, w_first, w_middle, w_last):
    contract = (((0,), (0,)), ((), ()))
    hidden = jax.nn.gelu(
        lax.dot_general(w_first, features, contract, preferred_element_type=jnp.float32)
    ).astype(jnp.bfloat16)
    for layer_no in range(w_middle.shape[0]):
        hidden = jax.nn.gelu(
            lax.dot_general(
                w_middle[layer_no], hidden, contract, preferred_element_type=jnp.float32
            )
        ).astype(jnp.bfloat16)
    return lax.dot_general(w_last, hidden, contract, preferred_element_type=jnp.float32).astype(
        jnp.bfloat16
    )


def on_device(fields, diffusivity, cloudy_index, owners, w_in, w_mid, w_out):
    lat_rows = fields.shape[2]
    coefficients = clear_outside(padded_2(diffusivity, (("lat", 1), ("lon", 2)), 1), 1, lat_rows)
    values = fields
    for repeat in range(STEPS):
        padded = clear_outside(padded_2(values, (("lat", 2), ("lon", 3)), 1), 1, lat_rows)
        values = substep(padded, coefficients)
    lev_count = lax.axis_size("lev")
    lon_count = lax.axis_size("lon")
    level_rows = values.shape[1]
    cells = values.shape[2] * values.shape[3]
    column_ids = cloudy_index[0]
    cloudy = column_ids.shape[0]
    per_device = cloudy // lev_count
    capacity = min(per_device, 4 * per_device // lon_count)
    feature_count = 2 * LEVELS
    flat_values = values.reshape(2 * level_rows, cells)
    picker = (column_ids[:, None] == jnp.arange(cells, dtype=jnp.int32)[None, :]).astype(
        jnp.bfloat16
    )
    picked = lax.dot_general(
        flat_values.astype(jnp.bfloat16),
        picker,
        (((1,), (1,)), ((), ())),
        preferred_element_type=jnp.float32,
    )
    picked = picked.astype(jnp.bfloat16).reshape(2, level_rows, cloudy)
    routes = owners[0, :, 0]
    pieces = routes.reshape(lev_count, per_device)
    onehot = (pieces[:, :, None] == jnp.arange(lon_count, dtype=jnp.int32)).astype(jnp.int32)
    slot_rank = jnp.sum(jnp.cumsum(onehot, 1) * onehot, 2) - 1
    columns = lax.all_to_all(picked, "lev", split_axis=2, concat_axis=1, tiled=True).reshape(
        feature_count, per_device
    )
    lev_pos = lax.axis_index("lev")
    my_route = lax.dynamic_index_in_dim(pieces, lev_pos, 0, keepdims=False)
    my_rank = lax.dynamic_index_in_dim(slot_rank, lev_pos, 0, keepdims=False)
    slot_index = my_route * capacity + my_rank
    send_buffer = (
        jnp.zeros((feature_count, lon_count * capacity), jnp.bfloat16)
        .at[:, slot_index]
        .set(columns)
    )
    send_buffer = send_buffer.reshape(feature_count, lon_count, capacity)
    received = lax.all_to_all(send_buffer, "lon", split_axis=1, concat_axis=1, tiled=True)
    outcome = network(received.reshape(feature_count, -1), w_in[0], w_mid[0], w_out[0]).reshape(
        received.shape
    )
    returned = lax.all_to_all(outcome, "lon", split_axis=1, concat_axis=1, tiled=True).reshape(
        feature_count, lon_count * capacity
    )
    returned = returned[:, slot_index].reshape(2, LEVELS, per_device)
    tendency = lax.all_to_all(returned, "lev", split_axis=1, concat_axis=2, tiled=True)
    spread = jnp.dot(
        tendency.reshape(2 * level_rows, cloudy), picker, preferred_element_type=jnp.float32
    )
    updated = flat_values + spread
    return updated.reshape(values.shape)


def solution(mesh):
    in_specs = (
        P(None, "lev", "lat", "lon"),
        P("lev", "lat", "lon"),
        P("lat", "lon"),
        P("lat", "lon", None),
        P("lon", None, None),
        P("lon", None, None, None),
        P("lon", None, None),
    )
    out_specs = P(None, "lev", "lat", "lon")
    return jax.shard_map(
        on_device, mesh=mesh, in_specs=in_specs, out_specs=out_specs, check_vma=False
    )
```

profile of v0, /device:TPU:0, one launch (start us, length us, event | category | flops | bytes accessed | tf_op | source)
XLA Modules:
  0.0 159.0 jit_solution(291012053237129662)
XLA Ops:
  9.3 2.3 %collective-permute-start.6 = (f32[15,34,1]{2,1,0:T(8,128)}, f32[15,34,1]{2,1,0:T(8,128)S(1)}, u32[]{:S(2)}, u32[]{:S(2)}) collective-permute-start(f32[15,34,1]{2,1,0:T(8,128)} %get-tuple-element.21), channel_id=1, source_target_pairs={{0,4},{4,0},{1,5},{5,1},{2,6},{6,2},{3,7},{7,3},{8,12},{12,8},{9,1... | collective-permute-start | bytes 6128 | tf_op jit(solution)/shard_map/ppermute | solution.py:17
  12.6 7.3 %collective-permute-done.6 = f32[15,34,1]{2,1,0:T(8,128)S(1)} collective-permute-done((f32[15,34,1]{2,1,0:T(8,128)}, f32[15,34,1]{2,1,0:T(8,128)S(1)}, u32[]{:S(2)}, u32[]{:S(2)}) %collective-permute-start.6) | collective-permute-done | bytes 2072 | tf_op jit(solution)/shard_map/ppermute | solution.py:17
  19.9 6.2 %collective-permute-done.7 = f32[15,34,1]{2,1,0:T(8,128)} collective-permute-done((f32[15,34,1]{2,1,0:T(8,128)}, f32[15,34,1]{2,1,0:T(8,128)}, u32[]{:S(2)}, u32[]{:S(2)}) %collective-permute-start.7) | collective-permute-done | bytes 2072 | tf_op jit(solution)/shard_map/ppermute | solution.py:19
  27.4 2.1 %copy.132 = f32[2,15,1,128]{2,1,3,0:T(8,128)} copy(f32[2,15,1,128]{3,1,2,0:T(8,128)S(1)} %collective-permute-done) | data formatting | bytes 30720 | tf_op jit(solution)/shard_map/ppermute | solution.py:17
  29.5 2.8 %copy.134 = f32[2,15,1,128]{2,1,3,0:T(8,128)} copy(f32[2,15,1,128]{3,1,2,0:T(8,128)} %collective-permute-done.1) | data formatting | bytes 30720 | tf_op jit(solution)/shard_map/ppermute | solution.py:19
  37.9 2.3 %copy.136 = f32[15,32,128]{1,0,2:T(8,128)} copy(f32[15,32,128]{2,1,0:T(8,128)} %get-tuple-element.17) | data formatting | bytes 491520 | tf_op jit(solution)/shard_map/mul | solution.py:37
  40.3 2.3 %copy.137 = f32[15,32,128]{1,0,2:T(8,128)} copy(f32[15,32,128]{2,1,0:T(8,128)} %get-tuple-element.16) | data formatting | bytes 491520 | tf_op jit(solution)/shard_map/mul | solution.py:37
  42.6 2.3 %copy.138 = f32[15,32,128]{1,0,2:T(8,128)} copy(f32[15,32,128]{2,1,0:T(8,128)} %get-tuple-element.18) | data formatting | bytes 491520 | tf_op jit(solution)/shard_map/mul | solution.py:37
  44.9 3.5 %maximum_select_fusion = f32[2,15,34,130]{2,1,3,0:T(8,128)S(1)} fusion(f32[2,15,34,1]{2,1,3,0:T(8,128)S(1)} %collective-permute-done.3, f32[2,15,1,128]{2,1,3,0:T(8,128)} %copy.134, f32[2,15,32,128]{2,1,3,0:T(8,128)S(1)} %copy.133, f32[2,15,1,128]{2,1,3,0:T(8,128)} %copy.132, f32[2,15,34,1]{2,1,3,0:T(8,128)S(1)} %collective-permute-done.2, ...), kind=kLoop, calls=%fused_computation.11 | loop fusion | flops 663000 | bytes 1060834 | tf_op jit(solution)/shard_map/jit(_where)/select_n | solution.py:47
  48.5 2.4 %fusion.46 = f32[2,15,32,128]{2,1,3,0:T(8,128)S(1)} fusion(f32[2,15,34,130]{2,1,3,0:T(8,128)S(1)} %maximum_select_fusion, f32[15,32,128]{1,0,2:T(8,128)S(1)} %copy-done.7, f32[15,32,128]{1,0,2:T(8,128)S(1)} %copy-done.4, f32[15,32,128]{1,0,2:T(8,128)S(1)} %copy-done.1, f32[15,32,128]{1,0,2:T(8,128)S(1)} %copy.135), kind=kLoop, calls=%fused_computation.64 | loop fusion | flops 1474560 | bytes 3932160 | tf_op jit(solution)/shard_map/add | solution.py:38
  50.8 2.6 %fusion.99 = (f32[2,15,1,128]{2,1,3,0:T(8,128)}, f32[2,15,1,128]{2,1,3,0:T(8,128)}) fusion(f32[2,15,32,128]{2,1,3,0:T(8,128)S(1)} %fusion.46), kind=kLoop, calls=%fused_computation.134 | loop fusion | bytes 61440 | tf_op jit(solution)/shard_map/slice | solution.py:14
  53.5 2.3 %copy.139 = f32[2,15,1,128]{3,1,2,0:T(8,128)S(1)} copy(f32[2,15,1,128]{2,1,3,0:T(8,128)} %get-tuple-element.13) | data formatting | bytes 30720 | tf_op jit(solution)/shard_map/slice | solution.py:14
  55.9 2.3 %copy.140 = f32[2,15,1,128]{3,1,2,0:T(8,128)S(1)} copy(f32[2,15,1,128]{2,1,3,0:T(8,128)} %get-tuple-element.14) | data formatting | bytes 30720 | tf_op jit(solution)/shard_map/slice | solution.py:13
  62.2 2.1 %copy.142 = f32[2,15,1,128]{2,1,3,0:T(8,128)} copy(f32[2,15,1,128]{3,1,2,0:T(8,128)S(1)} %collective-permute-done.9) | data formatting | bytes 30720 | tf_op jit(solution)/shard_map/ppermute | solution.py:19
  67.3 2.4 %reduce-window.6 = s32[4,2,2,128]{3,2,1,0:T(2,128)S(1)} reduce-window(s32[4,2,2,128]{3,2,1,0:T(2,128)S(1)} %compare_convert_fusion, s32[]{:T(128)} %constant.17.clone.1), window={size=1x1x1x128 pad=0_0x0_0x0_0x127_0}, to_apply=%region_0.1 | reduce-window | flops 260096 | bytes 16388 | tf_op jit(solution)/shard_map/reduce-window
  70.5 3.6 %maximum_select_fusion.1 = f32[2,15,34,130]{2,1,3,0:T(8,128)S(1)} fusion(f32[2,15,34,1]{2,1,3,0:T(8,128)S(1)} %collective-permute-done.11, f32[2,15,1,128]{2,1,3,0:T(8,128)} %copy.142, f32[2,15,32,128]{2,1,3,0:T(8,128)S(1)} %fusion.46, f32[2,15,1,128]{2,1,3,0:T(8,128)} %copy.141, f32[2,15,34,1]{2,1,3,0:T(8,128)S(1)} %collective-permute-done.10, ...), kind=kLoop, calls=%fused_computation.12 | loop fusion | flops 663000 | bytes 1060834 | tf_op jit(solution)/shard_map/jit(_where)/select_n | solution.py:47
  74.1 2.4 %fusion.38 = f32[2,15,32,128]{2,1,3,0:T(8,128)S(1)} fusion(f32[2,15,34,130]{2,1,3,0:T(8,128)S(1)} %maximum_select_fusion.1, f32[15,32,128]{1,0,2:T(8,128)S(1)} %copy-done.8, f32[15,32,128]{1,0,2:T(8,128)S(1)} %copy-done.5, f32[15,32,128]{1,0,2:T(8,128)S(1)} %copy-done.2, f32[15,32,128]{1,0,2:T(8,128)S(1)} %copy.135), kind=kLoop, calls=%fused_computation.52 | loop fusion | flops 1474560 | bytes 3932160 | tf_op jit(solution)/shard_map/add | solution.py:38
  76.5 2.6 %fusion.98 = (f32[2,15,1,128]{2,1,3,0:T(8,128)}, f32[2,15,1,128]{2,1,3,0:T(8,128)}) fusion(f32[2,15,32,128]{2,1,3,0:T(8,128)S(1)} %fusion.38), kind=kLoop, calls=%fused_computation.133 | loop fusion | bytes 61440 | tf_op jit(solution)/shard_map/slice | solution.py:14
  79.1 2.3 %copy.143 = f32[2,15,1,128]{3,1,2,0:T(8,128)S(1)} copy(f32[2,15,1,128]{2,1,3,0:T(8,128)} %get-tuple-element.11) | data formatting | bytes 30720 | tf_op jit(solution)/shard_map/slice | solution.py:14
  81.5 2.3 %copy.144 = f32[2,15,1,128]{3,1,2,0:T(8,128)S(1)} copy(f32[2,15,1,128]{2,1,3,0:T(8,128)} %get-tuple-element.12) | data formatting | bytes 30720 | tf_op jit(solution)/shard_map/slice | solution.py:13
  97.0 3.4 %maximum_select_fusion.2 = f32[2,15,34,130]{2,1,3,0:T(8,128)S(1)} fusion(f32[2,15,34,1]{2,1,3,0:T(8,128)S(1)} %collective-permute-done.15, f32[2,15,1,128]{2,1,3,0:T(8,128)} %copy.146, f32[2,15,32,128]{2,1,3,0:T(8,128)S(1)} %fusion.38, f32[2,15,1,128]{2,1,3,0:T(8,128)} %copy.145, f32[2,15,34,1]{2,1,3,0:T(8,128)S(1)} %collective-permute-done.14, ...), kind=kLoop, calls=%fused_computation.13 | loop fusion | flops 663000 | bytes 1060834 | tf_op jit(solution)/shard_map/jit(_where)/select_n | solution.py:47
  100.4 2.4 %fusion.30 = f32[2,15,32,128]{2,1,3,0:T(8,128)S(1)} fusion(f32[2,15,34,130]{2,1,3,0:T(8,128)S(1)} %maximum_select_fusion.2, f32[15,32,128]{1,0,2:T(8,128)S(1)} %copy-done.9, f32[15,32,128]{1,0,2:T(8,128)S(1)} %copy-done.6, f32[15,32,128]{1,0,2:T(8,128)S(1)} %copy-done.3, f32[15,32,128]{1,0,2:T(8,128)S(1)} %copy.135), kind=kLoop, calls=%fused_computation.40 | loop fusion | flops 1474560 | bytes 3932160 | tf_op jit(solution)/shard_map/add | solution.py:38
  103.9 3.4 %fusion.69 = bf16[30,1024]{1,0:T(8,128)(2,1)S(1)} fusion(s32[1024]{0:T(1024)S(1)} %bitcast.101, f32[30,4096]{1,0:T(8,128)S(1)} %bitcast.83), kind=kOutput, calls=%fused_computation.82 | convolution fusion | flops 256006144 | bytes 557056 | tf_op jit(solution)/shard_map/dot_general | solution.py:86
  109.2 4.9 %all-to-all-start = ((bf16[4,2,3840]{2,1,0:T(2,128)(2,1)}), bf16[4,2,3840]{2,1,0:T(2,128)(2,1)S(1)}, u32[]{:S(2)}, u32[]{:S(2)}) async-start(bf16[4,2,3840]{2,1,0:T(2,128)(2,1)} %reshape.124), calls=%async_computation | async-start | bytes 122880 | tf_op jit(solution)/shard_map/all_to_all | solution.py:97
  114.1 5.7 %all-to-all-done = bf16[4,2,3840]{2,1,0:T(2,128)(2,1)S(1)} async-done(((bf16[4,2,3840]{2,1,0:T(2,128)(2,1)}), bf16[4,2,3840]{2,1,0:T(2,128)(2,1)S(1)}, u32[]{:S(2)}, u32[]{:S(2)}) %all-to-all-start) | async-done | bytes 61472 | tf_op jit(solution)/shard_map/all_to_all | solution.py:97
  122.8 6.8 %all_to_all.40 = bf16[120,2,256]{2,0,1:T(8,128)(2,1)S(1)} all-to-all(bf16[120,2,256]{2,0,1:T(8,128)(2,1)S(1)} %copy.154), channel_id=1, replica_groups=mesh['lat'=4,'lon'=2,'lev'=4] {'lon'}, dimensions={1} | all-to-all | bytes 245760 | tf_op jit(solution)/shard_map/all_to_all | solution.py:110
  129.6 3.7 %fusion.20 = bf16[1024,512]{0,1:T(8,128)(2,1)S(1)} fusion(bf16[1,2,1024,1024]{3,2,1,0:T(8,128)(2,1)} %param.12, bf16[120,512]{1,0:T(8,128)(2,1)S(1)} %bitcast.94, bf16[1,120,1024]{2,1,0:T(8,128)(2,1)S(1)} %copy-done), kind=kOutput, calls=%fused_computation.29 | convolution fusion | flops 1209008128 | bytes 3514368 | tf_op jit(solution)/shard_map/dot_general | solution.py:57
  133.4 3.4 %fusion.66 = bf16[512,120]{0,1:T(8,128)(2,1)S(1)} fusion(bf16[1024,512]{0,1:T(8,128)(2,1)S(1)} %fusion.20, bf16[1,2,1024,1024]{3,2,1,0:T(8,128)(2,1)} %param.12, bf16[1,1024,120]{1,2,0:T(8,128)(2,1)S(1)} %copy-done.13), kind=kOutput, calls=%fused_computation.81 | convolution fusion | flops 1204350976 | bytes 3514368 | tf_op jit(solution)/shard_map/dot_general | solution.py:61
  137.5 3.4 %all-to-all-start.2 = ((bf16[120,2,256]{2,0,1:T(8,128)(2,1)}), bf16[120,2,256]{2,0,1:T(8,128)(2,1)S(1)}, u32[]{:S(2)}, u32[]{:S(2)}) async-start(bf16[120,2,256]{2,0,1:T(8,128)(2,1)} %bitcast.76), calls=%async_computation.2 | async-start | bytes 245760 | tf_op jit(solution)/shard_map/all_to_all | solution.py:114
  140.9 4.4 %all-to-all-done.2 = bf16[120,2,256]{2,0,1:T(8,128)(2,1)S(1)} async-done(((bf16[120,2,256]{2,0,1:T(8,128)(2,1)}), bf16[120,2,256]{2,0,1:T(8,128)(2,1)S(1)}, u32[]{:S(2)}, u32[]{:S(2)}) %all-to-all-start.2) | async-done | bytes 122912 | tf_op jit(solution)/shard_map/all_to_all | solution.py:114
  146.5 8.1 %all_to_all.41 = bf16[2,60,256]{2,0,1:T(2,128)(2,1)S(1)} all-to-all(bf16[2,60,256]{2,0,1:T(2,128)(2,1)S(1)} %copy.159), channel_id=1, replica_groups=mesh['lat'=4,'lon'=2,'lev'=4] {'lev'}, dimensions={1} | all-to-all | bytes 122880 | tf_op jit(solution)/shard_map/all_to_all | solution.py:118
  154.7 3.4 %fusion.4 = f32[30,4096]{1,0:T(8,128)S(1)} fusion(f32[30,4096]{1,0:T(8,128)S(1)} %bitcast.84, bf16[30,1024]{1,0:T(8,128)(2,1)S(1)} %bitcast.96, s32[1024]{0:T(1024)S(1)} %bitcast.102), kind=kOutput, calls=%fused_computation.7 | convolution fusion | flops 255975424 | bytes 1048576 | tf_op jit(solution)/shard_map/dot_general | solution.py:119
  (114 shorter events, 46.9 us)
Async XLA Ops:
  0.0 129.6 %copy-start = (bf16[1,120,1024]{2,1,0:T(8,128)(2,1)S(1)}, bf16[1,120,1024]{2,1,0:T(8,128)(2,1)}, u32[]{:S(2)}) copy-start(bf16[1,120,1024]{2,1,0:T(8,128)(2,1)} %param.11) | copy-start | bytes 737284
  0.0 11.7 %copy-start.11 = (f32[2,15,32,128]{3,2,1,0:T(8,128)S(1)}, f32[2,15,32,128]{3,2,1,0:T(8,128)}, u32[]{:S(2)}) copy-start(f32[2,15,32,128]{3,2,1,0:T(8,128)} %param.7) | copy-start | bytes 1474564
  0.9 6.4 %collective-permute-start.4 = (f32[15,1,128]{2,1,0:T(1,128)S(1)}, f32[15,1,128]{2,1,0:T(1,128)S(1)}, u32[]{:S(2)}, u32[]{:S(2)}) collective-permute-start(f32[15,1,128]{2,1,0:T(1,128)S(1)} %get-tuple-element.23), channel_id=1, source_target_pairs={{0,8},{8,16},{16,24},{24,0},{1,9},{9,17},{17,25},{25,1},{2,10},{10... | collective-permute-start | bytes 23048 | tf_op jit(solution)/shard_map/ppermute | solution.py:17
  1.5 5.9 %collective-permute-start.5 = (f32[15,1,128]{2,1,0:T(1,128)S(1)}, f32[15,1,128]{2,1,0:T(1,128)S(1)}, u32[]{:S(2)}, u32[]{:S(2)}) collective-permute-start(f32[15,1,128]{2,1,0:T(1,128)S(1)} %get-tuple-element.24), channel_id=1, source_target_pairs={{8,0},{16,8},{24,16},{0,24},{9,1},{17,9},{25,17},{1,25},{10,2},{18... | collective-permute-start | bytes 23048 | tf_op jit(solution)/shard_map/ppermute | solution.py:19
  5.0 22.4 %collective-permute-start = (f32[2,15,1,128]{3,1,2,0:T(8,128)}, f32[2,15,1,128]{3,1,2,0:T(8,128)S(1)}, u32[]{:S(2)}, u32[]{:S(2)}) collective-permute-start(f32[2,15,1,128]{3,1,2,0:T(8,128)} %copy.164), channel_id=1, source_target_pairs={{0,8},{8,16},{16,24},{24,0},{1,9},{9,17},{17,25},{25,1},{2,10},{10... | collective-permute-start | bytes 46088 | tf_op jit(solution)/shard_map/ppermute | solution.py:17
  6.2 23.3 %collective-permute-start.1 = (f32[2,15,1,128]{3,1,2,0:T(8,128)}, f32[2,15,1,128]{3,1,2,0:T(8,128)}, u32[]{:S(2)}, u32[]{:S(2)}) collective-permute-start(f32[2,15,1,128]{3,1,2,0:T(8,128)} %copy.165), channel_id=1, source_target_pairs={{8,0},{16,8},{24,16},{0,24},{9,1},{17,9},{25,17},{1,25},{10,2},{18... | collective-permute-start | bytes 46088 | tf_op jit(solution)/shard_map/ppermute | solution.py:19
  7.4 18.7 %copy-start.10 = (f32[15,32,128]{2,1,0:T(8,128)S(1)}, f32[15,32,128]{2,1,0:T(8,128)}, u32[]{:S(2)}) copy-start(f32[15,32,128]{2,1,0:T(8,128)} %param.8) | copy-start | bytes 737284
  9.3 10.5 %collective-permute-start.6 = (f32[15,34,1]{2,1,0:T(8,128)}, f32[15,34,1]{2,1,0:T(8,128)S(1)}, u32[]{:S(2)}, u32[]{:S(2)}) collective-permute-start(f32[15,34,1]{2,1,0:T(8,128)} %get-tuple-element.21), channel_id=1, source_target_pairs={{0,4},{4,0},{1,5},{5,1},{2,6},{6,2},{3,7},{7,3},{8,12},{12,8},{9,1... | collective-permute-start | bytes 6128 | tf_op jit(solution)/shard_map/ppermute | solution.py:17
  11.6 14.4 %collective-permute-start.7 = (f32[15,34,1]{2,1,0:T(8,128)}, f32[15,34,1]{2,1,0:T(8,128)}, u32[]{:S(2)}, u32[]{:S(2)}) collective-permute-start(f32[15,34,1]{2,1,0:T(8,128)} %get-tuple-element.22), channel_id=1, source_target_pairs={{4,0},{0,4},{5,1},{1,5},{6,2},{2,6},{7,3},{3,7},{12,8},{8,12},{13,... | collective-permute-start | bytes 6128 | tf_op jit(solution)/shard_map/ppermute | solution.py:19
  33.2 11.7 %collective-permute-start.2 = (f32[2,15,34,1]{2,1,3,0:T(8,128)S(1)}, f32[2,15,34,1]{2,1,3,0:T(8,128)S(1)}, u32[]{:S(2)}, u32[]{:S(2)}) collective-permute-start(f32[2,15,34,1]{2,1,3,0:T(8,128)S(1)} %get-tuple-element.9), channel_id=1, source_target_pairs={{0,4},{4,0},{1,5},{5,1},{2,6},{6,2},{3,7},{7,3},{8,12},{12,8},{9,1... | collective-permute-start | bytes 12248 | tf_op jit(solution)/shard_map/ppermute | solution.py:17
  34.7 10.2 %collective-permute-start.3 = (f32[2,15,34,1]{2,1,3,0:T(8,128)S(1)}, f32[2,15,34,1]{2,1,3,0:T(8,128)S(1)}, u32[]{:S(2)}, u32[]{:S(2)}) collective-permute-start(f32[2,15,34,1]{2,1,3,0:T(8,128)S(1)} %get-tuple-element.10), channel_id=1, source_target_pairs={{4,0},{0,4},{5,1},{1,5},{6,2},{2,6},{7,3},{3,7},{12,8},{8,12},{13,... | collective-permute-start | bytes 12248 | tf_op jit(solution)/shard_map/ppermute | solution.py:19
  44.9 3.6 %copy-start.1 = (f32[15,32,128]{1,0,2:T(8,128)S(1)}, f32[15,32,128]{1,0,2:T(8,128)}, u32[]{:S(2)}) copy-start(f32[15,32,128]{1,0,2:T(8,128)} %copy.136) | copy-start | bytes 737284
  44.9 3.6 %copy-start.4 = (f32[15,32,128]{1,0,2:T(8,128)S(1)}, f32[15,32,128]{1,0,2:T(8,128)}, u32[]{:S(2)}) copy-start(f32[15,32,128]{1,0,2:T(8,128)} %copy.137) | copy-start | bytes 737284
  44.9 3.6 %copy-start.7 = (f32[15,32,128]{1,0,2:T(8,128)S(1)}, f32[15,32,128]{1,0,2:T(8,128)}, u32[]{:S(2)}) copy-start(f32[15,32,128]{1,0,2:T(8,128)} %copy.138) | copy-start | bytes 737284
  55.8 4.3 %collective-permute-start.8 = (f32[2,15,1,128]{3,1,2,0:T(8,128)S(1)}, f32[2,15,1,128]{3,1,2,0:T(8,128)S(1)}, u32[]{:S(2)}, u32[]{:S(2)}) collective-permute-start(f32[2,15,1,128]{3,1,2,0:T(8,128)S(1)} %copy.139), channel_id=1, source_target_pairs={{0,8},{8,16},{16,24},{24,0},{1,9},{9,17},{17,25},{25,1},{2,10},{10... | collective-permute-start | bytes 46088 | tf_op jit(solution)/shard_map/ppermute | solution.py:17
  58.2 4.0 %collective-permute-start.9 = (f32[2,15,1,128]{3,1,2,0:T(8,128)S(1)}, f32[2,15,1,128]{3,1,2,0:T(8,128)S(1)}, u32[]{:S(2)}, u32[]{:S(2)}) collective-permute-start(f32[2,15,1,128]{3,1,2,0:T(8,128)S(1)} %copy.140), channel_id=1, source_target_pairs={{8,0},{16,8},{24,16},{0,24},{9,1},{17,9},{25,17},{1,25},{10,2},{18... | collective-permute-start | bytes 46088 | tf_op jit(solution)/shard_map/ppermute | solution.py:19
  64.3 3.0 %copy-start.12 = (s32[1,1024,1]{1,2,0:T(1,128)S(1)}, s32[1,1024,1]{1,2,0:T(1,128)}, u32[]{:S(2)}) copy-start(s32[1,1024,1]{1,2,0:T(1,128)} %param.10) | copy-start | bytes 12292
  65.2 4.9 %collective-permute-start.10 = (f32[2,15,34,1]{2,1,3,0:T(8,128)S(1)}, f32[2,15,34,1]{2,1,3,0:T(8,128)S(1)}, u32[]{:S(2)}, u32[]{:S(2)}) collective-permute-start(f32[2,15,34,1]{2,1,3,0:T(8,128)S(1)} %get-tuple-element.7), channel_id=1, source_target_pairs={{0,4},{4,0},{1,5},{5,1},{2,6},{6,2},{3,7},{7,3},{8,12},{12,8},{9,1... | collective-permute-start | bytes 12248 | tf_op jit(solution)/shard_map/ppermute | solution.py:17
  66.8 3.7 %collective-permute-start.11 = (f32[2,15,34,1]{2,1,3,0:T(8,128)S(1)}, f32[2,15,34,1]{2,1,3,0:T(8,128)S(1)}, u32[]{:S(2)}, u32[]{:S(2)}) collective-permute-start(f32[2,15,34,1]{2,1,3,0:T(8,128)S(1)} %get-tuple-element.8), channel_id=1, source_target_pairs={{4,0},{0,4},{5,1},{1,5},{6,2},{2,6},{7,3},{3,7},{12,8},{8,12},{13,... | collective-permute-start | bytes 12248 | tf_op jit(solution)/shard_map/ppermute | solution.py:19
  70.1 4.0 %copy-start.2 = (f32[15,32,128]{1,0,2:T(8,128)S(1)}, f32[15,32,128]{1,0,2:T(8,128)}, u32[]{:S(2)}) copy-start(f32[15,32,128]{1,0,2:T(8,128)} %copy.136) | copy-start | bytes 737284
  70.1 4.1 %copy-start.5 = (f32[15,32,128]{1,0,2:T(8,128)S(1)}, f32[15,32,128]{1,0,2:T(8,128)}, u32[]{:S(2)}) copy-start(f32[15,32,128]{1,0,2:T(8,128)} %copy.137) | copy-start | bytes 737284
  70.1 4.1 %copy-start.8 = (f32[15,32,128]{1,0,2:T(8,128)S(1)}, f32[15,32,128]{1,0,2:T(8,128)}, u32[]{:S(2)}) copy-start(f32[15,32,128]{1,0,2:T(8,128)} %copy.138) | copy-start | bytes 737284
  81.5 5.6 %collective-permute-start.12 = (f32[2,15,1,128]{3,1,2,0:T(8,128)S(1)}, f32[2,15,1,128]{3,1,2,0:T(8,128)S(1)}, u32[]{:S(2)}, u32[]{:S(2)}) collective-permute-start(f32[2,15,1,128]{3,1,2,0:T(8,128)S(1)} %copy.143), channel_id=1, source_target_pairs={{0,8},{8,16},{16,24},{24,0},{1,9},{9,17},{17,25},{25,1},{2,10},{10... | collective-permute-start | bytes 46088 | tf_op jit(solution)/shard_map/ppermute | solution.py:17
  83.9 5.3 %collective-permute-start.13 = (f32[2,15,1,128]{3,1,2,0:T(8,128)S(1)}, f32[2,15,1,128]{3,1,2,0:T(8,128)S(1)}, u32[]{:S(2)}, u32[]{:S(2)}) collective-permute-start(f32[2,15,1,128]{3,1,2,0:T(8,128)S(1)} %copy.144), channel_id=1, source_target_pairs={{8,0},{16,8},{24,16},{0,24},{9,1},{17,9},{25,17},{1,25},{10,2},{18... | collective-permute-start | bytes 46088 | tf_op jit(solution)/shard_map/ppermute | solution.py:19
  92.2 3.8 %collective-permute-start.14 = (f32[2,15,34,1]{2,1,3,0:T(8,128)S(1)}, f32[2,15,34,1]{2,1,3,0:T(8,128)S(1)}, u32[]{:S(2)}, u32[]{:S(2)}) collective-permute-start(f32[2,15,34,1]{2,1,3,0:T(8,128)S(1)} %get-tuple-element.5), channel_id=1, source_target_pairs={{0,4},{4,0},{1,5},{5,1},{2,6},{6,2},{3,7},{7,3},{8,12},{12,8},{9,1... | collective-permute-start | bytes 12248 | tf_op jit(solution)/shard_map/ppermute | solution.py:17
  93.3 3.7 %collective-permute-start.15 = (f32[2,15,34,1]{2,1,3,0:T(8,128)S(1)}, f32[2,15,34,1]{2,1,3,0:T(8,128)S(1)}, u32[]{:S(2)}, u32[]{:S(2)}) collective-permute-start(f32[2,15,34,1]{2,1,3,0:T(8,128)S(1)} %get-tuple-element.6), channel_id=1, source_target_pairs={{4,0},{0,4},{5,1},{1,5},{6,2},{2,6},{7,3},{3,7},{12,8},{8,12},{13,... | collective-permute-start | bytes 12248 | tf_op jit(solution)/shard_map/ppermute | solution.py:19
  94.3 6.1 %copy-start.3 = (f32[15,32,128]{1,0,2:T(8,128)S(1)}, f32[15,32,128]{1,0,2:T(8,128)}, u32[]{:S(2)}) copy-start(f32[15,32,128]{1,0,2:T(8,128)} %copy.136) | copy-start | bytes 737284
  94.3 6.1 %copy-start.6 = (f32[15,32,128]{1,0,2:T(8,128)S(1)}, f32[15,32,128]{1,0,2:T(8,128)}, u32[]{:S(2)}) copy-start(f32[15,32,128]{1,0,2:T(8,128)} %copy.137) | copy-start | bytes 737284
  94.3 6.1 %copy-start.9 = (f32[15,32,128]{1,0,2:T(8,128)S(1)}, f32[15,32,128]{1,0,2:T(8,128)}, u32[]{:S(2)}) copy-start(f32[15,32,128]{1,0,2:T(8,128)} %copy.138) | copy-start | bytes 737284
  109.2 10.6 %all-to-all-start = ((bf16[4,2,3840]{2,1,0:T(2,128)(2,1)}), bf16[4,2,3840]{2,1,0:T(2,128)(2,1)S(1)}, u32[]{:S(2)}, u32[]{:S(2)}) async-start(bf16[4,2,3840]{2,1,0:T(2,128)(2,1)} %reshape.124), calls=%async_computation | async-start | bytes 122880 | tf_op jit(solution)/shard_map/all_to_all | solution.py:97
  129.6 3.8 %copy-start.13 = (bf16[1,1024,120]{1,2,0:T(8,128)(2,1)S(1)}, bf16[1,1024,120]{1,2,0:T(8,128)(2,1)}, u32[]{:S(2)}) copy-start(bf16[1,1024,120]{1,2,0:T(8,128)(2,1)} %param.13) | copy-start | bytes 737284
  137.5 7.8 %all-to-all-start.2 = ((bf16[120,2,256]{2,0,1:T(8,128)(2,1)}), bf16[120,2,256]{2,0,1:T(8,128)(2,1)S(1)}, u32[]{:S(2)}, u32[]{:S(2)}) async-start(bf16[120,2,256]{2,0,1:T(8,128)(2,1)} %bitcast.76), calls=%async_computation.2 | async-start | bytes 245760 | tf_op jit(solution)/shard_map/all_to_all | solution.py:114
  (1 other events, 1.1 us)
where the time goes:
time: 160 us; the launch traced here: 159 us
  local copies, waits for them, and re-layouts  50.9 us (32%)
  other arithmetic  27 us (17%)
  waiting for transfers between devices  26.7 us (17%)
  starting transfers between devices  25 us (16%)
  blocking collectives  14.9 us (9%)
  matrix products  14 us (9%)
    slice x7, local copies, waits for them, and re-layouts, padded_2(): lax.slice_in_dim(cells, cells.shape[dim] - width, cells.shape[dim], axis=...  12.8 us
    select_n x4, other arithmetic, clear_outside(): return jnp.where(inside[:, None], values, 0.0)  11.8 us
    ppermute x8, starting transfers between devices, padded_2(): lax.ppermute(head, axis, [((i + 1) % count, i) for i in range(count)])  9.04 us
    ppermute x8, waiting for transfers between devices, padded_2(): lax.ppermute(tail, axis, [(i, (i + 1) % count) for i in range(count)])  8.97 us
    mul x4, local copies, waits for them, and re-layouts, substep(): face_coef = 0.5 * (middle + coefficients[:, lat_cut, lon_cut])  8.39 us
    all_to_all x1, blocking collectives, on_device(): lax.all_to_all(returned, 'lev', split_axis=1, concat_axis=2, tiled=True)  8.09 us
    ppermute x8, starting transfers between devices, padded_2(): lax.ppermute(tail, axis, [(i, (i + 1) % count) for i in range(count)])  7.69 us
    ppermute x8, waiting for transfers between devices, padded_2(): lax.ppermute(head, axis, [((i + 1) % count, i) for i in range(count)])  7.63 us
  transfers between devices with their start and end apart: 18, of which 7 were waited for; matrix products, arithmetic and copies ran while one was open for 20% of the time, Pallas kernels for 0%

commit v1 on v0

--- a/solution.py
+++ b/solution.py
@@ -7,20 +7,25 @@
 STEPS = 3
 
 
-def padded_2(cells, sides, width):
-    for axis, dim in sides:
-        count = lax.axis_size(axis)
-        head = lax.slice_in_dim(cells, 0, width, axis=dim)
-        tail = lax.slice_in_dim(cells, cells.shape[dim] - width, cells.shape[dim], axis=dim)
-        cells = jnp.concatenate(
-            [
-                lax.ppermute(tail, axis, [(i, (i + 1) % count) for i in range(count)]),
-                cells,
-                lax.ppermute(head, axis, [((i + 1) % count, i) for i in range(count)]),
-            ],
-            axis=dim,
-        )
-    return cells
+def halo_exchange(cells, width):
+    lat_count = lax.axis_size("lat")
+    from_above = lax.ppermute(
+        cells[..., cells.shape[-2] - width :, :], "lat", [(i, i + 1) for i in range(lat_count - 1)]
+    )
+    from_below = lax.ppermute(
+        cells[..., :width, :], "lat", [(i + 1, i) for i in range(lat_count - 1)]
+    )
+    cells = jnp.concatenate([from_above, cells, from_below], axis=-2)
+    lon_count = lax.axis_size("lon")
+    left = cells[..., :width]
+    right = cells[..., cells.shape[-1] - width :]
+    if lon_count == 2:
+        both = lax.ppermute(jnp.concatenate([right, left], axis=-1), "lon", [(0, 1), (1, 0)])
+        from_left, from_right = both[..., :width], both[..., width:]
+    else:
+        from_left = lax.ppermute(right, "lon", [(i, (i + 1) % lon_count) for i in range(lon_count)])
+        from_right = lax.ppermute(left, "lon", [((i + 1) % lon_count, i) for i in range(lon_count)])
+    return jnp.concatenate([from_left, cells, from_right], axis=-1)
 
 
 def substep(values, coefficients):
@@ -47,6 +52,26 @@
     return jnp.where(inside[:, None], values, 0.0)
 
 
+def dynamics(fields, diffusivity):
+    kinds, level_rows, lat_rows, lon_cols = fields.shape
+    stacked = jnp.concatenate(
+        [fields.reshape(kinds * level_rows, lat_rows, lon_cols), diffusivity], axis=0
+    )
+    stacked = halo_exchange(stacked, STEPS)
+    values = stacked[: kinds * level_rows].reshape(
+        kinds, level_rows, lat_rows + 2 * STEPS, lon_cols + 2 * STEPS
+    )
+    kappa = stacked[kinds * level_rows :]
+    for repeat in range(STEPS):
+        trim = repeat
+        coefficients = kappa[:, trim : kappa.shape[1] - trim, trim : kappa.shape[2] - trim]
+        values = substep(values, coefficients)
+        rim = STEPS - repeat - 1
+        if rim:
+            values = clear_outside(values, rim, lat_rows)
+    return values
+
+
 def network(features, w_first, w_middle, w_last):
     contract = (((0,), (0,)), ((), ()))
     hidden = jax.nn.gelu(
@@ -64,12 +89,7 @@
 
 
 def on_device(fields, diffusivity, cloudy_index, owners, w_in, w_mid, w_out):
-    lat_rows = fields.shape[2]
-    coefficients = clear_outside(padded_2(diffusivity, (("lat", 1), ("lon", 2)), 1), 1, lat_rows)
-    values = fields
-    for repeat in range(STEPS):
-        padded = clear_outside(padded_2(values, (("lat", 2), ("lon", 3)), 1), 1, lat_rows)
-        values = substep(padded, coefficients)
+    values = dynamics(fields, diffusivity)
     lev_count = lax.axis_size("lev")
     lon_count = lax.axis_size("lon")
     level_rows = values.shape[1]

time: 160 us -> 85.2 us (0.53)
  local copies, waits for them, and re-layouts: 50.9 us -> 11.5 us
  other arithmetic: 27 us -> 13.4 us
  waiting for transfers between devices: 26.7 us -> 13.7 us
  starting transfers between devices: 25 us -> 16.5 us
    slice x11 -> x7, local copies, waits for them, and re-layouts: 17.7 us -> 1.45 us  [the longest x2 0.74 us: halo_exchange(): right = cells[..., cells.shape[-1] - width:]]
    ppermute x6 -> x0, local copies, waits for them, and re-layouts: 13.3 us -> none  [the longest x3 7.03 us: padded_2(): lax.ppermute(head, axis, [((i + 1) % count, i) for i in range(count)])]
    ppermute x16 -> x3, waiting for transfers between devices: 16.6 us -> 3.59 us  [the longest x1 3.58 us: halo_exchange(): lax.ppermute(jnp.concatenate([right, left], axis=-1), 'lon', [(0, 1), (1,...]
    ppermute x16 -> x3, starting transfers between devices: 16.7 us -> 7.36 us  [the longest x1 3.04 us: halo_exchange(): lax.ppermute(cells[..., cells.shape[-2] - width:, :], 'lat', [(i, i + 1)...]
    select_n x4 -> x2, other arithmetic: 11.8 us -> 2.81 us  [clear_outside(): return jnp.where(inside[:, None], values, 0.0)]
    mul x4 -> x0, local copies, waits for them, and re-layouts: 8.39 us -> none  [substep(): face_coef = 0.5 * (middle + coefficients[:, lat_cut, lon_cut])]
    add x3 -> x1, other arithmetic: 7.08 us -> 0.6 us  [substep(): updated = updated + face_coef * (neighbour - centre)]
    unnamed x42 -> x21, local copies, waits for them, and re-layouts: 6.43 us -> 5.51 us
  transfers between devices with their start and end apart: 18 -> 5, of which waited for: 7 -> 3; matrix products, arithmetic and copies ran while one was open for 20% -> 6% of each run, Pallas kernels for 0% -> 0%
where the time goes in v1:
time: 85.2 us; the launch traced here: 84.6 us
  starting transfers between devices  16.5 us (19%)
  blocking collectives  15.1 us (18%)
  matrix products  14 us (16%)
  waiting for transfers between devices  13.7 us (16%)
  other arithmetic  13.4 us (16%)
  local copies, waits for them, and re-layouts  11.5 us (13%)
    all_to_all x1, blocking collectives, on_device(): lax.all_to_all(returned, 'lev', split_axis=1, concat_axis=2, tiled=True)  8.09 us
    all_to_all x1, blocking collectives, on_device(): lax.all_to_all(send_buffer, 'lon', split_axis=1, concat_axis=1, tiled=True)  7.02 us
    all_to_all x1, starting transfers between devices, on_device(): lax.all_to_all(picked, 'lev', split_axis=2, concat_axis=1, tiled=True)  5.82 us
    all_to_all x1, waiting for transfers between devices, on_device(): lax.all_to_all(picked, 'lev', split_axis=2, concat_axis=1, tiled=True)  5.72 us
    unnamed x21, local copies, waits for them, and re-layouts  5.51 us
    all_to_all x1, waiting for transfers between devices, on_device(): lax.all_to_all(outcome, 'lon', split_axis=1, concat_axis=1, tiled=True)  4.4 us
    dot_general x1, matrix products, network(): lax.dot_general(w_middle[layer_no], hidden, contract, preferred_element_t...  3.73 us
    ppermute x1, waiting for transfers between devices, halo_exchange(): lax.ppermute(jnp.concatenate([right, left], axis=-1), 'lon', [(0, 1), (1,...  3.58 us
  transfers between devices with their start and end apart: 5, of which 3 were waited for; matrix products, arithmetic and copies ran while one was open for 6% of the time, Pallas kernels for 0%

profile of v1, /device:TPU:0, one launch (start us, length us, event | category | flops | bytes accessed | tf_op | source)
XLA Modules:
  0.0 84.6 jit_solution(4896823482996957519)
XLA Ops:
  0.0 1.1 %pad_maximum_fusion.16 = (f32[45,3,128]{2,1,0:T(4,128)S(1)}, f32[45,3,128]{2,1,0:T(4,128)S(1)}) fusion(f32[15,32,128]{2,1,0:T(8,128)} %param.8, f32[30,32,128]{2,1,0:T(8,128)} %bitcast.80), kind=kLoop, calls=%fused_computation.134 | loop fusion | flops 34560 | bytes 875520 | tf_op jit(solution)/shard_map/slice | solution.py:13
  1.1 1.3 %collective-permute-start.1 = (f32[45,3,128]{2,1,0:T(4,128)S(1)}, f32[45,3,128]{2,1,0:T(4,128)S(1)}, u32[]{:S(2)}, u32[]{:S(2)}) collective-permute-start(f32[45,3,128]{2,1,0:T(4,128)S(1)} %get-tuple-element.22), channel_id=1, source_target_pairs={{8,0},{16,8},{24,16},{9,1},{17,9},{25,17},{10,2},{18,10},{26,18},{... | collective-permute-start | bytes 207368 | tf_op jit(solution)/shard_map/ppermute | solution.py:15
  2.4 3.0 %collective-permute-start = (f32[45,3,128]{2,1,0:T(4,128)S(1)}, f32[45,3,128]{2,1,0:T(4,128)S(1)}, u32[]{:S(2)}, u32[]{:S(2)}) collective-permute-start(f32[45,3,128]{2,1,0:T(4,128)S(1)} %get-tuple-element.21), channel_id=1, source_target_pairs={{0,8},{8,16},{16,24},{1,9},{9,17},{17,25},{2,10},{10,18},{18,26},{... | collective-permute-start | bytes 207368 | tf_op jit(solution)/shard_map/ppermute | solution.py:12
  5.5 0.7 compare_convert_fusion
  6.2 2.4 %reduce-window.6 = s32[4,2,2,128]{3,2,1,0:T(2,128)S(1)} reduce-window(s32[4,2,2,128]{3,2,1,0:T(2,128)S(1)} %compare_convert_fusion, s32[]{:T(128)} %constant.18.clone.1), window={size=1x1x1x128 pad=0_0x0_0x0_0x127_0}, to_apply=%region_0.1 | reduce-window | flops 260096 | bytes 16388 | tf_op jit(solution)/shard_map/reduce-window
  9.5 1.3 %reduce.3 = s32[1024]{0:T(1024)S(1)} reduce(s32[1,1024,1]{1,2,0:T(1,128)} %param.10, s32[]{:T(128)} %broadcast.151), dimensions={0,2}, to_apply=%param.10.reduce_sub_computation.3 | reduce | bytes 8196 | tf_op args[3]
  10.9 1.3 %pad_maximum_fusion.1 = f32[45,38,128]{2,1,0:T(8,128)S(1)} fusion(f32[45,3,128]{2,1,0:T(4,128)S(1)} %collective-permute-done.1, f32[15,32,128]{2,1,0:T(8,128)} %param.8, f32[30,32,128]{2,1,0:T(8,128)} %bitcast.81, f32[45,3,128]{2,1,0:T(4,128)S(1)} %collective-permute-done), kind=kLoop, calls=%fused_computation.79 | loop fusion | flops 656640 | bytes 1751040 | tf_op jit(solution)/shard_map/concatenate | solution.py:18
  13.4 3.0 %collective-permute-start.2 = (f32[45,38,6]{0,1,2:T(8,128)S(1)}, f32[45,38,6]{0,1,2:T(8,128)S(1)}, u32[]{:S(2)}, u32[]{:S(2)}) collective-permute-start(f32[45,38,6]{0,1,2:T(8,128)S(1)} %pad_maximum_fusion.14), channel_id=1, source_target_pairs={{0,4},{4,0},{1,5},{5,1},{2,6},{6,2},{3,7},{7,3},{8,12},{12,8},{9,1... | collective-permute-start | bytes 123128 | tf_op jit(solution)/shard_map/ppermute | solution.py:23
  16.5 3.6 %collective-permute-done.2 = f32[45,38,6]{0,1,2:T(8,128)S(1)} collective-permute-done((f32[45,38,6]{0,1,2:T(8,128)S(1)}, f32[45,38,6]{0,1,2:T(8,128)S(1)}, u32[]{:S(2)}, u32[]{:S(2)}) %collective-permute-start.2) | collective-permute-done | bytes 41072 | tf_op jit(solution)/shard_map/ppermute | solution.py:23
  21.0 1.0 %pad_maximum_fusion = f32[45,38,134]{2,1,0:T(8,128)S(1)} fusion(f32[45,38,3]{2,1,0:T(8,128)S(1)} %copy.77, f32[45,3,128]{2,1,0:T(4,128)S(1)} %collective-permute-done.1, f32[15,32,128]{2,1,0:T(8,128)S(1)} %copy-done.2, f32[30,32,128]{2,1,0:T(8,128)S(1)} %bitcast.82, f32[45,3,128]{2,1,0:T(4,128)S(1)} %collective-permute-done, f32[45,38,3]{2,1,0:T(8,128)S(1)} %copy.76), kind=kLoop, calls=%fused_computation.41 | loop fusion | flops 1145700 | bytes 1833120 | tf_op jit(solution)/shard_map/concatenate | solution.py:28
  22.1 0.7 fusion.79
  22.8 1.4 %fusion.46 = f32[2,15,36,132]{3,2,1,0:T(8,128)S(1)} fusion(f32[2,15,38,134]{3,2,1,0:T(8,128)S(1)} %bitcast.79, f32[15,36,132]{2,1,0:T(8,128)S(1)} %get-tuple-element.12, f32[15,36,132]{2,1,0:T(8,128)S(1)} %get-tuple-element.13, f32[15,36,132]{2,1,0:T(8,128)S(1)} %get-tuple-element.14, f32[15,36,132]{2,1,0:T(8,128)S(1)} %get-tuple-element.11, ...), kind=kLoop, calls=%fused_computation.58 | loop fusion | flops 1853280 | bytes 4561956 | tf_op jit(solution)/shard_map/jit(_where)/select_n | solution.py:52
  24.2 0.9 %fusion.75 = (f32[15,34,130]{2,1,0:T(8,128)S(1)}, f32[15,34,130]{2,1,0:T(8,128)S(1)}, f32[15,34,130]{2,1,0:T(8,128)S(1)}, f32[15,34,130]{2,1,0:T(8,128)S(1)}) fusion(f32[45,38,134]{2,1,0:T(8,128)S(1)} %pad_maximum_fusion, f32[45,38,3]{2,1,0:T(8,128)S(1)} %copy.77, f32[45,3,128]{2,1,0:T(4,128)S(1)} %collective-permute-done.1, ...), kind=kLoop, calls=%fused_computation.87 | loop fusion | flops 1060800 | bytes 2772960 | tf_op jit(solution)/shard_map/mul | solution.py:42
  25.1 1.4 %fusion.37 = f32[2,15,34,130]{3,2,1,0:T(8,128)S(1)} fusion(f32[2,15,36,132]{3,2,1,0:T(8,128)S(1)} %fusion.46, f32[15,34,130]{2,1,0:T(8,128)S(1)} %get-tuple-element.9, f32[15,34,130]{2,1,0:T(8,128)S(1)} %get-tuple-element.10, f32[15,34,130]{2,1,0:T(8,128)S(1)} %get-tuple-element.8, f32[15,34,130]{2,1,0:T(8,128)S(1)} %get-tuple-element.7, ...), kind=kLoop, calls=%fused_computation.45 | loop fusion | flops 1723800 | bytes 4243234 | tf_op jit(solution)/shard_map/jit(_where)/select_n | solution.py:52
  26.9 0.6 fusion.81
  28.2 3.4 %fusion.63 = bf16[30,1024]{1,0:T(8,128)(2,1)S(1)} fusion(s32[1024]{0:T(1024)S(1)} %bitcast.109, f32[30,4096]{1,0:T(8,128)S(1)} %bitcast.91), kind=kOutput, calls=%fused_computation.70 | convolution fusion | flops 256006144 | bytes 557056 | tf_op jit(solution)/shard_map/dot_general | solution.py:106
  31.7 0.6 copy.62
  32.3 1.4 %reshape.140 = bf16[4,2,3840]{2,1,0:T(2,128)(2,1)} reshape(bf16[1024,2,15]{2,1,0:T(2,128)(2,1)S(1)} %bitcast.87) | data formatting | bytes 122880
  33.6 5.8 %all-to-all-start = ((bf16[4,2,3840]{2,1,0:T(2,128)(2,1)}), bf16[4,2,3840]{2,1,0:T(2,128)(2,1)S(1)}, u32[]{:S(2)}, u32[]{:S(2)}) async-start(bf16[4,2,3840]{2,1,0:T(2,128)(2,1)} %reshape.140), calls=%async_computation | async-start | bytes 122880 | tf_op jit(solution)/shard_map/all_to_all | solution.py:117
  39.5 5.7 %all-to-all-done = bf16[4,2,3840]{2,1,0:T(2,128)(2,1)S(1)} async-done(((bf16[4,2,3840]{2,1,0:T(2,128)(2,1)}), bf16[4,2,3840]{2,1,0:T(2,128)(2,1)S(1)}, u32[]{:S(2)}, u32[]{:S(2)}) %all-to-all-start) | async-done | bytes 61472 | tf_op jit(solution)/shard_map/all_to_all | solution.py:117
  45.2 1.1 %reshape.141 = bf16[1024,2,15]{2,1,0:T(2,128)(2,1)S(1)} reshape(bf16[4,2,3840]{2,1,0:T(2,128)(2,1)S(1)} %all-to-all-done) | data formatting | bytes 122880
  46.9 1.2 %scatter_custom_fusion = bf16[120,512]{0,1:T(8,128)(2,1)S(1)} fusion(s32[256]{0:T(256)S(1)} %bitcast.107, bf16[256,120]{1,0:T(8,128)(2,1)S(1)} %copy.65, bf16[]{:T(256)} %constant.23.clone.1), kind=kCustom, calls=%fused_computation.135 | custom fusion | bytes 122882 | tf_op jit(solution)/shard_map/scatter | solution.py:127
  48.2 7.0 %all_to_all.40 = bf16[120,2,256]{2,0,1:T(8,128)(2,1)S(1)} all-to-all(bf16[120,2,256]{2,0,1:T(8,128)(2,1)S(1)} %copy.66), channel_id=1, replica_groups=mesh['lat'=4,'lon'=2,'lev'=4] {'lon'}, dimensions={1} | all-to-all | bytes 245760 | tf_op jit(solution)/shard_map/all_to_all | solution.py:130
  55.3 3.7 %fusion.20 = bf16[1024,512]{0,1:T(8,128)(2,1)S(1)} fusion(bf16[1,2,1024,1024]{3,2,1,0:T(8,128)(2,1)} %param.12, bf16[120,512]{1,0:T(8,128)(2,1)S(1)} %bitcast.102, bf16[1,120,1024]{2,1,0:T(8,128)(2,1)S(1)} %copy-done), kind=kOutput, calls=%fused_computation.26 | convolution fusion | flops 1209008128 | bytes 3514368 | tf_op jit(solution)/shard_map/dot_general | solution.py:82
  59.0 3.5 %fusion.60 = bf16[512,120]{0,1:T(8,128)(2,1)S(1)} fusion(bf16[1024,512]{0,1:T(8,128)(2,1)S(1)} %fusion.20, bf16[1,2,1024,1024]{3,2,1,0:T(8,128)(2,1)} %param.12, bf16[1,1024,120]{1,2,0:T(8,128)(2,1)S(1)} %copy-done.3), kind=kOutput, calls=%fused_computation.69 | convolution fusion | flops 1204350976 | bytes 3514368 | tf_op jit(solution)/shard_map/dot_general | solution.py:86
  62.5 0.7 copy.84
  63.1 3.4 %all-to-all-start.2 = ((bf16[120,2,256]{2,0,1:T(8,128)(2,1)}), bf16[120,2,256]{2,0,1:T(8,128)(2,1)S(1)}, u32[]{:S(2)}, u32[]{:S(2)}) async-start(bf16[120,2,256]{2,0,1:T(8,128)(2,1)} %bitcast.78), calls=%async_computation.2 | async-start | bytes 245760 | tf_op jit(solution)/shard_map/all_to_all | solution.py:134
  66.5 4.4 %all-to-all-done.2 = bf16[120,2,256]{2,0,1:T(8,128)(2,1)S(1)} async-done(((bf16[120,2,256]{2,0,1:T(8,128)(2,1)}), bf16[120,2,256]{2,0,1:T(8,128)(2,1)S(1)}, u32[]{:S(2)}, u32[]{:S(2)}) %all-to-all-start.2) | async-done | bytes 122912 | tf_op jit(solution)/shard_map/all_to_all | solution.py:134
  71.1 0.9 %gather_fusion = bf16[256,120]{1,0:T(8,128)(2,1)S(1)} fusion(bf16[120,512]{0,1:T(8,128)(2,1)S(1)} %bitcast.85, s32[1024]{0:T(1024)S(1)} %pad_clamp_fusion), kind=kCustom, calls=%fused_computation | custom fusion | bytes 123904 | tf_op jit(solution)/shard_map/gather | solution.py:137
  72.2 8.1 %all_to_all.41 = bf16[2,60,256]{2,0,1:T(2,128)(2,1)S(1)} all-to-all(bf16[2,60,256]{2,0,1:T(2,128)(2,1)S(1)} %copy.71), channel_id=1, replica_groups=mesh['lat'=4,'lon'=2,'lev'=4] {'lev'}, dimensions={1} | all-to-all | bytes 122880 | tf_op jit(solution)/shard_map/all_to_all | solution.py:138
  80.3 3.4 %fusion.4 = f32[30,4096]{1,0:T(8,128)S(1)} fusion(f32[30,4096]{1,0:T(8,128)S(1)} %bitcast.92, bf16[30,1024]{1,0:T(8,128)(2,1)S(1)} %bitcast.104, s32[1024]{0:T(1024)S(1)} %bitcast.110), kind=kOutput, calls=%fused_computation.7 | convolution fusion | flops 255975424 | bytes 1048576 | tf_op jit(solution)/shard_map/dot_general | solution.py:139
  83.8 0.8 slice.224
  (51 shorter events, 5.5 us)
Async XLA Ops:
  0.0 55.3 %copy-start = (bf16[1,120,1024]{2,1,0:T(8,128)(2,1)S(1)}, bf16[1,120,1024]{2,1,0:T(8,128)(2,1)}, u32[]{:S(2)}) copy-start(bf16[1,120,1024]{2,1,0:T(8,128)(2,1)} %param.11) | copy-start | bytes 737284
  1.1 9.8 %collective-permute-start.1 = (f32[45,3,128]{2,1,0:T(4,128)S(1)}, f32[45,3,128]{2,1,0:T(4,128)S(1)}, u32[]{:S(2)}, u32[]{:S(2)}) collective-permute-start(f32[45,3,128]{2,1,0:T(4,128)S(1)} %get-tuple-element.22), channel_id=1, source_target_pairs={{8,0},{16,8},{24,16},{9,1},{17,9},{25,17},{10,2},{18,10},{26,18},{... | collective-permute-start | bytes 207368 | tf_op jit(solution)/shard_map/ppermute | solution.py:15
  2.4 8.5 %collective-permute-start = (f32[45,3,128]{2,1,0:T(4,128)S(1)}, f32[45,3,128]{2,1,0:T(4,128)S(1)}, u32[]{:S(2)}, u32[]{:S(2)}) collective-permute-start(f32[45,3,128]{2,1,0:T(4,128)S(1)} %get-tuple-element.21), channel_id=1, source_target_pairs={{0,8},{8,16},{16,24},{1,9},{9,17},{17,25},{2,10},{10,18},{18,26},{... | collective-permute-start | bytes 207368 | tf_op jit(solution)/shard_map/ppermute | solution.py:12
  13.0 8.0 %copy-start.1 = (f32[2,15,32,128]{3,2,1,0:T(8,128)S(1)}, f32[2,15,32,128]{3,2,1,0:T(8,128)}, u32[]{:S(2)}) copy-start(f32[2,15,32,128]{3,2,1,0:T(8,128)} %param.7) | copy-start | bytes 1474564
  13.0 8.0 %copy-start.2 = (f32[15,32,128]{2,1,0:T(8,128)S(1)}, f32[15,32,128]{2,1,0:T(8,128)}, u32[]{:S(2)}) copy-start(f32[15,32,128]{2,1,0:T(8,128)} %param.8) | copy-start | bytes 737284
  13.4 6.6 %collective-permute-start.2 = (f32[45,38,6]{0,1,2:T(8,128)S(1)}, f32[45,38,6]{0,1,2:T(8,128)S(1)}, u32[]{:S(2)}, u32[]{:S(2)}) collective-permute-start(f32[45,38,6]{0,1,2:T(8,128)S(1)} %pad_maximum_fusion.14), channel_id=1, source_target_pairs={{0,4},{4,0},{1,5},{5,1},{2,6},{6,2},{3,7},{7,3},{8,12},{12,8},{9,1... | collective-permute-start | bytes 123128 | tf_op jit(solution)/shard_map/ppermute | solution.py:23
  27.5 0.7 copy-start.4
  33.6 11.5 %all-to-all-start = ((bf16[4,2,3840]{2,1,0:T(2,128)(2,1)}), bf16[4,2,3840]{2,1,0:T(2,128)(2,1)S(1)}, u32[]{:S(2)}, u32[]{:S(2)}) async-start(bf16[4,2,3840]{2,1,0:T(2,128)(2,1)} %reshape.140), calls=%async_computation | async-start | bytes 122880 | tf_op jit(solution)/shard_map/all_to_all | solution.py:117
  55.3 3.7 %copy-start.3 = (bf16[1,1024,120]{1,2,0:T(8,128)(2,1)S(1)}, bf16[1,1024,120]{1,2,0:T(8,128)(2,1)}, u32[]{:S(2)}) copy-start(bf16[1,1024,120]{1,2,0:T(8,128)(2,1)} %param.13) | copy-start | bytes 737284
  63.1 7.8 %all-to-all-start.2 = ((bf16[120,2,256]{2,0,1:T(8,128)(2,1)}), bf16[120,2,256]{2,0,1:T(8,128)(2,1)S(1)}, u32[]{:S(2)}, u32[]{:S(2)}) async-start(bf16[120,2,256]{2,0,1:T(8,128)(2,1)} %bitcast.78), calls=%async_computation.2 | async-start | bytes 245760 | tf_op jit(solution)/shard_map/all_to_all | solution.py:134

commit v2 on v1

--- a/solution.py
+++ b/solution.py
@@ -109,35 +109,40 @@
         (((1,), (1,)), ((), ())),
         preferred_element_type=jnp.float32,
     )
-    picked = picked.astype(jnp.bfloat16).reshape(2, level_rows, cloudy)
+    picked = picked.astype(jnp.bfloat16)
     routes = owners[0, :, 0]
     pieces = routes.reshape(lev_count, per_device)
     onehot = (pieces[:, :, None] == jnp.arange(lon_count, dtype=jnp.int32)).astype(jnp.int32)
     slot_rank = jnp.sum(jnp.cumsum(onehot, 1) * onehot, 2) - 1
-    columns = lax.all_to_all(picked, "lev", split_axis=2, concat_axis=1, tiled=True).reshape(
-        feature_count, per_device
+    piece_of = jnp.arange(lev_count, dtype=jnp.int32)[:, None]
+    slot_index = ((pieces * lev_count + piece_of) * capacity + slot_rank).reshape(cloudy)
+    group = lon_count * lev_count
+    local_features = 2 * level_rows
+    send_buffer = (
+        jnp.zeros((local_features, group * capacity), jnp.bfloat16)
+        .at[:, slot_index]
+        .set(picked)
+    ).reshape(local_features, group, capacity)
+    received = lax.all_to_all(
+        send_buffer, ("lon", "lev"), split_axis=1, concat_axis=1, tiled=True
     )
-    lev_pos = lax.axis_index("lev")
-    my_route = lax.dynamic_index_in_dim(pieces, lev_pos, 0, keepdims=False)
-    my_rank = lax.dynamic_index_in_dim(slot_rank, lev_pos, 0, keepdims=False)
-    slot_index = my_route * capacity + my_rank
-    send_buffer = (
-        jnp.zeros((feature_count, lon_count * capacity), jnp.bfloat16)
-        .at[:, slot_index]
-        .set(columns)
+    inputs = (
+        received.reshape(2, level_rows, lon_count, lev_count, capacity)
+        .transpose(0, 3, 1, 2, 4)
+        .reshape(feature_count, lon_count * capacity)
     )
-    send_buffer = send_buffer.reshape(feature_count, lon_count, capacity)
-    received = lax.all_to_all(send_buffer, "lon", split_axis=1, concat_axis=1, tiled=True)
-    outcome = network(received.reshape(feature_count, -1), w_in[0], w_mid[0], w_out[0]).reshape(
-        received.shape
+    outcome = network(inputs, w_in[0], w_mid[0], w_out[0])
+    outgoing = (
+        outcome.reshape(2, lev_count, level_rows, lon_count, capacity)
+        .transpose(0, 2, 3, 1, 4)
+        .reshape(local_features, group, capacity)
     )
-    returned = lax.all_to_all(outcome, "lon", split_axis=1, concat_axis=1, tiled=True).reshape(
-        feature_count, lon_count * capacity
-    )
-    returned = returned[:, slot_index].reshape(2, LEVELS, per_device)
-    tendency = lax.all_to_all(returned, "lev", split_axis=1, concat_axis=2, tiled=True)
+    returned = lax.all_to_all(
+        outgoing, ("lon", "lev"), split_axis=1, concat_axis=1, tiled=True
+    ).reshape(local_features, group * capacity)
+    tendency = returned[:, slot_index]
     spread = jnp.dot(
-        tendency.reshape(2 * level_rows, cloudy), picker, preferred_element_type=jnp.float32
+        tendency, picker, preferred_element_type=jnp.float32
     )
     updated = flat_values + spread
     return updated.reshape(values.shape)

time: 85.2 us -> 77.9 us (0.914)
  starting transfers between devices: 16.5 us -> 10.7 us
  waiting for transfers between devices: 13.7 us -> 11 us
  local copies, waits for them, and re-layouts: 11.5 us -> 13.1 us
  blocking collectives: 15.1 us -> 14.2 us
    all_to_all x2 -> x1, starting transfers between devices: 9.18 us -> 3.37 us  [on_device(): lax.all_to_all(outgoing, ('lon', 'lev'), split_axis=1, concat_axis=1, til...]
    all_to_all x2 -> x1, waiting for transfers between devices: 10.1 us -> 7.44 us  [on_device(): lax.all_to_all(outgoing, ('lon', 'lev'), split_axis=1, concat_axis=1, til...]
    unnamed x21, local copies, waits for them, and re-layouts: 5.51 us -> 3.07 us
    gather x1, local copies, waits for them, and re-layouts: 0.86 us -> 3.2 us  [on_device(): tendency = returned[:, slot_index]]
    scatter x1, local copies, waits for them, and re-layouts: 1.22 us -> 3.51 us  [on_device(): send_buffer = jnp.zeros((local_features, group * capacity), jnp.bfloat16)...]
    all_to_all x2 -> x1, blocking collectives: 15.1 us -> 14.2 us  [on_device(): lax.all_to_all(send_buffer, ('lon', 'lev'), split_axis=1, concat_axis=1,...]
    reshape x9 -> x7, local copies, waits for them, and re-layouts: 1.8 us -> 1.17 us  [the longest x2 0.72 us: on_device(): outgoing = outcome.reshape(2, lev_count, level_rows, lon_count, capacity)...]
  transfers between devices with their start and end apart: 5 -> 4, of which waited for: 3 -> 2; matrix products, arithmetic and copies ran while one was open for 6% -> 8% of each run, Pallas kernels for 0% -> 0%
where the time goes in v2:
time: 77.9 us; the launch traced here: 77.4 us
  blocking collectives  14.2 us (18%)
  other arithmetic  14 us (18%)
  matrix products  13.9 us (18%)
  local copies, waits for them, and re-layouts  13.1 us (17%)
  waiting for transfers between devices  11 us (14%)
  starting transfers between devices  10.7 us (14%)
    all_to_all x1, blocking collectives, on_device(): lax.all_to_all(send_buffer, ('lon', 'lev'), split_axis=1, concat_axis=1,...  14.2 us
    all_to_all x1, waiting for transfers between devices, on_device(): lax.all_to_all(outgoing, ('lon', 'lev'), split_axis=1, concat_axis=1, til...  7.44 us
    dot_general x1, matrix products, network(): lax.dot_general(w_middle[layer_no], hidden, contract, preferred_element_t...  3.74 us
    ppermute x1, waiting for transfers between devices, halo_exchange(): lax.ppermute(jnp.concatenate([right, left], axis=-1), 'lon', [(0, 1), (1,...  3.58 us
    scatter x1, local copies, waits for them, and re-layouts, on_device(): send_buffer = jnp.zeros((local_features, group * capacity), jnp.bfloat16)...  3.51 us
    dot_general x1, matrix products, network(): lax.dot_general(w_last, hidden, contract, preferred_element_type=jnp.floa...  3.46 us
    dot_general x1, matrix products, on_device(): lax.dot_general(flat_values.astype(jnp.bfloat16), picker, (((1,), (1,)),...  3.41 us
    all_to_all x1, starting transfers between devices, on_device(): lax.all_to_all(outgoing, ('lon', 'lev'), split_axis=1, concat_axis=1, til...  3.37 us
  transfers between devices with their start and end apart: 4, of which 2 were waited for; matrix products, arithmetic and copies ran while one was open for 8% of the time, Pallas kernels for 0%

profile of v2, /device:TPU:0, one launch (start us, length us, event | category | flops | bytes accessed | tf_op | source)
XLA Modules:
  0.0 77.4 jit_solution(5720988606565134992)
XLA Ops:
  0.0 1.1 %pad_maximum_fusion.16 = (f32[45,3,128]{2,1,0:T(4,128)S(1)}, f32[45,3,128]{2,1,0:T(4,128)S(1)}) fusion(f32[15,32,128]{2,1,0:T(8,128)} %param.8, f32[30,32,128]{2,1,0:T(8,128)} %bitcast.93), kind=kLoop, calls=%fused_computation.139 | loop fusion | flops 34560 | bytes 875520 | tf_op jit(solution)/shard_map/slice | solution.py:13
  1.1 1.3 %collective-permute-start.1 = (f32[45,3,128]{2,1,0:T(4,128)S(1)}, f32[45,3,128]{2,1,0:T(4,128)S(1)}, u32[]{:S(2)}, u32[]{:S(2)}) collective-permute-start(f32[45,3,128]{2,1,0:T(4,128)S(1)} %get-tuple-element.22), channel_id=1, source_target_pairs={{8,0},{16,8},{24,16},{9,1},{17,9},{25,17},{10,2},{18,10},{26,18},{... | collective-permute-start | bytes 207368 | tf_op jit(solution)/shard_map/ppermute | solution.py:15
  2.4 3.0 %collective-permute-start = (f32[45,3,128]{2,1,0:T(4,128)S(1)}, f32[45,3,128]{2,1,0:T(4,128)S(1)}, u32[]{:S(2)}, u32[]{:S(2)}) collective-permute-start(f32[45,3,128]{2,1,0:T(4,128)S(1)} %get-tuple-element.21), channel_id=1, source_target_pairs={{0,8},{8,16},{16,24},{1,9},{9,17},{17,25},{2,10},{10,18},{18,26},{... | collective-permute-start | bytes 207368 | tf_op jit(solution)/shard_map/ppermute | solution.py:12
  5.5 0.7 compare_convert_fusion
  6.2 2.4 %reduce-window.6 = s32[4,2,2,128]{3,2,1,0:T(2,128)S(1)} reduce-window(s32[4,2,2,128]{3,2,1,0:T(2,128)S(1)} %compare_convert_fusion, s32[]{:T(128)} %constant.18.clone.1), window={size=1x1x1x128 pad=0_0x0_0x0_0x127_0}, to_apply=%region_0.1 | reduce-window | flops 260096 | bytes 16388 | tf_op jit(solution)/shard_map/reduce-window
  9.0 0.5 broadcast.170
  9.5 1.3 %reduce.3 = s32[1024]{0:T(1024)S(1)} reduce(s32[1,1024,1]{1,2,0:T(1,128)} %param.10, s32[]{:T(128)} %broadcast.170), dimensions={0,2}, to_apply=%param.10.reduce_sub_computation.3 | reduce | bytes 8196 | tf_op args[3]
  11.0 0.7 compare_select_fusion
  11.7 1.3 %pad_maximum_fusion.1 = f32[45,38,128]{2,1,0:T(8,128)S(1)} fusion(f32[45,3,128]{2,1,0:T(4,128)S(1)} %collective-permute-done.1, f32[15,32,128]{2,1,0:T(8,128)} %param.8, f32[30,32,128]{2,1,0:T(8,128)} %bitcast.94, f32[45,3,128]{2,1,0:T(4,128)S(1)} %collective-permute-done), kind=kLoop, calls=%fused_computation.81 | loop fusion | flops 656640 | bytes 1751040 | tf_op jit(solution)/shard_map/concatenate | solution.py:18
  13.3 0.4 copy.51
  13.7 0.4 copy.50
  14.2 3.0 %collective-permute-start.2 = (f32[45,38,6]{0,1,2:T(8,128)S(1)}, f32[45,38,6]{0,1,2:T(8,128)S(1)}, u32[]{:S(2)}, u32[]{:S(2)}) collective-permute-start(f32[45,38,6]{0,1,2:T(8,128)S(1)} %pad_maximum_fusion.14), channel_id=1, source_target_pairs={{0,4},{4,0},{1,5},{5,1},{2,6},{6,2},{3,7},{7,3},{8,12},{12,8},{9,1... | collective-permute-start | bytes 123128 | tf_op jit(solution)/shard_map/ppermute | solution.py:23
  17.2 3.6 %collective-permute-done.2 = f32[45,38,6]{0,1,2:T(8,128)S(1)} collective-permute-done((f32[45,38,6]{0,1,2:T(8,128)S(1)}, f32[45,38,6]{0,1,2:T(8,128)S(1)}, u32[]{:S(2)}, u32[]{:S(2)}) %collective-permute-start.2) | collective-permute-done | bytes 41072 | tf_op jit(solution)/shard_map/ppermute | solution.py:23
  20.8 0.5 copy.65
  21.3 0.5 copy.64
  21.7 1.0 %pad_maximum_fusion = f32[45,38,134]{2,1,0:T(8,128)S(1)} fusion(f32[45,38,3]{2,1,0:T(8,128)S(1)} %copy.65, f32[45,3,128]{2,1,0:T(4,128)S(1)} %collective-permute-done.1, f32[15,32,128]{2,1,0:T(8,128)S(1)} %copy-done.2, f32[30,32,128]{2,1,0:T(8,128)S(1)} %bitcast.95, f32[45,3,128]{2,1,0:T(4,128)S(1)} %collective-permute-done, f32[45,38,3]{2,1,0:T(8,128)S(1)} %copy.64), kind=kLoop, calls=%fused_computation.41 | loop fusion | flops 1145700 | bytes 1833120 | tf_op jit(solution)/shard_map/concatenate | solution.py:28
  22.8 0.7 fusion.83
  23.5 1.4 %fusion.46 = f32[2,15,36,132]{3,2,1,0:T(8,128)S(1)} fusion(f32[2,15,38,134]{3,2,1,0:T(8,128)S(1)} %bitcast.92, f32[15,36,132]{2,1,0:T(8,128)S(1)} %get-tuple-element.12, f32[15,36,132]{2,1,0:T(8,128)S(1)} %get-tuple-element.13, f32[15,36,132]{2,1,0:T(8,128)S(1)} %get-tuple-element.14, f32[15,36,132]{2,1,0:T(8,128)S(1)} %get-tuple-element.11, ...), kind=kLoop, calls=%fused_computation.58 | loop fusion | flops 1853280 | bytes 4561956 | tf_op jit(solution)/shard_map/jit(_where)/select_n | solution.py:52
  25.0 0.9 %fusion.79 = (f32[15,34,130]{2,1,0:T(8,128)S(1)}, f32[15,34,130]{2,1,0:T(8,128)S(1)}, f32[15,34,130]{2,1,0:T(8,128)S(1)}, f32[15,34,130]{2,1,0:T(8,128)S(1)}) fusion(f32[45,38,134]{2,1,0:T(8,128)S(1)} %pad_maximum_fusion, f32[45,38,3]{2,1,0:T(8,128)S(1)} %copy.65, f32[45,3,128]{2,1,0:T(4,128)S(1)} %collective-permute-done.1, ...), kind=kLoop, calls=%fused_computation.89 | loop fusion | flops 1060800 | bytes 2772960 | tf_op jit(solution)/shard_map/mul | solution.py:42
  25.8 1.4 %fusion.37 = f32[2,15,34,130]{3,2,1,0:T(8,128)S(1)} fusion(f32[2,15,36,132]{3,2,1,0:T(8,128)S(1)} %fusion.46, f32[15,34,130]{2,1,0:T(8,128)S(1)} %get-tuple-element.9, f32[15,34,130]{2,1,0:T(8,128)S(1)} %get-tuple-element.10, f32[15,34,130]{2,1,0:T(8,128)S(1)} %get-tuple-element.8, f32[15,34,130]{2,1,0:T(8,128)S(1)} %get-tuple-element.7, ...), kind=kLoop, calls=%fused_computation.45 | loop fusion | flops 1723800 | bytes 4243234 | tf_op jit(solution)/shard_map/jit(_where)/select_n | solution.py:52
  27.6 0.6 fusion.85
  28.9 3.4 %fusion.67 = bf16[1024,30]{0,1:T(8,128)(2,1)S(1)} fusion(s32[1024]{0:T(1024)S(1)} %bitcast.116, f32[30,4096]{1,0:T(8,128)S(1)} %bitcast.103), kind=kOutput, calls=%fused_computation.72 | convolution fusion | flops 256006144 | bytes 557056 | tf_op jit(solution)/shard_map/dot_general | solution.py:106
  32.5 3.5 %scatter_custom_fusion = bf16[30,2048]{0,1:T(8,128)(2,1)S(1)} fusion(s32[1024]{0:T(1024)S(1)} %bitcast.111, bf16[1024,30]{1,0:T(8,128)(2,1)S(1)} %copy.56, bf16[]{:T(256)} %constant.23.clone.1), kind=kCustom, calls=%fused_computation.111 | custom fusion | bytes 122882 | tf_op jit(solution)/shard_map/scatter | solution.py:124
  36.3 14.2 %all_to_all.10 = bf16[30,8,256]{2,0,1:T(8,128)(2,1)S(1)} all-to-all(bf16[30,8,256]{2,0,1:T(8,128)(2,1)S(1)} %copy.57), channel_id=1, replica_groups=mesh['lat'=4,'lon'=2,'lev'=4] {'lon','lev'}, dimensions={1} | all-to-all | bytes 245760 | tf_op jit(solution)/shard_map/all_to_all | solution.py:126
  50.8 3.7 %fusion.20 = bf16[1024,512]{0,1:T(8,128)(2,1)S(1)} fusion(bf16[1,2,1024,1024]{3,2,1,0:T(8,128)(2,1)} %param.12, bf16[120,512]{1,0:T(8,128)(2,1)S(1)} %bitcast.109, bf16[1,120,1024]{2,1,0:T(8,128)(2,1)S(1)} %copy-done), kind=kOutput, calls=%fused_computation.26 | convolution fusion | flops 1209008128 | bytes 3514368 | tf_op jit(solution)/shard_map/dot_general | solution.py:82
  54.6 3.5 %fusion.63 = bf16[120,512]{1,0:T(8,128)(2,1)S(1)} fusion(bf16[1024,512]{0,1:T(8,128)(2,1)S(1)} %fusion.20, bf16[1,2,1024,1024]{3,2,1,0:T(8,128)(2,1)} %param.12, bf16[1,1024,120]{1,2,0:T(8,128)(2,1)S(1)} %copy-done.3), kind=kOutput, calls=%fused_computation.70 | convolution fusion | flops 1204350976 | bytes 3514368 | tf_op jit(solution)/shard_map/dot_general | solution.py:86
  58.2 0.7 copy.61
  58.9 3.4 %all-to-all-start.1 = ((bf16[30,8,256]{2,0,1:T(8,128)(2,1)}), bf16[30,8,256]{2,0,1:T(8,128)(2,1)S(1)}, u32[]{:S(2)}, u32[]{:S(2)}) async-start(bf16[30,8,256]{2,0,1:T(8,128)(2,1)} %copy.61), calls=%async_computation.1 | async-start | bytes 262144 | tf_op jit(solution)/shard_map/all_to_all | solution.py:140
  62.3 7.4 %all-to-all-done.1 = bf16[30,8,256]{2,0,1:T(8,128)(2,1)S(1)} async-done(((bf16[30,8,256]{2,0,1:T(8,128)(2,1)}), bf16[30,8,256]{2,0,1:T(8,128)(2,1)S(1)}, u32[]{:S(2)}, u32[]{:S(2)}) %all-to-all-start.1) | async-done | bytes 122912 | tf_op jit(solution)/shard_map/all_to_all | solution.py:140
  70.0 3.2 %gather_fusion = bf16[1024,30]{1,0:T(8,128)(2,1)S(1)} fusion(bf16[30,2048]{0,1:T(8,128)(2,1)S(1)} %bitcast.99, s32[1024]{0:T(1024)S(1)} %broadcast_clamp_fusion), kind=kCustom, calls=%fused_computation | custom fusion | bytes 126976 | tf_op jit(solution)/shard_map/gather | solution.py:143
  73.2 3.3 %fusion.4 = f32[30,4096]{1,0:T(8,128)S(1)} fusion(f32[30,4096]{1,0:T(8,128)S(1)} %bitcast.104, bf16[1024,30]{1,0:T(8,128)(2,1)S(1)} %gather_fusion, s32[1024]{0:T(1024)S(1)} %bitcast.117), kind=kOutput, calls=%fused_computation.7 | convolution fusion | flops 255975424 | bytes 1048576 | tf_op jit(solution)/shard_map/dot_general | solution.py:144
  76.6 0.8 %slice.224 = f32[30,32,128]{2,1,0:T(8,128)} slice(f32[32,32,128]{2,1,0:T(8,128)S(1)} %bitcast.101), slice={[0:30], [0:32], [0:128]} | slice | bytes 983040
  (46 shorter events, 3.2 us)
Async XLA Ops:
  0.0 50.8 %copy-start = (bf16[1,120,1024]{2,1,0:T(8,128)(2,1)S(1)}, bf16[1,120,1024]{2,1,0:T(8,128)(2,1)}, u32[]{:S(2)}) copy-start(bf16[1,120,1024]{2,1,0:T(8,128)(2,1)} %param.11) | copy-start | bytes 737284
  1.1 10.6 %collective-permute-start.1 = (f32[45,3,128]{2,1,0:T(4,128)S(1)}, f32[45,3,128]{2,1,0:T(4,128)S(1)}, u32[]{:S(2)}, u32[]{:S(2)}) collective-permute-start(f32[45,3,128]{2,1,0:T(4,128)S(1)} %get-tuple-element.22), channel_id=1, source_target_pairs={{8,0},{16,8},{24,16},{9,1},{17,9},{25,17},{10,2},{18,10},{26,18},{... | collective-permute-start | bytes 207368 | tf_op jit(solution)/shard_map/ppermute | solution.py:15
  2.4 9.3 %collective-permute-start = (f32[45,3,128]{2,1,0:T(4,128)S(1)}, f32[45,3,128]{2,1,0:T(4,128)S(1)}, u32[]{:S(2)}, u32[]{:S(2)}) collective-permute-start(f32[45,3,128]{2,1,0:T(4,128)S(1)} %get-tuple-element.21), channel_id=1, source_target_pairs={{0,8},{8,16},{16,24},{1,9},{9,17},{17,25},{2,10},{10,18},{18,26},{... | collective-permute-start | bytes 207368 | tf_op jit(solution)/shard_map/ppermute | solution.py:12
  13.7 8.0 %copy-start.1 = (f32[2,15,32,128]{3,2,1,0:T(8,128)S(1)}, f32[2,15,32,128]{3,2,1,0:T(8,128)}, u32[]{:S(2)}) copy-start(f32[2,15,32,128]{3,2,1,0:T(8,128)} %param.7) | copy-start | bytes 1474564
  13.7 8.0 %copy-start.2 = (f32[15,32,128]{2,1,0:T(8,128)S(1)}, f32[15,32,128]{2,1,0:T(8,128)}, u32[]{:S(2)}) copy-start(f32[15,32,128]{2,1,0:T(8,128)} %param.8) | copy-start | bytes 737284
  14.2 6.6 %collective-permute-start.2 = (f32[45,38,6]{0,1,2:T(8,128)S(1)}, f32[45,38,6]{0,1,2:T(8,128)S(1)}, u32[]{:S(2)}, u32[]{:S(2)}) collective-permute-start(f32[45,38,6]{0,1,2:T(8,128)S(1)} %pad_maximum_fusion.14), channel_id=1, source_target_pairs={{0,4},{4,0},{1,5},{5,1},{2,6},{6,2},{3,7},{7,3},{8,12},{12,8},{9,1... | collective-permute-start | bytes 123128 | tf_op jit(solution)/shard_map/ppermute | solution.py:23
  28.2 0.7 copy-start.4
  50.8 3.8 %copy-start.3 = (bf16[1,1024,120]{1,2,0:T(8,128)(2,1)S(1)}, bf16[1,1024,120]{1,2,0:T(8,128)(2,1)}, u32[]{:S(2)}) copy-start(bf16[1,1024,120]{1,2,0:T(8,128)(2,1)} %param.13) | copy-start | bytes 737284
  58.9 10.8 %all-to-all-start.1 = ((bf16[30,8,256]{2,0,1:T(8,128)(2,1)}), bf16[30,8,256]{2,0,1:T(8,128)(2,1)S(1)}, u32[]{:S(2)}, u32[]{:S(2)}) async-start(bf16[30,8,256]{2,0,1:T(8,128)(2,1)} %copy.61), calls=%async_computation.1 | async-start | bytes 262144 | tf_op jit(solution)/shard_map/all_to_all | solution.py:140

commit v3 on v2

--- a/solution.py
+++ b/solution.py
@@ -111,18 +111,25 @@
     )
     picked = picked.astype(jnp.bfloat16)
     routes = owners[0, :, 0]
-    pieces = routes.reshape(lev_count, per_device)
-    onehot = (pieces[:, :, None] == jnp.arange(lon_count, dtype=jnp.int32)).astype(jnp.int32)
-    slot_rank = jnp.sum(jnp.cumsum(onehot, 1) * onehot, 2) - 1
-    piece_of = jnp.arange(lev_count, dtype=jnp.int32)[:, None]
-    slot_index = ((pieces * lev_count + piece_of) * capacity + slot_rank).reshape(cloudy)
     group = lon_count * lev_count
     local_features = 2 * level_rows
-    send_buffer = (
-        jnp.zeros((local_features, group * capacity), jnp.bfloat16)
-        .at[:, slot_index]
-        .set(picked)
-    ).reshape(local_features, group, capacity)
+    whole_slices = capacity == per_device
+    if whole_slices:
+        send_buffer = jnp.broadcast_to(
+            picked.reshape(local_features, 1, lev_count, per_device),
+            (local_features, lon_count, lev_count, per_device),
+        ).reshape(local_features, group, capacity)
+    else:
+        pieces = routes.reshape(lev_count, per_device)
+        onehot = (pieces[:, :, None] == jnp.arange(lon_count, dtype=jnp.int32)).astype(jnp.int32)
+        slot_rank = jnp.sum(jnp.cumsum(onehot, 1) * onehot, 2) - 1
+        piece_of = jnp.arange(lev_count, dtype=jnp.int32)[:, None]
+        slot_index = ((pieces * lev_count + piece_of) * capacity + slot_rank).reshape(cloudy)
+        send_buffer = (
+            jnp.zeros((local_features, group * capacity), jnp.bfloat16)
+            .at[:, slot_index]
+            .set(picked)
+        ).reshape(local_features, group, capacity)
     received = lax.all_to_all(
         send_buffer, ("lon", "lev"), split_axis=1, concat_axis=1, tiled=True
     )
@@ -139,8 +146,14 @@
     )
     returned = lax.all_to_all(
         outgoing, ("lon", "lev"), split_axis=1, concat_axis=1, tiled=True
-    ).reshape(local_features, group * capacity)
-    tendency = returned[:, slot_index]
+    )
+    if whole_slices:
+        returned = returned.reshape(local_features, lon_count, cloudy)
+        tendency = returned[:, 0]
+        for regime in range(1, lon_count):
+            tendency = jnp.where(routes[None, :] == regime, returned[:, regime], tendency)
+    else:
+        tendency = returned.reshape(local_features, group * capacity)[:, slot_index]
     spread = jnp.dot(
         tendency, picker, preferred_element_type=jnp.float32
     )

time: 77.9 us -> 65.3 us (0.84)
  local copies, waits for them, and re-layouts: 13.1 us -> 5.19 us
  other arithmetic: 14 us -> 8.77 us
    scatter x1 -> x0, local copies, waits for them, and re-layouts: 3.51 us -> none  [on_device(): send_buffer = jnp.zeros((local_features, group * capacity), jnp.bfloat16)...]
    gather x1 -> x0, local copies, waits for them, and re-layouts: 3.2 us -> none  [on_device(): tendency = returned[:, slot_index]]
    another operation x3 -> x0, other arithmetic: 2.52 us -> none
    unnamed x2 -> x0, other arithmetic: 1.35 us -> none
    ppermute x1, waiting for transfers between devices: 0.01 us -> 0.88 us  [halo_exchange(): lax.ppermute(cells[..., cells.shape[-2] - width:, :], 'lat', [(i, i + 1)...]
    unnamed x21 -> x19, local copies, waits for them, and re-layouts: 3.07 us -> 2.53 us
  transfers between devices with their start and end apart: 4 -> 4, of which waited for: 2 -> 3; matrix products, arithmetic and copies ran while one was open for 8% -> 0% of each run, Pallas kernels for 0% -> 0%
where the time goes in v3:
time: 65.3 us; the launch traced here: 64.7 us
  blocking collectives  14.5 us (22%)
  matrix products  14 us (21%)
  waiting for transfers between devices  11.3 us (17%)
  starting transfers between devices  10.7 us (16%)
  other arithmetic  8.77 us (13%)
  local copies, waits for them, and re-layouts  5.19 us (8%)
    all_to_all x1, blocking collectives, on_device(): lax.all_to_all(send_buffer, ('lon', 'lev'), split_axis=1, concat_axis=1,...  14.5 us
    all_to_all x1, waiting for transfers between devices, on_device(): lax.all_to_all(outgoing, ('lon', 'lev'), split_axis=1, concat_axis=1, til...  7.42 us
    dot_general x1, matrix products, network(): lax.dot_general(w_middle[layer_no], hidden, contract, preferred_element_t...  3.73 us
    dot_general x1, matrix products, network(): lax.dot_general(w_last, hidden, contract, preferred_element_type=jnp.floa...  3.45 us
    dot_general x1, matrix products, on_device(): lax.dot_general(flat_values.astype(jnp.bfloat16), picker, (((1,), (1,)),...  3.41 us
    dot_general x1, matrix products, on_device(): spread = jnp.dot(tendency, picker, preferred_element_type=jnp.float32)  3.39 us
    all_to_all x1, starting transfers between devices, on_device(): lax.all_to_all(outgoing, ('lon', 'lev'), split_axis=1, concat_axis=1, til...  3.37 us
    ppermute x1, starting transfers between devices, halo_exchange(): lax.ppermute(cells[..., cells.shape[-2] - width:, :], 'lat', [(i, i + 1)...  3.04 us
  transfers between devices with their start and end apart: 4, of which 3 were waited for; matrix products, arithmetic and copies ran while one was open for 0% of the time, Pallas kernels for 0%

profile of v3, /device:TPU:0, one launch (start us, length us, event | category | flops | bytes accessed | tf_op | source)
XLA Modules:
  0.0 64.7 jit_solution(6390719495106276549)
XLA Ops:
  0.0 1.1 %pad_maximum_fusion.16 = (f32[45,3,128]{2,1,0:T(4,128)S(1)}, f32[45,3,128]{2,1,0:T(4,128)S(1)}) fusion(f32[15,32,128]{2,1,0:T(8,128)} %param.8, f32[30,32,128]{2,1,0:T(8,128)} %bitcast.73), kind=kLoop, calls=%fused_computation.134 | loop fusion | flops 34560 | bytes 875520 | tf_op jit(solution)/shard_map/slice | solution.py:13
  1.1 1.3 %collective-permute-start.1 = (f32[45,3,128]{2,1,0:T(4,128)S(1)}, f32[45,3,128]{2,1,0:T(4,128)S(1)}, u32[]{:S(2)}, u32[]{:S(2)}) collective-permute-start(f32[45,3,128]{2,1,0:T(4,128)S(1)} %get-tuple-element.22), channel_id=1, source_target_pairs={{8,0},{16,8},{24,16},{9,1},{17,9},{25,17},{10,2},{18,10},{26,18},{... | collective-permute-start | bytes 207368 | tf_op jit(solution)/shard_map/ppermute | solution.py:15
  2.4 3.0 %collective-permute-start = (f32[45,3,128]{2,1,0:T(4,128)S(1)}, f32[45,3,128]{2,1,0:T(4,128)S(1)}, u32[]{:S(2)}, u32[]{:S(2)}) collective-permute-start(f32[45,3,128]{2,1,0:T(4,128)S(1)} %get-tuple-element.21), channel_id=1, source_target_pairs={{0,8},{8,16},{16,24},{1,9},{9,17},{17,25},{2,10},{10,18},{18,26},{... | collective-permute-start | bytes 207368 | tf_op jit(solution)/shard_map/ppermute | solution.py:12
  5.5 0.9 %collective-permute-done = f32[45,3,128]{2,1,0:T(4,128)S(1)} collective-permute-done((f32[45,3,128]{2,1,0:T(4,128)S(1)}, f32[45,3,128]{2,1,0:T(4,128)S(1)}, u32[]{:S(2)}, u32[]{:S(2)}) %collective-permute-start) | collective-permute-done | bytes 69152 | tf_op jit(solution)/shard_map/ppermute | solution.py:12
  6.4 1.3 %pad_maximum_fusion.1 = f32[45,38,128]{2,1,0:T(8,128)S(1)} fusion(f32[45,3,128]{2,1,0:T(4,128)S(1)} %collective-permute-done.1, f32[15,32,128]{2,1,0:T(8,128)} %param.8, f32[30,32,128]{2,1,0:T(8,128)} %bitcast.74, f32[45,3,128]{2,1,0:T(4,128)S(1)} %collective-permute-done), kind=kLoop, calls=%fused_computation.78 | loop fusion | flops 656640 | bytes 1751040 | tf_op jit(solution)/shard_map/concatenate | solution.py:18
  7.6 0.3 fusion.115
  7.9 0.4 copy.44
  8.4 0.4 copy.43
  8.9 3.0 %collective-permute-start.2 = (f32[45,38,6]{0,1,2:T(8,128)S(1)}, f32[45,38,6]{0,1,2:T(8,128)S(1)}, u32[]{:S(2)}, u32[]{:S(2)}) collective-permute-start(f32[45,38,6]{0,1,2:T(8,128)S(1)} %pad_maximum_fusion.14), channel_id=1, source_target_pairs={{0,4},{4,0},{1,5},{5,1},{2,6},{6,2},{3,7},{7,3},{8,12},{12,8},{9,1... | collective-permute-start | bytes 123128 | tf_op jit(solution)/shard_map/ppermute | solution.py:23
  11.9 3.0 %collective-permute-done.2 = f32[45,38,6]{0,1,2:T(8,128)S(1)} collective-permute-done((f32[45,38,6]{0,1,2:T(8,128)S(1)}, f32[45,38,6]{0,1,2:T(8,128)S(1)}, u32[]{:S(2)}, u32[]{:S(2)}) %collective-permute-start.2) | collective-permute-done | bytes 41072 | tf_op jit(solution)/shard_map/ppermute | solution.py:23
  14.9 0.5 copy.57
  15.3 0.5 copy.56
  15.8 1.0 %pad_maximum_fusion = f32[45,38,134]{2,1,0:T(8,128)S(1)} fusion(f32[45,38,3]{2,1,0:T(8,128)S(1)} %copy.57, f32[45,3,128]{2,1,0:T(4,128)S(1)} %collective-permute-done.1, f32[15,32,128]{2,1,0:T(8,128)S(1)} %copy-done.2, f32[30,32,128]{2,1,0:T(8,128)S(1)} %bitcast.75, f32[45,3,128]{2,1,0:T(4,128)S(1)} %collective-permute-done, f32[45,38,3]{2,1,0:T(8,128)S(1)} %copy.56), kind=kLoop, calls=%fused_computation.39 | loop fusion | flops 1145700 | bytes 1833120 | tf_op jit(solution)/shard_map/concatenate | solution.py:28
  16.9 0.7 %fusion.82 = (f32[15,36,132]{2,1,0:T(8,128)S(1)}, f32[15,36,132]{2,1,0:T(8,128)S(1)}, f32[15,36,132]{2,1,0:T(8,128)S(1)}, f32[15,36,132]{2,1,0:T(8,128)S(1)}) fusion(f32[45,38,134]{2,1,0:T(8,128)S(1)} %pad_maximum_fusion), kind=kLoop, calls=%fused_computation.94 | loop fusion | flops 570240 | bytes 2566080 | tf_op jit(solution)/shard_map/mul | solution.py:42
  17.6 1.4 %fusion.46 = f32[2,15,36,132]{3,2,1,0:T(8,128)S(1)} fusion(f32[2,15,38,134]{3,2,1,0:T(8,128)S(1)} %bitcast.72, f32[15,36,132]{2,1,0:T(8,128)S(1)} %get-tuple-element.12, f32[15,36,132]{2,1,0:T(8,128)S(1)} %get-tuple-element.13, f32[15,36,132]{2,1,0:T(8,128)S(1)} %get-tuple-element.14, f32[15,36,132]{2,1,0:T(8,128)S(1)} %get-tuple-element.11, ...), kind=kLoop, calls=%fused_computation.56 | loop fusion | flops 1853280 | bytes 4561956 | tf_op jit(solution)/shard_map/jit(_where)/select_n | solution.py:52
  19.0 0.9 %fusion.78 = (f32[15,34,130]{2,1,0:T(8,128)S(1)}, f32[15,34,130]{2,1,0:T(8,128)S(1)}, f32[15,34,130]{2,1,0:T(8,128)S(1)}, f32[15,34,130]{2,1,0:T(8,128)S(1)}) fusion(f32[45,38,134]{2,1,0:T(8,128)S(1)} %pad_maximum_fusion, f32[45,38,3]{2,1,0:T(8,128)S(1)} %copy.57, f32[45,3,128]{2,1,0:T(4,128)S(1)} %collective-permute-done.1, ...), kind=kLoop, calls=%fused_computation.86 | loop fusion | flops 1060800 | bytes 2772960 | tf_op jit(solution)/shard_map/mul | solution.py:42
  19.9 1.4 %fusion.37 = f32[2,15,34,130]{3,2,1,0:T(8,128)S(1)} fusion(f32[2,15,36,132]{3,2,1,0:T(8,128)S(1)} %fusion.46, f32[15,34,130]{2,1,0:T(8,128)S(1)} %get-tuple-element.9, f32[15,34,130]{2,1,0:T(8,128)S(1)} %get-tuple-element.10, f32[15,34,130]{2,1,0:T(8,128)S(1)} %get-tuple-element.8, f32[15,34,130]{2,1,0:T(8,128)S(1)} %get-tuple-element.7, ...), kind=kLoop, calls=%fused_computation.43 | loop fusion | flops 1723800 | bytes 4243234 | tf_op jit(solution)/shard_map/jit(_where)/select_n | solution.py:52
  21.3 0.4 fusion.95
  21.7 0.6 fusion.84
  22.3 0.3 copy.58
  22.7 0.3 copy-done.5
  23.0 3.4 %fusion.66 = bf16[30,1024]{1,0:T(8,128)(2,1)S(1)} fusion(s32[1024]{0:T(1024)S(1)} %bitcast.89, f32[30,4096]{1,0:T(8,128)S(1)} %bitcast.81), kind=kOutput, calls=%fused_computation.69 | convolution fusion | flops 256006144 | bytes 557056 | tf_op jit(solution)/shard_map/dot_general | solution.py:106
  26.5 14.5 %all_to_all.10 = bf16[30,8,256]{2,0,1:T(8,128)(2,1)S(1)} all-to-all(bf16[30,8,256]{2,0,1:T(8,128)(2,1)S(1)} %bitcast.84), channel_id=1, replica_groups=mesh['lat'=4,'lon'=2,'lev'=4] {'lon','lev'}, dimensions={1} | all-to-all | bytes 245760 | tf_op jit(solution)/shard_map/all_to_all | solution.py:133
  41.0 0.1 copy.71
  41.2 3.7 %fusion.20 = bf16[1024,512]{0,1:T(8,128)(2,1)S(1)} fusion(bf16[1,2,1024,1024]{3,2,1,0:T(8,128)(2,1)} %param.12, bf16[120,512]{1,0:T(8,128)(2,1)S(1)} %bitcast.88, bf16[1,120,1024]{2,1,0:T(8,128)(2,1)S(1)} %copy-done), kind=kOutput, calls=%fused_computation.24 | convolution fusion | flops 1209008128 | bytes 3514368 | tf_op jit(solution)/shard_map/dot_general | solution.py:82
  45.0 3.5 %fusion.63 = bf16[120,512]{1,0:T(8,128)(2,1)S(1)} fusion(bf16[1024,512]{0,1:T(8,128)(2,1)S(1)} %fusion.20, bf16[1,2,1024,1024]{3,2,1,0:T(8,128)(2,1)} %param.12, bf16[1,1024,120]{1,2,0:T(8,128)(2,1)S(1)} %copy-done.4), kind=kOutput, calls=%fused_computation.68 | convolution fusion | flops 1204350976 | bytes 3514368 | tf_op jit(solution)/shard_map/dot_general | solution.py:86
  48.6 0.7 %copy.51 = bf16[30,8,256]{2,0,1:T(8,128)(2,1)} copy(bf16[30,8,256]{2,1,0:T(8,128)(2,1)S(1)} %reshape.65) | data formatting | bytes 245760 | tf_op jit(solution)/shard_map/reshape | solution.py:145
  49.3 3.4 %all-to-all-start.1 = ((bf16[30,8,256]{2,0,1:T(8,128)(2,1)}), bf16[30,8,256]{2,0,1:T(8,128)(2,1)S(1)}, u32[]{:S(2)}, u32[]{:S(2)}) async-start(bf16[30,8,256]{2,0,1:T(8,128)(2,1)} %copy.51), calls=%async_computation.1 | async-start | bytes 262144 | tf_op jit(solution)/shard_map/all_to_all | solution.py:147
  52.7 7.4 %all-to-all-done.1 = bf16[30,8,256]{2,0,1:T(8,128)(2,1)S(1)} async-done(((bf16[30,8,256]{2,0,1:T(8,128)(2,1)}), bf16[30,8,256]{2,0,1:T(8,128)(2,1)S(1)}, u32[]{:S(2)}, u32[]{:S(2)}) %all-to-all-start.1) | async-done | bytes 122912 | tf_op jit(solution)/shard_map/all_to_all | solution.py:147
  60.3 0.2 fusion.116
  60.4 3.4 %fusion.4 = f32[30,4096]{1,0:T(8,128)S(1)} fusion(f32[30,4096]{1,0:T(8,128)S(1)} %bitcast.82, s32[1024]{0:T(1024)S(1)} %bitcast.90, bf16[30,1,1024]{2,1,0:T(2,128)(2,1)S(1)} %get-tuple-element.24, bf16[30,1,1024]{2,1,0:T(2,128)(2,1)S(1)} %get-tuple-element.23, pred[1024]{0:T(1024)(128)(4,1)S(1)} %compare_reduce_fusion), kind=kOutput, calls=%fused_computation.5 | convolution fusion | flops 256006144 | bytes 1111040 | tf_op jit(solution)/shard_map/dot_general | solution.py:157
  63.9 0.8 %slice.222 = f32[30,32,128]{2,1,0:T(8,128)} slice(f32[32,32,128]{2,1,0:T(8,128)S(1)} %bitcast.79), slice={[0:30], [0:32], [0:128]} | slice | bytes 983040
  (31 shorter events, 0.8 us)
Async XLA Ops:
  0.0 41.2 %copy-start = (bf16[1,120,1024]{2,1,0:T(8,128)(2,1)S(1)}, bf16[1,120,1024]{2,1,0:T(8,128)(2,1)}, u32[]{:S(2)}) copy-start(bf16[1,120,1024]{2,1,0:T(8,128)(2,1)} %param.11) | copy-start | bytes 737284
  1.1 4.4 %collective-permute-start.1 = (f32[45,3,128]{2,1,0:T(4,128)S(1)}, f32[45,3,128]{2,1,0:T(4,128)S(1)}, u32[]{:S(2)}, u32[]{:S(2)}) collective-permute-start(f32[45,3,128]{2,1,0:T(4,128)S(1)} %get-tuple-element.22), channel_id=1, source_target_pairs={{8,0},{16,8},{24,16},{9,1},{17,9},{25,17},{10,2},{18,10},{26,18},{... | collective-permute-start | bytes 207368 | tf_op jit(solution)/shard_map/ppermute | solution.py:15
  2.4 4.0 %collective-permute-start = (f32[45,3,128]{2,1,0:T(4,128)S(1)}, f32[45,3,128]{2,1,0:T(4,128)S(1)}, u32[]{:S(2)}, u32[]{:S(2)}) collective-permute-start(f32[45,3,128]{2,1,0:T(4,128)S(1)} %get-tuple-element.21), channel_id=1, source_target_pairs={{0,8},{8,16},{16,24},{1,9},{9,17},{17,25},{2,10},{10,18},{18,26},{... | collective-permute-start | bytes 207368 | tf_op jit(solution)/shard_map/ppermute | solution.py:12
  8.4 7.4 %copy-start.1 = (f32[2,15,32,128]{3,2,1,0:T(8,128)S(1)}, f32[2,15,32,128]{3,2,1,0:T(8,128)}, u32[]{:S(2)}) copy-start(f32[2,15,32,128]{3,2,1,0:T(8,128)} %param.7) | copy-start | bytes 1474564
  8.4 7.4 %copy-start.2 = (f32[15,32,128]{2,1,0:T(8,128)S(1)}, f32[15,32,128]{2,1,0:T(8,128)}, u32[]{:S(2)}) copy-start(f32[15,32,128]{2,1,0:T(8,128)} %param.8) | copy-start | bytes 737284
  8.9 6.0 %collective-permute-start.2 = (f32[45,38,6]{0,1,2:T(8,128)S(1)}, f32[45,38,6]{0,1,2:T(8,128)S(1)}, u32[]{:S(2)}, u32[]{:S(2)}) collective-permute-start(f32[45,38,6]{0,1,2:T(8,128)S(1)} %pad_maximum_fusion.14), channel_id=1, source_target_pairs={{0,4},{4,0},{1,5},{5,1},{2,6},{6,2},{3,7},{7,3},{8,12},{12,8},{9,1... | collective-permute-start | bytes 123128 | tf_op jit(solution)/shard_map/ppermute | solution.py:23
  22.3 0.7 %copy-start.5 = (s32[1,1024]{1,0:T(1,128)S(1)}, s32[1,1024]{1,0:T(1,128)}, u32[]{:S(2)}) copy-start(s32[1,1024]{1,0:T(1,128)} %param.9) | copy-start | bytes 12292
  41.2 3.7 %copy-start.4 = (bf16[1,1024,120]{1,2,0:T(8,128)(2,1)S(1)}, bf16[1,1024,120]{1,2,0:T(8,128)(2,1)}, u32[]{:S(2)}) copy-start(bf16[1,1024,120]{1,2,0:T(8,128)(2,1)} %param.13) | copy-start | bytes 737284
  45.0 7.7 %copy-start.3 = (s32[1,1024,1]{1,2,0:T(1,128)S(1)}, s32[1,1024,1]{1,2,0:T(1,128)}, u32[]{:S(2)}) copy-start(s32[1,1024,1]{1,2,0:T(1,128)} %param.10) | copy-start | bytes 12292
  49.3 10.8 %all-to-all-start.1 = ((bf16[30,8,256]{2,0,1:T(8,128)(2,1)}), bf16[30,8,256]{2,0,1:T(8,128)(2,1)S(1)}, u32[]{:S(2)}, u32[]{:S(2)}) async-start(bf16[30,8,256]{2,0,1:T(8,128)(2,1)} %copy.51), calls=%async_computation.1 | async-start | bytes 262144 | tf_op jit(solution)/shard_map/all_to_all | solution.py:147

commit v4 on v3

--- a/solution.py
+++ b/solution.py
@@ -8,24 +8,55 @@
 
 
 def halo_exchange(cells, width):
-    lat_count = lax.axis_size("lat")
-    from_above = lax.ppermute(
-        cells[..., cells.shape[-2] - width :, :], "lat", [(i, i + 1) for i in range(lat_count - 1)]
-    )
-    from_below = lax.ppermute(
-        cells[..., :width, :], "lat", [(i + 1, i) for i in range(lat_count - 1)]
-    )
-    cells = jnp.concatenate([from_above, cells, from_below], axis=-2)
-    lon_count = lax.axis_size("lon")
-    left = cells[..., :width]
-    right = cells[..., cells.shape[-1] - width :]
+    lat_count, lon_count = lax.axis_size("lat"), lax.axis_size("lon")
+    rows, cols = cells.shape[-2], cells.shape[-1]
+    top, bottom = cells[..., :width, :], cells[..., rows - width :, :]
+
+    def lat_shift(piece, step):
+        pairs = [(i, i + step) for i in range(lat_count) if 0 <= i + step < lat_count]
+        return lax.ppermute(piece, "lat", pairs)
+
+    def lon_shift(piece, step):
+        pairs = [(j, (j + step) % lon_count) for j in range(lon_count)]
+        return lax.ppermute(piece, "lon", pairs)
+
+    def diagonal_shift(piece, lat_step, lon_step):
+        pairs = [
+            (i * lon_count + j, (i + lat_step) * lon_count + (j + lon_step) % lon_count)
+            for i in range(lat_count)
+            for j in range(lon_count)
+            if 0 <= i + lat_step < lat_count
+        ]
+        return lax.ppermute(piece, ("lat", "lon"), pairs)
+
+    def left_right(piece):
+        return piece[..., :width], piece[..., cols - width :]
+
+    north, south = lat_shift(bottom, 1), lat_shift(top, -1)
+    left, right = left_right(cells)
+    bottom_left, bottom_right = left_right(bottom)
+    top_left, top_right = left_right(top)
     if lon_count == 2:
-        both = lax.ppermute(jnp.concatenate([right, left], axis=-1), "lon", [(0, 1), (1, 0)])
-        from_left, from_right = both[..., :width], both[..., width:]
+        west_east = lon_shift(jnp.concatenate([right, left], axis=-1), 1)
+        west, east = west_east[..., :width], west_east[..., width:]
+        upper = diagonal_shift(jnp.concatenate([bottom_right, bottom_left], axis=-1), 1, 1)
+        north_west, north_east = upper[..., :width], upper[..., width:]
+        lower = diagonal_shift(jnp.concatenate([top_right, top_left], axis=-1), -1, 1)
+        south_west, south_east = lower[..., :width], lower[..., width:]
     else:
-        from_left = lax.ppermute(right, "lon", [(i, (i + 1) % lon_count) for i in range(lon_count)])
-        from_right = lax.ppermute(left, "lon", [((i + 1) % lon_count, i) for i in range(lon_count)])
-    return jnp.concatenate([from_left, cells, from_right], axis=-1)
+        west, east = lon_shift(right, 1), lon_shift(left, -1)
+        north_west = diagonal_shift(bottom_right, 1, 1)
+        north_east = diagonal_shift(bottom_left, 1, -1)
+        south_west = diagonal_shift(top_right, -1, 1)
+        south_east = diagonal_shift(top_left, -1, -1)
+    return jnp.concatenate(
+        [
+            jnp.concatenate([north_west, north, north_east], axis=-1),
+            jnp.concatenate([west, cells, east], axis=-1),
+            jnp.concatenate([south_west, south, south_east], axis=-1),
+        ],
+        axis=-2,
+    )
 
 
 def substep(values, coefficients):

time: 65.3 us -> 68.7 us (1.052)
  starting transfers between devices: 10.7 us -> 17.4 us
  waiting for transfers between devices: 11.3 us -> 7.43 us
  blocking collectives: 14.5 us -> 12.3 us
  other arithmetic: 8.77 us -> 10.8 us
    ppermute x3 -> x5, starting transfers between devices: 7.36 us -> 14 us  [the longest x2 5.9 us: diagonal_shift(): return lax.ppermute(piece, ('lat', 'lon'), pairs)]
    ppermute x3 -> x5, waiting for transfers between devices: 3.84 us -> 0.01 us  [the longest x2 0.01 us: diagonal_shift(): return lax.ppermute(piece, ('lat', 'lon'), pairs)]
    concatenate x3 -> x7, other arithmetic: 2.29 us -> 4.65 us  [the longest x3 2.67 us: dynamics(): jnp.concatenate([fields.reshape(kinds * level_rows, lat_rows, lon_cols),...]
    all_to_all x1, blocking collectives: 14.5 us -> 12.3 us  [on_device(): lax.all_to_all(send_buffer, ('lon', 'lev'), split_axis=1, concat_axis=1,...]
    slice x1 -> x0, other arithmetic: 1.1 us -> none  [halo_exchange(): cells[..., cells.shape[-2] - width:, :]]
    mul x3 -> x5, other arithmetic: 1.93 us -> 2.74 us  [substep(): face_coef = 0.5 * (middle + coefficients[:, lat_cut, lon_cut])]
  transfers between devices with their start and end apart: 4 -> 6, of which waited for: 3 -> 1; matrix products, arithmetic and copies ran while one was open for 0% -> 6% of each run, Pallas kernels for 0% -> 0%
where the time goes in v4:
time: 68.7 us; the launch traced here: 68.3 us
  starting transfers between devices  17.4 us (25%)
  matrix products  14.1 us (21%)
  blocking collectives  12.3 us (18%)
  other arithmetic  10.8 us (16%)
  waiting for transfers between devices  7.43 us (11%)
  local copies, waits for them, and re-layouts  5.78 us (8%)
    all_to_all x1, blocking collectives, on_device(): lax.all_to_all(send_buffer, ('lon', 'lev'), split_axis=1, concat_axis=1,...  12.3 us
    all_to_all x1, waiting for transfers between devices, on_device(): lax.all_to_all(outgoing, ('lon', 'lev'), split_axis=1, concat_axis=1, til...  7.42 us
    ppermute x2, starting transfers between devices, diagonal_shift(): return lax.ppermute(piece, ('lat', 'lon'), pairs)  5.9 us
    ppermute x2, starting transfers between devices, lat_shift(): return lax.ppermute(piece, 'lat', pairs)  5.05 us
    dot_general x1, matrix products, network(): lax.dot_general(w_middle[layer_no], hidden, contract, preferred_element_t...  3.73 us
    dot_general x1, matrix products, on_device(): lax.dot_general(flat_values.astype(jnp.bfloat16), picker, (((1,), (1,)),...  3.59 us
    dot_general x1, matrix products, network(): lax.dot_general(w_last, hidden, contract, preferred_element_type=jnp.floa...  3.44 us
    dot_general x1, matrix products, on_device(): spread = jnp.dot(tendency, picker, preferred_element_type=jnp.float32)  3.39 us
  transfers between devices with their start and end apart: 6, of which 1 were waited for; matrix products, arithmetic and copies ran while one was open for 6% of the time, Pallas kernels for 0%

profile of v4, /device:TPU:0, one launch (start us, length us, event | category | flops | bytes accessed | tf_op | source)
XLA Modules:
  0.0 68.3 jit_solution(11806023475652009907)
XLA Ops:
  0.0 1.4 %fusion.108 = (f32[45,3,3]{2,1,0:T(4,128)S(1)}, f32[45,3,3]{2,1,0:T(4,128)S(1)}, f32[45,3,3]{2,1,0:T(4,128)S(1)}, f32[45,3,3]{2,1,0:T(4,128)S(1)}) fusion(f32[30,32,128]{2,1,0:T(8,128)} %bitcast.73, f32[15,32,128]{2,1,0:T(8,128)} %param.8), kind=kLoop, calls=%fused_computation.153 | loop fusion | flops 1620 | bytes 743760 | tf_op jit(solution)/shard_map/concatenate | solution.py:88
  1.4 0.8 %pad_maximum_fusion.17 = f32[45,3,6]{2,1,0:T(4,128)} fusion(f32[45,3,3]{2,1,0:T(4,128)S(1)} %get-tuple-element.20, f32[45,3,3]{2,1,0:T(4,128)S(1)} %get-tuple-element.19), kind=kLoop, calls=%fused_computation.159 | loop fusion | flops 810 | bytes 6480 | tf_op jit(solution)/shard_map/concatenate | solution.py:44
  2.2 1.3 %collective-permute-start.3 = (f32[45,3,6]{2,1,0:T(4,128)}, f32[45,3,6]{2,1,0:T(4,128)S(1)}, u32[]{:S(2)}, u32[]{:S(2)}) collective-permute-start(f32[45,3,6]{2,1,0:T(4,128)} %pad_maximum_fusion.17), channel_id=1, source_target_pairs={{8,4},{12,0},{16,12},{20,8},{24,20},{28,16},{9,5},{13,1},{17,13},{... | collective-permute-start | bytes 9728 | tf_op jit(solution)/shard_map/ppermute | solution.py:30
  3.4 1.0 %fusion.110 = (f32[45,3,128]{2,1,0:T(4,128)S(1)}, f32[45,3,128]{2,1,0:T(4,128)S(1)}) fusion(f32[30,32,128]{2,1,0:T(8,128)} %bitcast.74, f32[15,32,128]{2,1,0:T(8,128)} %param.8), kind=kLoop, calls=%fused_computation.155 | loop fusion | flops 34560 | bytes 875520 | tf_op jit(solution)/shard_map/concatenate | solution.py:88
  4.5 1.3 %collective-permute-start.4 = (f32[45,3,128]{2,1,0:T(4,128)S(1)}, f32[45,3,128]{2,1,0:T(4,128)S(1)}, u32[]{:S(2)}, u32[]{:S(2)}) collective-permute-start(f32[45,3,128]{2,1,0:T(4,128)S(1)} %get-tuple-element.16), channel_id=1, source_target_pairs={{8,0},{16,8},{24,16},{9,1},{17,9},{25,17},{10,2},{18,10},{26,18},{... | collective-permute-start | bytes 207368 | tf_op jit(solution)/shard_map/ppermute | solution.py:17
  5.8 0.3 fusion.75
  6.1 0.5 copy.100
  6.6 0.5 copy.99
  7.1 3.0 %collective-permute-start.2 = (f32[45,32,6]{0,1,2:T(8,128)S(1)}, f32[45,32,6]{0,1,2:T(8,128)S(1)}, u32[]{:S(2)}, u32[]{:S(2)}) collective-permute-start(f32[45,32,6]{0,1,2:T(8,128)S(1)} %pad_maximum_fusion.14), channel_id=1, source_target_pairs={{0,4},{4,0},{1,5},{5,1},{2,6},{6,2},{3,7},{7,3},{8,12},{12,8},{9,1... | collective-permute-start | bytes 103688 | tf_op jit(solution)/shard_map/ppermute | solution.py:21
  10.3 4.6 %collective-permute-start = (f32[45,3,6]{2,1,0:T(4,128)S(1)}, f32[45,3,6]{2,1,0:T(4,128)S(1)}, u32[]{:S(2)}, u32[]{:S(2)}) collective-permute-start(f32[45,3,6]{2,1,0:T(4,128)S(1)} %pad_maximum_fusion.16), channel_id=1, source_target_pairs={{0,12},{4,8},{8,20},{12,16},{16,28},{20,24},{1,13},{5,9},{9,21},{1... | collective-permute-start | bytes 9728 | tf_op jit(solution)/shard_map/ppermute | solution.py:30
  14.9 3.8 %collective-permute-start.1 = (f32[45,3,128]{2,1,0:T(4,128)S(1)}, f32[45,3,128]{2,1,0:T(4,128)S(1)}, u32[]{:S(2)}, u32[]{:S(2)}) collective-permute-start(f32[45,3,128]{2,1,0:T(4,128)S(1)} %get-tuple-element.15), channel_id=1, source_target_pairs={{0,8},{8,16},{16,24},{1,9},{9,17},{17,25},{2,10},{10,18},{18,26},{... | collective-permute-start | bytes 207368 | tf_op jit(solution)/shard_map/ppermute | solution.py:17
  19.0 0.7 %copy.112 = f32[45,32,3]{2,1,0:T(8,128)S(1)} copy(f32[45,32,3]{0,1,2:T(8,128)S(1)} %get-tuple-element.25) | data formatting | bytes 34560
  19.9 0.7 %copy.113 = f32[45,32,3]{2,1,0:T(8,128)S(1)} copy(f32[45,32,3]{0,1,2:T(8,128)S(1)} %get-tuple-element.26) | data formatting | bytes 34560
  20.7 1.1 %maximum_maximum_fusion = f32[45,38,134]{2,1,0:T(8,128)S(1)} fusion(f32[45,3,3]{2,1,0:T(4,128)S(1)} %get-tuple-element.30, f32[45,3,128]{2,1,0:T(4,128)S(1)} %collective-permute-done.4, f32[45,3,3]{2,1,0:T(4,128)S(1)} %get-tuple-element.29, f32[45,32,3]{2,1,0:T(8,128)S(1)} %copy.113, f32[15,32,128]{2,1,0:T(8,128)S(1)} %copy-done.2, ...), kind=kLoop, calls=%fused_computation.46 | loop fusion | flops 2062260 | bytes 1833120 | tf_op jit(solution)/shard_map/concatenate | solution.py:52
  21.8 0.7 %fusion.84 = (f32[15,36,132]{2,1,0:T(8,128)S(1)}, f32[15,36,132]{2,1,0:T(8,128)S(1)}, f32[15,36,132]{2,1,0:T(8,128)S(1)}, f32[15,36,132]{2,1,0:T(8,128)S(1)}) fusion(f32[45,38,134]{2,1,0:T(8,128)S(1)} %maximum_maximum_fusion), kind=kLoop, calls=%fused_computation.109 | loop fusion | flops 570240 | bytes 2566080 | tf_op jit(solution)/shard_map/mul | solution.py:73
  22.6 0.4 fusion.78
  22.9 1.4 %fusion.46 = f32[2,15,36,132]{3,2,1,0:T(8,128)S(1)} fusion(f32[2,15,38,134]{3,2,1,0:T(8,128)S(1)} %bitcast.72, f32[15,36,132]{2,1,0:T(8,128)S(1)} %get-tuple-element.11, f32[15,36,132]{2,1,0:T(8,128)S(1)} %get-tuple-element.12, f32[15,36,132]{2,1,0:T(8,128)S(1)} %get-tuple-element.13, f32[15,36,132]{2,1,0:T(8,128)S(1)} %get-tuple-element.10, ...), kind=kLoop, calls=%fused_computation.63 | loop fusion | flops 1853280 | bytes 4561956 | tf_op jit(solution)/shard_map/jit(_where)/select_n | solution.py:83
  24.3 1.1 %fusion.80 = (f32[15,34,130]{2,1,0:T(8,128)S(1)}, f32[15,34,130]{2,1,0:T(8,128)S(1)}, f32[15,34,130]{2,1,0:T(8,128)S(1)}) fusion(f32[45,32,3]{2,1,0:T(8,128)S(1)} %copy.113, f32[45,3,3]{2,1,0:T(4,128)S(1)} %get-tuple-element.28, f32[45,32,3]{2,1,0:T(8,128)S(1)} %copy.112, f32[45,3,128]{2,1,0:T(4,128)S(1)} %collective-permute-done.1, ...), kind=kLoop, calls=%fused_computation.101 | loop fusion | flops 1193400 | bytes 2242560 | tf_op jit(solution)/shard_map/mul | solution.py:73
  25.4 1.4 %fusion.37 = f32[2,15,34,130]{3,2,1,0:T(8,128)S(1)} fusion(f32[2,15,36,132]{3,2,1,0:T(8,128)S(1)} %fusion.46, f32[15,34,130]{2,1,0:T(8,128)S(1)} %get-tuple-element.9, f32[15,34,130]{2,1,0:T(8,128)S(1)} %fusion.78, f32[15,34,130]{2,1,0:T(8,128)S(1)} %get-tuple-element.6, f32[15,34,130]{2,1,0:T(8,128)S(1)} %get-tuple-element.5, ...), kind=kLoop, calls=%fused_computation.50 | loop fusion | flops 1723800 | bytes 4243234 | tf_op jit(solution)/shard_map/jit(_where)/select_n | solution.py:83
  26.8 0.4 fusion.103
  27.2 0.6 fusion.86
  27.9 0.3 copy.114
  28.2 0.3 copy-done.5
  28.5 3.6 %fusion.66 = bf16[30,1024]{1,0:T(8,128)(2,1)S(1)} fusion(s32[1024]{0:T(1024)S(1)} %bitcast.91, f32[30,4096]{1,0:T(8,128)S(1)} %bitcast.83), kind=kOutput, calls=%fused_computation.83 | convolution fusion | flops 256006144 | bytes 557056 | tf_op jit(solution)/shard_map/dot_general | solution.py:137
  32.2 12.3 %all_to_all.10 = bf16[30,8,256]{2,0,1:T(8,128)(2,1)S(1)} all-to-all(bf16[30,8,256]{2,0,1:T(8,128)(2,1)S(1)} %bitcast.86), channel_id=1, replica_groups=mesh['lat'=4,'lon'=2,'lev'=4] {'lon','lev'}, dimensions={1} | all-to-all | bytes 245760 | tf_op jit(solution)/shard_map/all_to_all | solution.py:164
  44.8 3.7 %fusion.20 = bf16[1024,512]{0,1:T(8,128)(2,1)S(1)} fusion(bf16[1,2,1024,1024]{3,2,1,0:T(8,128)(2,1)} %param.12, bf16[120,512]{1,0:T(8,128)(2,1)S(1)} %bitcast.90, bf16[1,120,1024]{2,1,0:T(8,128)(2,1)S(1)} %copy-done), kind=kOutput, calls=%fused_computation.24 | convolution fusion | flops 1209008128 | bytes 3514368 | tf_op jit(solution)/shard_map/dot_general | solution.py:113
  48.6 3.4 %fusion.63 = bf16[120,512]{1,0:T(8,128)(2,1)S(1)} fusion(bf16[1024,512]{0,1:T(8,128)(2,1)S(1)} %fusion.20, bf16[1,2,1024,1024]{3,2,1,0:T(8,128)(2,1)} %param.12, bf16[1,1024,120]{1,2,0:T(8,128)(2,1)S(1)} %copy-done.4), kind=kOutput, calls=%fused_computation.82 | convolution fusion | flops 1204350976 | bytes 3514368 | tf_op jit(solution)/shard_map/dot_general | solution.py:117
  52.1 0.7 copy.107
  52.8 3.4 %all-to-all-start.1 = ((bf16[30,8,256]{2,0,1:T(8,128)(2,1)}), bf16[30,8,256]{2,0,1:T(8,128)(2,1)S(1)}, u32[]{:S(2)}, u32[]{:S(2)}) async-start(bf16[30,8,256]{2,0,1:T(8,128)(2,1)} %copy.107), calls=%async_computation.1 | async-start | bytes 262144 | tf_op jit(solution)/shard_map/all_to_all | solution.py:178
  56.2 7.4 %all-to-all-done.1 = bf16[30,8,256]{2,0,1:T(8,128)(2,1)S(1)} async-done(((bf16[30,8,256]{2,0,1:T(8,128)(2,1)}), bf16[30,8,256]{2,0,1:T(8,128)(2,1)S(1)}, u32[]{:S(2)}, u32[]{:S(2)}) %all-to-all-start.1) | async-done | bytes 122912 | tf_op jit(solution)/shard_map/all_to_all | solution.py:178
  64.0 3.4 %fusion.4 = f32[30,4096]{1,0:T(8,128)S(1)} fusion(f32[30,4096]{1,0:T(8,128)S(1)} %bitcast.84, s32[1024]{0:T(1024)S(1)} %bitcast.92, bf16[30,1,1024]{2,1,0:T(2,128)(2,1)S(1)} %get-tuple-element.24, bf16[30,1,1024]{2,1,0:T(2,128)(2,1)S(1)} %get-tuple-element.23, pred[1024]{0:T(1024)(128)(4,1)S(1)} %compare_reduce_fusion), kind=kOutput, calls=%fused_computation.5 | convolution fusion | flops 256006144 | bytes 1111040 | tf_op jit(solution)/shard_map/dot_general | solution.py:188
  67.5 0.8 %slice.274 = f32[30,32,128]{2,1,0:T(8,128)} slice(f32[32,32,128]{2,1,0:T(8,128)S(1)} %bitcast.81), slice={[0:30], [0:32], [0:128]} | slice | bytes 983040
  (41 shorter events, 1.6 us)
Async XLA Ops:
  0.0 44.8 %copy-start = (bf16[1,120,1024]{2,1,0:T(8,128)(2,1)S(1)}, bf16[1,120,1024]{2,1,0:T(8,128)(2,1)}, u32[]{:S(2)}) copy-start(bf16[1,120,1024]{2,1,0:T(8,128)(2,1)} %param.11) | copy-start | bytes 737284
  0.0 5.8 %copy-start.1 = (f32[2,15,32,128]{3,2,1,0:T(8,128)S(1)}, f32[2,15,32,128]{3,2,1,0:T(8,128)}, u32[]{:S(2)}) copy-start(f32[2,15,32,128]{3,2,1,0:T(8,128)} %param.7) | copy-start | bytes 1474564
  0.0 5.8 %copy-start.2 = (f32[15,32,128]{2,1,0:T(8,128)S(1)}, f32[15,32,128]{2,1,0:T(8,128)}, u32[]{:S(2)}) copy-start(f32[15,32,128]{2,1,0:T(8,128)} %param.8) | copy-start | bytes 737284
  2.2 16.6 %collective-permute-start.3 = (f32[45,3,6]{2,1,0:T(4,128)}, f32[45,3,6]{2,1,0:T(4,128)S(1)}, u32[]{:S(2)}, u32[]{:S(2)}) collective-permute-start(f32[45,3,6]{2,1,0:T(4,128)} %pad_maximum_fusion.17), channel_id=1, source_target_pairs={{8,4},{12,0},{16,12},{20,8},{24,20},{28,16},{9,5},{13,1},{17,13},{... | collective-permute-start | bytes 9728 | tf_op jit(solution)/shard_map/ppermute | solution.py:30
  4.5 16.2 %collective-permute-start.4 = (f32[45,3,128]{2,1,0:T(4,128)S(1)}, f32[45,3,128]{2,1,0:T(4,128)S(1)}, u32[]{:S(2)}, u32[]{:S(2)}) collective-permute-start(f32[45,3,128]{2,1,0:T(4,128)S(1)} %get-tuple-element.16), channel_id=1, source_target_pairs={{8,0},{16,8},{24,16},{9,1},{17,9},{25,17},{10,2},{18,10},{26,18},{... | collective-permute-start | bytes 207368 | tf_op jit(solution)/shard_map/ppermute | solution.py:17
  7.1 11.8 %collective-permute-start.2 = (f32[45,32,6]{0,1,2:T(8,128)S(1)}, f32[45,32,6]{0,1,2:T(8,128)S(1)}, u32[]{:S(2)}, u32[]{:S(2)}) collective-permute-start(f32[45,32,6]{0,1,2:T(8,128)S(1)} %pad_maximum_fusion.14), channel_id=1, source_target_pairs={{0,4},{4,0},{1,5},{5,1},{2,6},{6,2},{3,7},{7,3},{8,12},{12,8},{9,1... | collective-permute-start | bytes 103688 | tf_op jit(solution)/shard_map/ppermute | solution.py:21
  10.3 8.6 %collective-permute-start = (f32[45,3,6]{2,1,0:T(4,128)S(1)}, f32[45,3,6]{2,1,0:T(4,128)S(1)}, u32[]{:S(2)}, u32[]{:S(2)}) collective-permute-start(f32[45,3,6]{2,1,0:T(4,128)S(1)} %pad_maximum_fusion.16), channel_id=1, source_target_pairs={{0,12},{4,8},{8,20},{12,16},{16,28},{20,24},{1,13},{5,9},{9,21},{1... | collective-permute-start | bytes 9728 | tf_op jit(solution)/shard_map/ppermute | solution.py:30
  14.9 5.7 %collective-permute-start.1 = (f32[45,3,128]{2,1,0:T(4,128)S(1)}, f32[45,3,128]{2,1,0:T(4,128)S(1)}, u32[]{:S(2)}, u32[]{:S(2)}) collective-permute-start(f32[45,3,128]{2,1,0:T(4,128)S(1)} %get-tuple-element.15), channel_id=1, source_target_pairs={{0,8},{8,16},{16,24},{1,9},{9,17},{17,25},{2,10},{10,18},{18,26},{... | collective-permute-start | bytes 207368 | tf_op jit(solution)/shard_map/ppermute | solution.py:17
  27.8 0.7 %copy-start.5 = (s32[1,1024]{1,0:T(1,128)S(1)}, s32[1,1024]{1,0:T(1,128)}, u32[]{:S(2)}) copy-start(s32[1,1024]{1,0:T(1,128)} %param.9) | copy-start | bytes 12292
  44.8 3.7 %copy-start.4 = (bf16[1,1024,120]{1,2,0:T(8,128)(2,1)S(1)}, bf16[1,1024,120]{1,2,0:T(8,128)(2,1)}, u32[]{:S(2)}) copy-start(bf16[1,1024,120]{1,2,0:T(8,128)(2,1)} %param.13) | copy-start | bytes 737284
  48.5 7.7 %copy-start.3 = (s32[1,1024,1]{1,2,0:T(1,128)S(1)}, s32[1,1024,1]{1,2,0:T(1,128)}, u32[]{:S(2)}) copy-start(s32[1,1024,1]{1,2,0:T(1,128)} %param.10) | copy-start | bytes 12292
  52.8 10.8 %all-to-all-start.1 = ((bf16[30,8,256]{2,0,1:T(8,128)(2,1)}), bf16[30,8,256]{2,0,1:T(8,128)(2,1)S(1)}, u32[]{:S(2)}, u32[]{:S(2)}) async-start(bf16[30,8,256]{2,0,1:T(8,128)(2,1)} %copy.107), calls=%async_computation.1 | async-start | bytes 262144 | tf_op jit(solution)/shard_map/all_to_all | solution.py:178

commit v5 on v3

--- a/solution.py
+++ b/solution.py
@@ -99,20 +99,23 @@
     per_device = cloudy // lev_count
     capacity = min(per_device, 4 * per_device // lon_count)
     feature_count = 2 * LEVELS
-    flat_values = values.reshape(2 * level_rows, cells)
-    picker = (column_ids[:, None] == jnp.arange(cells, dtype=jnp.int32)[None, :]).astype(
+    lat_rows, lon_cols = values.shape[2], values.shape[3]
+    local_features = 2 * level_rows
+    planes = values.reshape(local_features, lat_rows, lon_cols)
+    row_of = column_ids // lon_cols
+    col_of = column_ids % lon_cols
+    col_picker = (jnp.arange(lon_cols, dtype=jnp.int32)[:, None] == col_of[None, :]).astype(
         jnp.bfloat16
     )
-    picked = lax.dot_general(
-        flat_values.astype(jnp.bfloat16),
-        picker,
-        (((1,), (1,)), ((), ())),
-        preferred_element_type=jnp.float32,
-    )
-    picked = picked.astype(jnp.bfloat16)
+    row_match = jnp.arange(lat_rows, dtype=jnp.int32)[:, None] == row_of[None, :]
+    by_row = jnp.dot(
+        planes.astype(jnp.bfloat16).reshape(local_features * lat_rows, lon_cols),
+        col_picker,
+        preferred_element_type=jnp.bfloat16,
+    ).reshape(local_features, lat_rows, cloudy)
+    picked = jnp.sum(jnp.where(row_match[None], by_row, jnp.zeros_like(by_row)), axis=1)
     routes = owners[0, :, 0]
     group = lon_count * lev_count
-    local_features = 2 * level_rows
     whole_slices = capacity == per_device
     if whole_slices:
         send_buffer = jnp.broadcast_to(
@@ -154,10 +157,14 @@
             tendency = jnp.where(routes[None, :] == regime, returned[:, regime], tendency)
     else:
         tendency = returned.reshape(local_features, group * capacity)[:, slot_index]
-    spread = jnp.dot(
-        tendency, picker, preferred_element_type=jnp.float32
+    spread_rows = jnp.where(row_match[None], tendency[:, None, :], jnp.zeros_like(tendency)[:, None, :])
+    spread = lax.dot_general(
+        spread_rows.reshape(local_features * lat_rows, cloudy),
+        col_picker,
+        (((1,), (1,)), ((), ())),
+        preferred_element_type=jnp.float32,
     )
-    updated = flat_values + spread
+    updated = planes + spread.reshape(planes.shape)
     return updated.reshape(values.shape)
 
 

time: 65.3 us -> 60 us (0.919)
  matrix products: 14 us -> 9.36 us
  local copies, waits for them, and re-layouts: 5.19 us -> 3.44 us
  other arithmetic: 8.77 us -> 10.5 us
    dot_general x2, matrix products: 6.8 us -> 2.19 us  [the longest x1 1.48 us: on_device(): lax.dot_general(spread_rows.reshape(local_features * lat_rows, cloudy), c...]
    select_n x0 -> x3, other arithmetic: none -> 1.63 us  [the longest x1 0.71 us: on_device(): row_of = column_ids // lon_cols]
    unnamed x19 -> x14, local copies, waits for them, and re-layouts: 2.53 us -> 0.98 us
    ppermute x1, waiting for transfers between devices: 0.88 us -> 0.01 us  [halo_exchange(): lax.ppermute(cells[..., cells.shape[-2] - width:, :], 'lat', [(i, i + 1)...]
  transfers between devices with their start and end apart: 4 -> 4, of which waited for: 3 -> 2; matrix products, arithmetic and copies ran while one was open for 0% -> 2% of each run, Pallas kernels for 0% -> 0%
where the time goes in v5:
time: 60 us; the launch traced here: 59.5 us
  blocking collectives  14.3 us (24%)
  waiting for transfers between devices  10.9 us (18%)
  starting transfers between devices  10.7 us (18%)
  other arithmetic  10.5 us (18%)
  matrix products  9.36 us (16%)
  local copies, waits for them, and re-layouts  3.44 us (6%)
    all_to_all x1, blocking collectives, on_device(): lax.all_to_all(send_buffer, ('lon', 'lev'), split_axis=1, concat_axis=1,...  14.3 us
    all_to_all x1, waiting for transfers between devices, on_device(): lax.all_to_all(outgoing, ('lon', 'lev'), split_axis=1, concat_axis=1, til...  7.42 us
    dot_general x1, matrix products, network(): lax.dot_general(w_middle[layer_no], hidden, contract, preferred_element_t...  3.73 us
    ppermute x1, waiting for transfers between devices, halo_exchange(): lax.ppermute(jnp.concatenate([right, left], axis=-1), 'lon', [(0, 1), (1,...  3.51 us
    dot_general x1, matrix products, network(): lax.dot_general(w_last, hidden, contract, preferred_element_type=jnp.floa...  3.44 us
    all_to_all x1, starting transfers between devices, on_device(): lax.all_to_all(outgoing, ('lon', 'lev'), split_axis=1, concat_axis=1, til...  3.37 us
    ppermute x1, starting transfers between devices, halo_exchange(): lax.ppermute(cells[..., cells.shape[-2] - width:, :], 'lat', [(i, i + 1)...  3.04 us
    ppermute x1, starting transfers between devices, halo_exchange(): lax.ppermute(jnp.concatenate([right, left], axis=-1), 'lon', [(0, 1), (1,...  3.03 us
  transfers between devices with their start and end apart: 4, of which 2 were waited for; matrix products, arithmetic and copies ran while one was open for 2% of the time, Pallas kernels for 0%

profile of v5, /device:TPU:0, one launch (start us, length us, event | category | flops | bytes accessed | tf_op | source)
XLA Modules:
  0.0 59.5 jit_solution(7515766200177670401)
XLA Ops:
  0.0 1.1 %pad_maximum_fusion.16 = (f32[45,3,128]{2,1,0:T(4,128)S(1)}, f32[45,3,128]{2,1,0:T(4,128)S(1)}) fusion(f32[15,32,128]{2,1,0:T(8,128)} %param.8, f32[30,32,128]{2,1,0:T(8,128)} %bitcast.69), kind=kLoop, calls=%fused_computation.140 | loop fusion | flops 34560 | bytes 875520 | tf_op jit(solution)/shard_map/slice | solution.py:13
  1.1 1.3 %collective-permute-start.1 = (f32[45,3,128]{2,1,0:T(4,128)S(1)}, f32[45,3,128]{2,1,0:T(4,128)S(1)}, u32[]{:S(2)}, u32[]{:S(2)}) collective-permute-start(f32[45,3,128]{2,1,0:T(4,128)S(1)} %get-tuple-element.24), channel_id=1, source_target_pairs={{8,0},{16,8},{24,16},{9,1},{17,9},{25,17},{10,2},{18,10},{26,18},{... | collective-permute-start | bytes 207368 | tf_op jit(solution)/shard_map/ppermute | solution.py:15
  2.4 3.0 %collective-permute-start = (f32[45,3,128]{2,1,0:T(4,128)S(1)}, f32[45,3,128]{2,1,0:T(4,128)S(1)}, u32[]{:S(2)}, u32[]{:S(2)}) collective-permute-start(f32[45,3,128]{2,1,0:T(4,128)S(1)} %get-tuple-element.23), channel_id=1, source_target_pairs={{0,8},{8,16},{16,24},{1,9},{9,17},{17,25},{2,10},{10,18},{18,26},{... | collective-permute-start | bytes 207368 | tf_op jit(solution)/shard_map/ppermute | solution.py:12
  5.5 0.7 %and_select_fusion = (s32[1,1024]{1,0:T(1,128)S(1)}, s32[1,1024]{1,0:T(1,128)S(1)}) fusion(s32[1,1024]{1,0:T(1,128)} %param.9), kind=kLoop, calls=%fused_computation.142 | loop fusion | flops 11264 | bytes 12288 | tf_op jit(solution)/shard_map/jit(remainder)/select_n | solution.py:106
  6.2 0.7 %and_select_fusion.1 = s32[1,1024]{1,0:T(1,128)S(1)} fusion(s32[1,1024]{1,0:T(1,128)S(1)} %get-tuple-element.6, s32[1,1024]{1,0:T(1,128)} %param.9), kind=kLoop, calls=%fused_computation.144 | loop fusion | flops 12288 | bytes 12288 | tf_op jit(solution)/shard_map/jit(floor_divide)/jit(_where)/select_n | solution.py:105
  6.9 1.3 %pad_maximum_fusion.1 = f32[45,38,128]{2,1,0:T(8,128)S(1)} fusion(f32[45,3,128]{2,1,0:T(4,128)S(1)} %collective-permute-done.1, f32[15,32,128]{2,1,0:T(8,128)} %param.8, f32[30,32,128]{2,1,0:T(8,128)} %bitcast.70, f32[45,3,128]{2,1,0:T(4,128)S(1)} %collective-permute-done), kind=kLoop, calls=%fused_computation.78 | loop fusion | flops 656640 | bytes 1751040 | tf_op jit(solution)/shard_map/concatenate | solution.py:18
  8.2 0.3 fusion.118
  8.5 0.4 copy.40
  9.0 0.4 copy.39
  9.4 3.0 %collective-permute-start.2 = (f32[45,38,6]{0,1,2:T(8,128)S(1)}, f32[45,38,6]{0,1,2:T(8,128)S(1)}, u32[]{:S(2)}, u32[]{:S(2)}) collective-permute-start(f32[45,38,6]{0,1,2:T(8,128)S(1)} %pad_maximum_fusion.14), channel_id=1, source_target_pairs={{0,4},{4,0},{1,5},{5,1},{2,6},{6,2},{3,7},{7,3},{8,12},{12,8},{9,1... | collective-permute-start | bytes 123128 | tf_op jit(solution)/shard_map/ppermute | solution.py:23
  12.5 3.5 %collective-permute-done.2 = f32[45,38,6]{0,1,2:T(8,128)S(1)} collective-permute-done((f32[45,38,6]{0,1,2:T(8,128)S(1)}, f32[45,38,6]{0,1,2:T(8,128)S(1)}, u32[]{:S(2)}, u32[]{:S(2)}) %collective-permute-start.2) | collective-permute-done | bytes 41072 | tf_op jit(solution)/shard_map/ppermute | solution.py:23
  16.0 0.5 copy.52
  16.4 0.5 copy.51
  16.9 1.0 %pad_maximum_fusion = f32[45,38,134]{2,1,0:T(8,128)S(1)} fusion(f32[45,38,3]{2,1,0:T(8,128)S(1)} %copy.52, f32[45,3,128]{2,1,0:T(4,128)S(1)} %collective-permute-done.1, f32[15,32,128]{2,1,0:T(8,128)S(1)} %copy-done.2, f32[30,32,128]{2,1,0:T(8,128)S(1)} %bitcast.71, f32[45,3,128]{2,1,0:T(4,128)S(1)} %collective-permute-done, f32[45,38,3]{2,1,0:T(8,128)S(1)} %copy.51), kind=kLoop, calls=%fused_computation.37 | loop fusion | flops 1145700 | bytes 1833120 | tf_op jit(solution)/shard_map/concatenate | solution.py:28
  17.9 0.1 slice.196
  18.0 0.7 %fusion.84 = (f32[15,36,132]{2,1,0:T(8,128)S(1)}, f32[15,36,132]{2,1,0:T(8,128)S(1)}, f32[15,36,132]{2,1,0:T(8,128)S(1)}, f32[15,36,132]{2,1,0:T(8,128)S(1)}) fusion(f32[45,38,134]{2,1,0:T(8,128)S(1)} %pad_maximum_fusion), kind=kLoop, calls=%fused_computation.94 | loop fusion | flops 570240 | bytes 2566080 | tf_op jit(solution)/shard_map/mul | solution.py:42
  18.7 1.4 %fusion.44 = f32[2,15,36,132]{3,2,1,0:T(8,128)S(1)} fusion(f32[2,15,38,134]{3,2,1,0:T(8,128)S(1)} %bitcast.68, f32[15,36,132]{2,1,0:T(8,128)S(1)} %get-tuple-element.14, f32[15,36,132]{2,1,0:T(8,128)S(1)} %get-tuple-element.15, f32[15,36,132]{2,1,0:T(8,128)S(1)} %get-tuple-element.16, f32[15,36,132]{2,1,0:T(8,128)S(1)} %get-tuple-element.13, ...), kind=kLoop, calls=%fused_computation.54 | loop fusion | flops 1853280 | bytes 4561956 | tf_op jit(solution)/shard_map/jit(_where)/select_n | solution.py:52
  20.1 0.9 %fusion.80 = (f32[15,34,130]{2,1,0:T(8,128)S(1)}, f32[15,34,130]{2,1,0:T(8,128)S(1)}, f32[15,34,130]{2,1,0:T(8,128)S(1)}, f32[15,34,130]{2,1,0:T(8,128)S(1)}) fusion(f32[45,38,134]{2,1,0:T(8,128)S(1)} %pad_maximum_fusion, f32[45,38,3]{2,1,0:T(8,128)S(1)} %copy.52, f32[45,3,128]{2,1,0:T(4,128)S(1)} %collective-permute-done.1, ...), kind=kLoop, calls=%fused_computation.86 | loop fusion | flops 1060800 | bytes 2772960 | tf_op jit(solution)/shard_map/mul | solution.py:42
  21.0 1.4 %fusion.35 = f32[2,15,34,130]{3,2,1,0:T(8,128)S(1)} fusion(f32[2,15,36,132]{3,2,1,0:T(8,128)S(1)} %fusion.44, f32[15,34,130]{2,1,0:T(8,128)S(1)} %get-tuple-element.11, f32[15,34,130]{2,1,0:T(8,128)S(1)} %get-tuple-element.12, f32[15,34,130]{2,1,0:T(8,128)S(1)} %get-tuple-element.10, f32[15,34,130]{2,1,0:T(8,128)S(1)} %get-tuple-element.9, ...), kind=kLoop, calls=%fused_computation.41 | loop fusion | flops 1723800 | bytes 4243234 | tf_op jit(solution)/shard_map/jit(_where)/select_n | solution.py:52
  22.4 0.4 fusion.101
  22.8 0.6 %fusion.89 = f32[2,15,32,128]{3,2,1,0:T(8,128)S(1)} fusion(f32[2,15,34,130]{3,2,1,0:T(8,128)S(1)} %fusion.35, f32[15,32,128]{2,1,0:T(8,128)S(1)} %get-tuple-element.18, f32[15,32,128]{2,1,0:T(8,128)S(1)} %get-tuple-element.17, f32[15,32,128]{2,1,0:T(8,128)S(1)} %get-tuple-element.22, f32[15,32,128]{2,1,0:T(8,128)S(1)} %get-tuple-element.21), kind=kLoop, calls=%fused_computation.99 | loop fusion | flops 1474560 | bytes 3932160 | tf_op jit(solution)/shard_map/add | solution.py:43
  23.4 0.7 %select_reduce_fusion = bf16[30,1024]{1,0:T(8,128)(2,1)S(1)} fusion(pred[32,1024]{1,0:T(8,128)(4,1)S(1)} %iota_compare_fusion.1, bf16[30,32,128]{2,1,0:T(8,128)(2,1)S(1)} %bitcast_convert_fusion, s32[1024]{0:T(1024)S(1)} %bitcast.82), kind=kOutput, calls=%fused_computation.35 | convolution fusion | flops 253724672 | bytes 344064 | tf_op jit(solution)/shard_map/dot_general | solution.py:111
  24.2 14.3 %all_to_all.10 = bf16[30,8,256]{2,0,1:T(8,128)(2,1)S(1)} all-to-all(bf16[30,8,256]{2,0,1:T(8,128)(2,1)S(1)} %bitcast.75), channel_id=1, replica_groups=mesh['lat'=4,'lon'=2,'lev'=4] {'lon','lev'}, dimensions={1} | all-to-all | bytes 245760 | tf_op jit(solution)/shard_map/all_to_all | solution.py:136
  38.5 0.1 copy.57
  38.6 0.1 copy.45
  38.8 3.7 %fusion.15 = bf16[1024,512]{0,1:T(8,128)(2,1)S(1)} fusion(bf16[1,2,1024,1024]{3,2,1,0:T(8,128)(2,1)} %param.12, bf16[120,512]{1,0:T(8,128)(2,1)S(1)} %bitcast.79, bf16[1,120,1024]{2,1,0:T(8,128)(2,1)S(1)} %copy-done), kind=kOutput, calls=%fused_computation.18 | convolution fusion | flops 1209008128 | bytes 3514368 | tf_op jit(solution)/shard_map/dot_general | solution.py:82
  42.5 3.4 %fusion.64 = bf16[120,512]{1,0:T(8,128)(2,1)S(1)} fusion(bf16[1024,512]{0,1:T(8,128)(2,1)S(1)} %fusion.15, bf16[1,2,1024,1024]{3,2,1,0:T(8,128)(2,1)} %param.12, bf16[1,1024,120]{1,2,0:T(8,128)(2,1)S(1)} %copy-done.4), kind=kOutput, calls=%fused_computation.67 | convolution fusion | flops 1204350976 | bytes 3514368 | tf_op jit(solution)/shard_map/dot_general | solution.py:86
  46.1 0.7 %copy.47 = bf16[30,8,256]{2,0,1:T(8,128)(2,1)} copy(bf16[30,8,256]{2,1,0:T(8,128)(2,1)S(1)} %reshape.103) | data formatting | bytes 245760 | tf_op jit(solution)/shard_map/reshape | solution.py:148
  46.8 3.4 %all-to-all-start.1 = ((bf16[30,8,256]{2,0,1:T(8,128)(2,1)}), bf16[30,8,256]{2,0,1:T(8,128)(2,1)S(1)}, u32[]{:S(2)}, u32[]{:S(2)}) async-start(bf16[30,8,256]{2,0,1:T(8,128)(2,1)} %copy.47), calls=%async_computation.1 | async-start | bytes 262144 | tf_op jit(solution)/shard_map/all_to_all | solution.py:150
  50.2 7.4 %all-to-all-done.1 = bf16[30,8,256]{2,0,1:T(8,128)(2,1)S(1)} async-done(((bf16[30,8,256]{2,0,1:T(8,128)(2,1)}), bf16[30,8,256]{2,0,1:T(8,128)(2,1)S(1)}, u32[]{:S(2)}, u32[]{:S(2)}) %all-to-all-start.1) | async-done | bytes 122912 | tf_op jit(solution)/shard_map/all_to_all | solution.py:150
  57.8 0.2 broadcast_select_fusion
  58.0 1.5 %fusion.51 = f32[30,32,128]{2,1,0:T(8,128)} fusion(f32[30,32,128]{2,1,0:T(8,128)S(1)} %bitcast.74, pred[32,1024]{1,0:T(8,128)(4,1)S(1)} %iota_compare_fusion.1, bf16[30,1024]{1,0:T(8,128)(2,1)S(1)} %bitcast.80, s32[1024]{0:T(1024)S(1)} %bitcast.83), kind=kOutput, calls=%fused_computation.64 | convolution fusion | flops 252895232 | bytes 1081344 | tf_op jit(solution)/shard_map/dot_general | solution.py:161
  (30 shorter events, 0.5 us)
Async XLA Ops:
  0.0 38.8 %copy-start = (bf16[1,120,1024]{2,1,0:T(8,128)(2,1)S(1)}, bf16[1,120,1024]{2,1,0:T(8,128)(2,1)}, u32[]{:S(2)}) copy-start(bf16[1,120,1024]{2,1,0:T(8,128)(2,1)} %param.11) | copy-start | bytes 737284
  1.1 5.8 %collective-permute-start.1 = (f32[45,3,128]{2,1,0:T(4,128)S(1)}, f32[45,3,128]{2,1,0:T(4,128)S(1)}, u32[]{:S(2)}, u32[]{:S(2)}) collective-permute-start(f32[45,3,128]{2,1,0:T(4,128)S(1)} %get-tuple-element.24), channel_id=1, source_target_pairs={{8,0},{16,8},{24,16},{9,1},{17,9},{25,17},{10,2},{18,10},{26,18},{... | collective-permute-start | bytes 207368 | tf_op jit(solution)/shard_map/ppermute | solution.py:15
  2.4 4.5 %collective-permute-start = (f32[45,3,128]{2,1,0:T(4,128)S(1)}, f32[45,3,128]{2,1,0:T(4,128)S(1)}, u32[]{:S(2)}, u32[]{:S(2)}) collective-permute-start(f32[45,3,128]{2,1,0:T(4,128)S(1)} %get-tuple-element.23), channel_id=1, source_target_pairs={{0,8},{8,16},{16,24},{1,9},{9,17},{17,25},{2,10},{10,18},{18,26},{... | collective-permute-start | bytes 207368 | tf_op jit(solution)/shard_map/ppermute | solution.py:12
  8.9 8.0 %copy-start.1 = (f32[2,15,32,128]{3,2,1,0:T(8,128)S(1)}, f32[2,15,32,128]{3,2,1,0:T(8,128)}, u32[]{:S(2)}) copy-start(f32[2,15,32,128]{3,2,1,0:T(8,128)} %param.7) | copy-start | bytes 1474564
  8.9 8.0 %copy-start.2 = (f32[15,32,128]{2,1,0:T(8,128)S(1)}, f32[15,32,128]{2,1,0:T(8,128)}, u32[]{:S(2)}) copy-start(f32[15,32,128]{2,1,0:T(8,128)} %param.8) | copy-start | bytes 737284
  9.4 6.6 %collective-permute-start.2 = (f32[45,38,6]{0,1,2:T(8,128)S(1)}, f32[45,38,6]{0,1,2:T(8,128)S(1)}, u32[]{:S(2)}, u32[]{:S(2)}) collective-permute-start(f32[45,38,6]{0,1,2:T(8,128)S(1)} %pad_maximum_fusion.14), channel_id=1, source_target_pairs={{0,4},{4,0},{1,5},{5,1},{2,6},{6,2},{3,7},{7,3},{8,12},{12,8},{9,1... | collective-permute-start | bytes 123128 | tf_op jit(solution)/shard_map/ppermute | solution.py:23
  38.8 3.8 %copy-start.4 = (bf16[1,1024,120]{1,2,0:T(8,128)(2,1)S(1)}, bf16[1,1024,120]{1,2,0:T(8,128)(2,1)}, u32[]{:S(2)}) copy-start(bf16[1,1024,120]{1,2,0:T(8,128)(2,1)} %param.13) | copy-start | bytes 737284
  42.5 7.7 %copy-start.3 = (s32[1,1024,1]{1,2,0:T(1,128)S(1)}, s32[1,1024,1]{1,2,0:T(1,128)}, u32[]{:S(2)}) copy-start(s32[1,1024,1]{1,2,0:T(1,128)} %param.10) | copy-start | bytes 12292
  46.8 10.8 %all-to-all-start.1 = ((bf16[30,8,256]{2,0,1:T(8,128)(2,1)}), bf16[30,8,256]{2,0,1:T(8,128)(2,1)S(1)}, u32[]{:S(2)}, u32[]{:S(2)}) async-start(bf16[30,8,256]{2,0,1:T(8,128)(2,1)} %copy.47), calls=%async_computation.1 | async-start | bytes 262144 | tf_op jit(solution)/shard_map/all_to_all | solution.py:150

commit v6 on v5

--- a/solution.py
+++ b/solution.py
@@ -7,12 +7,17 @@
 STEPS = 3
 
 
+def dense_ppermute(piece, axis, pairs):
+    flat = piece.reshape(piece.shape[0], -1)
+    return lax.ppermute(flat, axis, pairs).reshape(piece.shape)
+
+
 def halo_exchange(cells, width):
     lat_count = lax.axis_size("lat")
-    from_above = lax.ppermute(
+    from_above = dense_ppermute(
         cells[..., cells.shape[-2] - width :, :], "lat", [(i, i + 1) for i in range(lat_count - 1)]
     )
-    from_below = lax.ppermute(
+    from_below = dense_ppermute(
         cells[..., :width, :], "lat", [(i + 1, i) for i in range(lat_count - 1)]
     )
     cells = jnp.concatenate([from_above, cells, from_below], axis=-2)
@@ -20,11 +25,15 @@
     left = cells[..., :width]
     right = cells[..., cells.shape[-1] - width :]
     if lon_count == 2:
-        both = lax.ppermute(jnp.concatenate([right, left], axis=-1), "lon", [(0, 1), (1, 0)])
+        both = dense_ppermute(jnp.concatenate([right, left], axis=-1), "lon", [(0, 1), (1, 0)])
         from_left, from_right = both[..., :width], both[..., width:]
     else:
-        from_left = lax.ppermute(right, "lon", [(i, (i + 1) % lon_count) for i in range(lon_count)])
-        from_right = lax.ppermute(left, "lon", [((i + 1) % lon_count, i) for i in range(lon_count)])
+        from_left = dense_ppermute(
+            right, "lon", [(i, (i + 1) % lon_count) for i in range(lon_count)]
+        )
+        from_right = dense_ppermute(
+            left, "lon", [((i + 1) % lon_count, i) for i in range(lon_count)]
+        )
     return jnp.concatenate([from_left, cells, from_right], axis=-1)
 
 

time: 60 us -> 60.3 us (level)
  local copies, waits for them, and re-layouts: 3.44 us -> 4.54 us
  other arithmetic: 10.5 us -> 9.62 us
    concatenate x1, other arithmetic: 1.27 us -> 0.13 us  [halo_exchange(): cells = jnp.concatenate([from_above, cells, from_below], axis=-2)]
    slice x1 -> x2, local copies, waits for them, and re-layouts: 0.08 us -> 0.91 us  [dynamics(): stacked[:kinds * level_rows]]
    unnamed x14 -> x20, local copies, waits for them, and re-layouts: 0.98 us -> 1.6 us
  transfers between devices with their start and end apart: 4 -> 4, of which waited for: 2 -> 2; matrix products, arithmetic and copies ran while one was open for 2% -> 3% of each run, Pallas kernels for 0% -> 0%
where the time goes in v6:
time: 60.3 us; the launch traced here: 59.9 us
  blocking collectives  14.2 us (24%)
  waiting for transfers between devices  10.9 us (18%)
  starting transfers between devices  10.7 us (18%)
  other arithmetic  9.62 us (16%)
  matrix products  9.39 us (16%)
  local copies, waits for them, and re-layouts  4.54 us (8%)
    all_to_all x1, blocking collectives, on_device(): lax.all_to_all(send_buffer, ('lon', 'lev'), split_axis=1, concat_axis=1,...  14.2 us
    all_to_all x1, waiting for transfers between devices, on_device(): lax.all_to_all(outgoing, ('lon', 'lev'), split_axis=1, concat_axis=1, til...  7.42 us
    ppermute x3, starting transfers between devices, dense_ppermute(): return lax.ppermute(flat, axis, pairs).reshape(piece.shape)  7.36 us
    dot_general x1, matrix products, network(): lax.dot_general(w_middle[layer_no], hidden, contract, preferred_element_t...  3.73 us
    ppermute x3, waiting for transfers between devices, dense_ppermute(): return lax.ppermute(flat, axis, pairs).reshape(piece.shape)  3.5 us
    dot_general x1, matrix products, network(): lax.dot_general(w_last, hidden, contract, preferred_element_type=jnp.floa...  3.46 us
    all_to_all x1, starting transfers between devices, on_device(): lax.all_to_all(outgoing, ('lon', 'lev'), split_axis=1, concat_axis=1, til...  3.37 us
    select_n x2, other arithmetic, clear_outside(): return jnp.where(inside[:, None], values, 0.0)  2.81 us
  transfers between devices with their start and end apart: 4, of which 2 were waited for; matrix products, arithmetic and copies ran while one was open for 3% of the time, Pallas kernels for 0%

profile of v6, /device:TPU:0, one launch (start us, length us, event | category | flops | bytes accessed | tf_op | source)
XLA Modules:
  0.0 59.9 jit_solution(9298963875839943835)
XLA Ops:
  0.0 1.1 %pad_maximum_fusion.16 = (f32[45,3,128]{2,1,0:T(4,128)S(1)}, f32[45,3,128]{2,1,0:T(4,128)S(1)}) fusion(f32[15,32,128]{2,1,0:T(8,128)} %param.8, f32[30,32,128]{2,1,0:T(8,128)} %bitcast.77), kind=kLoop, calls=%fused_computation.140 | loop fusion | flops 34560 | bytes 875520 | tf_op jit(solution)/shard_map/slice | solution.py:18
  1.2 1.3 %collective-permute-start.1 = (f32[45,384]{1,0:T(8,128)S(1)}, f32[45,384]{1,0:T(8,128)S(1)}, u32[]{:S(2)}, u32[]{:S(2)}) collective-permute-start(f32[45,384]{1,0:T(8,128)S(1)} %bitcast.90), channel_id=1, source_target_pairs={{8,0},{16,8},{24,16},{9,1},{17,9},{25,17},{10,2},{18,10},{26,18},{... | collective-permute-start | bytes 207368 | tf_op jit(solution)/shard_map/ppermute | solution.py:12
  2.5 3.0 %collective-permute-start = (f32[45,384]{1,0:T(8,128)S(1)}, f32[45,384]{1,0:T(8,128)S(1)}, u32[]{:S(2)}, u32[]{:S(2)}) collective-permute-start(f32[45,384]{1,0:T(8,128)S(1)} %bitcast.91), channel_id=1, source_target_pairs={{0,8},{8,16},{16,24},{1,9},{9,17},{17,25},{2,10},{10,18},{18,26},{... | collective-permute-start | bytes 207368 | tf_op jit(solution)/shard_map/ppermute | solution.py:12
  5.6 0.7 %and_select_fusion = (s32[1,1024]{1,0:T(1,128)S(1)}, s32[1,1024]{1,0:T(1,128)S(1)}) fusion(s32[1,1024]{1,0:T(1,128)} %param.9), kind=kLoop, calls=%fused_computation.142 | loop fusion | flops 11264 | bytes 12288 | tf_op jit(solution)/shard_map/jit(remainder)/select_n | solution.py:115
  6.3 0.7 %and_select_fusion.1 = s32[1,1024]{1,0:T(1,128)S(1)} fusion(s32[1,1024]{1,0:T(1,128)S(1)} %get-tuple-element.6, s32[1,1024]{1,0:T(1,128)} %param.9), kind=kLoop, calls=%fused_computation.144 | loop fusion | flops 12288 | bytes 12288 | tf_op jit(solution)/shard_map/jit(floor_divide)/jit(_where)/select_n | solution.py:114
  7.2 0.1 pad_maximum_fusion.1
  7.3 0.3 fusion.118
  7.6 0.3 pad_maximum_fusion.2
  7.9 0.3 reshape.131
  8.2 0.1 copy.80
  8.3 3.0 %collective-permute-start.2 = (f32[45,228]{0,1:T(8,128)S(1)}, f32[45,228]{0,1:T(8,128)S(1)}, u32[]{:S(2)}, u32[]{:S(2)}) collective-permute-start(f32[45,228]{0,1:T(8,128)S(1)} %copy.80), channel_id=1, source_target_pairs={{0,4},{4,0},{1,5},{5,1},{2,6},{6,2},{3,7},{7,3},{8,12},{12,8},{9,1... | collective-permute-start | bytes 123128 | tf_op jit(solution)/shard_map/ppermute | solution.py:12
  11.4 3.5 %collective-permute-done.2 = f32[45,228]{0,1:T(8,128)S(1)} collective-permute-done((f32[45,228]{0,1:T(8,128)S(1)}, f32[45,228]{0,1:T(8,128)S(1)}, u32[]{:S(2)}, u32[]{:S(2)}) %collective-permute-start.2) | collective-permute-done | bytes 41072 | tf_op jit(solution)/shard_map/ppermute | solution.py:12
  14.9 0.5 copy.84
  15.4 0.5 copy.83
  15.9 1.0 %pad_maximum_fusion = f32[45,38,134]{2,1,0:T(8,128)S(1)} fusion(f32[45,38,3]{2,1,0:T(8,128)S(1)} %copy.84, f32[45,3,128]{2,1,0:T(4,128)S(1)} %reshape.118, f32[15,32,128]{2,1,0:T(8,128)S(1)} %copy-done.3, f32[30,32,128]{2,1,0:T(8,128)S(1)} %bitcast.79, f32[45,3,128]{2,1,0:T(4,128)S(1)} %reshape.116, f32[45,38,3]{2,1,0:T(8,128)S(1)} %copy.83), kind=kLoop, calls=%fused_computation.37 | loop fusion | flops 1145700 | bytes 1833120 | tf_op jit(solution)/shard_map/concatenate | solution.py:37
  16.9 0.7 %fusion.84 = (f32[15,36,132]{2,1,0:T(8,128)S(1)}, f32[15,36,132]{2,1,0:T(8,128)S(1)}, f32[15,36,132]{2,1,0:T(8,128)S(1)}, f32[15,36,132]{2,1,0:T(8,128)S(1)}) fusion(f32[45,38,134]{2,1,0:T(8,128)S(1)} %pad_maximum_fusion), kind=kLoop, calls=%fused_computation.95 | loop fusion | flops 570240 | bytes 2566080 | tf_op jit(solution)/shard_map/mul | solution.py:51
  17.6 0.6 copy-done.1
  18.1 0.9 %fusion.80 = (f32[15,34,130]{2,1,0:T(8,128)S(1)}, f32[15,34,130]{2,1,0:T(8,128)S(1)}, f32[15,34,130]{2,1,0:T(8,128)S(1)}, f32[15,34,130]{2,1,0:T(8,128)S(1)}) fusion(f32[45,38,134]{2,1,0:T(8,128)S(1)} %pad_maximum_fusion, f32[45,38,3]{2,1,0:T(8,128)S(1)} %copy.84, f32[45,3,128]{2,1,0:T(4,128)S(1)} %reshape.118, f32[15,32,128]{2,1,0:T(8,128)S(1)} %copy-done.3, ...), kind=kLoop, calls=%fused_computation.87 | loop fusion | flops 1060800 | bytes 2772960 | tf_op jit(solution)/shard_map/mul | solution.py:51
  19.0 0.4 fusion.101
  19.4 0.9 %slice-done = f32[30,38,134]{2,1,0:T(8,128)S(1)} async-done(((f32[45,38,134]{2,1,0:T(8,128)}), f32[30,38,134]{2,1,0:T(8,128)S(1)}, s32[]{:S(2)}) %slice-start) | async-done | bytes 611064 | tf_op jit(solution)/shard_map/slice | solution.py:70
  20.3 1.4 %fusion.44 = f32[2,15,36,132]{3,2,1,0:T(8,128)S(1)} fusion(f32[2,15,38,134]{3,2,1,0:T(8,128)S(1)} %bitcast.76, f32[15,36,132]{2,1,0:T(8,128)S(1)} %get-tuple-element.14, f32[15,36,132]{2,1,0:T(8,128)S(1)} %get-tuple-element.15, f32[15,36,132]{2,1,0:T(8,128)S(1)} %get-tuple-element.16, f32[15,36,132]{2,1,0:T(8,128)S(1)} %get-tuple-element.13, ...), kind=kLoop, calls=%fused_computation.54 | loop fusion | flops 1853280 | bytes 4561956 | tf_op jit(solution)/shard_map/jit(_where)/select_n | solution.py:61
  21.7 1.4 %fusion.35 = f32[2,15,34,130]{3,2,1,0:T(8,128)S(1)} fusion(f32[2,15,36,132]{3,2,1,0:T(8,128)S(1)} %fusion.44, f32[15,34,130]{2,1,0:T(8,128)S(1)} %get-tuple-element.11, f32[15,34,130]{2,1,0:T(8,128)S(1)} %get-tuple-element.12, f32[15,34,130]{2,1,0:T(8,128)S(1)} %get-tuple-element.10, f32[15,34,130]{2,1,0:T(8,128)S(1)} %get-tuple-element.9, ...), kind=kLoop, calls=%fused_computation.41 | loop fusion | flops 1723800 | bytes 4243234 | tf_op jit(solution)/shard_map/jit(_where)/select_n | solution.py:61
  23.1 0.6 fusion.89
  23.8 0.7 %select_reduce_fusion = bf16[30,1024]{1,0:T(8,128)(2,1)S(1)} fusion(pred[32,1024]{1,0:T(8,128)(4,1)S(1)} %iota_compare_fusion.1, bf16[30,32,128]{2,1,0:T(8,128)(2,1)S(1)} %bitcast_convert_fusion, s32[1024]{0:T(1024)S(1)} %bitcast.94), kind=kOutput, calls=%fused_computation.35 | convolution fusion | flops 253724672 | bytes 344064 | tf_op jit(solution)/shard_map/dot_general | solution.py:120
  24.5 14.2 %all_to_all.10 = bf16[30,8,256]{2,0,1:T(8,128)(2,1)S(1)} all-to-all(bf16[30,8,256]{2,0,1:T(8,128)(2,1)S(1)} %bitcast.83), channel_id=1, replica_groups=mesh['lat'=4,'lon'=2,'lev'=4] {'lon','lev'}, dimensions={1} | all-to-all | bytes 245760 | tf_op jit(solution)/shard_map/all_to_all | solution.py:145
  39.1 3.7 %fusion.15 = bf16[1024,512]{0,1:T(8,128)(2,1)S(1)} fusion(bf16[1,2,1024,1024]{3,2,1,0:T(8,128)(2,1)} %param.12, bf16[120,512]{1,0:T(8,128)(2,1)S(1)} %bitcast.89, bf16[1,120,1024]{2,1,0:T(8,128)(2,1)S(1)} %copy-done), kind=kOutput, calls=%fused_computation.18 | convolution fusion | flops 1209008128 | bytes 3514368 | tf_op jit(solution)/shard_map/dot_general | solution.py:91
  42.8 3.5 %fusion.64 = bf16[120,512]{1,0:T(8,128)(2,1)S(1)} fusion(bf16[1024,512]{0,1:T(8,128)(2,1)S(1)} %fusion.15, bf16[1,2,1024,1024]{3,2,1,0:T(8,128)(2,1)} %param.12, bf16[1,1024,120]{1,2,0:T(8,128)(2,1)S(1)} %copy-done.5), kind=kOutput, calls=%fused_computation.67 | convolution fusion | flops 1204350976 | bytes 3514368 | tf_op jit(solution)/shard_map/dot_general | solution.py:95
  46.5 0.7 %copy.78 = bf16[30,8,256]{2,0,1:T(8,128)(2,1)} copy(bf16[30,8,256]{2,1,0:T(8,128)(2,1)S(1)} %reshape.127) | data formatting | bytes 245760 | tf_op jit(solution)/shard_map/reshape | solution.py:157
  47.1 3.4 %all-to-all-start.1 = ((bf16[30,8,256]{2,0,1:T(8,128)(2,1)}), bf16[30,8,256]{2,0,1:T(8,128)(2,1)S(1)}, u32[]{:S(2)}, u32[]{:S(2)}) async-start(bf16[30,8,256]{2,0,1:T(8,128)(2,1)} %copy.78), calls=%async_computation.1 | async-start | bytes 262144 | tf_op jit(solution)/shard_map/all_to_all | solution.py:159
  50.6 7.4 %all-to-all-done.1 = bf16[30,8,256]{2,0,1:T(8,128)(2,1)S(1)} async-done(((bf16[30,8,256]{2,0,1:T(8,128)(2,1)}), bf16[30,8,256]{2,0,1:T(8,128)(2,1)S(1)}, u32[]{:S(2)}, u32[]{:S(2)}) %all-to-all-start.1) | async-done | bytes 122912 | tf_op jit(solution)/shard_map/all_to_all | solution.py:159
  58.1 0.2 broadcast_select_fusion
  58.4 1.5 %fusion.51 = f32[30,32,128]{2,1,0:T(8,128)} fusion(f32[30,32,128]{2,1,0:T(8,128)S(1)} %bitcast.82, pred[32,1024]{1,0:T(8,128)(4,1)S(1)} %iota_compare_fusion.1, bf16[30,1024]{1,0:T(8,128)(2,1)S(1)} %bitcast.92, s32[1024]{0:T(1024)S(1)} %bitcast.95), kind=kOutput, calls=%fused_computation.64 | convolution fusion | flops 252895232 | bytes 1081344 | tf_op jit(solution)/shard_map/dot_general | solution.py:170
  (40 shorter events, 0.9 us)
Async XLA Ops:
  0.0 39.1 %copy-start = (bf16[1,120,1024]{2,1,0:T(8,128)(2,1)S(1)}, bf16[1,120,1024]{2,1,0:T(8,128)(2,1)}, u32[]{:S(2)}) copy-start(bf16[1,120,1024]{2,1,0:T(8,128)(2,1)} %param.11) | copy-start | bytes 737284
  0.0 7.1 %copy-start.3 = (f32[15,32,128]{2,1,0:T(8,128)S(1)}, f32[15,32,128]{2,1,0:T(8,128)}, u32[]{:S(2)}) copy-start(f32[15,32,128]{2,1,0:T(8,128)} %param.8) | copy-start | bytes 737284
  0.0 7.2 %copy-start.2 = (f32[2,15,32,128]{3,2,1,0:T(8,128)S(1)}, f32[2,15,32,128]{3,2,1,0:T(8,128)}, u32[]{:S(2)}) copy-start(f32[2,15,32,128]{3,2,1,0:T(8,128)} %param.7) | copy-start | bytes 1474564
  1.2 5.9 %collective-permute-start.1 = (f32[45,384]{1,0:T(8,128)S(1)}, f32[45,384]{1,0:T(8,128)S(1)}, u32[]{:S(2)}, u32[]{:S(2)}) collective-permute-start(f32[45,384]{1,0:T(8,128)S(1)} %bitcast.90), channel_id=1, source_target_pairs={{8,0},{16,8},{24,16},{9,1},{17,9},{25,17},{10,2},{18,10},{26,18},{... | collective-permute-start | bytes 207368 | tf_op jit(solution)/shard_map/ppermute | solution.py:12
  2.5 4.6 %collective-permute-start = (f32[45,384]{1,0:T(8,128)S(1)}, f32[45,384]{1,0:T(8,128)S(1)}, u32[]{:S(2)}, u32[]{:S(2)}) collective-permute-start(f32[45,384]{1,0:T(8,128)S(1)} %bitcast.91), channel_id=1, source_target_pairs={{0,8},{8,16},{16,24},{1,9},{9,17},{17,25},{2,10},{10,18},{18,26},{... | collective-permute-start | bytes 207368 | tf_op jit(solution)/shard_map/ppermute | solution.py:12
  8.3 6.5 %collective-permute-start.2 = (f32[45,228]{0,1:T(8,128)S(1)}, f32[45,228]{0,1:T(8,128)S(1)}, u32[]{:S(2)}, u32[]{:S(2)}) collective-permute-start(f32[45,228]{0,1:T(8,128)S(1)} %copy.80), channel_id=1, source_target_pairs={{0,4},{4,0},{1,5},{5,1},{2,6},{6,2},{3,7},{7,3},{8,12},{12,8},{9,1... | collective-permute-start | bytes 123128 | tf_op jit(solution)/shard_map/ppermute | solution.py:12
  16.9 1.3 %copy-start.1 = (f32[45,38,134]{2,1,0:T(8,128)}, f32[45,38,134]{2,1,0:T(8,128)S(1)}, u32[]{:S(2)}) copy-start(f32[45,38,134]{2,1,0:T(8,128)S(1)} %pad_maximum_fusion) | copy-start | bytes 2749684
  19.0 1.3 %slice-start = ((f32[45,38,134]{2,1,0:T(8,128)}), f32[30,38,134]{2,1,0:T(8,128)S(1)}, s32[]{:S(2)}) async-start(f32[45,38,134]{2,1,0:T(8,128)} %copy-done.1), calls=%async_computation.2 | async-start | bytes 2457600 | tf_op jit(solution)/shard_map/slice | solution.py:70
  39.1 3.8 %copy-start.5 = (bf16[1,1024,120]{1,2,0:T(8,128)(2,1)S(1)}, bf16[1,1024,120]{1,2,0:T(8,128)(2,1)}, u32[]{:S(2)}) copy-start(bf16[1,1024,120]{1,2,0:T(8,128)(2,1)} %param.13) | copy-start | bytes 737284
  42.8 7.7 %copy-start.4 = (s32[1,1024,1]{1,2,0:T(1,128)S(1)}, s32[1,1024,1]{1,2,0:T(1,128)}, u32[]{:S(2)}) copy-start(s32[1,1024,1]{1,2,0:T(1,128)} %param.10) | copy-start | bytes 12292
  47.1 10.8 %all-to-all-start.1 = ((bf16[30,8,256]{2,0,1:T(8,128)(2,1)}), bf16[30,8,256]{2,0,1:T(8,128)(2,1)S(1)}, u32[]{:S(2)}, u32[]{:S(2)}) async-start(bf16[30,8,256]{2,0,1:T(8,128)(2,1)} %copy.78), calls=%async_computation.1 | async-start | bytes 262144 | tf_op jit(solution)/shard_map/all_to_all | solution.py:159

commit v7 on v6

--- a/solution.py
+++ b/solution.py
@@ -12,7 +12,7 @@
     return lax.ppermute(flat, axis, pairs).reshape(piece.shape)
 
 
-def halo_exchange(cells, width):
+def lat_exchange(cells, width):
     lat_count = lax.axis_size("lat")
     from_above = dense_ppermute(
         cells[..., cells.shape[-2] - width :, :], "lat", [(i, i + 1) for i in range(lat_count - 1)]
@@ -20,21 +20,19 @@
     from_below = dense_ppermute(
         cells[..., :width, :], "lat", [(i + 1, i) for i in range(lat_count - 1)]
     )
-    cells = jnp.concatenate([from_above, cells, from_below], axis=-2)
+    return jnp.concatenate([from_above, cells, from_below], axis=-2)
+
+
+def lon_exchange(cells, width):
     lon_count = lax.axis_size("lon")
     left = cells[..., :width]
     right = cells[..., cells.shape[-1] - width :]
     if lon_count == 2:
         both = dense_ppermute(jnp.concatenate([right, left], axis=-1), "lon", [(0, 1), (1, 0)])
-        from_left, from_right = both[..., :width], both[..., width:]
-    else:
-        from_left = dense_ppermute(
-            right, "lon", [(i, (i + 1) % lon_count) for i in range(lon_count)]
-        )
-        from_right = dense_ppermute(
-            left, "lon", [((i + 1) % lon_count, i) for i in range(lon_count)]
-        )
-    return jnp.concatenate([from_left, cells, from_right], axis=-1)
+        return both[..., :width], both[..., width:]
+    from_left = dense_ppermute(right, "lon", [(i, (i + 1) % lon_count) for i in range(lon_count)])
+    from_right = dense_ppermute(left, "lon", [((i + 1) % lon_count, i) for i in range(lon_count)])
+    return from_left, from_right
 
 
 def substep(values, coefficients):
@@ -61,14 +59,9 @@
     return jnp.where(inside[:, None], values, 0.0)
 
 
-def dynamics(fields, diffusivity):
-    kinds, level_rows, lat_rows, lon_cols = fields.shape
-    stacked = jnp.concatenate(
-        [fields.reshape(kinds * level_rows, lat_rows, lon_cols), diffusivity], axis=0
-    )
-    stacked = halo_exchange(stacked, STEPS)
+def run_steps(stacked, kinds, level_rows, lat_rows):
     values = stacked[: kinds * level_rows].reshape(
-        kinds, level_rows, lat_rows + 2 * STEPS, lon_cols + 2 * STEPS
+        (kinds, level_rows) + stacked.shape[1:]
     )
     kappa = stacked[kinds * level_rows :]
     for repeat in range(STEPS):
@@ -79,6 +72,21 @@
         if rim:
             values = clear_outside(values, rim, lat_rows)
     return values
+
+
+def dynamics(fields, diffusivity):
+    kinds, level_rows, lat_rows, lon_cols = fields.shape
+    stacked = jnp.concatenate(
+        [fields.reshape(kinds * level_rows, lat_rows, lon_cols), diffusivity], axis=0
+    )
+    stacked = lat_exchange(stacked, STEPS)
+    from_left, from_right = lon_exchange(stacked, STEPS)
+    interior = run_steps(stacked, kinds, level_rows, lat_rows)
+    left_strip = jnp.concatenate([from_left, stacked[..., : 2 * STEPS]], axis=-1)
+    right_strip = jnp.concatenate([stacked[..., lon_cols - 2 * STEPS :], from_right], axis=-1)
+    left_part = run_steps(left_strip, kinds, level_rows, lat_rows)
+    right_part = run_steps(right_strip, kinds, level_rows, lat_rows)
+    return jnp.concatenate([left_part, interior, right_part], axis=-1)
 
 
 def network(features, w_first, w_middle, w_last):

time: 60.3 us -> 131 us (2.17)
  local copies, waits for them, and re-layouts: 4.54 us -> 54.2 us
  other arithmetic: 9.62 us -> 35 us
  waiting for transfers between devices: 10.9 us -> 8.19 us
  blocking collectives: 14.2 us -> 12.4 us
  starting transfers between devices: 10.7 us -> 9.37 us
    mul x3 -> x10, other arithmetic: 1.93 us -> 23.1 us  [substep(): face_coef = 0.5 * (middle + coefficients[:, lat_cut, lon_cut])]
    unnamed x20 -> x104, local copies, waits for them, and re-layouts: 1.6 us -> 20.4 us
    mul x0 -> x8, local copies, waits for them, and re-layouts: none -> 15.6 us  [substep(): face_coef = 0.5 * (middle + coefficients[:, lat_cut, lon_cut])]
    reshape x3 -> x5, local copies, waits for them, and re-layouts: 0.08 us -> 5.78 us  [dense_ppermute(): return lax.ppermute(flat, axis, pairs).reshape(piece.shape)]
    concatenate x3 -> x7, other arithmetic: 1.44 us -> 6.24 us  [the longest x2 2.28 us: dynamics(): jnp.concatenate([fields.reshape(kinds * level_rows, lat_rows, lon_cols),...]
    ppermute x3, waiting for transfers between devices: 3.5 us -> 0.01 us  [dense_ppermute(): return lax.ppermute(flat, axis, pairs).reshape(piece.shape)]
    reshape x0 -> x2, local copies, waits for them, and re-layouts: none -> 3.16 us  [run_steps(): stacked[:kinds * level_rows]]
    slice x4 -> x9, local copies, waits for them, and re-layouts: 1.25 us -> 3.76 us  [the longest x4 1.87 us: substep(): face_coef = 0.5 * (middle + coefficients[:, lat_cut, lon_cut])]
  transfers between devices with their start and end apart: 4 -> 4, of which waited for: 2 -> 1; matrix products, arithmetic and copies ran while one was open for 3% -> 42% of each run, Pallas kernels for 0% -> 0%
where the time goes in v7:
time: 131 us; the launch traced here: 129 us
  local copies, waits for them, and re-layouts  54.2 us (41%)
  other arithmetic  35 us (27%)
  blocking collectives  12.4 us (9%)
  matrix products  9.38 us (7%)
  starting transfers between devices  9.37 us (7%)
  waiting for transfers between devices  8.19 us (6%)
    mul x10, other arithmetic, substep(): face_coef = 0.5 * (middle + coefficients[:, lat_cut, lon_cut])  23.1 us
    unnamed x104, local copies, waits for them, and re-layouts  20.4 us
    mul x8, local copies, waits for them, and re-layouts, substep(): face_coef = 0.5 * (middle + coefficients[:, lat_cut, lon_cut])  15.6 us
    all_to_all x1, blocking collectives, on_device(): lax.all_to_all(send_buffer, ('lon', 'lev'), split_axis=1, concat_axis=1,...  12.4 us
    all_to_all x1, waiting for transfers between devices, on_device(): lax.all_to_all(outgoing, ('lon', 'lev'), split_axis=1, concat_axis=1, til...  8.18 us
    ppermute x3, starting transfers between devices, dense_ppermute(): return lax.ppermute(flat, axis, pairs).reshape(piece.shape)  6 us
    reshape x5, local copies, waits for them, and re-layouts, dense_ppermute(): return lax.ppermute(flat, axis, pairs).reshape(piece.shape)  5.78 us
    dot_general x1, matrix products, network(): lax.dot_general(w_middle[layer_no], hidden, contract, preferred_element_t...  3.74 us
  transfers between devices with their start and end apart: 4, of which 1 were waited for; matrix products, arithmetic and copies ran while one was open for 42% of the time, Pallas kernels for 0%

profile of v7, /device:TPU:0, one launch (start us, length us, event | category | flops | bytes accessed | tf_op | source)
XLA Modules:
  0.0 129.4 jit_solution(3453059920269658943)
XLA Ops:
  1.1 2.4 %collective-permute-start = (f32[45,384]{1,0:T(8,128)S(1)}, f32[45,384]{1,0:T(8,128)S(1)}, u32[]{:S(2)}, u32[]{:S(2)}) collective-permute-start(f32[45,384]{1,0:T(8,128)S(1)} %bitcast.92), channel_id=1, source_target_pairs={{0,8},{8,16},{16,24},{1,9},{9,17},{17,25},{2,10},{10,18},{18,26},{... | collective-permute-start | bytes 207368 | tf_op jit(solution)/shard_map/ppermute | solution.py:12
  6.6 2.5 %copy.260 = f32[45,32,128]{1,0,2:T(8,128)} copy(f32[45,32,128]{2,1,0:T(8,128)S(1)} %pad_maximum_fusion) | data formatting | bytes 1474560 | tf_op jit(solution)/shard_map/concatenate | solution.py:79
  17.6 1.6 %fusion.227 = (f32[45,38,6]{2,1,0:T(8,128)}, f32[45,38,6]{2,1,0:T(8,128)}) fusion(f32[45,38,128]{2,1,0:T(8,128)S(1)} %pad_maximum_fusion.1), kind=kLoop, calls=%fused_computation.333 | loop fusion | bytes 164160 | tf_op jit(solution)/shard_map/slice | solution.py:85
  19.2 2.4 %copy.259 = f32[45,3,128]{1,0,2:T(8,128)} copy(f32[45,3,128]{2,1,0:T(4,128)S(1)} %reshape.146) | data formatting | bytes 138240 | tf_op jit(solution)/shard_map/reshape | solution.py:12
  21.6 2.4 %copy.262 = f32[45,3,128]{1,0,2:T(8,128)} copy(f32[45,3,128]{2,1,0:T(4,128)S(1)} %reshape.148) | data formatting | bytes 138240 | tf_op jit(solution)/shard_map/reshape | solution.py:12
  28.0 2.3 %collective-permute-start.2 = (f32[45,228]{0,1:T(8,128)}, f32[45,228]{0,1:T(8,128)}, u32[]{:S(2)}, u32[]{:S(2)}) collective-permute-start(f32[45,228]{0,1:T(8,128)} %copy.291), channel_id=1, source_target_pairs={{0,4},{4,0},{1,5},{5,1},{2,6},{6,2},{3,7},{7,3},{8,12},{12,8},{9,1... | collective-permute-start | bytes 123128 | tf_op jit(solution)/shard_map/ppermute | solution.py:12
  30.3 2.4 %copy.299 = f32[15,34,124]{1,0,2:T(8,128)} copy(f32[15,34,124]{2,1,0:T(8,128)} %get-tuple-element.35) | data formatting | bytes 505920
  32.7 2.4 %copy.300 = f32[15,34,124]{1,0,2:T(8,128)} copy(f32[15,34,124]{2,1,0:T(8,128)} %get-tuple-element.33) | data formatting | bytes 505920
  35.1 2.4 %copy.301 = f32[15,34,124]{1,0,2:T(8,128)} copy(f32[15,34,124]{2,1,0:T(8,128)} %get-tuple-element.34) | data formatting | bytes 505920
  37.5 5.7 %fusion.58 = (f32[15,34,124]{1,0,2:T(8,128)}, f32[15,34,124]{1,0,2:T(8,128)}, f32[15,34,124]{1,0,2:T(8,128)}, f32[15,34,124]{1,0,2:T(8,128)}) fusion(f32[15,34,124]{1,0,2:T(8,128)} %copy.299, f32[45,32,128]{1,0,2:T(8,128)S(1)} %copy-done.3, f32[45,3,128]{1,0,2:T(8,128)} %copy.259, f32[45,3,128]{1,0,2:T(8,128)} %copy.262, f32[15,34,124]{1,0,2:T(8,128)} %copy.301, ...), kind=kLoop, calls=%fused_computation.55 | loop fusion | flops 632400 | bytes 2646240 | tf_op jit(solution)/shard_map/mul | solution.py:49
  43.2 2.3 %copy.265 = f32[15,34,124]{2,1,0:T(8,128)} copy(f32[15,34,124]{1,0,2:T(8,128)} %get-tuple-element.19) | data formatting | bytes 505920 | tf_op jit(solution)/shard_map/mul | solution.py:49
  45.6 2.3 %copy.266 = f32[15,34,124]{2,1,0:T(8,128)} copy(f32[15,34,124]{1,0,2:T(8,128)} %get-tuple-element.20) | data formatting | bytes 505920 | tf_op jit(solution)/shard_map/mul | solution.py:49
  47.9 2.3 %copy.268 = f32[15,34,124]{2,1,0:T(8,128)} copy(f32[15,34,124]{1,0,2:T(8,128)} %get-tuple-element.26) | data formatting | bytes 505920 | tf_op jit(solution)/shard_map/mul | solution.py:49
  50.2 2.3 %copy.270 = f32[15,34,124]{2,1,0:T(8,128)} copy(f32[15,34,124]{1,0,2:T(8,128)} %get-tuple-element.25) | data formatting | bytes 505920 | tf_op jit(solution)/shard_map/mul | solution.py:49
  52.6 5.7 %fusion.60 = (f32[15,32,122]{1,0,2:T(8,128)}, f32[15,32,122]{1,0,2:T(8,128)}, f32[15,32,122]{1,0,2:T(8,128)}, f32[15,32,122]{1,0,2:T(8,128)}) fusion(f32[15,32,122]{1,0,2:T(8,128)} %copy.302, f32[45,32,128]{1,0,2:T(8,128)S(1)} %copy-done.3, f32[45,3,128]{1,0,2:T(8,128)} %copy.259, f32[45,3,128]{1,0,2:T(8,128)} %copy.262, f32[15,32,122]{1,0,2:T(8,128)} %copy.304, ...), kind=kLoop, calls=%fused_computation.61 | loop fusion | flops 585600 | bytes 2515200 | tf_op jit(solution)/shard_map/mul | solution.py:49
  58.3 2.4 %copy.272 = f32[15,32,122]{2,1,0:T(8,128)} copy(f32[15,32,122]{1,0,2:T(8,128)} %get-tuple-element.21) | data formatting | bytes 468480 | tf_op jit(solution)/shard_map/mul | solution.py:49
  60.7 2.4 %copy.273 = f32[15,32,122]{2,1,0:T(8,128)} copy(f32[15,32,122]{1,0,2:T(8,128)} %get-tuple-element.22) | data formatting | bytes 468480 | tf_op jit(solution)/shard_map/mul | solution.py:49
  64.6 1.9 %fusion.74 = f32[2,15,36,126]{3,2,1,0:T(8,128)S(1)} fusion(f32[2,15,38,128]{3,2,1,0:T(8,128)S(1)} %bitcast.80, f32[15,36,126]{2,1,0:T(8,128)} %get-tuple-element.39, f32[15,36,126]{2,1,0:T(8,128)S(1)} %copy-done.19, f32[15,36,126]{2,1,0:T(8,128)} %get-tuple-element.38, f32[15,36,126]{2,1,0:T(8,128)S(1)} %copy-done.18, pred[36]{0:T(512)(128)(4,1)S(1)} %compare_and_fusion), kind=kLoop, calls=%fused_computation.106 | loop fusion | flops 1769040 | bytes 4354596 | tf_op jit(solution)/shard_map/jit(_where)/select_n | solution.py:59
  75.5 1.7 %fusion.101 = f32[30,38,9]{1,0,2:T(8,128)} fusion(f32[45,38,6]{1,0,2:T(8,128)} %copy.305, f32[45,38,3]{1,0,2:T(8,128)} %copy.306), kind=kLoop, calls=%fused_computation.165 | loop fusion | flops 10260 | bytes 102600 | tf_op jit(solution)/shard_map/concatenate | solution.py:86
  77.2 1.7 %fusion.144 = (f32[15,36,7]{1,0,2:T(8,128)}, f32[15,36,7]{1,0,2:T(8,128)S(1)}, f32[15,36,7]{1,0,2:T(8,128)}, f32[15,36,7]{1,0,2:T(8,128)S(1)}) fusion(f32[45,38,6]{1,0,2:T(8,128)} %copy.305, f32[45,38,3]{1,0,2:T(8,128)} %copy.306, f32[45,38,6]{1,0,2:T(8,128)S(1)} %copy.295, f32[45,38,3]{1,0,2:T(8,128)} %copy.294), kind=kLoop, calls=%fused_computation.228 | loop fusion | flops 30240 | bytes 183600 | tf_op jit(solution)/shard_map/mul | solution.py:49
  80.3 1.6 %fusion.189 = (f32[15,34,5]{1,0,2:T(8,128)}, f32[15,34,5]{1,0,2:T(8,128)}, f32[15,34,5]{1,0,2:T(8,128)}, f32[15,34,5]{1,0,2:T(8,128)}) fusion(f32[45,38,6]{1,0,2:T(8,128)} %copy.305, f32[45,38,3]{1,0,2:T(8,128)} %copy.306, f32[45,38,6]{1,0,2:T(8,128)S(1)} %copy.295, f32[45,38,3]{1,0,2:T(8,128)} %copy.294), kind=kLoop, calls=%fused_computation.281 | loop fusion | flops 20400 | bytes 163920 | tf_op jit(solution)/shard_map/mul | solution.py:49
  82.0 1.7 %fusion.147 = (f32[15,36,7]{1,0,2:T(8,128)}, f32[15,36,7]{1,0,2:T(8,128)}, f32[15,36,7]{1,0,2:T(8,128)}) fusion(f32[15,36,7]{1,0,2:T(8,128)S(1)} %get-tuple-element.14, f32[45,38,6]{1,0,2:T(8,128)} %copy.305, f32[45,38,3]{1,0,2:T(8,128)} %copy.306), kind=kLoop, calls=%fused_computation.231 | loop fusion | flops 34020 | bytes 122040 | tf_op jit(solution)/shard_map/mul | solution.py:49
  83.7 1.6 %fusion.160 = (f32[15,36,7]{1,0,2:T(8,128)}, f32[15,36,7]{1,0,2:T(8,128)}, f32[15,36,7]{1,0,2:T(8,128)}) fusion(f32[15,36,7]{1,0,2:T(8,128)S(1)} %get-tuple-element.74, f32[45,38,6]{1,0,2:T(8,128)S(1)} %copy.295, f32[45,38,3]{1,0,2:T(8,128)} %copy.294), kind=kLoop, calls=%fused_computation.244 | loop fusion | flops 34020 | bytes 122040 | tf_op jit(solution)/shard_map/mul | solution.py:49
  85.3 1.6 %reshape.153 = f32[2,15,38,9]{2,1,0,3:T(8,128)} reshape(f32[30,38,9]{1,0,2:T(8,128)} %fusion.101) | data formatting | bytes 82080 | tf_op jit(solution)/shard_map/reshape | solution.py:63
  86.9 1.6 %reshape.151 = f32[2,15,38,9]{2,1,0,3:T(8,128)} reshape(f32[30,38,9]{1,0,2:T(8,128)} %fusion.102) | data formatting | bytes 82080 | tf_op jit(solution)/shard_map/reshape | solution.py:63
  90.5 1.8 %fusion.211 = (f32[15,32,3]{1,0,2:T(8,128)S(1)}, f32[15,32,3]{1,0,2:T(8,128)}, f32[15,32,3]{1,0,2:T(8,128)}, f32[15,32,3]{1,0,2:T(8,128)S(1)}, f32[15,32,3]{1,0,...) fusion(f32[15,32,3]{1,0,2:T(8,128)} %copy.297, f32[45,3,128]{1,0,2:T(8,128)} %copy.262, ...), kind=kLoop, calls=%fused_computation.310 | loop fusion | flops 31680 | bytes 1067760 | tf_op jit(solution)/shard_map/mul | solution.py:49
  95.2 12.4 %all_to_all.10 = bf16[30,8,256]{2,0,1:T(8,128)(2,1)S(1)} all-to-all(bf16[30,8,256]{2,0,1:T(8,128)(2,1)S(1)} %bitcast.85), channel_id=1, replica_groups=mesh['lat'=4,'lon'=2,'lev'=4] {'lon','lev'}, dimensions={1} | all-to-all | bytes 245760 | tf_op jit(solution)/shard_map/all_to_all | solution.py:153
  107.9 3.7 %fusion.15 = bf16[1024,512]{0,1:T(8,128)(2,1)S(1)} fusion(bf16[1,2,1024,1024]{3,2,1,0:T(8,128)(2,1)} %param.12, bf16[120,512]{1,0:T(8,128)(2,1)S(1)} %bitcast.91, bf16[1,120,1024]{2,1,0:T(8,128)(2,1)S(1)} %copy-done), kind=kOutput, calls=%fused_computation.18 | convolution fusion | flops 1209008128 | bytes 3514368 | tf_op jit(solution)/shard_map/dot_general | solution.py:99
  111.6 3.4 %fusion.46 = bf16[120,512]{1,0:T(8,128)(2,1)S(1)} fusion(bf16[1024,512]{0,1:T(8,128)(2,1)S(1)} %fusion.15, bf16[1,2,1024,1024]{3,2,1,0:T(8,128)(2,1)} %param.12, bf16[1,1024,120]{1,2,0:T(8,128)(2,1)S(1)} %copy-done.40), kind=kOutput, calls=%fused_computation.43 | convolution fusion | flops 1204350976 | bytes 3514368 | tf_op jit(solution)/shard_map/dot_general | solution.py:103
  115.9 3.4 %all-to-all-start.1 = ((bf16[30,8,256]{2,0,1:T(8,128)(2,1)}), bf16[30,8,256]{2,0,1:T(8,128)(2,1)S(1)}, u32[]{:S(2)}, u32[]{:S(2)}) async-start(bf16[30,8,256]{2,0,1:T(8,128)(2,1)} %copy.289), calls=%async_computation.1 | async-start | bytes 262144 | tf_op jit(solution)/shard_map/all_to_all | solution.py:167
  119.3 8.2 %all-to-all-done.1 = bf16[30,8,256]{2,0,1:T(8,128)(2,1)S(1)} async-done(((bf16[30,8,256]{2,0,1:T(8,128)(2,1)}), bf16[30,8,256]{2,0,1:T(8,128)(2,1)S(1)}, u32[]{:S(2)}, u32[]{:S(2)}) %all-to-all-start.1) | async-done | bytes 122912 | tf_op jit(solution)/shard_map/all_to_all | solution.py:167
  127.9 1.5 %fusion.33 = f32[30,32,128]{2,1,0:T(8,128)} fusion(f32[30,32,128]{2,1,0:T(8,128)S(1)} %bitcast.84, pred[32,1024]{1,0:T(8,128)(4,1)S(1)} %copy-done.37, bf16[30,1024]{1,0:T(8,128)(2,1)S(1)} %bitcast.94, s32[1024]{0:T(1024)S(1)} %bitcast.97), kind=kOutput, calls=%fused_computation.37 | convolution fusion | flops 252895232 | bytes 1081344 | tf_op jit(solution)/shard_map/dot_general | solution.py:178
  (158 shorter events, 34.5 us)
Async XLA Ops:
  0.0 107.8 %copy-start = (bf16[1,120,1024]{2,1,0:T(8,128)(2,1)S(1)}, bf16[1,120,1024]{2,1,0:T(8,128)(2,1)}, u32[]{:S(2)}) copy-start(bf16[1,120,1024]{2,1,0:T(8,128)(2,1)} %param.11) | copy-start | bytes 737284
  0.0 6.1 %copy-start.5 = (f32[15,32,128]{2,1,0:T(8,128)S(1)}, f32[15,32,128]{2,1,0:T(8,128)}, u32[]{:S(2)}) copy-start(f32[15,32,128]{2,1,0:T(8,128)} %param.8) | copy-start | bytes 737284
  1.1 16.0 %collective-permute-start = (f32[45,384]{1,0:T(8,128)S(1)}, f32[45,384]{1,0:T(8,128)S(1)}, u32[]{:S(2)}, u32[]{:S(2)}) collective-permute-start(f32[45,384]{1,0:T(8,128)S(1)} %bitcast.92), channel_id=1, source_target_pairs={{0,8},{8,16},{16,24},{1,9},{9,17},{17,25},{2,10},{10,18},{18,26},{... | collective-permute-start | bytes 207368 | tf_op jit(solution)/shard_map/ppermute | solution.py:12
  3.5 13.6 %collective-permute-start.1 = (f32[45,384]{1,0:T(8,128)S(1)}, f32[45,384]{1,0:T(8,128)S(1)}, u32[]{:S(2)}, u32[]{:S(2)}) collective-permute-start(f32[45,384]{1,0:T(8,128)S(1)} %bitcast.93), channel_id=1, source_target_pairs={{8,0},{16,8},{24,16},{9,1},{17,9},{25,17},{10,2},{18,10},{26,18},{... | collective-permute-start | bytes 207368 | tf_op jit(solution)/shard_map/ppermute | solution.py:12
  10.6 5.8 %copy-start.38 = (s32[1,1024]{1,0:T(1,128)S(1)}, s32[1,1024]{1,0:T(1,128)}, u32[]{:S(2)}) copy-start(s32[1,1024]{1,0:T(1,128)} %param.9) | copy-start | bytes 12292
  12.2 5.0 %copy-start.6 = (f32[2,15,32,128]{3,2,1,0:T(8,128)S(1)}, f32[2,15,32,128]{3,2,1,0:T(8,128)}, u32[]{:S(2)}) copy-start(f32[2,15,32,128]{3,2,1,0:T(8,128)} %param.7) | copy-start | bytes 1474564
  17.3 8.1 %copy-start.1 = (f32[45,38,128]{2,1,0:T(8,128)}, f32[45,38,128]{2,1,0:T(8,128)S(1)}, u32[]{:S(2)}) copy-start(f32[45,38,128]{2,1,0:T(8,128)S(1)} %pad_maximum_fusion.1) | copy-start | bytes 2626564
  27.2 10.3 %copy-start.3 = (f32[45,32,128]{1,0,2:T(8,128)S(1)}, f32[45,32,128]{1,0,2:T(8,128)}, u32[]{:S(2)}) copy-start(f32[45,32,128]{1,0,2:T(8,128)} %copy.260) | copy-start | bytes 2211844
  28.0 45.1 %collective-permute-start.2 = (f32[45,228]{0,1:T(8,128)}, f32[45,228]{0,1:T(8,128)}, u32[]{:S(2)}, u32[]{:S(2)}) collective-permute-start(f32[45,228]{0,1:T(8,128)} %copy.291), channel_id=1, source_target_pairs={{0,4},{4,0},{1,5},{5,1},{2,6},{6,2},{3,7},{7,3},{8,12},{12,8},{9,1... | collective-permute-start | bytes 123128 | tf_op jit(solution)/shard_map/ppermute | solution.py:12
  58.2 4.8 %copy-start.8 = (f32[15,32,122]{1,0,2:T(8,128)S(1)}, f32[15,32,122]{1,0,2:T(8,128)}, u32[]{:S(2)}) copy-start(f32[15,32,122]{1,0,2:T(8,128)} %get-tuple-element.28) | copy-start | bytes 702724
  58.2 5.9 %copy-start.7 = (f32[15,32,122]{1,0,2:T(8,128)S(1)}, f32[15,32,122]{1,0,2:T(8,128)}, u32[]{:S(2)}) copy-start(f32[15,32,122]{1,0,2:T(8,128)} %get-tuple-element.27) | copy-start | bytes 702724
  60.7 3.9 %slice-start = ((f32[45,38,128]{2,1,0:T(8,128)}), f32[30,38,128]{2,1,0:T(8,128)S(1)}, s32[]{:S(2)}) async-start(f32[45,38,128]{2,1,0:T(8,128)} %copy-done.1), calls=%async_computation.2 | async-start | bytes 1228800 | tf_op jit(solution)/shard_map/slice | solution.py:63
  60.7 3.9 %copy-start.18 = (f32[15,36,126]{2,1,0:T(8,128)S(1)}, f32[15,36,126]{2,1,0:T(8,128)}, u32[]{:S(2)}) copy-start(f32[15,36,126]{2,1,0:T(8,128)} %get-tuple-element.36) | copy-start | bytes 816484
  60.7 3.9 %copy-start.19 = (f32[15,36,126]{2,1,0:T(8,128)S(1)}, f32[15,36,126]{2,1,0:T(8,128)}, u32[]{:S(2)}) copy-start(f32[15,36,126]{2,1,0:T(8,128)} %get-tuple-element.37) | copy-start | bytes 816484
  64.6 1.9 %copy-start.14 = (f32[15,34,124]{2,1,0:T(8,128)S(1)}, f32[15,34,124]{2,1,0:T(8,128)}, u32[]{:S(2)}) copy-start(f32[15,34,124]{2,1,0:T(8,128)} %copy.265) | copy-start | bytes 758884
  64.6 1.9 %copy-start.15 = (f32[15,34,124]{2,1,0:T(8,128)S(1)}, f32[15,34,124]{2,1,0:T(8,128)}, u32[]{:S(2)}) copy-start(f32[15,34,124]{2,1,0:T(8,128)} %copy.266) | copy-start | bytes 758884
  64.6 1.9 %copy-start.16 = (f32[15,34,124]{2,1,0:T(8,128)S(1)}, f32[15,34,124]{2,1,0:T(8,128)}, u32[]{:S(2)}) copy-start(f32[15,34,124]{2,1,0:T(8,128)} %copy.268) | copy-start | bytes 758884
  64.6 1.9 %copy-start.17 = (f32[15,34,124]{2,1,0:T(8,128)S(1)}, f32[15,34,124]{2,1,0:T(8,128)}, u32[]{:S(2)}) copy-start(f32[15,34,124]{2,1,0:T(8,128)} %copy.270) | copy-start | bytes 758884
  75.5 14.9 %copy-start.4 = (f32[45,32,128]{1,0,2:T(8,128)S(1)}, f32[45,32,128]{1,0,2:T(8,128)}, u32[]{:S(2)}) copy-start(f32[45,32,128]{1,0,2:T(8,128)} %copy.260) | copy-start | bytes 2211844
  90.4 1.9 %copy-start.11 = (f32[2,15,38,9]{2,1,0,3:T(8,128)S(1)}, f32[2,15,38,9]{2,1,0,3:T(8,128)}, u32[]{:S(2)}) copy-start(f32[2,15,38,9]{2,1,0,3:T(8,128)} %reshape.153) | copy-start | bytes 123124
  90.4 1.9 %copy-start.12 = (f32[2,15,38,9]{2,1,0,3:T(8,128)S(1)}, f32[2,15,38,9]{2,1,0,3:T(8,128)}, u32[]{:S(2)}) copy-start(f32[2,15,38,9]{2,1,0,3:T(8,128)} %reshape.151) | copy-start | bytes 123124
  90.4 1.9 %copy-start.23 = (f32[15,36,7]{1,0,2:T(8,128)S(1)}, f32[15,36,7]{1,0,2:T(8,128)}, u32[]{:S(2)}) copy-start(f32[15,36,7]{1,0,2:T(8,128)} %get-tuple-element.47) | copy-start | bytes 45364
  90.4 1.9 %copy-start.24 = (f32[15,36,7]{1,0,2:T(8,128)S(1)}, f32[15,36,7]{1,0,2:T(8,128)}, u32[]{:S(2)}) copy-start(f32[15,36,7]{1,0,2:T(8,128)} %get-tuple-element.48) | copy-start | bytes 45364
  90.4 1.9 %copy-start.25 = (f32[15,36,7]{1,0,2:T(8,128)S(1)}, f32[15,36,7]{1,0,2:T(8,128)}, u32[]{:S(2)}) copy-start(f32[15,36,7]{1,0,2:T(8,128)} %get-tuple-element.49) | copy-start | bytes 45364
  90.4 1.9 %copy-start.26 = (f32[15,36,7]{1,0,2:T(8,128)S(1)}, f32[15,36,7]{1,0,2:T(8,128)}, u32[]{:S(2)}) copy-start(f32[15,36,7]{1,0,2:T(8,128)} %get-tuple-element.44) | copy-start | bytes 45364
  90.5 1.9 %copy-start.27 = (f32[15,36,7]{1,0,2:T(8,128)S(1)}, f32[15,36,7]{1,0,2:T(8,128)}, u32[]{:S(2)}) copy-start(f32[15,36,7]{1,0,2:T(8,128)} %get-tuple-element.45) | copy-start | bytes 45364
  90.5 1.9 %copy-start.28 = (f32[15,36,7]{1,0,2:T(8,128)S(1)}, f32[15,36,7]{1,0,2:T(8,128)}, u32[]{:S(2)}) copy-start(f32[15,36,7]{1,0,2:T(8,128)} %get-tuple-element.46) | copy-start | bytes 45364
  90.5 2.2 %copy-start.31 = (f32[15,34,5]{1,0,2:T(8,128)S(1)}, f32[15,34,5]{1,0,2:T(8,128)}, u32[]{:S(2)}) copy-start(f32[15,34,5]{1,0,2:T(8,128)} %get-tuple-element.11) | copy-start | bytes 30604
  90.5 2.2 %copy-start.32 = (f32[15,34,5]{1,0,2:T(8,128)S(1)}, f32[15,34,5]{1,0,2:T(8,128)}, u32[]{:S(2)}) copy-start(f32[15,34,5]{1,0,2:T(8,128)} %get-tuple-element.75) | copy-start | bytes 30604
  107.9 3.8 %copy-start.40 = (bf16[1,1024,120]{1,2,0:T(8,128)(2,1)S(1)}, bf16[1,1024,120]{1,2,0:T(8,128)(2,1)}, u32[]{:S(2)}) copy-start(bf16[1,1024,120]{1,2,0:T(8,128)(2,1)} %param.13) | copy-start | bytes 737284
  111.6 7.7 %copy-start.39 = (s32[1,1024,1]{1,2,0:T(1,128)S(1)}, s32[1,1024,1]{1,2,0:T(1,128)}, u32[]{:S(2)}) copy-start(s32[1,1024,1]{1,2,0:T(1,128)} %param.10) | copy-start | bytes 12292
  115.9 11.6 %all-to-all-start.1 = ((bf16[30,8,256]{2,0,1:T(8,128)(2,1)}), bf16[30,8,256]{2,0,1:T(8,128)(2,1)S(1)}, u32[]{:S(2)}, u32[]{:S(2)}) async-start(bf16[30,8,256]{2,0,1:T(8,128)(2,1)} %copy.289), calls=%async_computation.1 | async-start | bytes 262144 | tf_op jit(solution)/shard_map/all_to_all | solution.py:167
  (14 other events, 19.3 us)

commit v8 on v5

--- a/solution.py
+++ b/solution.py
@@ -54,14 +54,38 @@
 
 def dynamics(fields, diffusivity):
     kinds, level_rows, lat_rows, lon_cols = fields.shape
-    stacked = jnp.concatenate(
-        [fields.reshape(kinds * level_rows, lat_rows, lon_cols), diffusivity], axis=0
-    )
-    stacked = halo_exchange(stacked, STEPS)
-    values = stacked[: kinds * level_rows].reshape(
-        kinds, level_rows, lat_rows + 2 * STEPS, lon_cols + 2 * STEPS
-    )
-    kappa = stacked[kinds * level_rows :]
+    planes = fields.reshape(kinds * level_rows, lat_rows, lon_cols)
+    lat_count, lon_count = lax.axis_size("lat"), lax.axis_size("lon")
+    width = STEPS
+
+    def both(cut):
+        return jnp.concatenate([planes[cut], diffusivity[cut]], axis=0)
+
+    bottom_rows = both((slice(None), slice(lat_rows - width, None)))
+    top_rows = both((slice(None), slice(0, width)))
+    north = lax.ppermute(bottom_rows, "lat", [(i, i + 1) for i in range(lat_count - 1)])
+    south = lax.ppermute(top_rows, "lat", [(i + 1, i) for i in range(lat_count - 1)])
+
+    def edge(cut):
+        return jnp.concatenate([north[..., cut], both((slice(None), slice(None), cut)), south[..., cut]], axis=-2)
+
+    left, right = edge(slice(0, width)), edge(slice(lon_cols - width, None))
+    if lon_count == 2:
+        swapped = lax.ppermute(jnp.concatenate([right, left], axis=-1), "lon", [(0, 1), (1, 0)])
+        west, east = swapped[..., :width], swapped[..., width:]
+    else:
+        west = lax.ppermute(right, "lon", [(i, (i + 1) % lon_count) for i in range(lon_count)])
+        east = lax.ppermute(left, "lon", [((i + 1) % lon_count, i) for i in range(lon_count)])
+    count = kinds * level_rows
+
+    def assemble(own, first, last):
+        middle = jnp.concatenate([north[first:last], own, south[first:last]], axis=-2)
+        return jnp.concatenate([west[first:last], middle, east[first:last]], axis=-1)
+
+    values = assemble(planes, 0, count).reshape(
+        kinds, level_rows, lat_rows + 2 * width, lon_cols + 2 * width
+    )
+    kappa = assemble(diffusivity, count, count + diffusivity.shape[0])
     for repeat in range(STEPS):
         trim = repeat
         coefficients = kappa[:, trim : kappa.shape[1] - trim, trim : kappa.shape[2] - trim]

time: 60 us -> 64.7 us (1.078)
  local copies, waits for them, and re-layouts: 3.44 us -> 9 us
  other arithmetic: 10.5 us -> 9.35 us
    slice x5 -> x24, local copies, waits for them, and re-layouts: 1.25 us -> 6.55 us  [the longest x6 4.12 us: both(): return jnp.concatenate([planes[cut], diffusivity[cut]], axis=0)]
    slice x1 -> x0, other arithmetic: 1.1 us -> none  [halo_exchange(): cells[..., cells.shape[-2] - width:, :]]
    mul x3, other arithmetic: 1.94 us -> 2.68 us  [substep(): face_coef = 0.5 * (middle + coefficients[:, lat_cut, lon_cut])]
    select_n x1, other arithmetic: 0.7 us -> 0.02 us  [on_device(): col_of = column_ids % lon_cols]
    select_n x1, other arithmetic: 0.71 us -> 0.02 us  [on_device(): row_of = column_ids // lon_cols]
    concatenate x3 -> x6, other arithmetic: 2.29 us -> 2.35 us  [the longest x3 2.2 us: assemble(): jnp.concatenate([west[first:last], middle, east[first:last]], axis=-1)]
  transfers between devices with their start and end apart: 4 -> 4, of which waited for: 2 -> 2; matrix products, arithmetic and copies ran while one was open for 2% -> 6% of each run, Pallas kernels for 0% -> 0%
where the time goes in v8:
time: 64.7 us; the launch traced here: 64.2 us
  blocking collectives  14.2 us (22%)
  waiting for transfers between devices  11 us (17%)
  starting transfers between devices  10.7 us (17%)
  matrix products  9.36 us (14%)
  other arithmetic  9.35 us (14%)
  local copies, waits for them, and re-layouts  9 us (14%)
    all_to_all x1, blocking collectives, on_device(): lax.all_to_all(send_buffer, ('lon', 'lev'), split_axis=1, concat_axis=1,...  14.2 us
    all_to_all x1, waiting for transfers between devices, on_device(): lax.all_to_all(outgoing, ('lon', 'lev'), split_axis=1, concat_axis=1, til...  7.42 us
    slice x6, local copies, waits for them, and re-layouts, both(): return jnp.concatenate([planes[cut], diffusivity[cut]], axis=0)  4.12 us
    dot_general x1, matrix products, network(): lax.dot_general(w_middle[layer_no], hidden, contract, preferred_element_t...  3.73 us
    ppermute x1, waiting for transfers between devices, dynamics(): lax.ppermute(jnp.concatenate([right, left], axis=-1), 'lon', [(0, 1), (1,...  3.56 us
    dot_general x1, matrix products, network(): lax.dot_general(w_last, hidden, contract, preferred_element_type=jnp.floa...  3.44 us
    all_to_all x1, starting transfers between devices, on_device(): lax.all_to_all(outgoing, ('lon', 'lev'), split_axis=1, concat_axis=1, til...  3.37 us
    ppermute x1, starting transfers between devices, dynamics(): lax.ppermute(bottom_rows, 'lat', [(i, i + 1) for i in range(lat_count - 1)])  3.04 us
  transfers between devices with their start and end apart: 4, of which 2 were waited for; matrix products, arithmetic and copies ran while one was open for 6% of the time, Pallas kernels for 0%

profile of v8, /device:TPU:0, one launch (start us, length us, event | category | flops | bytes accessed | tf_op | source)
XLA Modules:
  0.0 64.2 jit_solution(17760173293702306249)
XLA Ops:
  0.0 0.9 %fusion.119 = (f32[15,3,128]{2,1,0:T(4,128)S(1)}, f32[15,3,128]{2,1,0:T(4,128)S(1)}) fusion(f32[15,32,128]{2,1,0:T(8,128)} %param.8), kind=kLoop, calls=%fused_computation.154 | loop fusion | bytes 92160 | tf_op jit(solution)/shard_map/slice | solution.py:62
  0.9 1.0 %fusion.117 = (f32[30,3,128]{2,1,0:T(4,128)S(1)}, f32[30,3,128]{2,1,0:T(4,128)S(1)}) fusion(f32[30,32,128]{2,1,0:T(8,128)} %bitcast.69), kind=kLoop, calls=%fused_computation.152 | loop fusion | bytes 184320 | tf_op jit(solution)/shard_map/slice | solution.py:62
  2.0 1.3 %collective-permute-start.1 = (f32[45,3,128]{2,1,0:T(4,128)S(1)}, f32[45,3,128]{2,1,0:T(4,128)S(1)}, u32[]{:S(2)}, u32[]{:S(2)}) collective-permute-start(f32[45,3,128]{2,1,0:T(4,128)S(1)} %pad_maximum_fusion.6), channel_id=1, source_target_pairs={{8,0},{16,8},{24,16},{9,1},{17,9},{25,17},{10,2},{18,10},{26,18},{... | collective-permute-start | bytes 207368 | tf_op jit(solution)/shard_map/ppermute | solution.py:67
  3.3 3.0 %collective-permute-start = (f32[45,3,128]{2,1,0:T(4,128)S(1)}, f32[45,3,128]{2,1,0:T(4,128)S(1)}, u32[]{:S(2)}, u32[]{:S(2)}) collective-permute-start(f32[45,3,128]{2,1,0:T(4,128)S(1)} %pad_maximum_fusion.5), channel_id=1, source_target_pairs={{0,8},{8,16},{16,24},{1,9},{9,17},{17,25},{2,10},{10,18},{18,26},{... | collective-permute-start | bytes 207368 | tf_op jit(solution)/shard_map/ppermute | solution.py:66
  6.3 1.2 %fusion.118 = (f32[15,32,3]{2,1,0:T(8,128)S(1)}, f32[15,32,3]{2,1,0:T(8,128)S(1)}) fusion(f32[15,32,128]{2,1,0:T(8,128)} %param.8), kind=kLoop, calls=%fused_computation.153 | loop fusion | bytes 23040 | tf_op jit(solution)/shard_map/slice | solution.py:62
  8.1 0.4 copy.73
  8.8 0.4 copy.69
  9.3 0.6 iota_compare_fusion.1
  10.7 3.0 %collective-permute-start.2 = (f32[45,38,6]{0,1,2:T(8,128)S(1)}, f32[45,38,6]{0,1,2:T(8,128)S(1)}, u32[]{:S(2)}, u32[]{:S(2)}) collective-permute-start(f32[45,38,6]{0,1,2:T(8,128)S(1)} %maximum_maximum_fusion.1), channel_id=1, source_target_pairs={{0,4},{4,0},{1,5},{5,1},{2,6},{6,2},{3,7},{7,3},{8,12},{12,8},{9,1... | collective-permute-start | bytes 123128 | tf_op jit(solution)/shard_map/ppermute | solution.py:74
  13.8 3.6 %collective-permute-done.2 = f32[45,38,6]{0,1,2:T(8,128)S(1)} collective-permute-done((f32[45,38,6]{0,1,2:T(8,128)S(1)}, f32[45,38,6]{0,1,2:T(8,128)S(1)}, u32[]{:S(2)}, u32[]{:S(2)}) %collective-permute-start.2) | collective-permute-done | bytes 41072 | tf_op jit(solution)/shard_map/ppermute | solution.py:74
  17.5 0.4 copy.79
  17.9 0.4 copy.78
  18.2 0.4 pad_maximum_fusion.1
  18.6 1.1 %maximum_maximum_fusion = (f32[15,38,131]{2,1,0:T(8,128)S(1)}, f32[15,38,131]{2,1,0:T(8,128)}) fusion(f32[15,3,128]{2,1,0:T(4,128)S(1)} %slice.257, f32[15,32,128]{2,1,0:T(8,128)S(1)} %copy-done.1, f32[15,3,128]{2,1,0:T(4,128)S(1)} %slice.256, f32[15,38,3]{2,1,0:T(8,128)S(1)} %copy.78, f32[15,38,3]{2,1,0:T(8,128)S(1)} %copy.79), kind=kLoop, calls=%fused_computation.95 | loop fusion | flops 448020 | bytes 902880 | tf_op jit(solution)/shard_map/concatenate | solution.py:83
  19.8 1.2 %fusion.99 = (f32[15,32,128]{2,1,0:T(8,128)}, f32[15,32,128]{2,1,0:T(8,128)}, f32[15,32,128]{2,1,0:T(8,128)}, f32[15,32,128]{2,1,0:T(8,128)}) fusion(f32[15,32,128]{2,1,0:T(8,128)S(1)} %copy-done.1, f32[15,38,3]{2,1,0:T(8,128)S(1)} %copy.78, f32[15,3,128]{2,1,0:T(4,128)S(1)} %slice.257, f32[15,3,128]{2,1,0:T(4,128)S(1)} %slice.256, f32[15,38,3]{2,1,0:T(8,128)S(1)} %copy.79), kind=kLoop, calls=%fused_computation.117 | loop fusion | flops 983040 | bytes 1288560 | tf_op jit(solution)/shard_map/mul | solution.py:42
  21.0 0.4 copy.77
  21.4 0.4 copy.76
  21.8 0.7 %fusion.84 = (f32[15,36,132]{2,1,0:T(8,128)S(1)}, f32[15,36,132]{2,1,0:T(8,128)S(1)}, f32[15,36,132]{2,1,0:T(8,128)S(1)}, f32[15,36,132]{2,1,0:T(8,128)S(1)}) fusion(f32[15,38,134]{2,1,0:T(8,128)S(1)} %pad_maximum_fusion.1), kind=kLoop, calls=%fused_computation.93 | loop fusion | flops 570240 | bytes 2566080 | tf_op jit(solution)/shard_map/mul | solution.py:42
  22.5 0.4 copy-done.3
  22.9 0.7 %fusion.80 = (f32[15,34,130]{2,1,0:T(8,128)S(1)}, f32[15,34,130]{2,1,0:T(8,128)S(1)}, f32[15,34,130]{2,1,0:T(8,128)S(1)}, f32[15,34,130]{2,1,0:T(8,128)S(1)}) fusion(f32[15,38,134]{2,1,0:T(8,128)S(1)} %pad_maximum_fusion.1, f32[15,38,131]{2,1,0:T(8,128)S(1)} %get-tuple-element.21, f32[15,38,131]{2,1,0:T(8,128)S(1)} %copy-done.3), kind=kLoop, calls=%fused_computation.85 | loop fusion | flops 530400 | bytes 2386800 | tf_op jit(solution)/shard_map/mul | solution.py:42
  23.8 0.7 %pad_maximum_fusion = f32[30,38,134]{2,1,0:T(8,128)S(1)} fusion(f32[30,38,3]{2,1,0:T(8,128)S(1)} %copy.77, f32[30,3,128]{2,1,0:T(4,128)S(1)} %slice-done, f32[30,32,128]{2,1,0:T(8,128)S(1)} %bitcast.71, f32[30,3,128]{2,1,0:T(4,128)S(1)} %slice-done.1, f32[30,38,3]{2,1,0:T(8,128)S(1)} %copy.76), kind=kLoop, calls=%fused_computation.63 | loop fusion | flops 611040 | bytes 1222080 | tf_op jit(solution)/shard_map/concatenate | solution.py:83
  24.4 1.4 %fusion.44 = f32[2,15,36,132]{3,2,1,0:T(8,128)S(1)} fusion(f32[2,15,38,134]{3,2,1,0:T(8,128)S(1)} %bitcast.68, f32[15,36,132]{2,1,0:T(8,128)S(1)} %get-tuple-element.12, f32[15,36,132]{2,1,0:T(8,128)S(1)} %get-tuple-element.13, f32[15,36,132]{2,1,0:T(8,128)S(1)} %get-tuple-element.14, f32[15,36,132]{2,1,0:T(8,128)S(1)} %get-tuple-element.11, ...), kind=kLoop, calls=%fused_computation.53 | loop fusion | flops 1853280 | bytes 4561956 | tf_op jit(solution)/shard_map/jit(_where)/select_n | solution.py:52
  25.9 1.4 %fusion.35 = f32[2,15,34,130]{3,2,1,0:T(8,128)S(1)} fusion(f32[2,15,36,132]{3,2,1,0:T(8,128)S(1)} %fusion.44, f32[15,34,130]{2,1,0:T(8,128)S(1)} %get-tuple-element.10, f32[15,34,130]{2,1,0:T(8,128)S(1)} %get-tuple-element.9, f32[15,34,130]{2,1,0:T(8,128)S(1)} %get-tuple-element.8, f32[15,34,130]{2,1,0:T(8,128)S(1)} %get-tuple-element.7, ...), kind=kLoop, calls=%fused_computation.40 | loop fusion | flops 1723800 | bytes 4243234 | tf_op jit(solution)/shard_map/jit(_where)/select_n | solution.py:52
  27.3 0.6 fusion.89
  28.1 0.7 %select_reduce_fusion = bf16[30,1024]{1,0:T(8,128)(2,1)S(1)} fusion(pred[32,1024]{1,0:T(8,128)(4,1)S(1)} %copy-done.10, bf16[30,32,128]{2,1,0:T(8,128)(2,1)S(1)} %bitcast_convert_fusion, s32[1024]{0:T(1024)S(1)} %bitcast.80), kind=kOutput, calls=%fused_computation.35 | convolution fusion | flops 253724672 | bytes 344064 | tf_op jit(solution)/shard_map/dot_general | solution.py:135
  28.9 14.2 %all_to_all.10 = bf16[30,8,256]{2,0,1:T(8,128)(2,1)S(1)} all-to-all(bf16[30,8,256]{2,0,1:T(8,128)(2,1)S(1)} %bitcast.73), channel_id=1, replica_groups=mesh['lat'=4,'lon'=2,'lev'=4] {'lon','lev'}, dimensions={1} | all-to-all | bytes 245760 | tf_op jit(solution)/shard_map/all_to_all | solution.py:160
  43.4 3.7 %fusion.15 = bf16[1024,512]{0,1:T(8,128)(2,1)S(1)} fusion(bf16[1,2,1024,1024]{3,2,1,0:T(8,128)(2,1)} %param.12, bf16[120,512]{1,0:T(8,128)(2,1)S(1)} %bitcast.77, bf16[1,120,1024]{2,1,0:T(8,128)(2,1)S(1)} %copy-done), kind=kOutput, calls=%fused_computation.18 | convolution fusion | flops 1209008128 | bytes 3514368 | tf_op jit(solution)/shard_map/dot_general | solution.py:106
  47.2 3.4 %fusion.64 = bf16[120,512]{1,0:T(8,128)(2,1)S(1)} fusion(bf16[1024,512]{0,1:T(8,128)(2,1)S(1)} %fusion.15, bf16[1,2,1024,1024]{3,2,1,0:T(8,128)(2,1)} %param.12, bf16[1,1024,120]{1,2,0:T(8,128)(2,1)S(1)} %copy-done.13), kind=kOutput, calls=%fused_computation.67 | convolution fusion | flops 1204350976 | bytes 3514368 | tf_op jit(solution)/shard_map/dot_general | solution.py:110
  50.8 0.7 %copy.86 = bf16[30,8,256]{2,0,1:T(8,128)(2,1)} copy(bf16[30,8,256]{2,1,0:T(8,128)(2,1)S(1)} %reshape.103) | data formatting | bytes 245760 | tf_op jit(solution)/shard_map/reshape | solution.py:172
  51.4 3.4 %all-to-all-start.1 = ((bf16[30,8,256]{2,0,1:T(8,128)(2,1)}), bf16[30,8,256]{2,0,1:T(8,128)(2,1)S(1)}, u32[]{:S(2)}, u32[]{:S(2)}) async-start(bf16[30,8,256]{2,0,1:T(8,128)(2,1)} %copy.86), calls=%async_computation.1 | async-start | bytes 262144 | tf_op jit(solution)/shard_map/all_to_all | solution.py:174
  54.9 7.4 %all-to-all-done.1 = bf16[30,8,256]{2,0,1:T(8,128)(2,1)S(1)} async-done(((bf16[30,8,256]{2,0,1:T(8,128)(2,1)}), bf16[30,8,256]{2,0,1:T(8,128)(2,1)S(1)}, u32[]{:S(2)}, u32[]{:S(2)}) %all-to-all-start.1) | async-done | bytes 122912 | tf_op jit(solution)/shard_map/all_to_all | solution.py:174
  62.7 1.5 %fusion.51 = f32[30,32,128]{2,1,0:T(8,128)} fusion(f32[30,32,128]{2,1,0:T(8,128)S(1)} %bitcast.72, pred[32,1024]{1,0:T(8,128)(4,1)S(1)} %copy-done.10, bf16[30,1024]{1,0:T(8,128)(2,1)S(1)} %bitcast.78, s32[1024]{0:T(1024)S(1)} %bitcast.81), kind=kOutput, calls=%fused_computation.64 | convolution fusion | flops 252895232 | bytes 1081344 | tf_op jit(solution)/shard_map/dot_general | solution.py:185
  (69 shorter events, 3.0 us)
Async XLA Ops:
  0.0 43.4 %copy-start = (bf16[1,120,1024]{2,1,0:T(8,128)(2,1)S(1)}, bf16[1,120,1024]{2,1,0:T(8,128)(2,1)}, u32[]{:S(2)}) copy-start(bf16[1,120,1024]{2,1,0:T(8,128)(2,1)} %param.11) | copy-start | bytes 737284
  0.0 7.5 %copy-start.2 = (f32[2,15,32,128]{3,2,1,0:T(8,128)S(1)}, f32[2,15,32,128]{3,2,1,0:T(8,128)}, u32[]{:S(2)}) copy-start(f32[2,15,32,128]{3,2,1,0:T(8,128)} %param.7) | copy-start | bytes 1474564
  2.0 7.9 %collective-permute-start.1 = (f32[45,3,128]{2,1,0:T(4,128)S(1)}, f32[45,3,128]{2,1,0:T(4,128)S(1)}, u32[]{:S(2)}, u32[]{:S(2)}) collective-permute-start(f32[45,3,128]{2,1,0:T(4,128)S(1)} %pad_maximum_fusion.6), channel_id=1, source_target_pairs={{8,0},{16,8},{24,16},{9,1},{17,9},{25,17},{10,2},{18,10},{26,18},{... | collective-permute-start | bytes 207368 | tf_op jit(solution)/shard_map/ppermute | solution.py:67
  3.3 6.9 %collective-permute-start = (f32[45,3,128]{2,1,0:T(4,128)S(1)}, f32[45,3,128]{2,1,0:T(4,128)S(1)}, u32[]{:S(2)}, u32[]{:S(2)}) collective-permute-start(f32[45,3,128]{2,1,0:T(4,128)S(1)} %pad_maximum_fusion.5), channel_id=1, source_target_pairs={{0,8},{8,16},{16,24},{1,9},{9,17},{17,25},{2,10},{10,18},{18,26},{... | collective-permute-start | bytes 207368 | tf_op jit(solution)/shard_map/ppermute | solution.py:66
  7.7 1.5 %copy-start.11 = (s32[1,1024]{1,0:T(1,128)S(1)}, s32[1,1024]{1,0:T(1,128)}, u32[]{:S(2)}) copy-start(s32[1,1024]{1,0:T(1,128)} %param.9) | copy-start | bytes 12292
  9.9 7.9 %copy-start.8 = (f32[45,3,128]{2,1,0:T(4,128)}, f32[45,3,128]{2,1,0:T(4,128)S(1)}, u32[]{:S(2)}) copy-start(f32[45,3,128]{2,1,0:T(4,128)S(1)} %collective-permute-done.1) | copy-start | bytes 207364
  10.0 8.2 %copy-start.1 = (f32[15,32,128]{2,1,0:T(8,128)S(1)}, f32[15,32,128]{2,1,0:T(8,128)}, u32[]{:S(2)}) copy-start(f32[15,32,128]{2,1,0:T(8,128)} %param.8) | copy-start | bytes 737284
  10.2 8.5 %copy-start.9 = (f32[45,3,128]{2,1,0:T(4,128)}, f32[45,3,128]{2,1,0:T(4,128)S(1)}, u32[]{:S(2)}) copy-start(f32[45,3,128]{2,1,0:T(4,128)S(1)} %collective-permute-done) | copy-start | bytes 207364
  10.7 6.6 %collective-permute-start.2 = (f32[45,38,6]{0,1,2:T(8,128)S(1)}, f32[45,38,6]{0,1,2:T(8,128)S(1)}, u32[]{:S(2)}, u32[]{:S(2)}) collective-permute-start(f32[45,38,6]{0,1,2:T(8,128)S(1)} %maximum_maximum_fusion.1), channel_id=1, source_target_pairs={{0,4},{4,0},{1,5},{5,1},{2,6},{6,2},{3,7},{7,3},{8,12},{12,8},{9,1... | collective-permute-start | bytes 123128 | tf_op jit(solution)/shard_map/ppermute | solution.py:74
  21.8 1.1 %copy-start.3 = (f32[15,38,131]{2,1,0:T(8,128)S(1)}, f32[15,38,131]{2,1,0:T(8,128)}, u32[]{:S(2)}) copy-start(f32[15,38,131]{2,1,0:T(8,128)} %get-tuple-element.22) | copy-start | bytes 896044
  22.9 0.8 %slice-start = ((f32[45,3,128]{2,1,0:T(4,128)}), f32[30,3,128]{2,1,0:T(4,128)S(1)}, s32[]{:S(2)}) async-start(f32[45,3,128]{2,1,0:T(4,128)} %copy-done.8), calls=%async_computation.2 | async-start | bytes 122880 | tf_op jit(solution)/shard_map/slice | solution.py:82
  22.9 0.9 %slice-start.1 = ((f32[45,3,128]{2,1,0:T(4,128)}), f32[30,3,128]{2,1,0:T(4,128)S(1)}, s32[]{:S(2)}) async-start(f32[45,3,128]{2,1,0:T(4,128)} %copy-done.9), calls=%async_computation.3 | async-start | bytes 122880 | tf_op jit(solution)/shard_map/slice | solution.py:82
  25.8 1.4 %copy-start.4 = (f32[15,32,128]{2,1,0:T(8,128)S(1)}, f32[15,32,128]{2,1,0:T(8,128)}, u32[]{:S(2)}) copy-start(f32[15,32,128]{2,1,0:T(8,128)} %get-tuple-element.19) | copy-start | bytes 737284
  25.9 1.4 %copy-start.5 = (f32[15,32,128]{2,1,0:T(8,128)S(1)}, f32[15,32,128]{2,1,0:T(8,128)}, u32[]{:S(2)}) copy-start(f32[15,32,128]{2,1,0:T(8,128)} %get-tuple-element.20) | copy-start | bytes 737284
  25.9 1.4 %copy-start.6 = (f32[15,32,128]{2,1,0:T(8,128)S(1)}, f32[15,32,128]{2,1,0:T(8,128)}, u32[]{:S(2)}) copy-start(f32[15,32,128]{2,1,0:T(8,128)} %get-tuple-element.23) | copy-start | bytes 737284
  25.9 1.4 %copy-start.7 = (f32[15,32,128]{2,1,0:T(8,128)S(1)}, f32[15,32,128]{2,1,0:T(8,128)}, u32[]{:S(2)}) copy-start(f32[15,32,128]{2,1,0:T(8,128)} %get-tuple-element.24) | copy-start | bytes 737284
  27.3 0.8 %copy-start.10 = (pred[32,1024]{1,0:T(8,128)(4,1)S(1)}, pred[32,1024]{1,0:T(8,128)(4,1)}, u32[]{:S(2)}) copy-start(pred[32,1024]{1,0:T(8,128)(4,1)} %iota_compare_fusion.1) | copy-start | bytes 98308
  43.4 3.8 %copy-start.13 = (bf16[1,1024,120]{1,2,0:T(8,128)(2,1)S(1)}, bf16[1,1024,120]{1,2,0:T(8,128)(2,1)}, u32[]{:S(2)}) copy-start(bf16[1,1024,120]{1,2,0:T(8,128)(2,1)} %param.13) | copy-start | bytes 737284
  50.6 4.2 %copy-start.12 = (s32[1,1024,1]{1,2,0:T(1,128)S(1)}, s32[1,1024,1]{1,2,0:T(1,128)}, u32[]{:S(2)}) copy-start(s32[1,1024,1]{1,2,0:T(1,128)} %param.10) | copy-start | bytes 12292
  51.4 10.8 %all-to-all-start.1 = ((bf16[30,8,256]{2,0,1:T(8,128)(2,1)}), bf16[30,8,256]{2,0,1:T(8,128)(2,1)S(1)}, u32[]{:S(2)}, u32[]{:S(2)}) async-start(bf16[30,8,256]{2,0,1:T(8,128)(2,1)} %copy.86), calls=%async_computation.1 | async-start | bytes 262144 | tf_op jit(solution)/shard_map/all_to_all | solution.py:174

commit v9 on v5

--- a/solution.py
+++ b/solution.py
@@ -20,26 +20,32 @@
     left = cells[..., :width]
     right = cells[..., cells.shape[-1] - width :]
     if lon_count == 2:
-        both = lax.ppermute(jnp.concatenate([right, left], axis=-1), "lon", [(0, 1), (1, 0)])
-        from_left, from_right = both[..., :width], both[..., width:]
+        both = lax.ppermute(jnp.stack([right, left]), "lon", [(0, 1), (1, 0)])
+        from_left, from_right = both[0], both[1]
     else:
         from_left = lax.ppermute(right, "lon", [(i, (i + 1) % lon_count) for i in range(lon_count)])
         from_right = lax.ppermute(left, "lon", [((i + 1) % lon_count, i) for i in range(lon_count)])
     return jnp.concatenate([from_left, cells, from_right], axis=-1)
 
 
-def substep(values, coefficients):
+NEIGHBOURS = (
+    (slice(0, -2), slice(1, -1)),
+    (slice(2, None), slice(1, -1)),
+    (slice(1, -1), slice(0, -2)),
+    (slice(1, -1), slice(2, None)),
+)
+
+
+def face_coefficients(coefficients):
+    middle = coefficients[:, 1:-1, 1:-1]
+    return [0.5 * (middle + coefficients[:, lat_cut, lon_cut]) for lat_cut, lon_cut in NEIGHBOURS]
+
+
+def substep(values, faces):
     centre = values[..., 1:-1, 1:-1]
-    middle = coefficients[:, 1:-1, 1:-1]
     updated = centre
-    for lat_cut, lon_cut in (
-        (slice(0, -2), slice(1, -1)),
-        (slice(2, None), slice(1, -1)),
-        (slice(1, -1), slice(0, -2)),
-        (slice(1, -1), slice(2, None)),
-    ):
+    for (lat_cut, lon_cut), face_coef in zip(NEIGHBOURS, faces):
         neighbour = values[..., lat_cut, lon_cut]
-        face_coef = 0.5 * (middle + coefficients[:, lat_cut, lon_cut])
         updated = updated + face_coef * (neighbour - centre)
     return updated
 
@@ -62,10 +68,12 @@
         kinds, level_rows, lat_rows + 2 * STEPS, lon_cols + 2 * STEPS
     )
     kappa = stacked[kinds * level_rows :]
+    faces = face_coefficients(kappa)
     for repeat in range(STEPS):
         trim = repeat
-        coefficients = kappa[:, trim : kappa.shape[1] - trim, trim : kappa.shape[2] - trim]
-        values = substep(values, coefficients)
+        values = substep(
+            values, [f[:, trim : f.shape[1] - trim, trim : f.shape[2] - trim] for f in faces]
+        )
         rim = STEPS - repeat - 1
         if rim:
             values = clear_outside(values, rim, lat_rows)

time: 60 us -> 61.4 us (1.023)
  waiting for transfers between devices: 10.9 us -> 13.9 us
  local copies, waits for them, and re-layouts: 3.44 us -> 5.94 us
  starting transfers between devices: 10.7 us -> 8.61 us
  other arithmetic: 10.5 us -> 9.34 us
  blocking collectives: 14.3 us -> 13.4 us
    ppermute x1, waiting for transfers between devices: 0.01 us -> 2.51 us  [halo_exchange(): lax.ppermute(cells[..., :width, :], 'lat', [(i + 1, i) for i in range(lat...]
    ppermute x1, starting transfers between devices: 3.03 us -> 1.58 us  [halo_exchange(): both = lax.ppermute(jnp.stack([right, left]), 'lon', [(0, 1), (1, 0)])]
    mul x3 -> x1, other arithmetic: 1.94 us -> 0.7 us  [face_coefficients(): 0.5 * (middle + coefficients[:, lat_cut, lon_cut])]
    another operation x0 -> x3, local copies, waits for them, and re-layouts: none -> 1.15 us  [halo_exchange(): both = lax.ppermute(jnp.stack([right, left]), 'lon', [(0, 1), (1, 0)])]
    squeeze x0 -> x2, local copies, waits for them, and re-layouts: none -> 0.92 us  [halo_exchange(): from_left, from_right = (both[0], both[1])]
    all_to_all x1, blocking collectives: 14.3 us -> 13.4 us  [on_device(): lax.all_to_all(send_buffer, ('lon', 'lev'), split_axis=1, concat_axis=1,...]
    ppermute x1, starting transfers between devices: 3.04 us -> 2.36 us  [halo_exchange(): lax.ppermute(cells[..., cells.shape[-2] - width:, :], 'lat', [(i, i + 1)...]
    all_to_all x1, waiting for transfers between devices: 7.42 us -> 8.08 us  [on_device(): lax.all_to_all(outgoing, ('lon', 'lev'), split_axis=1, concat_axis=1, til...]
  transfers between devices with their start and end apart: 4 -> 4, of which waited for: 2 -> 3; matrix products, arithmetic and copies ran while one was open for 2% -> 2% of each run, Pallas kernels for 0% -> 0%
where the time goes in v9:
time: 61.4 us; the launch traced here: 61 us
  waiting for transfers between devices  13.9 us (23%)
  blocking collectives  13.4 us (22%)
  matrix products  9.38 us (15%)
  other arithmetic  9.34 us (15%)
  starting transfers between devices  8.61 us (14%)
  local copies, waits for them, and re-layouts  5.94 us (10%)
    all_to_all x1, blocking collectives, on_device(): lax.all_to_all(send_buffer, ('lon', 'lev'), split_axis=1, concat_axis=1,...  13.4 us
    all_to_all x1, waiting for transfers between devices, on_device(): lax.all_to_all(outgoing, ('lon', 'lev'), split_axis=1, concat_axis=1, til...  8.08 us
    dot_general x1, matrix products, network(): lax.dot_general(w_middle[layer_no], hidden, contract, preferred_element_t...  3.73 us
    dot_general x1, matrix products, network(): lax.dot_general(w_last, hidden, contract, preferred_element_type=jnp.floa...  3.46 us
    all_to_all x1, starting transfers between devices, on_device(): lax.all_to_all(outgoing, ('lon', 'lev'), split_axis=1, concat_axis=1, til...  3.37 us
    ppermute x1, waiting for transfers between devices, halo_exchange(): both = lax.ppermute(jnp.stack([right, left]), 'lon', [(0, 1), (1, 0)])  3.29 us
    select_n x2, other arithmetic, clear_outside(): return jnp.where(inside[:, None], values, 0.0)  2.83 us
    ppermute x1, waiting for transfers between devices, halo_exchange(): lax.ppermute(cells[..., :width, :], 'lat', [(i + 1, i) for i in range(lat...  2.51 us
  transfers between devices with their start and end apart: 4, of which 3 were waited for; matrix products, arithmetic and copies ran while one was open for 2% of the time, Pallas kernels for 0%

profile of v9, /device:TPU:0, one launch (start us, length us, event | category | flops | bytes accessed | tf_op | source)
XLA Modules:
  0.0 61.0 jit_solution(12055669717882886385)
XLA Ops:
  0.0 1.1 %pad_maximum_fusion.4 = (f32[45,3,128]{2,1,0:T(4,128)S(1)}, f32[45,3,128]{2,1,0:T(4,128)S(1)}) fusion(f32[15,32,128]{2,1,0:T(8,128)} %param.8, f32[30,32,128]{2,1,0:T(8,128)} %bitcast.77), kind=kLoop, calls=%fused_computation.114 | loop fusion | flops 34560 | bytes 875520 | tf_op jit(solution)/shard_map/slice | solution.py:13
  1.1 2.4 %collective-permute-start = (f32[45,3,128]{2,1,0:T(4,128)S(1)}, f32[45,3,128]{2,1,0:T(4,128)S(1)}, u32[]{:S(2)}, u32[]{:S(2)}) collective-permute-start(f32[45,3,128]{2,1,0:T(4,128)S(1)} %get-tuple-element.13), channel_id=1, source_target_pairs={{0,8},{8,16},{16,24},{1,9},{9,17},{17,25},{2,10},{10,18},{18,26},{... | collective-permute-start | bytes 207368 | tf_op jit(solution)/shard_map/ppermute | solution.py:12
  3.5 1.3 %collective-permute-start.1 = (f32[45,3,128]{2,1,0:T(4,128)S(1)}, f32[45,3,128]{2,1,0:T(4,128)S(1)}, u32[]{:S(2)}, u32[]{:S(2)}) collective-permute-start(f32[45,3,128]{2,1,0:T(4,128)S(1)} %get-tuple-element.14), channel_id=1, source_target_pairs={{8,0},{16,8},{24,16},{9,1},{17,9},{25,17},{10,2},{18,10},{26,18},{... | collective-permute-start | bytes 207368 | tf_op jit(solution)/shard_map/ppermute | solution.py:15
  4.8 0.7 %and_select_fusion = (s32[1,1024]{1,0:T(1,128)S(1)}, s32[1,1024]{1,0:T(1,128)S(1)}) fusion(s32[1,1024]{1,0:T(1,128)} %param.9), kind=kLoop, calls=%fused_computation.116 | loop fusion | flops 11264 | bytes 12288 | tf_op jit(solution)/shard_map/jit(remainder)/select_n | solution.py:114
  5.5 0.7 %and_select_fusion.1 = s32[1,1024]{1,0:T(1,128)S(1)} fusion(s32[1,1024]{1,0:T(1,128)S(1)} %get-tuple-element.6, s32[1,1024]{1,0:T(1,128)} %param.9), kind=kLoop, calls=%fused_computation.118 | loop fusion | flops 12288 | bytes 12288 | tf_op jit(solution)/shard_map/jit(floor_divide)/jit(_where)/select_n | solution.py:113
  6.3 2.5 %collective-permute-done.1 = f32[45,3,128]{2,1,0:T(4,128)S(1)} collective-permute-done((f32[45,3,128]{2,1,0:T(4,128)S(1)}, f32[45,3,128]{2,1,0:T(4,128)S(1)}, u32[]{:S(2)}, u32[]{:S(2)}) %collective-permute-start.1) | collective-permute-done | bytes 69152 | tf_op jit(solution)/shard_map/ppermute | solution.py:15
  8.8 1.3 %pad_maximum_fusion.1 = f32[45,38,128]{2,1,0:T(8,128)S(1)} fusion(f32[45,3,128]{2,1,0:T(4,128)S(1)} %collective-permute-done.1, f32[15,32,128]{2,1,0:T(8,128)} %param.8, f32[30,32,128]{2,1,0:T(8,128)} %bitcast.78, f32[45,3,128]{2,1,0:T(4,128)S(1)} %collective-permute-done), kind=kLoop, calls=%fused_computation.80 | loop fusion | flops 656640 | bytes 1751040 | tf_op jit(solution)/shard_map/concatenate | solution.py:18
  10.0 0.3 slice_bitcast_fusion.1
  10.3 0.4 copy.37
  10.8 0.4 copy.38
  11.3 1.6 %collective-permute-start.2 = (f32[2,45,38,3]{1,0,3,2:T(2,128)S(1)}, f32[2,45,38,3]{1,0,3,2:T(2,128)S(1)}, u32[]{:S(2)}, u32[]{:S(2)}) collective-permute-start(f32[2,45,38,3]{1,0,3,2:T(2,128)S(1)} %pad_maximum_fusion.2), channel_id=1, source_target_pairs={{0,4},{4,0},{1,5},{5,1},{2,6},{6,2},{3,7},{7,3},{8,12},{12,8},{9,1... | collective-permute-start | bytes 123128 | tf_op jit(solution)/shard_map/ppermute | solution.py:23
  12.9 3.3 %collective-permute-done.2 = f32[2,45,38,3]{1,0,3,2:T(2,128)S(1)} collective-permute-done((f32[2,45,38,3]{1,0,3,2:T(2,128)S(1)}, f32[2,45,38,3]{1,0,3,2:T(2,128)S(1)}, u32[]{:S(2)}, u32[]{:S(2)}) %collective-permute-start.2) | collective-permute-done | bytes 41072 | tf_op jit(solution)/shard_map/ppermute | solution.py:23
  16.3 0.5 copy.55
  16.8 0.5 copy.56
  17.3 1.0 %pad_maximum_fusion = f32[45,38,134]{2,1,0:T(8,128)S(1)} fusion(f32[45,38,3]{2,1,0:T(8,128)S(1)} %bitcast.81, f32[45,3,128]{2,1,0:T(4,128)S(1)} %collective-permute-done.1, f32[15,32,128]{2,1,0:T(8,128)S(1)} %copy-done.3, f32[30,32,128]{2,1,0:T(8,128)S(1)} %bitcast.79, f32[45,3,128]{2,1,0:T(4,128)S(1)} %collective-permute-done, f32[45,38,3]{2,1,0:T(8,128)S(1)} %bitcast.80), kind=kLoop, calls=%fused_computation.37 | loop fusion | flops 1145700 | bytes 1833120 | tf_op jit(solution)/shard_map/concatenate | solution.py:28
  18.3 0.7 %fusion.80 = (f32[15,36,132]{2,1,0:T(8,128)S(1)}, f32[15,36,132]{2,1,0:T(8,128)S(1)}, f32[15,36,132]{2,1,0:T(8,128)S(1)}, f32[15,36,132]{2,1,0:T(8,128)S(1)}) fusion(f32[45,38,134]{2,1,0:T(8,128)S(1)} %pad_maximum_fusion), kind=kLoop, calls=%fused_computation.88 | loop fusion | flops 570240 | bytes 2566080 | tf_op jit(solution)/shard_map/mul | solution.py:41
  19.0 0.5 copy-done.1
  19.7 0.2 slice.180
  20.0 0.2 slice.184
  20.4 0.2 slice.182
  21.0 0.5 slice-done
  21.6 1.4 %fusion.44 = f32[2,15,36,132]{3,2,1,0:T(8,128)S(1)} fusion(f32[2,15,38,134]{3,2,1,0:T(8,128)S(1)} %bitcast.76, f32[15,36,132]{2,1,0:T(8,128)S(1)} %get-tuple-element.10, f32[15,36,132]{2,1,0:T(8,128)S(1)} %get-tuple-element.8, f32[15,36,132]{2,1,0:T(8,128)S(1)} %get-tuple-element.9, f32[15,36,132]{2,1,0:T(8,128)S(1)} %get-tuple-element.7, ...), kind=kLoop, calls=%fused_computation.54 | loop fusion | flops 1853280 | bytes 4561956 | tf_op jit(solution)/shard_map/jit(_where)/select_n | solution.py:58
  23.0 1.4 %fusion.35 = f32[2,15,34,130]{3,2,1,0:T(8,128)S(1)} fusion(f32[2,15,36,132]{3,2,1,0:T(8,128)S(1)} %fusion.44, f32[15,34,130]{2,1,0:T(8,128)S(1)} %slice.186, f32[15,34,130]{2,1,0:T(8,128)S(1)} %slice.184, f32[15,34,130]{2,1,0:T(8,128)S(1)} %slice.182, f32[15,34,130]{2,1,0:T(8,128)S(1)} %slice.180, pred[34]{0:T(512)(128)(4,1)S(1)} %compare_and_fusion.1), kind=kLoop, calls=%fused_computation.41 | loop fusion | flops 1723800 | bytes 4243234 | tf_op jit(solution)/shard_map/jit(_where)/select_n | solution.py:58
  24.4 0.6 fusion.85
  25.0 0.7 %select_reduce_fusion = bf16[30,1024]{1,0:T(8,128)(2,1)S(1)} fusion(pred[32,1024]{1,0:T(8,128)(4,1)S(1)} %iota_compare_fusion.1, bf16[30,32,128]{2,1,0:T(8,128)(2,1)S(1)} %bitcast_convert_fusion, s32[1024]{0:T(1024)S(1)} %bitcast.90), kind=kOutput, calls=%fused_computation.35 | convolution fusion | flops 253724672 | bytes 344064 | tf_op jit(solution)/shard_map/dot_general | solution.py:119
  25.8 13.4 %all_to_all.10 = bf16[30,8,256]{2,0,1:T(8,128)(2,1)S(1)} all-to-all(bf16[30,8,256]{2,0,1:T(8,128)(2,1)S(1)} %bitcast.83), channel_id=1, replica_groups=mesh['lat'=4,'lon'=2,'lev'=4] {'lon','lev'}, dimensions={1} | all-to-all | bytes 245760 | tf_op jit(solution)/shard_map/all_to_all | solution.py:144
  39.6 3.7 %fusion.15 = bf16[1024,512]{0,1:T(8,128)(2,1)S(1)} fusion(bf16[1,2,1024,1024]{3,2,1,0:T(8,128)(2,1)} %param.12, bf16[120,512]{1,0:T(8,128)(2,1)S(1)} %bitcast.87, bf16[1,120,1024]{2,1,0:T(8,128)(2,1)S(1)} %copy-done), kind=kOutput, calls=%fused_computation.18 | convolution fusion | flops 1209008128 | bytes 3514368 | tf_op jit(solution)/shard_map/dot_general | solution.py:90
  43.3 3.5 %fusion.64 = bf16[120,512]{1,0:T(8,128)(2,1)S(1)} fusion(bf16[1024,512]{0,1:T(8,128)(2,1)S(1)} %fusion.15, bf16[1,2,1024,1024]{3,2,1,0:T(8,128)(2,1)} %param.12, bf16[1,1024,120]{1,2,0:T(8,128)(2,1)S(1)} %copy-done.5), kind=kOutput, calls=%fused_computation.67 | convolution fusion | flops 1204350976 | bytes 3514368 | tf_op jit(solution)/shard_map/dot_general | solution.py:94
  46.9 0.7 %copy.47 = bf16[30,8,256]{2,0,1:T(8,128)(2,1)} copy(bf16[30,8,256]{2,1,0:T(8,128)(2,1)S(1)} %reshape.103) | data formatting | bytes 245760 | tf_op jit(solution)/shard_map/reshape | solution.py:156
  47.6 3.4 %all-to-all-start.1 = ((bf16[30,8,256]{2,0,1:T(8,128)(2,1)}), bf16[30,8,256]{2,0,1:T(8,128)(2,1)S(1)}, u32[]{:S(2)}, u32[]{:S(2)}) async-start(bf16[30,8,256]{2,0,1:T(8,128)(2,1)} %copy.47), calls=%async_computation.1 | async-start | bytes 262144 | tf_op jit(solution)/shard_map/all_to_all | solution.py:158
  51.0 8.1 %all-to-all-done.1 = bf16[30,8,256]{2,0,1:T(8,128)(2,1)S(1)} async-done(((bf16[30,8,256]{2,0,1:T(8,128)(2,1)}), bf16[30,8,256]{2,0,1:T(8,128)(2,1)S(1)}, u32[]{:S(2)}, u32[]{:S(2)}) %all-to-all-start.1) | async-done | bytes 122912 | tf_op jit(solution)/shard_map/all_to_all | solution.py:158
  59.5 1.5 %fusion.51 = f32[30,32,128]{2,1,0:T(8,128)} fusion(f32[30,32,128]{2,1,0:T(8,128)S(1)} %bitcast.82, pred[32,1024]{1,0:T(8,128)(4,1)S(1)} %iota_compare_fusion.1, bf16[30,1024]{1,0:T(8,128)(2,1)S(1)} %bitcast.88, s32[1024]{0:T(1024)S(1)} %bitcast.91), kind=kOutput, calls=%fused_computation.64 | convolution fusion | flops 252895232 | bytes 1081344 | tf_op jit(solution)/shard_map/dot_general | solution.py:169
  (39 shorter events, 1.9 us)
Async XLA Ops:
  0.0 39.5 %copy-start = (bf16[1,120,1024]{2,1,0:T(8,128)(2,1)S(1)}, bf16[1,120,1024]{2,1,0:T(8,128)(2,1)}, u32[]{:S(2)}) copy-start(bf16[1,120,1024]{2,1,0:T(8,128)(2,1)} %param.11) | copy-start | bytes 737284
  1.1 5.1 %collective-permute-start = (f32[45,3,128]{2,1,0:T(4,128)S(1)}, f32[45,3,128]{2,1,0:T(4,128)S(1)}, u32[]{:S(2)}, u32[]{:S(2)}) collective-permute-start(f32[45,3,128]{2,1,0:T(4,128)S(1)} %get-tuple-element.13), channel_id=1, source_target_pairs={{0,8},{8,16},{16,24},{1,9},{9,17},{17,25},{2,10},{10,18},{18,26},{... | collective-permute-start | bytes 207368 | tf_op jit(solution)/shard_map/ppermute | solution.py:12
  3.5 5.3 %collective-permute-start.1 = (f32[45,3,128]{2,1,0:T(4,128)S(1)}, f32[45,3,128]{2,1,0:T(4,128)S(1)}, u32[]{:S(2)}, u32[]{:S(2)}) collective-permute-start(f32[45,3,128]{2,1,0:T(4,128)S(1)} %get-tuple-element.14), channel_id=1, source_target_pairs={{8,0},{16,8},{24,16},{9,1},{17,9},{25,17},{10,2},{18,10},{26,18},{... | collective-permute-start | bytes 207368 | tf_op jit(solution)/shard_map/ppermute | solution.py:15
  10.8 6.5 %copy-start.2 = (f32[2,15,32,128]{3,2,1,0:T(8,128)S(1)}, f32[2,15,32,128]{3,2,1,0:T(8,128)}, u32[]{:S(2)}) copy-start(f32[2,15,32,128]{3,2,1,0:T(8,128)} %param.7) | copy-start | bytes 1474564
  10.8 6.5 %copy-start.3 = (f32[15,32,128]{2,1,0:T(8,128)S(1)}, f32[15,32,128]{2,1,0:T(8,128)}, u32[]{:S(2)}) copy-start(f32[15,32,128]{2,1,0:T(8,128)} %param.8) | copy-start | bytes 737284
  11.3 4.9 %collective-permute-start.2 = (f32[2,45,38,3]{1,0,3,2:T(2,128)S(1)}, f32[2,45,38,3]{1,0,3,2:T(2,128)S(1)}, u32[]{:S(2)}, u32[]{:S(2)}) collective-permute-start(f32[2,45,38,3]{1,0,3,2:T(2,128)S(1)} %pad_maximum_fusion.2), channel_id=1, source_target_pairs={{0,4},{4,0},{1,5},{5,1},{2,6},{6,2},{3,7},{7,3},{8,12},{12,8},{9,1... | collective-permute-start | bytes 123128 | tf_op jit(solution)/shard_map/ppermute | solution.py:23
  18.3 1.3 %copy-start.1 = (f32[45,38,134]{2,1,0:T(8,128)}, f32[45,38,134]{2,1,0:T(8,128)S(1)}, u32[]{:S(2)}) copy-start(f32[45,38,134]{2,1,0:T(8,128)S(1)} %pad_maximum_fusion) | copy-start | bytes 2749684
  20.3 1.3 %slice-start = ((f32[45,38,134]{2,1,0:T(8,128)}), f32[30,38,134]{2,1,0:T(8,128)S(1)}, s32[]{:S(2)}) async-start(f32[45,38,134]{2,1,0:T(8,128)} %copy-done.1), calls=%async_computation.2 | async-start | bytes 2457600 | tf_op jit(solution)/shard_map/slice | solution.py:67
  39.5 3.8 %copy-start.5 = (bf16[1,1024,120]{1,2,0:T(8,128)(2,1)S(1)}, bf16[1,1024,120]{1,2,0:T(8,128)(2,1)}, u32[]{:S(2)}) copy-start(bf16[1,1024,120]{1,2,0:T(8,128)(2,1)} %param.13) | copy-start | bytes 737284
  43.3 7.7 %copy-start.4 = (s32[1,1024,1]{1,2,0:T(1,128)S(1)}, s32[1,1024,1]{1,2,0:T(1,128)}, u32[]{:S(2)}) copy-start(s32[1,1024,1]{1,2,0:T(1,128)} %param.10) | copy-start | bytes 12292
  47.6 11.5 %all-to-all-start.1 = ((bf16[30,8,256]{2,0,1:T(8,128)(2,1)}), bf16[30,8,256]{2,0,1:T(8,128)(2,1)S(1)}, u32[]{:S(2)}, u32[]{:S(2)}) async-start(bf16[30,8,256]{2,0,1:T(8,128)(2,1)} %copy.47), calls=%async_computation.1 | async-start | bytes 262144 | tf_op jit(solution)/shard_map/all_to_all | solution.py:158

commit v10 on v5

--- a/solution.py
+++ b/solution.py
@@ -7,25 +7,38 @@
 STEPS = 3
 
 
-def halo_exchange(cells, width):
-    lat_count = lax.axis_size("lat")
+def halo_exchange(planes, diffusivity, width):
+    lat_count, lon_count = lax.axis_size("lat"), lax.axis_size("lon")
+    rows, cols = planes.shape[-2], planes.shape[-1]
+
+    def both(cut):
+        return jnp.concatenate([planes[cut], diffusivity[cut]], axis=0)
+
     from_above = lax.ppermute(
-        cells[..., cells.shape[-2] - width :, :], "lat", [(i, i + 1) for i in range(lat_count - 1)]
+        both((slice(None), slice(rows - width, None))),
+        "lat",
+        [(i, i + 1) for i in range(lat_count - 1)],
     )
     from_below = lax.ppermute(
-        cells[..., :width, :], "lat", [(i + 1, i) for i in range(lat_count - 1)]
+        both((slice(None), slice(0, width))), "lat", [(i + 1, i) for i in range(lat_count - 1)]
     )
-    cells = jnp.concatenate([from_above, cells, from_below], axis=-2)
-    lon_count = lax.axis_size("lon")
-    left = cells[..., :width]
-    right = cells[..., cells.shape[-1] - width :]
+
+    def edge(cut):
+        return jnp.concatenate(
+            [from_above[..., cut], both((slice(None), slice(None), cut)), from_below[..., cut]],
+            axis=-2,
+        )
+
+    left, right = edge(slice(0, width)), edge(slice(cols - width, None))
     if lon_count == 2:
-        both = lax.ppermute(jnp.concatenate([right, left], axis=-1), "lon", [(0, 1), (1, 0)])
-        from_left, from_right = both[..., :width], both[..., width:]
+        swapped = lax.ppermute(jnp.concatenate([right, left], axis=-1), "lon", [(0, 1), (1, 0)])
+        from_left, from_right = swapped[..., :width], swapped[..., width:]
     else:
         from_left = lax.ppermute(right, "lon", [(i, (i + 1) % lon_count) for i in range(lon_count)])
         from_right = lax.ppermute(left, "lon", [((i + 1) % lon_count, i) for i in range(lon_count)])
-    return jnp.concatenate([from_left, cells, from_right], axis=-1)
+    stacked = jnp.concatenate([planes, diffusivity], axis=0)
+    stacked = jnp.concatenate([from_above, stacked, from_below], axis=-2)
+    return jnp.concatenate([from_left, stacked, from_right], axis=-1)
 
 
 def substep(values, coefficients):
@@ -54,10 +67,9 @@
 
 def dynamics(fields, diffusivity):
     kinds, level_rows, lat_rows, lon_cols = fields.shape
-    stacked = jnp.concatenate(
-        [fields.reshape(kinds * level_rows, lat_rows, lon_cols), diffusivity], axis=0
+    stacked = halo_exchange(
+        fields.reshape(kinds * level_rows, lat_rows, lon_cols), diffusivity, STEPS
     )
-    stacked = halo_exchange(stacked, STEPS)
     values = stacked[: kinds * level_rows].reshape(
         kinds, level_rows, lat_rows + 2 * STEPS, lon_cols + 2 * STEPS
     )

time: 60 us -> 60.7 us (1.012)
  local copies, waits for them, and re-layouts: 3.44 us -> 7.75 us
  other arithmetic: 10.5 us -> 6.83 us
    slice x4 -> x13, local copies, waits for them, and re-layouts: 1.16 us -> 4.8 us  [the longest x6 4.12 us: both(): return jnp.concatenate([planes[cut], diffusivity[cut]], axis=0)]
    concatenate x2 -> x3, other arithmetic: 2.27 us -> 1.03 us  [the longest x1 0.98 us: halo_exchange(): return jnp.concatenate([from_left, stacked, from_right], axis=-1)]
    slice x1 -> x0, other arithmetic: 1.1 us -> none  [halo_exchange(): cells[..., cells.shape[-2] - width:, :]]
    select_n x1, other arithmetic: 0.7 us -> 0.02 us  [on_device(): col_of = column_ids % lon_cols]
    select_n x1, other arithmetic: 0.71 us -> 0.02 us  [on_device(): row_of = column_ids // lon_cols]
    unnamed x14 -> x18, local copies, waits for them, and re-layouts: 0.98 us -> 1.66 us
  transfers between devices with their start and end apart: 4 -> 4, of which waited for: 2 -> 2; matrix products, arithmetic and copies ran while one was open for 2% -> 5% of each run, Pallas kernels for 0% -> 0%
where the time goes in v10:
time: 60.7 us; the launch traced here: 60.3 us
  blocking collectives  14.2 us (23%)
  waiting for transfers between devices  11 us (18%)
  starting transfers between devices  10.7 us (18%)
  matrix products  9.38 us (15%)
  local copies, waits for them, and re-layouts  7.75 us (13%)
  other arithmetic  6.83 us (11%)
    all_to_all x1, blocking collectives, on_device(): lax.all_to_all(send_buffer, ('lon', 'lev'), split_axis=1, concat_axis=1,...  14.2 us
    all_to_all x1, waiting for transfers between devices, on_device(): lax.all_to_all(outgoing, ('lon', 'lev'), split_axis=1, concat_axis=1, til...  7.42 us
    slice x6, local copies, waits for them, and re-layouts, both(): return jnp.concatenate([planes[cut], diffusivity[cut]], axis=0)  4.12 us
    dot_general x1, matrix products, network(): lax.dot_general(w_middle[layer_no], hidden, contract, preferred_element_t...  3.73 us
    ppermute x1, waiting for transfers between devices, halo_exchange(): lax.ppermute(jnp.concatenate([right, left], axis=-1), 'lon', [(0, 1), (1,...  3.58 us
    dot_general x1, matrix products, network(): lax.dot_general(w_last, hidden, contract, preferred_element_type=jnp.floa...  3.46 us
    all_to_all x1, starting transfers between devices, on_device(): lax.all_to_all(outgoing, ('lon', 'lev'), split_axis=1, concat_axis=1, til...  3.37 us
    ppermute x1, starting transfers between devices, halo_exchange(): lax.ppermute(both((slice(None), slice(rows - width, None))), 'lat', [(i,...  3.04 us
  transfers between devices with their start and end apart: 4, of which 2 were waited for; matrix products, arithmetic and copies ran while one was open for 5% of the time, Pallas kernels for 0%

profile of v10, /device:TPU:0, one launch (start us, length us, event | category | flops | bytes accessed | tf_op | source)
XLA Modules:
  0.0 60.3 jit_solution(12138951285382758091)
XLA Ops:
  0.0 0.9 %fusion.121 = (f32[15,3,128]{2,1,0:T(4,128)S(1)}, f32[15,3,128]{2,1,0:T(4,128)S(1)}) fusion(f32[15,32,128]{2,1,0:T(8,128)} %param.8), kind=kLoop, calls=%fused_computation.161 | loop fusion | bytes 92160 | tf_op jit(solution)/shard_map/slice | solution.py:15
  0.9 1.0 %fusion.119 = (f32[30,3,128]{2,1,0:T(4,128)S(1)}, f32[30,3,128]{2,1,0:T(4,128)S(1)}) fusion(f32[30,32,128]{2,1,0:T(8,128)} %bitcast.69), kind=kLoop, calls=%fused_computation.159 | loop fusion | bytes 184320 | tf_op jit(solution)/shard_map/slice | solution.py:15
  2.0 1.3 %collective-permute-start.1 = (f32[45,3,128]{2,1,0:T(4,128)S(1)}, f32[45,3,128]{2,1,0:T(4,128)S(1)}, u32[]{:S(2)}, u32[]{:S(2)}) collective-permute-start(f32[45,3,128]{2,1,0:T(4,128)S(1)} %pad_maximum_fusion.14), channel_id=1, source_target_pairs={{8,0},{16,8},{24,16},{9,1},{17,9},{25,17},{10,2},{18,10},{26,18},{... | collective-permute-start | bytes 207368 | tf_op jit(solution)/shard_map/ppermute | solution.py:22
  3.3 3.0 %collective-permute-start = (f32[45,3,128]{2,1,0:T(4,128)S(1)}, f32[45,3,128]{2,1,0:T(4,128)S(1)}, u32[]{:S(2)}, u32[]{:S(2)}) collective-permute-start(f32[45,3,128]{2,1,0:T(4,128)S(1)} %pad_maximum_fusion.13), channel_id=1, source_target_pairs={{0,8},{8,16},{16,24},{1,9},{9,17},{17,25},{2,10},{10,18},{18,26},{... | collective-permute-start | bytes 207368 | tf_op jit(solution)/shard_map/ppermute | solution.py:17
  6.3 1.2 %fusion.120 = (f32[15,32,3]{2,1,0:T(8,128)S(1)}, f32[15,32,3]{2,1,0:T(8,128)S(1)}) fusion(f32[15,32,128]{2,1,0:T(8,128)} %param.8), kind=kLoop, calls=%fused_computation.160 | loop fusion | bytes 23040 | tf_op jit(solution)/shard_map/slice | solution.py:15
  7.6 0.2 fusion.118
  7.8 0.3 copy.94
  8.1 0.4 copy.80
  8.5 0.3 copy.93
  8.8 0.4 copy.76
  9.6 0.1 fusion.123
  9.9 0.1 copy.77
  10.2 3.0 %collective-permute-start.2 = (f32[45,38,6]{0,1,2:T(8,128)S(1)}, f32[45,38,6]{0,1,2:T(8,128)S(1)}, u32[]{:S(2)}, u32[]{:S(2)}) collective-permute-start(f32[45,38,6]{0,1,2:T(8,128)S(1)} %maximum_maximum_fusion), channel_id=1, source_target_pairs={{0,4},{4,0},{1,5},{5,1},{2,6},{6,2},{3,7},{7,3},{8,12},{12,8},{9,1... | collective-permute-start | bytes 123128 | tf_op jit(solution)/shard_map/ppermute | solution.py:34
  13.2 3.6 %collective-permute-done.2 = f32[45,38,6]{0,1,2:T(8,128)S(1)} collective-permute-done((f32[45,38,6]{0,1,2:T(8,128)S(1)}, f32[45,38,6]{0,1,2:T(8,128)S(1)}, u32[]{:S(2)}, u32[]{:S(2)}) %collective-permute-start.2) | collective-permute-done | bytes 41072 | tf_op jit(solution)/shard_map/ppermute | solution.py:34
  16.8 0.5 copy.96
  17.3 0.5 copy.95
  17.7 1.0 %pad_maximum_fusion = f32[45,38,134]{2,1,0:T(8,128)S(1)} fusion(f32[45,38,3]{2,1,0:T(8,128)S(1)} %copy.96, f32[45,3,128]{2,1,0:T(4,128)S(1)} %collective-permute-done.1, f32[15,32,128]{2,1,0:T(8,128)S(1)} %copy-done.2, f32[30,32,128]{2,1,0:T(8,128)S(1)} %bitcast.71, f32[45,3,128]{2,1,0:T(4,128)S(1)} %collective-permute-done, f32[45,38,3]{2,1,0:T(8,128)S(1)} %copy.95), kind=kLoop, calls=%fused_computation.37 | loop fusion | flops 1145700 | bytes 1833120 | tf_op jit(solution)/shard_map/concatenate | solution.py:41
  18.8 0.7 %fusion.84 = (f32[15,36,132]{2,1,0:T(8,128)S(1)}, f32[15,36,132]{2,1,0:T(8,128)S(1)}, f32[15,36,132]{2,1,0:T(8,128)S(1)}, f32[15,36,132]{2,1,0:T(8,128)S(1)}) fusion(f32[45,38,134]{2,1,0:T(8,128)S(1)} %pad_maximum_fusion), kind=kLoop, calls=%fused_computation.93 | loop fusion | flops 570240 | bytes 2566080 | tf_op jit(solution)/shard_map/mul | solution.py:55
  19.5 1.4 %fusion.44 = f32[2,15,36,132]{3,2,1,0:T(8,128)S(1)} fusion(f32[2,15,38,134]{3,2,1,0:T(8,128)S(1)} %bitcast.68, f32[15,36,132]{2,1,0:T(8,128)S(1)} %get-tuple-element.14, f32[15,36,132]{2,1,0:T(8,128)S(1)} %get-tuple-element.15, f32[15,36,132]{2,1,0:T(8,128)S(1)} %get-tuple-element.16, f32[15,36,132]{2,1,0:T(8,128)S(1)} %get-tuple-element.13, ...), kind=kLoop, calls=%fused_computation.54 | loop fusion | flops 1853280 | bytes 4561956 | tf_op jit(solution)/shard_map/jit(_where)/select_n | solution.py:65
  20.9 0.9 %fusion.80 = (f32[15,34,130]{2,1,0:T(8,128)S(1)}, f32[15,34,130]{2,1,0:T(8,128)S(1)}, f32[15,34,130]{2,1,0:T(8,128)S(1)}, f32[15,34,130]{2,1,0:T(8,128)S(1)}) fusion(f32[45,38,134]{2,1,0:T(8,128)S(1)} %pad_maximum_fusion, f32[45,38,3]{2,1,0:T(8,128)S(1)} %copy.96, f32[45,3,128]{2,1,0:T(4,128)S(1)} %collective-permute-done.1, ...), kind=kLoop, calls=%fused_computation.85 | loop fusion | flops 1060800 | bytes 2772960 | tf_op jit(solution)/shard_map/mul | solution.py:55
  21.8 1.4 %fusion.35 = f32[2,15,34,130]{3,2,1,0:T(8,128)S(1)} fusion(f32[2,15,36,132]{3,2,1,0:T(8,128)S(1)} %fusion.44, f32[15,34,130]{2,1,0:T(8,128)S(1)} %get-tuple-element.11, f32[15,34,130]{2,1,0:T(8,128)S(1)} %get-tuple-element.12, f32[15,34,130]{2,1,0:T(8,128)S(1)} %get-tuple-element.10, f32[15,34,130]{2,1,0:T(8,128)S(1)} %get-tuple-element.9, ...), kind=kLoop, calls=%fused_computation.41 | loop fusion | flops 1723800 | bytes 4243234 | tf_op jit(solution)/shard_map/jit(_where)/select_n | solution.py:65
  23.2 0.4 fusion.101
  23.6 0.6 fusion.89
  24.2 0.7 %select_reduce_fusion = bf16[30,1024]{1,0:T(8,128)(2,1)S(1)} fusion(pred[32,1024]{1,0:T(8,128)(4,1)S(1)} %iota_compare_fusion.1, bf16[30,32,128]{2,1,0:T(8,128)(2,1)S(1)} %bitcast_convert_fusion, s32[1024]{0:T(1024)S(1)} %bitcast.82), kind=kOutput, calls=%fused_computation.35 | convolution fusion | flops 253724672 | bytes 344064 | tf_op jit(solution)/shard_map/dot_general | solution.py:123
  25.0 14.2 %all_to_all.10 = bf16[30,8,256]{2,0,1:T(8,128)(2,1)S(1)} all-to-all(bf16[30,8,256]{2,0,1:T(8,128)(2,1)S(1)} %bitcast.75), channel_id=1, replica_groups=mesh['lat'=4,'lon'=2,'lev'=4] {'lon','lev'}, dimensions={1} | all-to-all | bytes 245760 | tf_op jit(solution)/shard_map/all_to_all | solution.py:148
  39.6 3.7 %fusion.15 = bf16[1024,512]{0,1:T(8,128)(2,1)S(1)} fusion(bf16[1,2,1024,1024]{3,2,1,0:T(8,128)(2,1)} %param.12, bf16[120,512]{1,0:T(8,128)(2,1)S(1)} %bitcast.79, bf16[1,120,1024]{2,1,0:T(8,128)(2,1)S(1)} %copy-done), kind=kOutput, calls=%fused_computation.18 | convolution fusion | flops 1209008128 | bytes 3514368 | tf_op jit(solution)/shard_map/dot_general | solution.py:94
  43.3 3.5 %fusion.64 = bf16[120,512]{1,0:T(8,128)(2,1)S(1)} fusion(bf16[1024,512]{0,1:T(8,128)(2,1)S(1)} %fusion.15, bf16[1,2,1024,1024]{3,2,1,0:T(8,128)(2,1)} %param.12, bf16[1,1024,120]{1,2,0:T(8,128)(2,1)S(1)} %copy-done.5), kind=kOutput, calls=%fused_computation.67 | convolution fusion | flops 1204350976 | bytes 3514368 | tf_op jit(solution)/shard_map/dot_general | solution.py:98
  46.9 0.7 %copy.89 = bf16[30,8,256]{2,0,1:T(8,128)(2,1)} copy(bf16[30,8,256]{2,1,0:T(8,128)(2,1)S(1)} %reshape.103) | data formatting | bytes 245760 | tf_op jit(solution)/shard_map/reshape | solution.py:160
  47.6 3.4 %all-to-all-start.1 = ((bf16[30,8,256]{2,0,1:T(8,128)(2,1)}), bf16[30,8,256]{2,0,1:T(8,128)(2,1)S(1)}, u32[]{:S(2)}, u32[]{:S(2)}) async-start(bf16[30,8,256]{2,0,1:T(8,128)(2,1)} %copy.89), calls=%async_computation.1 | async-start | bytes 262144 | tf_op jit(solution)/shard_map/all_to_all | solution.py:162
  51.0 7.4 %all-to-all-done.1 = bf16[30,8,256]{2,0,1:T(8,128)(2,1)S(1)} async-done(((bf16[30,8,256]{2,0,1:T(8,128)(2,1)}), bf16[30,8,256]{2,0,1:T(8,128)(2,1)S(1)}, u32[]{:S(2)}, u32[]{:S(2)}) %all-to-all-start.1) | async-done | bytes 122912 | tf_op jit(solution)/shard_map/all_to_all | solution.py:162
  58.6 0.2 broadcast_select_fusion
  58.8 1.5 %fusion.51 = f32[30,32,128]{2,1,0:T(8,128)} fusion(f32[30,32,128]{2,1,0:T(8,128)S(1)} %bitcast.74, pred[32,1024]{1,0:T(8,128)(4,1)S(1)} %iota_compare_fusion.1, bf16[30,1024]{1,0:T(8,128)(2,1)S(1)} %bitcast.80, s32[1024]{0:T(1024)S(1)} %bitcast.83), kind=kOutput, calls=%fused_computation.64 | convolution fusion | flops 252895232 | bytes 1081344 | tf_op jit(solution)/shard_map/dot_general | solution.py:173
  (43 shorter events, 1.4 us)
Async XLA Ops:
  0.0 39.5 %copy-start = (bf16[1,120,1024]{2,1,0:T(8,128)(2,1)S(1)}, bf16[1,120,1024]{2,1,0:T(8,128)(2,1)}, u32[]{:S(2)}) copy-start(bf16[1,120,1024]{2,1,0:T(8,128)(2,1)} %param.11) | copy-start | bytes 737284
  0.0 7.5 %copy-start.1 = (f32[2,15,32,128]{3,2,1,0:T(8,128)S(1)}, f32[2,15,32,128]{3,2,1,0:T(8,128)}, u32[]{:S(2)}) copy-start(f32[2,15,32,128]{3,2,1,0:T(8,128)} %param.7) | copy-start | bytes 1474564
  2.0 7.4 %collective-permute-start.1 = (f32[45,3,128]{2,1,0:T(4,128)S(1)}, f32[45,3,128]{2,1,0:T(4,128)S(1)}, u32[]{:S(2)}, u32[]{:S(2)}) collective-permute-start(f32[45,3,128]{2,1,0:T(4,128)S(1)} %pad_maximum_fusion.14), channel_id=1, source_target_pairs={{8,0},{16,8},{24,16},{9,1},{17,9},{25,17},{10,2},{18,10},{26,18},{... | collective-permute-start | bytes 207368 | tf_op jit(solution)/shard_map/ppermute | solution.py:22
  3.3 6.3 %collective-permute-start = (f32[45,3,128]{2,1,0:T(4,128)S(1)}, f32[45,3,128]{2,1,0:T(4,128)S(1)}, u32[]{:S(2)}, u32[]{:S(2)}) collective-permute-start(f32[45,3,128]{2,1,0:T(4,128)S(1)} %pad_maximum_fusion.13), channel_id=1, source_target_pairs={{0,8},{8,16},{16,24},{1,9},{9,17},{17,25},{2,10},{10,18},{18,26},{... | collective-permute-start | bytes 207368 | tf_op jit(solution)/shard_map/ppermute | solution.py:17
  7.5 1.7 %copy-start.3 = (s32[1,1024]{1,0:T(1,128)S(1)}, s32[1,1024]{1,0:T(1,128)}, u32[]{:S(2)}) copy-start(s32[1,1024]{1,0:T(1,128)} %param.9) | copy-start | bytes 12292
  9.3 8.4 %copy-start.2 = (f32[15,32,128]{2,1,0:T(8,128)S(1)}, f32[15,32,128]{2,1,0:T(8,128)}, u32[]{:S(2)}) copy-start(f32[15,32,128]{2,1,0:T(8,128)} %param.8) | copy-start | bytes 737284
  10.2 6.6 %collective-permute-start.2 = (f32[45,38,6]{0,1,2:T(8,128)S(1)}, f32[45,38,6]{0,1,2:T(8,128)S(1)}, u32[]{:S(2)}, u32[]{:S(2)}) collective-permute-start(f32[45,38,6]{0,1,2:T(8,128)S(1)} %maximum_maximum_fusion), channel_id=1, source_target_pairs={{0,4},{4,0},{1,5},{5,1},{2,6},{6,2},{3,7},{7,3},{8,12},{12,8},{9,1... | collective-permute-start | bytes 123128 | tf_op jit(solution)/shard_map/ppermute | solution.py:34
  39.6 3.8 %copy-start.5 = (bf16[1,1024,120]{1,2,0:T(8,128)(2,1)S(1)}, bf16[1,1024,120]{1,2,0:T(8,128)(2,1)}, u32[]{:S(2)}) copy-start(bf16[1,1024,120]{1,2,0:T(8,128)(2,1)} %param.13) | copy-start | bytes 737284
  43.3 7.7 %copy-start.4 = (s32[1,1024,1]{1,2,0:T(1,128)S(1)}, s32[1,1024,1]{1,2,0:T(1,128)}, u32[]{:S(2)}) copy-start(s32[1,1024,1]{1,2,0:T(1,128)} %param.10) | copy-start | bytes 12292
  47.6 10.8 %all-to-all-start.1 = ((bf16[30,8,256]{2,0,1:T(8,128)(2,1)}), bf16[30,8,256]{2,0,1:T(8,128)(2,1)S(1)}, u32[]{:S(2)}, u32[]{:S(2)}) async-start(bf16[30,8,256]{2,0,1:T(8,128)(2,1)} %copy.89), calls=%async_computation.1 | async-start | bytes 262144 | tf_op jit(solution)/shard_map/all_to_all | solution.py:162

commit v11 on v5

--- a/solution.py
+++ b/solution.py
@@ -8,14 +8,6 @@
 
 
 def halo_exchange(cells, width):
-    lat_count = lax.axis_size("lat")
-    from_above = lax.ppermute(
-        cells[..., cells.shape[-2] - width :, :], "lat", [(i, i + 1) for i in range(lat_count - 1)]
-    )
-    from_below = lax.ppermute(
-        cells[..., :width, :], "lat", [(i + 1, i) for i in range(lat_count - 1)]
-    )
-    cells = jnp.concatenate([from_above, cells, from_below], axis=-2)
     lon_count = lax.axis_size("lon")
     left = cells[..., :width]
     right = cells[..., cells.shape[-1] - width :]
@@ -25,7 +17,15 @@
     else:
         from_left = lax.ppermute(right, "lon", [(i, (i + 1) % lon_count) for i in range(lon_count)])
         from_right = lax.ppermute(left, "lon", [((i + 1) % lon_count, i) for i in range(lon_count)])
-    return jnp.concatenate([from_left, cells, from_right], axis=-1)
+    cells = jnp.concatenate([from_left, cells, from_right], axis=-1)
+    lat_count = lax.axis_size("lat")
+    from_above = lax.ppermute(
+        cells[..., cells.shape[-2] - width :, :], "lat", [(i, i + 1) for i in range(lat_count - 1)]
+    )
+    from_below = lax.ppermute(
+        cells[..., :width, :], "lat", [(i + 1, i) for i in range(lat_count - 1)]
+    )
+    return jnp.concatenate([from_above, cells, from_below], axis=-2)
 
 
 def substep(values, coefficients):

time: 60 us -> 60.4 us (level)
  the two profiles are of different devices: /device:TPU:0 before, /device:TPU:2 now
where the time goes in v11:
time: 60.4 us; the launch traced here: 60.1 us
  waiting for transfers between devices  14.8 us (25%)
  blocking collectives  13.2 us (22%)
  matrix products  9.36 us (15%)
  starting transfers between devices  9.29 us (15%)
  other arithmetic  9.03 us (15%)
  local copies, waits for them, and re-layouts  4.04 us (7%)
    all_to_all x1, blocking collectives, on_device(): lax.all_to_all(send_buffer, ('lon', 'lev'), split_axis=1, concat_axis=1,...  13.2 us
    all_to_all x1, waiting for transfers between devices, on_device(): lax.all_to_all(outgoing, ('lon', 'lev'), split_axis=1, concat_axis=1, til...  7.42 us
    ppermute x1, waiting for transfers between devices, halo_exchange(): lax.ppermute(cells[..., cells.shape[-2] - width:, :], 'lat', [(i, i + 1)...  3.82 us
    dot_general x1, matrix products, network(): lax.dot_general(w_middle[layer_no], hidden, contract, preferred_element_t...  3.73 us
    dot_general x1, matrix products, network(): lax.dot_general(w_last, hidden, contract, preferred_element_type=jnp.floa...  3.44 us
    all_to_all x1, starting transfers between devices, on_device(): lax.all_to_all(outgoing, ('lon', 'lev'), split_axis=1, concat_axis=1, til...  3.37 us
    ppermute x1, waiting for transfers between devices, halo_exchange(): lax.ppermute(jnp.concatenate([right, left], axis=-1), 'lon', [(0, 1), (1,...  3 us
    select_n x2, other arithmetic, clear_outside(): return jnp.where(inside[:, None], values, 0.0)  2.78 us
  transfers between devices with their start and end apart: 4, of which 4 were waited for; matrix products, arithmetic and copies ran while one was open for 0% of the time, Pallas kernels for 0%

profile of v11, /device:TPU:2, one launch (start us, length us, event | category | flops | bytes accessed | tf_op | source)
XLA Modules:
  0.0 60.1 jit_solution(6795579929088353204)
XLA Ops:
  0.0 1.7 %slice_maximum_fusion = (f32[45,32,3]{2,1,0:T(8,128)S(1)}, f32[45,32,3]{2,1,0:T(8,128)S(1)}) fusion(f32[15,32,128]{2,1,0:T(8,128)} %param.8, f32[30,32,128]{2,1,0:T(8,128)} %bitcast.69), kind=kLoop, calls=%fused_computation.79 | loop fusion | flops 8640 | bytes 771840 | tf_op jit(solution)/shard_map/concatenate | solution.py:57
  1.8 0.6 copy.40
  2.3 0.6 copy.39
  2.9 1.6 %collective-permute-start = (f32[45,32,6]{0,1,2:T(8,128)S(1)}, f32[45,32,6]{0,1,2:T(8,128)S(1)}, u32[]{:S(2)}, u32[]{:S(2)}) collective-permute-start(f32[45,32,6]{0,1,2:T(8,128)S(1)} %pad_maximum_fusion.18), channel_id=1, source_target_pairs={{0,4},{4,0},{1,5},{5,1},{2,6},{6,2},{3,7},{7,3},{8,12},{12,8},{9,1... | collective-permute-start | bytes 103688 | tf_op jit(solution)/shard_map/ppermute | solution.py:15
  4.6 3.0 %collective-permute-done = f32[45,32,6]{0,1,2:T(8,128)S(1)} collective-permute-done((f32[45,32,6]{0,1,2:T(8,128)S(1)}, f32[45,32,6]{0,1,2:T(8,128)S(1)}, u32[]{:S(2)}, u32[]{:S(2)}) %collective-permute-start) | collective-permute-done | bytes 34592 | tf_op jit(solution)/shard_map/ppermute | solution.py:15
  7.6 0.8 %copy.52 = f32[45,32,3]{2,1,0:T(8,128)S(1)} copy(f32[45,32,3]{0,1,2:T(8,128)S(1)} %get-tuple-element.24) | data formatting | bytes 34560
  8.4 0.8 %copy.51 = f32[45,32,3]{2,1,0:T(8,128)S(1)} copy(f32[45,32,3]{0,1,2:T(8,128)S(1)} %get-tuple-element.23) | data formatting | bytes 34560
  9.2 0.4 pad_maximum_fusion.17
  9.5 1.9 %collective-permute-start.2 = (f32[45,3,134]{2,1,0:T(4,128)S(1)}, f32[45,3,134]{2,1,0:T(4,128)S(1)}, u32[]{:S(2)}, u32[]{:S(2)}) collective-permute-start(f32[45,3,134]{2,1,0:T(4,128)S(1)} %get-tuple-element.12), channel_id=1, source_target_pairs={{8,0},{16,8},{24,16},{9,1},{17,9},{25,17},{10,2},{18,10},{26,18},{... | collective-permute-start | bytes 217088 | tf_op jit(solution)/shard_map/ppermute | solution.py:25
  11.5 2.4 %collective-permute-start.1 = (f32[45,3,134]{2,1,0:T(4,128)S(1)}, f32[45,3,134]{2,1,0:T(4,128)S(1)}, u32[]{:S(2)}, u32[]{:S(2)}) collective-permute-start(f32[45,3,134]{2,1,0:T(4,128)S(1)} %get-tuple-element.11), channel_id=1, source_target_pairs={{0,8},{8,16},{16,24},{1,9},{9,17},{17,25},{2,10},{10,18},{18,26},{... | collective-permute-start | bytes 217088 | tf_op jit(solution)/shard_map/ppermute | solution.py:22
  13.9 0.6 collective-permute-done.2
  14.5 3.8 %collective-permute-done.1 = f32[45,3,134]{2,1,0:T(4,128)S(1)} collective-permute-done((f32[45,3,134]{2,1,0:T(4,128)S(1)}, f32[45,3,134]{2,1,0:T(4,128)S(1)}, u32[]{:S(2)}, u32[]{:S(2)}) %collective-permute-start.1) | collective-permute-done | bytes 72392 | tf_op jit(solution)/shard_map/ppermute | solution.py:22
  18.3 0.8 %pad_maximum_fusion = f32[45,38,134]{2,1,0:T(8,128)S(1)} fusion(f32[45,3,134]{2,1,0:T(4,128)S(1)} %collective-permute-done.2, f32[45,32,3]{2,1,0:T(8,128)S(1)} %copy.52, f32[15,32,128]{2,1,0:T(8,128)S(1)} %copy-done.2, f32[30,32,128]{2,1,0:T(8,128)S(1)} %bitcast.71, f32[45,32,3]{2,1,0:T(8,128)S(1)} %copy.51, f32[45,3,134]{2,1,0:T(4,128)S(1)} %collective-permute-done.1), kind=kLoop, calls=%fused_computation.37 | loop fusion | flops 1145700 | bytes 1833120 | tf_op jit(solution)/shard_map/concatenate | solution.py:28
  19.2 0.1 slice.196
  19.2 0.7 %fusion.84 = (f32[15,36,132]{2,1,0:T(8,128)S(1)}, f32[15,36,132]{2,1,0:T(8,128)S(1)}, f32[15,36,132]{2,1,0:T(8,128)S(1)}, f32[15,36,132]{2,1,0:T(8,128)S(1)}) fusion(f32[45,38,134]{2,1,0:T(8,128)S(1)} %pad_maximum_fusion), kind=kLoop, calls=%fused_computation.95 | loop fusion | flops 570240 | bytes 2566080 | tf_op jit(solution)/shard_map/mul | solution.py:42
  20.0 1.4 %fusion.44 = f32[2,15,36,132]{3,2,1,0:T(8,128)S(1)} fusion(f32[2,15,38,134]{3,2,1,0:T(8,128)S(1)} %bitcast.68, f32[15,36,132]{2,1,0:T(8,128)S(1)} %get-tuple-element.16, f32[15,36,132]{2,1,0:T(8,128)S(1)} %get-tuple-element.17, f32[15,36,132]{2,1,0:T(8,128)S(1)} %get-tuple-element.18, f32[15,36,132]{2,1,0:T(8,128)S(1)} %get-tuple-element.15, ...), kind=kLoop, calls=%fused_computation.54 | loop fusion | flops 1853280 | bytes 4561956 | tf_op jit(solution)/shard_map/jit(_where)/select_n | solution.py:52
  21.3 1.2 %fusion.80 = (f32[15,34,130]{2,1,0:T(8,128)S(1)}, f32[15,34,130]{2,1,0:T(8,128)S(1)}, f32[15,34,130]{2,1,0:T(8,128)S(1)}, f32[15,34,130]{2,1,0:T(8,128)S(1)}) fusion(f32[45,3,134]{2,1,0:T(4,128)S(1)} %collective-permute-done.1, f32[45,32,3]{2,1,0:T(8,128)S(1)} %copy.52, f32[45,32,3]{2,1,0:T(8,128)S(1)} %copy.51, f32[15,32,128]{2,1,0:T(8,128)S(1)} %copy-done.2, ...), kind=kLoop, calls=%fused_computation.87 | loop fusion | flops 1060800 | bytes 2772960 | tf_op jit(solution)/shard_map/mul | solution.py:42
  22.5 1.4 %fusion.35 = f32[2,15,34,130]{3,2,1,0:T(8,128)S(1)} fusion(f32[2,15,36,132]{3,2,1,0:T(8,128)S(1)} %fusion.44, f32[15,34,130]{2,1,0:T(8,128)S(1)} %get-tuple-element.13, f32[15,34,130]{2,1,0:T(8,128)S(1)} %get-tuple-element.14, f32[15,34,130]{2,1,0:T(8,128)S(1)} %get-tuple-element.8, f32[15,34,130]{2,1,0:T(8,128)S(1)} %get-tuple-element.7, ...), kind=kLoop, calls=%fused_computation.41 | loop fusion | flops 1723800 | bytes 4243234 | tf_op jit(solution)/shard_map/jit(_where)/select_n | solution.py:52
  23.9 0.5 fusion.105
  24.4 0.6 %fusion.89 = f32[2,15,32,128]{3,2,1,0:T(8,128)S(1)} fusion(f32[2,15,34,130]{3,2,1,0:T(8,128)S(1)} %fusion.35, f32[15,32,128]{2,1,0:T(8,128)S(1)} %get-tuple-element.19, f32[15,32,128]{2,1,0:T(8,128)S(1)} %get-tuple-element.20, f32[15,32,128]{2,1,0:T(8,128)S(1)} %get-tuple-element.10, f32[15,32,128]{2,1,0:T(8,128)S(1)} %get-tuple-element.9), kind=kLoop, calls=%fused_computation.100 | loop fusion | flops 1474560 | bytes 3932160 | tf_op jit(solution)/shard_map/add | solution.py:43
  25.1 0.7 %select_reduce_fusion = bf16[30,1024]{1,0:T(8,128)(2,1)S(1)} fusion(pred[32,1024]{1,0:T(8,128)(4,1)S(1)} %iota_compare_fusion.1, bf16[30,32,128]{2,1,0:T(8,128)(2,1)S(1)} %bitcast_convert_fusion, s32[1024]{0:T(1024)S(1)} %bitcast.82), kind=kOutput, calls=%fused_computation.35 | convolution fusion | flops 253724672 | bytes 344064 | tf_op jit(solution)/shard_map/dot_general | solution.py:111
  25.9 13.2 %all_to_all.10 = bf16[30,8,256]{2,0,1:T(8,128)(2,1)S(1)} all-to-all(bf16[30,8,256]{2,0,1:T(8,128)(2,1)S(1)} %bitcast.75), channel_id=1, replica_groups=mesh['lat'=4,'lon'=2,'lev'=4] {'lon','lev'}, dimensions={1} | all-to-all | bytes 245760 | tf_op jit(solution)/shard_map/all_to_all | solution.py:136
  39.1 0.1 copy.57
  39.2 0.1 copy.45
  39.3 3.7 %fusion.15 = bf16[1024,512]{0,1:T(8,128)(2,1)S(1)} fusion(bf16[1,2,1024,1024]{3,2,1,0:T(8,128)(2,1)} %param.12, bf16[120,512]{1,0:T(8,128)(2,1)S(1)} %bitcast.79, bf16[1,120,1024]{2,1,0:T(8,128)(2,1)S(1)} %copy-done), kind=kOutput, calls=%fused_computation.18 | convolution fusion | flops 1209008128 | bytes 3514368 | tf_op jit(solution)/shard_map/dot_general | solution.py:82
  43.1 3.4 %fusion.64 = bf16[120,512]{1,0:T(8,128)(2,1)S(1)} fusion(bf16[1024,512]{0,1:T(8,128)(2,1)S(1)} %fusion.15, bf16[1,2,1024,1024]{3,2,1,0:T(8,128)(2,1)} %param.12, bf16[1,1024,120]{1,2,0:T(8,128)(2,1)S(1)} %copy-done.5), kind=kOutput, calls=%fused_computation.67 | convolution fusion | flops 1204350976 | bytes 3514368 | tf_op jit(solution)/shard_map/dot_general | solution.py:86
  46.7 0.7 %copy.47 = bf16[30,8,256]{2,0,1:T(8,128)(2,1)} copy(bf16[30,8,256]{2,1,0:T(8,128)(2,1)S(1)} %reshape.103) | data formatting | bytes 245760 | tf_op jit(solution)/shard_map/reshape | solution.py:148
  47.4 3.4 %all-to-all-start.1 = ((bf16[30,8,256]{2,0,1:T(8,128)(2,1)}), bf16[30,8,256]{2,0,1:T(8,128)(2,1)S(1)}, u32[]{:S(2)}, u32[]{:S(2)}) async-start(bf16[30,8,256]{2,0,1:T(8,128)(2,1)} %copy.47), calls=%async_computation.1 | async-start | bytes 262144 | tf_op jit(solution)/shard_map/all_to_all | solution.py:150
  50.8 7.4 %all-to-all-done.1 = bf16[30,8,256]{2,0,1:T(8,128)(2,1)S(1)} async-done(((bf16[30,8,256]{2,0,1:T(8,128)(2,1)}), bf16[30,8,256]{2,0,1:T(8,128)(2,1)S(1)}, u32[]{:S(2)}, u32[]{:S(2)}) %all-to-all-start.1) | async-done | bytes 122912 | tf_op jit(solution)/shard_map/all_to_all | solution.py:150
  58.2 0.1 copy.48
  58.3 0.2 broadcast_select_fusion
  58.6 1.5 %fusion.51 = f32[30,32,128]{2,1,0:T(8,128)} fusion(f32[30,32,128]{2,1,0:T(8,128)S(1)} %bitcast.74, pred[32,1024]{1,0:T(8,128)(4,1)S(1)} %iota_compare_fusion.1, bf16[30,1024]{1,0:T(8,128)(2,1)S(1)} %bitcast.80, s32[1024]{0:T(1024)S(1)} %bitcast.83), kind=kOutput, calls=%fused_computation.64 | convolution fusion | flops 252895232 | bytes 1081344 | tf_op jit(solution)/shard_map/dot_general | solution.py:161
  (31 shorter events, 0.5 us)
Async XLA Ops:
  0.0 39.3 %copy-start = (bf16[1,120,1024]{2,1,0:T(8,128)(2,1)S(1)}, bf16[1,120,1024]{2,1,0:T(8,128)(2,1)}, u32[]{:S(2)}) copy-start(bf16[1,120,1024]{2,1,0:T(8,128)(2,1)} %param.11) | copy-start | bytes 737284
  0.0 4.5 %copy-start.3 = (s32[1,1024]{1,0:T(1,128)S(1)}, s32[1,1024]{1,0:T(1,128)}, u32[]{:S(2)}) copy-start(s32[1,1024]{1,0:T(1,128)} %param.9) | copy-start | bytes 12292
  1.8 7.4 %copy-start.1 = (f32[2,15,32,128]{3,2,1,0:T(8,128)S(1)}, f32[2,15,32,128]{3,2,1,0:T(8,128)}, u32[]{:S(2)}) copy-start(f32[2,15,32,128]{3,2,1,0:T(8,128)} %param.7) | copy-start | bytes 1474564
  1.8 7.4 %copy-start.2 = (f32[15,32,128]{2,1,0:T(8,128)S(1)}, f32[15,32,128]{2,1,0:T(8,128)}, u32[]{:S(2)}) copy-start(f32[15,32,128]{2,1,0:T(8,128)} %param.8) | copy-start | bytes 737284
  2.9 4.7 %collective-permute-start = (f32[45,32,6]{0,1,2:T(8,128)S(1)}, f32[45,32,6]{0,1,2:T(8,128)S(1)}, u32[]{:S(2)}, u32[]{:S(2)}) collective-permute-start(f32[45,32,6]{0,1,2:T(8,128)S(1)} %pad_maximum_fusion.18), channel_id=1, source_target_pairs={{0,4},{4,0},{1,5},{5,1},{2,6},{6,2},{3,7},{7,3},{8,12},{12,8},{9,1... | collective-permute-start | bytes 103688 | tf_op jit(solution)/shard_map/ppermute | solution.py:15
  9.5 5.0 %collective-permute-start.2 = (f32[45,3,134]{2,1,0:T(4,128)S(1)}, f32[45,3,134]{2,1,0:T(4,128)S(1)}, u32[]{:S(2)}, u32[]{:S(2)}) collective-permute-start(f32[45,3,134]{2,1,0:T(4,128)S(1)} %get-tuple-element.12), channel_id=1, source_target_pairs={{8,0},{16,8},{24,16},{9,1},{17,9},{25,17},{10,2},{18,10},{26,18},{... | collective-permute-start | bytes 217088 | tf_op jit(solution)/shard_map/ppermute | solution.py:25
  11.5 6.9 %collective-permute-start.1 = (f32[45,3,134]{2,1,0:T(4,128)S(1)}, f32[45,3,134]{2,1,0:T(4,128)S(1)}, u32[]{:S(2)}, u32[]{:S(2)}) collective-permute-start(f32[45,3,134]{2,1,0:T(4,128)S(1)} %get-tuple-element.11), channel_id=1, source_target_pairs={{0,8},{8,16},{16,24},{1,9},{9,17},{17,25},{2,10},{10,18},{18,26},{... | collective-permute-start | bytes 217088 | tf_op jit(solution)/shard_map/ppermute | solution.py:22
  39.3 3.8 %copy-start.5 = (bf16[1,1024,120]{1,2,0:T(8,128)(2,1)S(1)}, bf16[1,1024,120]{1,2,0:T(8,128)(2,1)}, u32[]{:S(2)}) copy-start(bf16[1,1024,120]{1,2,0:T(8,128)(2,1)} %param.13) | copy-start | bytes 737284
  43.1 7.7 %copy-start.4 = (s32[1,1024,1]{1,2,0:T(1,128)S(1)}, s32[1,1024,1]{1,2,0:T(1,128)}, u32[]{:S(2)}) copy-start(s32[1,1024,1]{1,2,0:T(1,128)} %param.10) | copy-start | bytes 12292
  47.4 10.8 %all-to-all-start.1 = ((bf16[30,8,256]{2,0,1:T(8,128)(2,1)}), bf16[30,8,256]{2,0,1:T(8,128)(2,1)S(1)}, u32[]{:S(2)}, u32[]{:S(2)}) async-start(bf16[30,8,256]{2,0,1:T(8,128)(2,1)} %copy.47), calls=%async_computation.1 | async-start | bytes 262144 | tf_op jit(solution)/shard_map/all_to_all | solution.py:150

commit v12 on v10

--- a/solution.py
+++ b/solution.py
@@ -1,87 +1,96 @@
 import jax
 import jax.numpy as jnp
 from jax import lax
+from jax.experimental import pallas as pl
+from jax.experimental.pallas import tpu as pltpu
 from jax.sharding import PartitionSpec as P
 
 LEVELS = 60
 STEPS = 3
 
 
-def halo_exchange(planes, diffusivity, width):
+def stencil_kernel(own_ref, kappa_ref, rows_ref, lanes_ref, mask_ref, out_ref):
+    kinds, levels = out_ref.shape[0], out_ref.shape[1]
+    lat_rows, lon_cols = out_ref.shape[2], out_ref.shape[3]
+    mask = mask_ref[...] > 0.5
+    tile_rows = lat_rows + rows_ref.shape[1]
+    tile_cols = lon_cols + lanes_ref.shape[2]
+    shifts = ((1, 0), (tile_rows - 1, 0), (1, 1), (tile_cols - 1, 1))
+
+    def tile(own, plane):
+        top = jnp.concatenate([own, rows_ref[plane]], axis=0)
+        return jnp.concatenate([top, lanes_ref[plane]], axis=1)
+
+    def level(index, carry):
+        kappa = tile(kappa_ref[index], kinds * levels + index)
+        faces = [0.5 * (kappa + pltpu.roll(kappa, shift, axis)) for shift, axis in shifts]
+        for kind in range(kinds):
+            plane = kind * levels + index
+            values = tile(own_ref[plane], plane)
+            for repeat in range(STEPS):
+                updated = values
+                for face, (shift, axis) in zip(faces, shifts):
+                    updated = updated + face * (pltpu.roll(values, shift, axis) - values)
+                values = jnp.where(mask, updated, 0.0)
+            out_ref[kind, index] = values[:lat_rows, :lon_cols]
+        return carry
+
+    lax.fori_loop(0, levels, level, 0)
+
+
+def dynamics(fields, diffusivity):
+    kinds, level_rows, lat_rows, lon_cols = fields.shape
+    planes = fields.reshape(kinds * level_rows, lat_rows, lon_cols)
     lat_count, lon_count = lax.axis_size("lat"), lax.axis_size("lon")
-    rows, cols = planes.shape[-2], planes.shape[-1]
+    width = STEPS
+    row_pad = 8 * ((2 * width + 7) // 8)
+    lane_pad = 128 * ((2 * width + 127) // 128)
 
     def both(cut):
         return jnp.concatenate([planes[cut], diffusivity[cut]], axis=0)
 
-    from_above = lax.ppermute(
-        both((slice(None), slice(rows - width, None))),
+    north = lax.ppermute(
+        both((slice(None), slice(lat_rows - width, None))),
         "lat",
         [(i, i + 1) for i in range(lat_count - 1)],
     )
-    from_below = lax.ppermute(
+    south = lax.ppermute(
         both((slice(None), slice(0, width))), "lat", [(i + 1, i) for i in range(lat_count - 1)]
     )
+    gap = jnp.zeros((north.shape[0], row_pad - 2 * width, lon_cols), north.dtype)
+    row_block = jnp.concatenate([south, gap, north], axis=1)
 
     def edge(cut):
         return jnp.concatenate(
-            [from_above[..., cut], both((slice(None), slice(None), cut)), from_below[..., cut]],
-            axis=-2,
+            [both((slice(None), slice(None), cut)), row_block[..., cut]], axis=1
         )
 
-    left, right = edge(slice(0, width)), edge(slice(cols - width, None))
+    left, right = edge(slice(0, width)), edge(slice(lon_cols - width, None))
     if lon_count == 2:
         swapped = lax.ppermute(jnp.concatenate([right, left], axis=-1), "lon", [(0, 1), (1, 0)])
-        from_left, from_right = swapped[..., :width], swapped[..., width:]
+        west, east = swapped[..., :width], swapped[..., width:]
     else:
-        from_left = lax.ppermute(right, "lon", [(i, (i + 1) % lon_count) for i in range(lon_count)])
-        from_right = lax.ppermute(left, "lon", [((i + 1) % lon_count, i) for i in range(lon_count)])
-    stacked = jnp.concatenate([planes, diffusivity], axis=0)
-    stacked = jnp.concatenate([from_above, stacked, from_below], axis=-2)
-    return jnp.concatenate([from_left, stacked, from_right], axis=-1)
-
-
-def substep(values, coefficients):
-    centre = values[..., 1:-1, 1:-1]
-    middle = coefficients[:, 1:-1, 1:-1]
-    updated = centre
-    for lat_cut, lon_cut in (
-        (slice(0, -2), slice(1, -1)),
-        (slice(2, None), slice(1, -1)),
-        (slice(1, -1), slice(0, -2)),
-        (slice(1, -1), slice(2, None)),
-    ):
-        neighbour = values[..., lat_cut, lon_cut]
-        face_coef = 0.5 * (middle + coefficients[:, lat_cut, lon_cut])
-        updated = updated + face_coef * (neighbour - centre)
-    return updated
-
-
-def clear_outside(values, rim_width, lat_rows):
-    lat_pos = (
-        lax.axis_index("lat") * lat_rows - rim_width + jnp.arange(values.shape[-2], dtype=jnp.int32)
-    )
-    inside = (lat_pos >= 0) & (lat_pos < lat_rows * lax.axis_size("lat"))
-    return jnp.where(inside[:, None], values, 0.0)
-
-
-def dynamics(fields, diffusivity):
-    kinds, level_rows, lat_rows, lon_cols = fields.shape
-    stacked = halo_exchange(
-        fields.reshape(kinds * level_rows, lat_rows, lon_cols), diffusivity, STEPS
-    )
-    values = stacked[: kinds * level_rows].reshape(
-        kinds, level_rows, lat_rows + 2 * STEPS, lon_cols + 2 * STEPS
-    )
-    kappa = stacked[kinds * level_rows :]
-    for repeat in range(STEPS):
-        trim = repeat
-        coefficients = kappa[:, trim : kappa.shape[1] - trim, trim : kappa.shape[2] - trim]
-        values = substep(values, coefficients)
-        rim = STEPS - repeat - 1
-        if rim:
-            values = clear_outside(values, rim, lat_rows)
-    return values
+        west = lax.ppermute(right, "lon", [(i, (i + 1) % lon_count) for i in range(lon_count)])
+        east = lax.ppermute(left, "lon", [((i + 1) % lon_count, i) for i in range(lon_count)])
+    lane_gap = jnp.zeros(east.shape[:2] + (lane_pad - 2 * width,), east.dtype)
+    lane_block = jnp.concatenate([east, lane_gap, west], axis=-1)
+    tile_rows = lat_rows + row_pad
+    row_ids = jnp.arange(tile_rows, dtype=jnp.int32)
+    offset = jnp.where(row_ids < lat_rows + row_pad - width, row_ids, row_ids - tile_rows)
+    global_row = lax.axis_index("lat") * lat_rows + offset
+    inside = (global_row >= 0) & (global_row < lat_rows * lat_count)
+    mask = jnp.broadcast_to(inside[:, None], (tile_rows, lon_cols + lane_pad)).astype(jnp.float32)
+    vmem = pl.BlockSpec(memory_space=pltpu.VMEM)
+    cells = kinds * level_rows * lat_rows * lon_cols
+    return pl.pallas_call(
+        stencil_kernel,
+        out_shape=jax.ShapeDtypeStruct(fields.shape, fields.dtype),
+        in_specs=[vmem] * 5,
+        out_specs=vmem,
+        cost_estimate=pl.CostEstimate(
+            flops=60 * cells, transcendentals=0, bytes_accessed=16 * cells
+        ),
+    )(planes, diffusivity, row_block, lane_block, mask)
 
 
 def network(features, w_first, w_middle, w_last):

time: 60.7 us -> 64.5 us (1.063)
  Pallas kernels: 0 us -> 7.12 us
  other arithmetic: 6.83 us -> 2.86 us
  local copies, waits for them, and re-layouts: 7.75 us -> 8.43 us
    pallas_call x0 -> x1, Pallas kernels: none -> 7.12 us  [dynamics(): pl.pallas_call(stencil_kernel, out_shape=jax.ShapeDtypeStruct(fields.shap...]
    select_n x2 -> x0, other arithmetic: 2.81 us -> none  [clear_outside(): return jnp.where(inside[:, None], values, 0.0)]
    mul x3 -> x0, other arithmetic: 1.93 us -> none  [substep(): face_coef = 0.5 * (middle + coefficients[:, lat_cut, lon_cut])]
    convert_element_type x1, other arithmetic: 0.04 us -> 1.06 us  [on_device(): planes.astype(jnp.bfloat16).reshape(local_features * lat_rows, lon_cols)]
    unnamed x18, local copies, waits for them, and re-layouts: 1.66 us -> 0.74 us
    broadcast_in_dim x0 -> x3, local copies, waits for them, and re-layouts: none -> 0.69 us  [the longest x1 0.69 us: dynamics(): jnp.broadcast_to(inside[:, None], (tile_rows, lon_cols + lane_pad))]
    slice x8 -> x6, local copies, waits for them, and re-layouts: 0.76 us -> 1.34 us  [the longest x3 0.93 us: dynamics(): west, east = (swapped[..., :width], swapped[..., width:])]
    concatenate x2 -> x3, other arithmetic: 1.09 us -> 1.44 us  [the longest x1 1.25 us: dynamics(): lane_block = jnp.concatenate([east, lane_gap, west], axis=-1)]
where the time goes in v12:
time: 64.5 us; the launch traced here: 64 us
  blocking collectives  14.2 us (22%)
  waiting for transfers between devices  10.9 us (17%)
  starting transfers between devices  10.7 us (17%)
  matrix products  9.37 us (15%)
  local copies, waits for them, and re-layouts  8.43 us (13%)
  Pallas kernels  7.12 us (11%)
  other arithmetic  2.86 us (4%)
    all_to_all x1, blocking collectives, on_device(): lax.all_to_all(send_buffer, ('lon', 'lev'), split_axis=1, concat_axis=1,...  14.2 us
    all_to_all x1, waiting for transfers between devices, on_device(): lax.all_to_all(outgoing, ('lon', 'lev'), split_axis=1, concat_axis=1, til...  7.42 us
    pallas_call x1, Pallas kernels, dynamics(): pl.pallas_call(stencil_kernel, out_shape=jax.ShapeDtypeStruct(fields.shap...  7.12 us
    slice x6, local copies, waits for them, and re-layouts, both(): return jnp.concatenate([planes[cut], diffusivity[cut]], axis=0)  4.31 us
    dot_general x1, matrix products, network(): lax.dot_general(w_middle[layer_no], hidden, contract, preferred_element_t...  3.73 us
    ppermute x1, waiting for transfers between devices, dynamics(): lax.ppermute(jnp.concatenate([right, left], axis=-1), 'lon', [(0, 1), (1,...  3.5 us
    dot_general x1, matrix products, network(): lax.dot_general(w_last, hidden, contract, preferred_element_type=jnp.floa...  3.45 us
    all_to_all x1, starting transfers between devices, on_device(): lax.all_to_all(outgoing, ('lon', 'lev'), split_axis=1, concat_axis=1, til...  3.37 us
  transfers between devices with their start and end apart: 4, of which 2 were waited for; matrix products, arithmetic and copies ran while one was open for 5% of the time, Pallas kernels for 0%

profile of v12, /device:TPU:0, one launch (start us, length us, event | category | flops | bytes accessed | tf_op | source)
XLA Modules:
  0.0 64.0 jit_solution(4804723204855004748)
XLA Ops:
  0.0 1.0 %fusion.78 = (f32[30,3,128]{2,1,0:T(4,128)S(1)}, f32[30,3,128]{2,1,0:T(4,128)S(1)}) fusion(f32[30,32,128]{2,1,0:T(8,128)} %bitcast.67), kind=kLoop, calls=%fused_computation.87 | loop fusion | bytes 184320 | tf_op jit(solution)/shard_map/slice | solution.py:50
  1.1 0.9 %fusion.80 = (f32[15,3,128]{2,1,0:T(4,128)S(1)}, f32[15,3,128]{2,1,0:T(4,128)S(1)}) fusion(f32[15,32,128]{2,1,0:T(8,128)} %kappa_ref.1), kind=kLoop, calls=%fused_computation.89 | loop fusion | bytes 92160 | tf_op jit(solution)/shard_map/slice | solution.py:50
  2.0 1.3 %collective-permute-start = (f32[45,3,128]{2,1,0:T(4,128)S(1)}, f32[45,3,128]{2,1,0:T(4,128)S(1)}, u32[]{:S(2)}, u32[]{:S(2)}) collective-permute-start(f32[45,3,128]{2,1,0:T(4,128)S(1)} %pad_maximum_fusion.2), channel_id=1, source_target_pairs={{8,0},{16,8},{24,16},{9,1},{17,9},{25,17},{10,2},{18,10},{26,18},{... | collective-permute-start | bytes 207368 | tf_op jit(solution)/shard_map/ppermute | solution.py:57
  3.3 3.0 %collective-permute-start.1 = (f32[45,3,128]{2,1,0:T(4,128)S(1)}, f32[45,3,128]{2,1,0:T(4,128)S(1)}, u32[]{:S(2)}, u32[]{:S(2)}) collective-permute-start(f32[45,3,128]{2,1,0:T(4,128)S(1)} %pad_maximum_fusion.3), channel_id=1, source_target_pairs={{0,8},{8,16},{16,24},{1,9},{9,17},{17,25},{2,10},{10,18},{18,26},{... | collective-permute-start | bytes 207368 | tf_op jit(solution)/shard_map/ppermute | solution.py:52
  6.3 1.4 %fusion.77 = (f32[30,32,3]{2,1,0:T(8,128)S(1)}, f32[30,32,3]{2,1,0:T(8,128)S(1)}) fusion(f32[30,32,128]{2,1,0:T(8,128)} %bitcast.68), kind=kLoop, calls=%fused_computation.86 | loop fusion | bytes 46080 | tf_op jit(solution)/shard_map/slice | solution.py:50
  7.7 0.1 fusion.79
  8.0 0.4 copy.25
  8.4 0.4 copy.28
  8.8 0.3 copy.40
  9.2 0.3 copy.41
  9.7 0.1 fusion.81
  9.8 0.1 copy.26
  10.0 0.2 copy.29
  10.1 0.1 maximum_maximum_fusion
  10.2 3.0 %collective-permute-start.2 = (f32[45,40,6]{0,1,2:T(8,128)S(1)}, f32[45,40,6]{0,1,2:T(8,128)S(1)}, u32[]{:S(2)}, u32[]{:S(2)}) collective-permute-start(f32[45,40,6]{0,1,2:T(8,128)S(1)} %maximum_maximum_fusion), channel_id=1, source_target_pairs={{0,4},{4,0},{1,5},{5,1},{2,6},{6,2},{3,7},{7,3},{8,12},{12,8},{9,1... | collective-permute-start | bytes 129608 | tf_op jit(solution)/shard_map/ppermute | solution.py:70
  13.4 3.5 %collective-permute-done.2 = f32[45,40,6]{0,1,2:T(8,128)S(1)} collective-permute-done((f32[45,40,6]{0,1,2:T(8,128)S(1)}, f32[45,40,6]{0,1,2:T(8,128)S(1)}, u32[]{:S(2)}, u32[]{:S(2)}) %collective-permute-start.2) | collective-permute-done | bytes 43232 | tf_op jit(solution)/shard_map/ppermute | solution.py:70
  16.9 0.5 copy.30
  17.3 0.5 copy.31
  17.8 1.2 %pad_maximum_fusion.lanes_ref = f32[45,40,128]{2,1,0:T(8,128)} fusion(f32[45,40,3]{2,1,0:T(8,128)S(1)} %copy.31, f32[45,40,3]{2,1,0:T(8,128)S(1)} %copy.30, f32[128]{0:T(128)S(1)} %pad.1.clone), kind=kLoop, calls=%fused_computation.51 | loop fusion | flops 460800 | bytes 965312 | tf_op jit(solution)/shard_map/concatenate | solution.py:76
  19.0 0.7 %broadcast_in_dim.69.mask_ref = f32[40,256]{1,0:T(8,128)} broadcast(f32[40]{0:T(128)S(1)} %and_convert_fusion), dimensions={0} | broadcast | bytes 41120 | tf_op jit(solution)/shard_map/broadcast_in_dim | solution.py:82
  19.7 7.1 %shard_map.73 = f32[2,15,32,128]{3,2,1,0:T(8,128)} custom-call(f32[30,32,128]{2,1,0:T(8,128)} %bitcast.69, f32[15,32,128]{2,1,0:T(8,128)} %kappa_ref.1, f32[45,8,128]{2,1,0:T(8,128)} %copy-done.1, f32[45,40,128]{2,1,0:T(8,128)} %pad_maximum_fusion.lanes_ref, f32[40,256]{1,0:T(8,128)} %broadcast_in_dim.69.mask_ref), custom_call_target="tpu_custom_call" | custom-call | flops 7372800 | bytes 1966080 | tf_op jit(solution)/shard_map/pallas_call | solution.py:85
  26.9 1.1 %bitcast_convert_fusion = bf16[30,32,128]{2,1,0:T(8,128)(2,1)S(1)} fusion(f32[2,15,32,128]{3,2,1,0:T(8,128)} %shard_map.73), kind=kLoop, calls=%fused_computation.54 | loop fusion | flops 122880 | bytes 737280 | tf_op jit(solution)/shard_map/convert_element_type | solution.py:133
  27.9 0.7 %select_reduce_fusion = bf16[30,1024]{1,0:T(8,128)(2,1)S(1)} fusion(pred[32,1024]{1,0:T(8,128)(4,1)S(1)} %iota_compare_fusion.1, bf16[30,32,128]{2,1,0:T(8,128)(2,1)S(1)} %bitcast_convert_fusion, s32[1024]{0:T(1024)S(1)} %bitcast.78), kind=kOutput, calls=%fused_computation.35 | convolution fusion | flops 253724672 | bytes 344064 | tf_op jit(solution)/shard_map/dot_general | solution.py:132
  28.7 14.2 %all_to_all.10 = bf16[30,8,256]{2,0,1:T(8,128)(2,1)S(1)} all-to-all(bf16[30,8,256]{2,0,1:T(8,128)(2,1)S(1)} %bitcast.71), channel_id=1, replica_groups=mesh['lat'=4,'lon'=2,'lev'=4] {'lon','lev'}, dimensions={1} | all-to-all | bytes 245760 | tf_op jit(solution)/shard_map/all_to_all | solution.py:157
  43.0 0.1 copy.46
  43.3 3.7 %fusion.15 = bf16[1024,512]{0,1:T(8,128)(2,1)S(1)} fusion(bf16[1,2,1024,1024]{3,2,1,0:T(8,128)(2,1)} %param.12, bf16[120,512]{1,0:T(8,128)(2,1)S(1)} %bitcast.75, bf16[1,120,1024]{2,1,0:T(8,128)(2,1)S(1)} %copy-done), kind=kOutput, calls=%fused_computation.18 | convolution fusion | flops 1209008128 | bytes 3514368 | tf_op jit(solution)/shard_map/dot_general | solution.py:103
  47.0 3.4 %fusion.46 = bf16[120,512]{1,0:T(8,128)(2,1)S(1)} fusion(bf16[1024,512]{0,1:T(8,128)(2,1)S(1)} %fusion.15, bf16[1,2,1024,1024]{3,2,1,0:T(8,128)(2,1)} %param.12, bf16[1,1024,120]{1,2,0:T(8,128)(2,1)S(1)} %copy-done.6), kind=kOutput, calls=%fused_computation.40 | convolution fusion | flops 1204350976 | bytes 3514368 | tf_op jit(solution)/shard_map/dot_general | solution.py:107
  50.6 0.7 %copy.36 = bf16[30,8,256]{2,0,1:T(8,128)(2,1)} copy(bf16[30,8,256]{2,1,0:T(8,128)(2,1)S(1)} %reshape.99) | data formatting | bytes 245760 | tf_op jit(solution)/shard_map/reshape | solution.py:169
  51.3 3.4 %all-to-all-start.1 = ((bf16[30,8,256]{2,0,1:T(8,128)(2,1)}), bf16[30,8,256]{2,0,1:T(8,128)(2,1)S(1)}, u32[]{:S(2)}, u32[]{:S(2)}) async-start(bf16[30,8,256]{2,0,1:T(8,128)(2,1)} %copy.36), calls=%async_computation.1 | async-start | bytes 262144 | tf_op jit(solution)/shard_map/all_to_all | solution.py:171
  54.7 7.4 %all-to-all-done.1 = bf16[30,8,256]{2,0,1:T(8,128)(2,1)S(1)} async-done(((bf16[30,8,256]{2,0,1:T(8,128)(2,1)}), bf16[30,8,256]{2,0,1:T(8,128)(2,1)S(1)}, u32[]{:S(2)}, u32[]{:S(2)}) %all-to-all-start.1) | async-done | bytes 122912 | tf_op jit(solution)/shard_map/all_to_all | solution.py:171
  62.3 0.2 broadcast_select_fusion
  62.5 1.5 %fusion.33 = f32[30,32,128]{2,1,0:T(8,128)} fusion(f32[30,32,128]{2,1,0:T(8,128)S(1)} %bitcast.70, pred[32,1024]{1,0:T(8,128)(4,1)S(1)} %iota_compare_fusion.1, bf16[30,1024]{1,0:T(8,128)(2,1)S(1)} %bitcast.76, s32[1024]{0:T(1024)S(1)} %bitcast.79), kind=kOutput, calls=%fused_computation.37 | convolution fusion | flops 252895232 | bytes 1081344 | tf_op jit(solution)/shard_map/dot_general | solution.py:182
  (41 shorter events, 0.9 us)
Async XLA Ops:
  0.0 43.2 %copy-start = (bf16[1,120,1024]{2,1,0:T(8,128)(2,1)S(1)}, bf16[1,120,1024]{2,1,0:T(8,128)(2,1)}, u32[]{:S(2)}) copy-start(bf16[1,120,1024]{2,1,0:T(8,128)(2,1)} %param.11) | copy-start | bytes 737284
  0.0 7.7 %copy-start.2 = (f32[15,32,128]{2,1,0:T(8,128)S(1)}, f32[15,32,128]{2,1,0:T(8,128)}, u32[]{:S(2)}) copy-start(f32[15,32,128]{2,1,0:T(8,128)} %kappa_ref.1) | copy-start | bytes 737284
  0.0 7.9 %copy-start.4 = (s32[1,1024]{1,0:T(1,128)S(1)}, s32[1,1024]{1,0:T(1,128)}, u32[]{:S(2)}) copy-start(s32[1,1024]{1,0:T(1,128)} %param.9) | copy-start | bytes 12292
  2.0 7.6 %collective-permute-start = (f32[45,3,128]{2,1,0:T(4,128)S(1)}, f32[45,3,128]{2,1,0:T(4,128)S(1)}, u32[]{:S(2)}, u32[]{:S(2)}) collective-permute-start(f32[45,3,128]{2,1,0:T(4,128)S(1)} %pad_maximum_fusion.2), channel_id=1, source_target_pairs={{8,0},{16,8},{24,16},{9,1},{17,9},{25,17},{10,2},{18,10},{26,18},{... | collective-permute-start | bytes 207368 | tf_op jit(solution)/shard_map/ppermute | solution.py:57
  3.3 6.3 %collective-permute-start.1 = (f32[45,3,128]{2,1,0:T(4,128)S(1)}, f32[45,3,128]{2,1,0:T(4,128)S(1)}, u32[]{:S(2)}, u32[]{:S(2)}) collective-permute-start(f32[45,3,128]{2,1,0:T(4,128)S(1)} %pad_maximum_fusion.3), channel_id=1, source_target_pairs={{0,8},{8,16},{16,24},{1,9},{9,17},{17,25},{2,10},{10,18},{18,26},{... | collective-permute-start | bytes 207368 | tf_op jit(solution)/shard_map/ppermute | solution.py:52
  9.7 9.4 %copy-start.1 = (f32[45,8,128]{2,1,0:T(8,128)}, f32[45,8,128]{2,1,0:T(8,128)S(1)}, u32[]{:S(2)}) copy-start(f32[45,8,128]{2,1,0:T(8,128)S(1)} %pad_maximum_fusion.1.rows_ref) | copy-start | bytes 552964
  10.2 6.6 %collective-permute-start.2 = (f32[45,40,6]{0,1,2:T(8,128)S(1)}, f32[45,40,6]{0,1,2:T(8,128)S(1)}, u32[]{:S(2)}, u32[]{:S(2)}) collective-permute-start(f32[45,40,6]{0,1,2:T(8,128)S(1)} %maximum_maximum_fusion), channel_id=1, source_target_pairs={{0,4},{4,0},{1,5},{5,1},{2,6},{6,2},{3,7},{7,3},{8,12},{12,8},{9,1... | collective-permute-start | bytes 129608 | tf_op jit(solution)/shard_map/ppermute | solution.py:70
  43.2 3.8 %copy-start.6 = (bf16[1,1024,120]{1,2,0:T(8,128)(2,1)S(1)}, bf16[1,1024,120]{1,2,0:T(8,128)(2,1)}, u32[]{:S(2)}) copy-start(bf16[1,1024,120]{1,2,0:T(8,128)(2,1)} %param.13) | copy-start | bytes 737284
  47.0 7.7 %copy-start.5 = (s32[1,1024,1]{1,2,0:T(1,128)S(1)}, s32[1,1024,1]{1,2,0:T(1,128)}, u32[]{:S(2)}) copy-start(s32[1,1024,1]{1,2,0:T(1,128)} %param.10) | copy-start | bytes 12292
  50.5 12.0 %copy-start.3 = (f32[2,15,32,128]{3,2,1,0:T(8,128)S(1)}, f32[2,15,32,128]{3,2,1,0:T(8,128)}, u32[]{:S(2)}) copy-start(f32[2,15,32,128]{3,2,1,0:T(8,128)} %shard_map.73) | copy-start | bytes 1474564
  51.3 10.8 %all-to-all-start.1 = ((bf16[30,8,256]{2,0,1:T(8,128)(2,1)}), bf16[30,8,256]{2,0,1:T(8,128)(2,1)S(1)}, u32[]{:S(2)}, u32[]{:S(2)}) async-start(bf16[30,8,256]{2,0,1:T(8,128)(2,1)} %copy.36), calls=%async_computation.1 | async-start | bytes 262144 | tf_op jit(solution)/shard_map/all_to_all | solution.py:171

commit v13 on v5

--- a/solution.py
+++ b/solution.py
@@ -133,15 +133,20 @@
             .at[:, slot_index]
             .set(picked)
         ).reshape(local_features, group, capacity)
+    send_buffer, late_routes, unit = lax.optimization_barrier(
+        (send_buffer, routes, jnp.ones((), w_in.dtype))
+    )
+    first_layer = lax.optimization_barrier(w_in[0] * unit)
     received = lax.all_to_all(
         send_buffer, ("lon", "lev"), split_axis=1, concat_axis=1, tiled=True
     )
+    owned = [late_routes[None, :] == regime for regime in range(lon_count)]
     inputs = (
         received.reshape(2, level_rows, lon_count, lev_count, capacity)
         .transpose(0, 3, 1, 2, 4)
         .reshape(feature_count, lon_count * capacity)
     )
-    outcome = network(inputs, w_in[0], w_mid[0], w_out[0])
+    outcome = network(inputs, first_layer, w_mid[0], w_out[0])
     outgoing = (
         outcome.reshape(2, lev_count, level_rows, lon_count, capacity)
         .transpose(0, 2, 3, 1, 4)
@@ -154,7 +159,7 @@
         returned = returned.reshape(local_features, lon_count, cloudy)
         tendency = returned[:, 0]
         for regime in range(1, lon_count):
-            tendency = jnp.where(routes[None, :] == regime, returned[:, regime], tendency)
+            tendency = jnp.where(owned[regime], returned[:, regime], tendency)
     else:
         tendency = returned.reshape(local_features, group * capacity)[:, slot_index]
     spread_rows = jnp.where(row_match[None], tendency[:, None, :], jnp.zeros_like(tendency)[:, None, :])

time: 60 us -> 61 us (1.017)
  blocking collectives: 14.3 us -> 0 us
  waiting for transfers between devices: 10.9 us -> 18.6 us
  starting transfers between devices: 10.7 us -> 17.5 us
  local copies, waits for them, and re-layouts: 3.44 us -> 4.09 us
    all_to_all x1 -> x0, blocking collectives: 14.3 us -> none  [on_device(): lax.all_to_all(send_buffer, ('lon', 'lev'), split_axis=1, concat_axis=1,...]
    all_to_all x0 -> x1, waiting for transfers between devices: none -> 7.64 us  [on_device(): lax.all_to_all(send_buffer, ('lon', 'lev'), split_axis=1, concat_axis=1,...]
    all_to_all x0 -> x1, starting transfers between devices: none -> 6.79 us  [on_device(): lax.all_to_all(send_buffer, ('lon', 'lev'), split_axis=1, concat_axis=1,...]
    broadcast_in_dim x3, local copies, waits for them, and re-layouts: 0.05 us -> 0.71 us  [on_device(): jnp.broadcast_to(picked.reshape(local_features, 1, lev_count, per_device)...]
  transfers between devices with their start and end apart: 4 -> 5, of which waited for: 2 -> 3; matrix products, arithmetic and copies ran while one was open for 2% -> 2% of each run, Pallas kernels for 0% -> 0%
where the time goes in v13:
time: 61 us; the launch traced here: 60.5 us
  waiting for transfers between devices  18.6 us (30%)
  starting transfers between devices  17.5 us (29%)
  other arithmetic  10.5 us (17%)
  matrix products  9.48 us (16%)
  local copies, waits for them, and re-layouts  4.09 us (7%)
    all_to_all x1, waiting for transfers between devices, on_device(): lax.all_to_all(send_buffer, ('lon', 'lev'), split_axis=1, concat_axis=1,...  7.64 us
    all_to_all x1, waiting for transfers between devices, on_device(): lax.all_to_all(outgoing, ('lon', 'lev'), split_axis=1, concat_axis=1, til...  7.43 us
    all_to_all x1, starting transfers between devices, on_device(): lax.all_to_all(send_buffer, ('lon', 'lev'), split_axis=1, concat_axis=1,...  6.79 us
    dot_general x1, matrix products, network(): lax.dot_general(w_middle[layer_no], hidden, contract, preferred_element_t...  3.8 us
    ppermute x1, waiting for transfers between devices, halo_exchange(): lax.ppermute(jnp.concatenate([right, left], axis=-1), 'lon', [(0, 1), (1,...  3.51 us
    dot_general x1, matrix products, network(): lax.dot_general(w_last, hidden, contract, preferred_element_type=jnp.floa...  3.48 us
    all_to_all x1, starting transfers between devices, on_device(): lax.all_to_all(outgoing, ('lon', 'lev'), split_axis=1, concat_axis=1, til...  3.37 us
    ppermute x1, starting transfers between devices, halo_exchange(): lax.ppermute(cells[..., cells.shape[-2] - width:, :], 'lat', [(i, i + 1)...  3.04 us
  transfers between devices with their start and end apart: 5, of which 3 were waited for; matrix products, arithmetic and copies ran while one was open for 2% of the time, Pallas kernels for 0%

profile of v13, /device:TPU:0, one launch (start us, length us, event | category | flops | bytes accessed | tf_op | source)
XLA Modules:
  0.0 60.5 jit_solution(11384309104307751077)
XLA Ops:
  0.0 1.1 %pad_maximum_fusion.16 = (f32[45,3,128]{2,1,0:T(4,128)S(1)}, f32[45,3,128]{2,1,0:T(4,128)S(1)}) fusion(f32[15,32,128]{2,1,0:T(8,128)} %param.8, f32[30,32,128]{2,1,0:T(8,128)} %bitcast.65), kind=kLoop, calls=%fused_computation.140 | loop fusion | flops 34560 | bytes 875520 | tf_op jit(solution)/shard_map/slice | solution.py:13
  1.1 1.3 %collective-permute-start.1 = (f32[45,3,128]{2,1,0:T(4,128)S(1)}, f32[45,3,128]{2,1,0:T(4,128)S(1)}, u32[]{:S(2)}, u32[]{:S(2)}) collective-permute-start(f32[45,3,128]{2,1,0:T(4,128)S(1)} %get-tuple-element.30), channel_id=1, source_target_pairs={{8,0},{16,8},{24,16},{9,1},{17,9},{25,17},{10,2},{18,10},{26,18},{... | collective-permute-start | bytes 207368 | tf_op jit(solution)/shard_map/ppermute | solution.py:15
  2.4 3.0 %collective-permute-start = (f32[45,3,128]{2,1,0:T(4,128)S(1)}, f32[45,3,128]{2,1,0:T(4,128)S(1)}, u32[]{:S(2)}, u32[]{:S(2)}) collective-permute-start(f32[45,3,128]{2,1,0:T(4,128)S(1)} %get-tuple-element.29), channel_id=1, source_target_pairs={{0,8},{8,16},{16,24},{1,9},{9,17},{17,25},{2,10},{10,18},{18,26},{... | collective-permute-start | bytes 207368 | tf_op jit(solution)/shard_map/ppermute | solution.py:12
  5.5 0.7 %and_select_fusion = (s32[1,1024]{1,0:T(1,128)S(1)}, s32[1,1024]{1,0:T(1,128)S(1)}) fusion(s32[1,1024]{1,0:T(1,128)} %param.9), kind=kLoop, calls=%fused_computation.142 | loop fusion | flops 11264 | bytes 12288 | tf_op jit(solution)/shard_map/jit(remainder)/select_n | solution.py:106
  6.2 0.7 %and_select_fusion.1 = s32[1,1024]{1,0:T(1,128)S(1)} fusion(s32[1,1024]{1,0:T(1,128)S(1)} %get-tuple-element.12, s32[1,1024]{1,0:T(1,128)} %param.9), kind=kLoop, calls=%fused_computation.143 | loop fusion | flops 12288 | bytes 12288 | tf_op jit(solution)/shard_map/jit(floor_divide)/jit(_where)/select_n | solution.py:105
  6.9 1.3 %pad_maximum_fusion.1 = f32[45,38,128]{2,1,0:T(8,128)S(1)} fusion(f32[45,3,128]{2,1,0:T(4,128)S(1)} %collective-permute-done.1, f32[15,32,128]{2,1,0:T(8,128)} %param.8, f32[30,32,128]{2,1,0:T(8,128)} %bitcast.66, f32[45,3,128]{2,1,0:T(4,128)S(1)} %collective-permute-done), kind=kLoop, calls=%fused_computation.78 | loop fusion | flops 656640 | bytes 1751040 | tf_op jit(solution)/shard_map/concatenate | solution.py:18
  8.2 0.3 fusion.116
  8.5 0.4 copy.48
  9.0 0.4 copy.47
  9.4 3.0 %collective-permute-start.2 = (f32[45,38,6]{0,1,2:T(8,128)S(1)}, f32[45,38,6]{0,1,2:T(8,128)S(1)}, u32[]{:S(2)}, u32[]{:S(2)}) collective-permute-start(f32[45,38,6]{0,1,2:T(8,128)S(1)} %pad_maximum_fusion.14), channel_id=1, source_target_pairs={{0,4},{4,0},{1,5},{5,1},{2,6},{6,2},{3,7},{7,3},{8,12},{12,8},{9,1... | collective-permute-start | bytes 123128 | tf_op jit(solution)/shard_map/ppermute | solution.py:23
  12.5 3.5 %collective-permute-done.2 = f32[45,38,6]{0,1,2:T(8,128)S(1)} collective-permute-done((f32[45,38,6]{0,1,2:T(8,128)S(1)}, f32[45,38,6]{0,1,2:T(8,128)S(1)}, u32[]{:S(2)}, u32[]{:S(2)}) %collective-permute-start.2) | collective-permute-done | bytes 41072 | tf_op jit(solution)/shard_map/ppermute | solution.py:23
  16.0 0.5 copy.64
  16.4 0.5 copy.63
  16.9 1.0 %pad_maximum_fusion = f32[45,38,134]{2,1,0:T(8,128)S(1)} fusion(f32[45,38,3]{2,1,0:T(8,128)S(1)} %copy.64, f32[45,3,128]{2,1,0:T(4,128)S(1)} %collective-permute-done.1, f32[15,32,128]{2,1,0:T(8,128)S(1)} %copy-done.2, f32[30,32,128]{2,1,0:T(8,128)S(1)} %bitcast.67, f32[45,3,128]{2,1,0:T(4,128)S(1)} %collective-permute-done, f32[45,38,3]{2,1,0:T(8,128)S(1)} %copy.63), kind=kLoop, calls=%fused_computation.37 | loop fusion | flops 1145700 | bytes 1833120 | tf_op jit(solution)/shard_map/concatenate | solution.py:28
  18.0 0.7 %fusion.84 = (f32[15,36,132]{2,1,0:T(8,128)S(1)}, f32[15,36,132]{2,1,0:T(8,128)S(1)}, f32[15,36,132]{2,1,0:T(8,128)S(1)}, f32[15,36,132]{2,1,0:T(8,128)S(1)}) fusion(f32[45,38,134]{2,1,0:T(8,128)S(1)} %pad_maximum_fusion), kind=kLoop, calls=%fused_computation.94 | loop fusion | flops 570240 | bytes 2566080 | tf_op jit(solution)/shard_map/mul | solution.py:42
  18.7 1.4 %fusion.44 = f32[2,15,36,132]{3,2,1,0:T(8,128)S(1)} fusion(f32[2,15,38,134]{3,2,1,0:T(8,128)S(1)} %bitcast.64, f32[15,36,132]{2,1,0:T(8,128)S(1)} %get-tuple-element.20, f32[15,36,132]{2,1,0:T(8,128)S(1)} %get-tuple-element.21, f32[15,36,132]{2,1,0:T(8,128)S(1)} %get-tuple-element.22, f32[15,36,132]{2,1,0:T(8,128)S(1)} %get-tuple-element.19, ...), kind=kLoop, calls=%fused_computation.54 | loop fusion | flops 1853280 | bytes 4561956 | tf_op jit(solution)/shard_map/jit(_where)/select_n | solution.py:52
  20.1 0.9 %fusion.80 = (f32[15,34,130]{2,1,0:T(8,128)S(1)}, f32[15,34,130]{2,1,0:T(8,128)S(1)}, f32[15,34,130]{2,1,0:T(8,128)S(1)}, f32[15,34,130]{2,1,0:T(8,128)S(1)}) fusion(f32[45,38,134]{2,1,0:T(8,128)S(1)} %pad_maximum_fusion, f32[45,38,3]{2,1,0:T(8,128)S(1)} %copy.64, f32[45,3,128]{2,1,0:T(4,128)S(1)} %collective-permute-done.1, ...), kind=kLoop, calls=%fused_computation.86 | loop fusion | flops 1060800 | bytes 2772960 | tf_op jit(solution)/shard_map/mul | solution.py:42
  21.0 1.4 %fusion.35 = f32[2,15,34,130]{3,2,1,0:T(8,128)S(1)} fusion(f32[2,15,36,132]{3,2,1,0:T(8,128)S(1)} %fusion.44, f32[15,34,130]{2,1,0:T(8,128)S(1)} %get-tuple-element.17, f32[15,34,130]{2,1,0:T(8,128)S(1)} %get-tuple-element.18, f32[15,34,130]{2,1,0:T(8,128)S(1)} %get-tuple-element.16, f32[15,34,130]{2,1,0:T(8,128)S(1)} %get-tuple-element.15, ...), kind=kLoop, calls=%fused_computation.41 | loop fusion | flops 1723800 | bytes 4243234 | tf_op jit(solution)/shard_map/jit(_where)/select_n | solution.py:52
  22.4 0.4 fusion.101
  22.8 0.6 fusion.89
  23.5 0.7 %select_reduce_fusion = bf16[30,1024]{1,0:T(8,128)(2,1)S(1)} fusion(pred[32,1024]{1,0:T(8,128)(4,1)S(1)} %iota_compare_fusion.1, bf16[30,32,128]{2,1,0:T(8,128)(2,1)S(1)} %bitcast_convert_fusion, s32[1024]{0:T(1024)S(1)} %bitcast.77), kind=kOutput, calls=%fused_computation.35 | convolution fusion | flops 253724672 | bytes 344064 | tf_op jit(solution)/shard_map/dot_general | solution.py:111
  24.2 0.7 %broadcast_in_dim.101 = bf16[30,2,4,256]{3,0,2,1:T(8,128)(2,1)} broadcast(bf16[30,4,256]{2,0,1:T(8,128)(2,1)S(1)} %copy.51), dimensions={0,2,3} | broadcast | bytes 184320 | tf_op jit(solution)/shard_map/broadcast_in_dim | solution.py:121
  24.9 6.8 %all-to-all-start = ((bf16[30,8,256]{2,0,1:T(8,128)(2,1)}), bf16[30,8,256]{2,0,1:T(8,128)(2,1)S(1)}, u32[]{:S(2)}, u32[]{:S(2)}) async-start(bf16[30,8,256]{2,0,1:T(8,128)(2,1)} %bitcast.6), calls=%async_computation | async-start | bytes 262144 | tf_op jit(solution)/shard_map/all_to_all | solution.py:140
  31.7 7.6 %all-to-all-done = bf16[30,8,256]{2,0,1:T(8,128)(2,1)S(1)} async-done(((bf16[30,8,256]{2,0,1:T(8,128)(2,1)}), bf16[30,8,256]{2,0,1:T(8,128)(2,1)S(1)}, u32[]{:S(2)}, u32[]{:S(2)}) %all-to-all-start) | async-done | bytes 122912 | tf_op jit(solution)/shard_map/all_to_all | solution.py:140
  39.4 0.1 copy.69
  39.6 3.8 %fusion.15 = bf16[1024,512]{1,0:T(8,128)(2,1)S(1)} fusion(bf16[1,2,1024,1024]{3,2,1,0:T(8,128)(2,1)} %param.12, bf16[120,1024]{1,0:T(8,128)(2,1)S(1)} %multiply_bitcast_fusion, bf16[120,512]{1,0:T(8,128)(2,1)S(1)} %bitcast.74), kind=kOutput, calls=%fused_computation.18 | convolution fusion | flops 1209008128 | bytes 3514368 | tf_op jit(solution)/shard_map/dot_general | solution.py:82
  43.5 3.5 %fusion.64 = bf16[120,512]{1,0:T(8,128)(2,1)S(1)} fusion(bf16[1024,512]{1,0:T(8,128)(2,1)S(1)} %fusion.15, bf16[1,2,1024,1024]{3,2,1,0:T(8,128)(2,1)} %param.12, bf16[1,1024,120]{1,2,0:T(8,128)(2,1)S(1)} %copy-done), kind=kOutput, calls=%fused_computation.67 | convolution fusion | flops 1204350976 | bytes 3514368 | tf_op jit(solution)/shard_map/dot_general | solution.py:86
  47.1 0.7 %copy.57 = bf16[30,8,256]{2,0,1:T(8,128)(2,1)} copy(bf16[30,8,256]{2,1,0:T(8,128)(2,1)S(1)} %reshape.97) | data formatting | bytes 245760 | tf_op jit(solution)/shard_map/reshape | solution.py:153
  47.8 3.4 %all-to-all-start.1 = ((bf16[30,8,256]{2,0,1:T(8,128)(2,1)}), bf16[30,8,256]{2,0,1:T(8,128)(2,1)S(1)}, u32[]{:S(2)}, u32[]{:S(2)}) async-start(bf16[30,8,256]{2,0,1:T(8,128)(2,1)} %copy.57), calls=%async_computation.1 | async-start | bytes 262144 | tf_op jit(solution)/shard_map/all_to_all | solution.py:155
  51.2 7.4 %all-to-all-done.1 = bf16[30,8,256]{2,0,1:T(8,128)(2,1)S(1)} async-done(((bf16[30,8,256]{2,0,1:T(8,128)(2,1)}), bf16[30,8,256]{2,0,1:T(8,128)(2,1)S(1)}, u32[]{:S(2)}, u32[]{:S(2)}) %all-to-all-start.1) | async-done | bytes 122912 | tf_op jit(solution)/shard_map/all_to_all | solution.py:155
  58.7 0.2 broadcast_select_fusion
  59.0 1.5 %fusion.51 = f32[30,32,128]{2,1,0:T(8,128)} fusion(f32[30,32,128]{2,1,0:T(8,128)S(1)} %bitcast.70, pred[32,1024]{1,0:T(8,128)(4,1)S(1)} %iota_compare_fusion.1, bf16[30,1024]{1,0:T(8,128)(2,1)S(1)} %bitcast.75, s32[1024]{0:T(1024)S(1)} %bitcast.78), kind=kOutput, calls=%fused_computation.64 | convolution fusion | flops 252895232 | bytes 1081344 | tf_op jit(solution)/shard_map/dot_general | solution.py:166
  (32 shorter events, 0.7 us)
Async XLA Ops:
  0.0 43.4 %copy-start = (bf16[1,1024,120]{1,2,0:T(8,128)(2,1)S(1)}, bf16[1,1024,120]{1,2,0:T(8,128)(2,1)}, u32[]{:S(2)}) copy-start(bf16[1,1024,120]{1,2,0:T(8,128)(2,1)} %param.13) | copy-start | bytes 737284
  1.1 5.8 %collective-permute-start.1 = (f32[45,3,128]{2,1,0:T(4,128)S(1)}, f32[45,3,128]{2,1,0:T(4,128)S(1)}, u32[]{:S(2)}, u32[]{:S(2)}) collective-permute-start(f32[45,3,128]{2,1,0:T(4,128)S(1)} %get-tuple-element.30), channel_id=1, source_target_pairs={{8,0},{16,8},{24,16},{9,1},{17,9},{25,17},{10,2},{18,10},{26,18},{... | collective-permute-start | bytes 207368 | tf_op jit(solution)/shard_map/ppermute | solution.py:15
  2.4 4.5 %collective-permute-start = (f32[45,3,128]{2,1,0:T(4,128)S(1)}, f32[45,3,128]{2,1,0:T(4,128)S(1)}, u32[]{:S(2)}, u32[]{:S(2)}) collective-permute-start(f32[45,3,128]{2,1,0:T(4,128)S(1)} %get-tuple-element.29), channel_id=1, source_target_pairs={{0,8},{8,16},{16,24},{1,9},{9,17},{17,25},{2,10},{10,18},{18,26},{... | collective-permute-start | bytes 207368 | tf_op jit(solution)/shard_map/ppermute | solution.py:12
  8.9 8.0 %copy-start.1 = (f32[2,15,32,128]{3,2,1,0:T(8,128)S(1)}, f32[2,15,32,128]{3,2,1,0:T(8,128)}, u32[]{:S(2)}) copy-start(f32[2,15,32,128]{3,2,1,0:T(8,128)} %param.7) | copy-start | bytes 1474564
  8.9 8.0 %copy-start.2 = (f32[15,32,128]{2,1,0:T(8,128)S(1)}, f32[15,32,128]{2,1,0:T(8,128)}, u32[]{:S(2)}) copy-start(f32[15,32,128]{2,1,0:T(8,128)} %param.8) | copy-start | bytes 737284
  9.4 6.6 %collective-permute-start.2 = (f32[45,38,6]{0,1,2:T(8,128)S(1)}, f32[45,38,6]{0,1,2:T(8,128)S(1)}, u32[]{:S(2)}, u32[]{:S(2)}) collective-permute-start(f32[45,38,6]{0,1,2:T(8,128)S(1)} %pad_maximum_fusion.14), channel_id=1, source_target_pairs={{0,4},{4,0},{1,5},{5,1},{2,6},{6,2},{3,7},{7,3},{8,12},{12,8},{9,1... | collective-permute-start | bytes 123128 | tf_op jit(solution)/shard_map/ppermute | solution.py:23
  23.4 8.2 %copy-start.3 = (bf16[1,120,1024]{2,1,0:T(8,128)(2,1)S(1)}, bf16[1,120,1024]{2,1,0:T(8,128)(2,1)}, u32[]{:S(2)}) copy-start(bf16[1,120,1024]{2,1,0:T(8,128)(2,1)} %param.11) | copy-start | bytes 737284
  24.9 14.5 %all-to-all-start = ((bf16[30,8,256]{2,0,1:T(8,128)(2,1)}), bf16[30,8,256]{2,0,1:T(8,128)(2,1)S(1)}, u32[]{:S(2)}, u32[]{:S(2)}) async-start(bf16[30,8,256]{2,0,1:T(8,128)(2,1)} %bitcast.6), calls=%async_computation | async-start | bytes 262144 | tf_op jit(solution)/shard_map/all_to_all | solution.py:140
  43.5 7.7 %copy-start.4 = (s32[1,1024,1]{1,2,0:T(1,128)S(1)}, s32[1,1024,1]{1,2,0:T(1,128)}, u32[]{:S(2)}) copy-start(s32[1,1024,1]{1,2,0:T(1,128)} %param.10) | copy-start | bytes 12292
  47.8 10.8 %all-to-all-start.1 = ((bf16[30,8,256]{2,0,1:T(8,128)(2,1)}), bf16[30,8,256]{2,0,1:T(8,128)(2,1)S(1)}, u32[]{:S(2)}, u32[]{:S(2)}) async-start(bf16[30,8,256]{2,0,1:T(8,128)(2,1)} %copy.57), calls=%async_computation.1 | async-start | bytes 262144 | tf_op jit(solution)/shard_map/all_to_all | solution.py:155

commit v14 on v5

--- a/solution.py
+++ b/solution.py
@@ -1,6 +1,8 @@
 import jax
 import jax.numpy as jnp
 from jax import lax
+from jax.experimental import pallas as pl
+from jax.experimental.pallas import tpu as pltpu
 from jax.sharding import PartitionSpec as P
 
 LEVELS = 60
@@ -72,20 +74,44 @@
     return values
 
 
-def network(features, w_first, w_middle, w_last):
-    contract = (((0,), (0,)), ((), ()))
-    hidden = jax.nn.gelu(
-        lax.dot_general(w_first, features, contract, preferred_element_type=jnp.float32)
-    ).astype(jnp.bfloat16)
-    for layer_no in range(w_middle.shape[0]):
+def network_kernel(rows_ref, first_ref, middle_ref, last_ref, out_ref):
+    tile = min(rows_ref.shape[0], 512)
+
+    def one_tile(index, carry):
+        rows = pl.ds(pl.multiple_of(index * tile, tile), tile)
         hidden = jax.nn.gelu(
-            lax.dot_general(
-                w_middle[layer_no], hidden, contract, preferred_element_type=jnp.float32
-            )
+            jnp.dot(rows_ref[rows, :], first_ref[...], preferred_element_type=jnp.float32)
         ).astype(jnp.bfloat16)
-    return lax.dot_general(w_last, hidden, contract, preferred_element_type=jnp.float32).astype(
-        jnp.bfloat16
-    )
+        for layer_no in range(middle_ref.shape[0]):
+            hidden = jax.nn.gelu(
+                jnp.dot(hidden, middle_ref[layer_no], preferred_element_type=jnp.float32)
+            ).astype(jnp.bfloat16)
+        out_ref[rows, :] = jnp.dot(
+            hidden, last_ref[...], preferred_element_type=jnp.float32
+        ).astype(jnp.bfloat16)
+        return carry
+
+    lax.fori_loop(0, rows_ref.shape[0] // tile, one_tile, 0)
+
+
+def network(rows, w_first, w_middle, w_last):
+    count, width = rows.shape
+    hid = w_first.shape[1]
+    vmem = pl.BlockSpec(memory_space=pltpu.VMEM)
+    flops = 2 * count * (width * hid + w_middle.shape[0] * hid * hid + hid * w_last.shape[1])
+    weight_bytes = 2 * (w_first.size + w_middle.size + w_last.size)
+    return pl.pallas_call(
+        network_kernel,
+        out_shape=jax.ShapeDtypeStruct((count, w_last.shape[1]), jnp.bfloat16),
+        in_specs=[vmem] * 4,
+        out_specs=vmem,
+        compiler_params=pltpu.CompilerParams(vmem_limit_bytes=48 * 1024 * 1024),
+        cost_estimate=pl.CostEstimate(
+            flops=flops,
+            transcendentals=(1 + w_middle.shape[0]) * count * hid,
+            bytes_accessed=weight_bytes + 2 * count * (width + w_last.shape[1]),
+        ),
+    )(rows, w_first, w_middle, w_last)
 
 
 def on_device(fields, diffusivity, cloudy_index, owners, w_in, w_mid, w_out):
@@ -138,13 +164,13 @@
     )
     inputs = (
         received.reshape(2, level_rows, lon_count, lev_count, capacity)
-        .transpose(0, 3, 1, 2, 4)
-        .reshape(feature_count, lon_count * capacity)
+        .transpose(2, 4, 0, 3, 1)
+        .reshape(lon_count * capacity, feature_count)
     )
     outcome = network(inputs, w_in[0], w_mid[0], w_out[0])
     outgoing = (
-        outcome.reshape(2, lev_count, level_rows, lon_count, capacity)
-        .transpose(0, 2, 3, 1, 4)
+        outcome.reshape(lon_count, capacity, 2, lev_count, level_rows)
+        .transpose(2, 4, 0, 3, 1)
         .reshape(local_features, group, capacity)
     )
     returned = lax.all_to_all(

time: 60 us -> 59.1 us (0.985)
  blocking collectives: 14.3 us -> 0 us
  waiting for transfers between devices: 10.9 us -> 18.4 us
  matrix products: 9.36 us -> 2.19 us
  starting transfers between devices: 10.7 us -> 17.5 us
  Pallas kernels: 0 us -> 3.23 us
  local copies, waits for them, and re-layouts: 3.44 us -> 6.63 us
    all_to_all x1 -> x0, blocking collectives: 14.3 us -> none  [on_device(): lax.all_to_all(send_buffer, ('lon', 'lev'), split_axis=1, concat_axis=1,...]
    all_to_all x0 -> x1, waiting for transfers between devices: none -> 7.49 us  [on_device(): lax.all_to_all(send_buffer, ('lon', 'lev'), split_axis=1, concat_axis=1,...]
    dot_general x2 -> x0, matrix products: 7.17 us -> none  [the longest x1 3.73 us: network(): lax.dot_general(w_middle[layer_no], hidden, contract, preferred_element_t...]
    all_to_all x0 -> x1, starting transfers between devices: none -> 6.79 us  [on_device(): lax.all_to_all(send_buffer, ('lon', 'lev'), split_axis=1, concat_axis=1,...]
    pallas_call x0 -> x1, Pallas kernels: none -> 3.23 us  [network(): pl.pallas_call(network_kernel, out_shape=jax.ShapeDtypeStruct((count, w_l...]
    unnamed x14 -> x17, local copies, waits for them, and re-layouts: 0.98 us -> 3.34 us
    broadcast_in_dim x3, local copies, waits for them, and re-layouts: 0.05 us -> 0.71 us  [on_device(): jnp.broadcast_to(picked.reshape(local_features, 1, lev_count, per_device)...]
  transfers between devices with their start and end apart: 4 -> 5, of which waited for: 2 -> 3; matrix products, arithmetic and copies ran while one was open for 2% -> 3% of each run, Pallas kernels for 0% -> 0%
where the time goes in v14:
time: 59.1 us; the launch traced here: 58.7 us
  waiting for transfers between devices  18.4 us (31%)
  starting transfers between devices  17.5 us (30%)
  other arithmetic  10.3 us (17%)
  local copies, waits for them, and re-layouts  6.63 us (11%)
  Pallas kernels  3.23 us (5%)
  matrix products  2.19 us (4%)
    all_to_all x1, waiting for transfers between devices, on_device(): lax.all_to_all(send_buffer, ('lon', 'lev'), split_axis=1, concat_axis=1,...  7.49 us
    all_to_all x1, waiting for transfers between devices, on_device(): lax.all_to_all(outgoing, ('lon', 'lev'), split_axis=1, concat_axis=1, til...  7.42 us
    all_to_all x1, starting transfers between devices, on_device(): lax.all_to_all(send_buffer, ('lon', 'lev'), split_axis=1, concat_axis=1,...  6.79 us
    ppermute x1, waiting for transfers between devices, halo_exchange(): lax.ppermute(jnp.concatenate([right, left], axis=-1), 'lon', [(0, 1), (1,...  3.52 us
    all_to_all x1, starting transfers between devices, on_device(): lax.all_to_all(outgoing, ('lon', 'lev'), split_axis=1, concat_axis=1, til...  3.37 us
    unnamed x17, local copies, waits for them, and re-layouts  3.34 us
    pallas_call x1, Pallas kernels, network(): pl.pallas_call(network_kernel, out_shape=jax.ShapeDtypeStruct((count, w_l...  3.23 us
    ppermute x1, starting transfers between devices, halo_exchange(): lax.ppermute(cells[..., cells.shape[-2] - width:, :], 'lat', [(i, i + 1)...  3.04 us
  transfers between devices with their start and end apart: 5, of which 3 were waited for; matrix products, arithmetic and copies ran while one was open for 3% of the time, Pallas kernels for 0%

profile of v14, /device:TPU:0, one launch (start us, length us, event | category | flops | bytes accessed | tf_op | source)
XLA Modules:
  0.0 58.7 jit_solution(8102304932339166036)
XLA Ops:
  0.0 1.1 %pad_maximum_fusion.16 = (f32[45,3,128]{2,1,0:T(4,128)S(1)}, f32[45,3,128]{2,1,0:T(4,128)S(1)}) fusion(f32[15,32,128]{2,1,0:T(8,128)} %param.8, f32[30,32,128]{2,1,0:T(8,128)} %bitcast.38), kind=kLoop, calls=%fused_computation.93 | loop fusion | flops 34560 | bytes 875520 | tf_op jit(solution)/shard_map/slice | solution.py:15
  1.1 1.3 %collective-permute-start.1 = (f32[45,3,128]{2,1,0:T(4,128)S(1)}, f32[45,3,128]{2,1,0:T(4,128)S(1)}, u32[]{:S(2)}, u32[]{:S(2)}) collective-permute-start(f32[45,3,128]{2,1,0:T(4,128)S(1)} %get-tuple-element.24), channel_id=1, source_target_pairs={{8,0},{16,8},{24,16},{9,1},{17,9},{25,17},{10,2},{18,10},{26,18},{... | collective-permute-start | bytes 207368 | tf_op jit(solution)/shard_map/ppermute | solution.py:17
  2.4 3.0 %collective-permute-start = (f32[45,3,128]{2,1,0:T(4,128)S(1)}, f32[45,3,128]{2,1,0:T(4,128)S(1)}, u32[]{:S(2)}, u32[]{:S(2)}) collective-permute-start(f32[45,3,128]{2,1,0:T(4,128)S(1)} %get-tuple-element.23), channel_id=1, source_target_pairs={{0,8},{8,16},{16,24},{1,9},{9,17},{17,25},{2,10},{10,18},{18,26},{... | collective-permute-start | bytes 207368 | tf_op jit(solution)/shard_map/ppermute | solution.py:14
  5.5 0.7 %and_select_fusion = (s32[1,1024]{1,0:T(1,128)S(1)}, s32[1,1024]{1,0:T(1,128)S(1)}) fusion(s32[1,1024]{1,0:T(1,128)} %param.9), kind=kLoop, calls=%fused_computation.95 | loop fusion | flops 11264 | bytes 12288 | tf_op jit(solution)/shard_map/jit(remainder)/select_n | solution.py:132
  6.2 0.7 %and_select_fusion.1 = s32[1,1024]{1,0:T(1,128)S(1)} fusion(s32[1,1024]{1,0:T(1,128)S(1)} %get-tuple-element.6, s32[1,1024]{1,0:T(1,128)} %param.9), kind=kLoop, calls=%fused_computation.97 | loop fusion | flops 12288 | bytes 12288 | tf_op jit(solution)/shard_map/jit(floor_divide)/jit(_where)/select_n | solution.py:131
  7.0 1.1 %pad_maximum_fusion.1 = f32[45,38,128]{2,1,0:T(8,128)S(1)} fusion(f32[45,3,128]{2,1,0:T(4,128)S(1)} %collective-permute-done.1, f32[15,32,128]{2,1,0:T(8,128)} %param.8, f32[30,32,128]{2,1,0:T(8,128)S(1)} %bitcast.39, f32[45,3,128]{2,1,0:T(4,128)S(1)} %collective-permute-done), kind=kLoop, calls=%fused_computation.34 | loop fusion | flops 656640 | bytes 1751040 | tf_op jit(solution)/shard_map/concatenate | solution.py:20
  8.0 0.3 fusion.56
  8.3 0.4 copy.51
  8.8 0.4 copy.50
  9.3 3.0 %collective-permute-start.2 = (f32[45,38,6]{0,1,2:T(8,128)S(1)}, f32[45,38,6]{0,1,2:T(8,128)S(1)}, u32[]{:S(2)}, u32[]{:S(2)}) collective-permute-start(f32[45,38,6]{0,1,2:T(8,128)S(1)} %pad_maximum_fusion.14), channel_id=1, source_target_pairs={{0,4},{4,0},{1,5},{5,1},{2,6},{6,2},{3,7},{7,3},{8,12},{12,8},{9,1... | collective-permute-start | bytes 123128 | tf_op jit(solution)/shard_map/ppermute | solution.py:25
  12.3 3.5 %collective-permute-done.2 = f32[45,38,6]{0,1,2:T(8,128)S(1)} collective-permute-done((f32[45,38,6]{0,1,2:T(8,128)S(1)}, f32[45,38,6]{0,1,2:T(8,128)S(1)}, u32[]{:S(2)}, u32[]{:S(2)}) %collective-permute-start.2) | collective-permute-done | bytes 41072 | tf_op jit(solution)/shard_map/ppermute | solution.py:25
  15.8 0.5 copy.68
  16.3 0.5 copy.67
  16.8 1.0 %pad_maximum_fusion = f32[45,38,134]{2,1,0:T(8,128)S(1)} fusion(f32[45,38,3]{2,1,0:T(8,128)S(1)} %copy.68, f32[45,3,128]{2,1,0:T(4,128)S(1)} %collective-permute-done.1, f32[15,32,128]{2,1,0:T(8,128)S(1)} %copy-done.3, f32[30,32,128]{2,1,0:T(8,128)S(1)} %bitcast.40, f32[45,3,128]{2,1,0:T(4,128)S(1)} %collective-permute-done, f32[45,38,3]{2,1,0:T(8,128)S(1)} %copy.67), kind=kLoop, calls=%fused_computation.4 | loop fusion | flops 1145700 | bytes 1833120 | tf_op jit(solution)/shard_map/concatenate | solution.py:30
  17.8 0.7 %fusion.33 = (f32[15,36,132]{2,1,0:T(8,128)S(1)}, f32[15,36,132]{2,1,0:T(8,128)S(1)}, f32[15,36,132]{2,1,0:T(8,128)S(1)}, f32[15,36,132]{2,1,0:T(8,128)S(1)}) fusion(f32[45,38,134]{2,1,0:T(8,128)S(1)} %pad_maximum_fusion), kind=kLoop, calls=%fused_computation.50 | loop fusion | flops 570240 | bytes 2566080 | tf_op jit(solution)/shard_map/mul | solution.py:44
  18.6 1.4 %fusion.14 = f32[2,15,36,132]{3,2,1,0:T(8,128)S(1)} fusion(f32[2,15,38,134]{3,2,1,0:T(8,128)S(1)} %bitcast.37, f32[15,36,132]{2,1,0:T(8,128)S(1)} %get-tuple-element.14, f32[15,36,132]{2,1,0:T(8,128)S(1)} %get-tuple-element.15, f32[15,36,132]{2,1,0:T(8,128)S(1)} %get-tuple-element.16, f32[15,36,132]{2,1,0:T(8,128)S(1)} %get-tuple-element.13, ...), kind=kLoop, calls=%fused_computation.21 | loop fusion | flops 1853280 | bytes 4561956 | tf_op jit(solution)/shard_map/jit(_where)/select_n | solution.py:54
  20.0 0.9 %fusion.29 = (f32[15,34,130]{2,1,0:T(8,128)S(1)}, f32[15,34,130]{2,1,0:T(8,128)S(1)}, f32[15,34,130]{2,1,0:T(8,128)S(1)}, f32[15,34,130]{2,1,0:T(8,128)S(1)}) fusion(f32[45,38,134]{2,1,0:T(8,128)S(1)} %pad_maximum_fusion, f32[45,38,3]{2,1,0:T(8,128)S(1)} %copy.68, f32[45,3,128]{2,1,0:T(4,128)S(1)} %collective-permute-done.1, ...), kind=kLoop, calls=%fused_computation.42 | loop fusion | flops 1060800 | bytes 2772960 | tf_op jit(solution)/shard_map/mul | solution.py:44
  20.9 1.4 %fusion.5 = f32[2,15,34,130]{3,2,1,0:T(8,128)S(1)} fusion(f32[2,15,36,132]{3,2,1,0:T(8,128)S(1)} %fusion.14, f32[15,34,130]{2,1,0:T(8,128)S(1)} %get-tuple-element.11, f32[15,34,130]{2,1,0:T(8,128)S(1)} %get-tuple-element.12, f32[15,34,130]{2,1,0:T(8,128)S(1)} %get-tuple-element.10, f32[15,34,130]{2,1,0:T(8,128)S(1)} %get-tuple-element.9, ...), kind=kLoop, calls=%fused_computation.8 | loop fusion | flops 1723800 | bytes 4243234 | tf_op jit(solution)/shard_map/jit(_where)/select_n | solution.py:54
  22.3 0.4 fusion.50
  22.7 0.6 %fusion.38 = f32[2,15,32,128]{3,2,1,0:T(8,128)S(1)} fusion(f32[2,15,34,130]{3,2,1,0:T(8,128)S(1)} %fusion.5, f32[15,32,128]{2,1,0:T(8,128)S(1)} %get-tuple-element.18, f32[15,32,128]{2,1,0:T(8,128)S(1)} %get-tuple-element.17, f32[15,32,128]{2,1,0:T(8,128)S(1)} %get-tuple-element.22, f32[15,32,128]{2,1,0:T(8,128)S(1)} %get-tuple-element.21), kind=kLoop, calls=%fused_computation.55 | loop fusion | flops 1474560 | bytes 3932160 | tf_op jit(solution)/shard_map/add | solution.py:45
  23.3 0.7 %select_reduce_fusion = bf16[30,1024]{1,0:T(8,128)(2,1)S(1)} fusion(pred[32,1024]{1,0:T(8,128)(4,1)S(1)} %iota_compare_fusion.1, bf16[30,32,128]{2,1,0:T(8,128)(2,1)S(1)} %bitcast_convert_fusion, s32[1024]{0:T(1024)S(1)} %bitcast.50), kind=kOutput, calls=%fused_computation.2 | convolution fusion | flops 253724672 | bytes 344064 | tf_op jit(solution)/shard_map/dot_general | solution.py:137
  24.1 0.7 %broadcast_in_dim.101 = bf16[30,2,4,256]{3,0,2,1:T(8,128)(2,1)} broadcast(bf16[30,4,256]{2,0,1:T(8,128)(2,1)S(1)} %copy.54), dimensions={0,2,3} | broadcast | bytes 184320 | tf_op jit(solution)/shard_map/broadcast_in_dim | solution.py:147
  24.8 6.8 %all-to-all-start = ((bf16[30,8,256]{2,0,1:T(8,128)(2,1)}), bf16[30,8,256]{2,0,1:T(8,128)(2,1)S(1)}, u32[]{:S(2)}, u32[]{:S(2)}) async-start(bf16[30,8,256]{2,0,1:T(8,128)(2,1)} %bitcast.6), calls=%async_computation | async-start | bytes 262144 | tf_op jit(solution)/shard_map/all_to_all | solution.py:162
  31.6 0.2 copy.57
  31.7 7.5 %all-to-all-done = bf16[30,8,256]{2,0,1:T(8,128)(2,1)S(1)} async-done(((bf16[30,8,256]{2,0,1:T(8,128)(2,1)}), bf16[30,8,256]{2,0,1:T(8,128)(2,1)S(1)}, u32[]{:S(2)}, u32[]{:S(2)}) %all-to-all-start) | async-done | bytes 122912 | tf_op jit(solution)/shard_map/all_to_all | solution.py:162
  39.6 2.2 %copy-done = bf16[1,2,1024,1024]{3,2,1,0:T(8,128)(2,1)S(1)} copy-done((bf16[1,2,1024,1024]{3,2,1,0:T(8,128)(2,1)S(1)}, bf16[1,2,1024,1024]{3,2,1,0:T(8,128)(2,1)}, u32[]{:S(2)}) %copy-start) | copy-done | bytes 4194328
  41.8 3.2 %shard_map.73 = bf16[512,120]{1,0:T(8,128)(2,1)S(1)} custom-call(bf16[512,120]{1,0:T(8,128)(2,1)S(1)} %copy.58.rows_ref, bf16[120,1024]{1,0:T(8,128)(2,1)S(1)} %bitcast.36, bf16[2,1024,1024]{2,1,0:T(8,128)(2,1)S(1)} %bitcast.35, bf16[1024,120]{1,0:T(8,128)(2,1)S(1)} %bitcast.34), custom_call_target="tpu_custom_call" | custom-call | flops 2399141888 | bytes 4931584 | tf_op jit(solution)/shard_map/pallas_call | solution.py:103
  45.3 0.7 %reshape.104 = bf16[30,8,256]{2,0,1:T(8,128)(2,1)} reshape(bf16[2,15,2,4,256]{4,1,0,3,2:T(8,128)(2,1)S(1)} %copy.64) | data formatting | bytes 245760 | tf_op jit(solution)/shard_map/reshape | solution.py:174
  45.9 3.4 %all-to-all-start.1 = ((bf16[30,8,256]{2,0,1:T(8,128)(2,1)}), bf16[30,8,256]{2,0,1:T(8,128)(2,1)S(1)}, u32[]{:S(2)}, u32[]{:S(2)}) async-start(bf16[30,8,256]{2,0,1:T(8,128)(2,1)} %reshape.104), calls=%async_computation.1 | async-start | bytes 262144 | tf_op jit(solution)/shard_map/all_to_all | solution.py:176
  49.4 7.4 %all-to-all-done.1 = bf16[30,8,256]{2,0,1:T(8,128)(2,1)S(1)} async-done(((bf16[30,8,256]{2,0,1:T(8,128)(2,1)}), bf16[30,8,256]{2,0,1:T(8,128)(2,1)S(1)}, u32[]{:S(2)}, u32[]{:S(2)}) %all-to-all-start.1) | async-done | bytes 122912 | tf_op jit(solution)/shard_map/all_to_all | solution.py:176
  56.9 0.2 broadcast_select_fusion
  57.2 1.5 %fusion.21 = f32[30,32,128]{2,1,0:T(8,128)} fusion(f32[30,32,128]{2,1,0:T(8,128)S(1)} %bitcast.43, pred[32,1024]{1,0:T(8,128)(4,1)S(1)} %iota_compare_fusion.1, bf16[30,1024]{1,0:T(8,128)(2,1)S(1)} %bitcast.48, s32[1024]{0:T(1024)S(1)} %bitcast.51), kind=kOutput, calls=%fused_computation.31 | convolution fusion | flops 252895232 | bytes 1081344 | tf_op jit(solution)/shard_map/dot_general | solution.py:187
  (34 shorter events, 1.0 us)
Async XLA Ops:
  0.0 7.0 %copy-start.2 = (f32[2,15,32,128]{3,2,1,0:T(8,128)S(1)}, f32[2,15,32,128]{3,2,1,0:T(8,128)}, u32[]{:S(2)}) copy-start(f32[2,15,32,128]{3,2,1,0:T(8,128)} %param.7) | copy-start | bytes 1474564
  1.1 5.8 %collective-permute-start.1 = (f32[45,3,128]{2,1,0:T(4,128)S(1)}, f32[45,3,128]{2,1,0:T(4,128)S(1)}, u32[]{:S(2)}, u32[]{:S(2)}) collective-permute-start(f32[45,3,128]{2,1,0:T(4,128)S(1)} %get-tuple-element.24), channel_id=1, source_target_pairs={{8,0},{16,8},{24,16},{9,1},{17,9},{25,17},{10,2},{18,10},{26,18},{... | collective-permute-start | bytes 207368 | tf_op jit(solution)/shard_map/ppermute | solution.py:17
  2.4 4.5 %collective-permute-start = (f32[45,3,128]{2,1,0:T(4,128)S(1)}, f32[45,3,128]{2,1,0:T(4,128)S(1)}, u32[]{:S(2)}, u32[]{:S(2)}) collective-permute-start(f32[45,3,128]{2,1,0:T(4,128)S(1)} %get-tuple-element.23), channel_id=1, source_target_pairs={{0,8},{8,16},{16,24},{1,9},{9,17},{17,25},{2,10},{10,18},{18,26},{... | collective-permute-start | bytes 207368 | tf_op jit(solution)/shard_map/ppermute | solution.py:14
  9.2 7.5 %copy-start.3 = (f32[15,32,128]{2,1,0:T(8,128)S(1)}, f32[15,32,128]{2,1,0:T(8,128)}, u32[]{:S(2)}) copy-start(f32[15,32,128]{2,1,0:T(8,128)} %param.8) | copy-start | bytes 737284
  9.3 6.6 %collective-permute-start.2 = (f32[45,38,6]{0,1,2:T(8,128)S(1)}, f32[45,38,6]{0,1,2:T(8,128)S(1)}, u32[]{:S(2)}, u32[]{:S(2)}) collective-permute-start(f32[45,38,6]{0,1,2:T(8,128)S(1)} %pad_maximum_fusion.14), channel_id=1, source_target_pairs={{0,4},{4,0},{1,5},{5,1},{2,6},{6,2},{3,7},{7,3},{8,12},{12,8},{9,1... | collective-permute-start | bytes 123128 | tf_op jit(solution)/shard_map/ppermute | solution.py:25
  23.3 8.3 %copy-start.4 = (bf16[1,1024,120]{1,2,0:T(8,128)(2,1)S(1)}, bf16[1,1024,120]{1,2,0:T(8,128)(2,1)}, u32[]{:S(2)}) copy-start(bf16[1,1024,120]{1,2,0:T(8,128)(2,1)} %param.13) | copy-start | bytes 737284
  24.0 15.6 %copy-start.1 = (bf16[1,120,1024]{2,1,0:T(8,128)(2,1)S(1)}, bf16[1,120,1024]{2,1,0:T(8,128)(2,1)}, u32[]{:S(2)}) copy-start(bf16[1,120,1024]{2,1,0:T(8,128)(2,1)} %param.11) | copy-start | bytes 737284
  24.8 14.5 %all-to-all-start = ((bf16[30,8,256]{2,0,1:T(8,128)(2,1)}), bf16[30,8,256]{2,0,1:T(8,128)(2,1)S(1)}, u32[]{:S(2)}, u32[]{:S(2)}) async-start(bf16[30,8,256]{2,0,1:T(8,128)(2,1)} %bitcast.6), calls=%async_computation | async-start | bytes 262144 | tf_op jit(solution)/shard_map/all_to_all | solution.py:162
  39.6 2.2 %copy-start = (bf16[1,2,1024,1024]{3,2,1,0:T(8,128)(2,1)S(1)}, bf16[1,2,1024,1024]{3,2,1,0:T(8,128)(2,1)}, u32[]{:S(2)}) copy-start(bf16[1,2,1024,1024]{3,2,1,0:T(8,128)(2,1)} %param.12) | copy-start | bytes 12582916
  45.1 4.3 %copy-start.5 = (s32[1,1024,1]{1,2,0:T(1,128)S(1)}, s32[1,1024,1]{1,2,0:T(1,128)}, u32[]{:S(2)}) copy-start(s32[1,1024,1]{1,2,0:T(1,128)} %param.10) | copy-start | bytes 12292
  45.9 10.8 %all-to-all-start.1 = ((bf16[30,8,256]{2,0,1:T(8,128)(2,1)}), bf16[30,8,256]{2,0,1:T(8,128)(2,1)S(1)}, u32[]{:S(2)}, u32[]{:S(2)}) async-start(bf16[30,8,256]{2,0,1:T(8,128)(2,1)} %reshape.104), calls=%async_computation.1 | async-start | bytes 262144 | tf_op jit(solution)/shard_map/all_to_all | solution.py:176

commit v15 on v14

--- a/solution.py
+++ b/solution.py
@@ -1,3 +1,5 @@
+import functools
+
 import jax
 import jax.numpy as jnp
 from jax import lax
@@ -74,44 +76,38 @@
     return values
 
 
-def network_kernel(rows_ref, first_ref, middle_ref, last_ref, out_ref):
-    tile = min(rows_ref.shape[0], 512)
-
-    def one_tile(index, carry):
-        rows = pl.ds(pl.multiple_of(index * tile, tile), tile)
-        hidden = jax.nn.gelu(
-            jnp.dot(rows_ref[rows, :], first_ref[...], preferred_element_type=jnp.float32)
-        ).astype(jnp.bfloat16)
-        for layer_no in range(middle_ref.shape[0]):
-            hidden = jax.nn.gelu(
-                jnp.dot(hidden, middle_ref[layer_no], preferred_element_type=jnp.float32)
-            ).astype(jnp.bfloat16)
-        out_ref[rows, :] = jnp.dot(
-            hidden, last_ref[...], preferred_element_type=jnp.float32
-        ).astype(jnp.bfloat16)
-        return carry
-
-    lax.fori_loop(0, rows_ref.shape[0] // tile, one_tile, 0)
-
-
-def network(rows, w_first, w_middle, w_last):
-    count, width = rows.shape
-    hid = w_first.shape[1]
+def layers_kernel(rows_ref, *refs, finals):
+    out_ref = refs[-1]
+    hidden = rows_ref[...]
+    for number, weight_ref in enumerate(refs[:-1]):
+        hidden = jnp.dot(hidden, weight_ref[...], preferred_element_type=jnp.float32)
+        if number < len(refs) - 2 or not finals:
+            hidden = jax.nn.gelu(hidden)
+        hidden = hidden.astype(jnp.bfloat16)
+    out_ref[...] = hidden
+
+
+def layers(rows, weights, finals):
+    count = rows.shape[0]
     vmem = pl.BlockSpec(memory_space=pltpu.VMEM)
-    flops = 2 * count * (width * hid + w_middle.shape[0] * hid * hid + hid * w_last.shape[1])
-    weight_bytes = 2 * (w_first.size + w_middle.size + w_last.size)
+    flops = sum(2 * count * w.shape[0] * w.shape[1] for w in weights)
     return pl.pallas_call(
-        network_kernel,
-        out_shape=jax.ShapeDtypeStruct((count, w_last.shape[1]), jnp.bfloat16),
-        in_specs=[vmem] * 4,
+        functools.partial(layers_kernel, finals=finals),
+        out_shape=jax.ShapeDtypeStruct((count, weights[-1].shape[1]), jnp.bfloat16),
+        in_specs=[vmem] * (1 + len(weights)),
         out_specs=vmem,
         compiler_params=pltpu.CompilerParams(vmem_limit_bytes=48 * 1024 * 1024),
         cost_estimate=pl.CostEstimate(
             flops=flops,
-            transcendentals=(1 + w_middle.shape[0]) * count * hid,
-            bytes_accessed=weight_bytes + 2 * count * (width + w_last.shape[1]),
+            transcendentals=count * sum(w.shape[1] for w in weights),
+            bytes_accessed=sum(2 * w.size for w in weights) + 2 * count * (rows.shape[1] + weights[-1].shape[1]),
         ),
-    )(rows, w_first, w_middle, w_last)
+    )(rows, *weights)
+
+
+def network(rows, w_first, w_middle, w_last):
+    hidden = layers(rows, [w_first, w_middle[0]], finals=False)
+    return layers(hidden, [w_middle[layer_no] for layer_no in range(1, w_middle.shape[0])] + [w_last], finals=True)
 
 
 def on_device(fields, diffusivity, cloudy_index, owners, w_in, w_mid, w_out):

time: 59.1 us -> 59.2 us (level)
  waiting for transfers between devices: 18.4 us -> 14.4 us
  local copies, waits for them, and re-layouts: 6.63 us -> 10 us
  Pallas kernels: 3.23 us -> 3.91 us
    squeeze x0 -> x1, local copies, waits for them, and re-layouts: none -> 4 us  [network(): w_middle[layer_no]]
    all_to_all x1, waiting for transfers between devices: 7.49 us -> 3.67 us  [on_device(): lax.all_to_all(send_buffer, ('lon', 'lev'), split_axis=1, concat_axis=1,...]
    pallas_call x1 -> x2, Pallas kernels: 3.23 us -> 3.91 us  [layers(): pl.pallas_call(functools.partial(layers_kernel, finals=finals), out_shape...]
    unnamed x17, local copies, waits for them, and re-layouts: 3.34 us -> 2.74 us
  transfers between devices with their start and end apart: 5 -> 5, of which waited for: 3 -> 3; matrix products, arithmetic and copies ran while one was open for 3% -> 10% of each run, Pallas kernels for 0% -> 0%
where the time goes in v15:
time: 59.2 us; the launch traced here: 58.7 us
  starting transfers between devices  17.5 us (30%)
  waiting for transfers between devices  14.4 us (24%)
  other arithmetic  10.3 us (17%)
  local copies, waits for them, and re-layouts  10 us (17%)
  Pallas kernels  3.91 us (7%)
  matrix products  2.19 us (4%)
    all_to_all x1, waiting for transfers between devices, on_device(): lax.all_to_all(outgoing, ('lon', 'lev'), split_axis=1, concat_axis=1, til...  7.42 us
    all_to_all x1, starting transfers between devices, on_device(): lax.all_to_all(send_buffer, ('lon', 'lev'), split_axis=1, concat_axis=1,...  6.79 us
    squeeze x1, local copies, waits for them, and re-layouts, network(): w_middle[layer_no]  4 us
    pallas_call x2, Pallas kernels, layers(): pl.pallas_call(functools.partial(layers_kernel, finals=finals), out_shape...  3.91 us
    all_to_all x1, waiting for transfers between devices, on_device(): lax.all_to_all(send_buffer, ('lon', 'lev'), split_axis=1, concat_axis=1,...  3.67 us
    all_to_all x1, starting transfers between devices, on_device(): lax.all_to_all(outgoing, ('lon', 'lev'), split_axis=1, concat_axis=1, til...  3.37 us
    ppermute x1, waiting for transfers between devices, halo_exchange(): lax.ppermute(jnp.concatenate([right, left], axis=-1), 'lon', [(0, 1), (1,...  3.33 us
    ppermute x1, starting transfers between devices, halo_exchange(): lax.ppermute(cells[..., cells.shape[-2] - width:, :], 'lat', [(i, i + 1)...  3.04 us
  transfers between devices with their start and end apart: 5, of which 3 were waited for; matrix products, arithmetic and copies ran while one was open for 10% of the time, Pallas kernels for 0%

profile of v15, /device:TPU:0, one launch (start us, length us, event | category | flops | bytes accessed | tf_op | source)
XLA Modules:
  0.0 58.7 jit_solution(15105728767027230441)
XLA Ops:
  0.0 1.1 %pad_maximum_fusion.16 = (f32[45,3,128]{2,1,0:T(4,128)S(1)}, f32[45,3,128]{2,1,0:T(4,128)S(1)}) fusion(f32[15,32,128]{2,1,0:T(8,128)} %param.8, f32[30,32,128]{2,1,0:T(8,128)} %bitcast.40), kind=kLoop, calls=%fused_computation.95 | loop fusion | flops 34560 | bytes 875520 | tf_op jit(solution)/shard_map/slice | solution.py:17
  1.1 1.3 %collective-permute-start.1 = (f32[45,3,128]{2,1,0:T(4,128)S(1)}, f32[45,3,128]{2,1,0:T(4,128)S(1)}, u32[]{:S(2)}, u32[]{:S(2)}) collective-permute-start(f32[45,3,128]{2,1,0:T(4,128)S(1)} %get-tuple-element.26), channel_id=1, source_target_pairs={{8,0},{16,8},{24,16},{9,1},{17,9},{25,17},{10,2},{18,10},{26,18},{... | collective-permute-start | bytes 207368 | tf_op jit(solution)/shard_map/ppermute | solution.py:19
  2.4 3.0 %collective-permute-start = (f32[45,3,128]{2,1,0:T(4,128)S(1)}, f32[45,3,128]{2,1,0:T(4,128)S(1)}, u32[]{:S(2)}, u32[]{:S(2)}) collective-permute-start(f32[45,3,128]{2,1,0:T(4,128)S(1)} %get-tuple-element.25), channel_id=1, source_target_pairs={{0,8},{8,16},{16,24},{1,9},{9,17},{17,25},{2,10},{10,18},{18,26},{... | collective-permute-start | bytes 207368 | tf_op jit(solution)/shard_map/ppermute | solution.py:16
  5.5 0.7 %and_select_fusion = (s32[1,1024]{1,0:T(1,128)S(1)}, s32[1,1024]{1,0:T(1,128)S(1)}) fusion(s32[1,1024]{1,0:T(1,128)} %param.9), kind=kLoop, calls=%fused_computation.97 | loop fusion | flops 11264 | bytes 12288 | tf_op jit(solution)/shard_map/jit(remainder)/select_n | solution.py:128
  6.2 0.7 %and_select_fusion.1 = s32[1,1024]{1,0:T(1,128)S(1)} fusion(s32[1,1024]{1,0:T(1,128)S(1)} %get-tuple-element.6, s32[1,1024]{1,0:T(1,128)} %param.9), kind=kLoop, calls=%fused_computation.99 | loop fusion | flops 12288 | bytes 12288 | tf_op jit(solution)/shard_map/jit(floor_divide)/jit(_where)/select_n | solution.py:127
  7.0 1.1 %pad_maximum_fusion.1 = f32[45,38,128]{2,1,0:T(8,128)S(1)} fusion(f32[45,3,128]{2,1,0:T(4,128)S(1)} %collective-permute-done.1, f32[15,32,128]{2,1,0:T(8,128)} %param.8, f32[30,32,128]{2,1,0:T(8,128)S(1)} %bitcast.41, f32[45,3,128]{2,1,0:T(4,128)S(1)} %collective-permute-done), kind=kLoop, calls=%fused_computation.36 | loop fusion | flops 656640 | bytes 1751040 | tf_op jit(solution)/shard_map/concatenate | solution.py:22
  8.0 0.3 fusion.56
  8.4 0.4 copy.51
  8.8 0.4 copy.50
  9.3 3.0 %collective-permute-start.2 = (f32[45,38,6]{0,1,2:T(8,128)S(1)}, f32[45,38,6]{0,1,2:T(8,128)S(1)}, u32[]{:S(2)}, u32[]{:S(2)}) collective-permute-start(f32[45,38,6]{0,1,2:T(8,128)S(1)} %pad_maximum_fusion.14), channel_id=1, source_target_pairs={{0,4},{4,0},{1,5},{5,1},{2,6},{6,2},{3,7},{7,3},{8,12},{12,8},{9,1... | collective-permute-start | bytes 123128 | tf_op jit(solution)/shard_map/ppermute | solution.py:27
  12.5 3.3 %collective-permute-done.2 = f32[45,38,6]{0,1,2:T(8,128)S(1)} collective-permute-done((f32[45,38,6]{0,1,2:T(8,128)S(1)}, f32[45,38,6]{0,1,2:T(8,128)S(1)}, u32[]{:S(2)}, u32[]{:S(2)}) %collective-permute-start.2) | collective-permute-done | bytes 41072 | tf_op jit(solution)/shard_map/ppermute | solution.py:27
  15.8 0.5 copy.68
  16.3 0.5 copy.67
  16.8 1.0 %pad_maximum_fusion = f32[45,38,134]{2,1,0:T(8,128)S(1)} fusion(f32[45,38,3]{2,1,0:T(8,128)S(1)} %copy.68, f32[45,3,128]{2,1,0:T(4,128)S(1)} %collective-permute-done.1, f32[15,32,128]{2,1,0:T(8,128)S(1)} %copy-done.3, f32[30,32,128]{2,1,0:T(8,128)S(1)} %bitcast.42, f32[45,3,128]{2,1,0:T(4,128)S(1)} %collective-permute-done, f32[45,38,3]{2,1,0:T(8,128)S(1)} %copy.67), kind=kLoop, calls=%fused_computation.6 | loop fusion | flops 1145700 | bytes 1833120 | tf_op jit(solution)/shard_map/concatenate | solution.py:32
  17.8 0.7 %fusion.33 = (f32[15,36,132]{2,1,0:T(8,128)S(1)}, f32[15,36,132]{2,1,0:T(8,128)S(1)}, f32[15,36,132]{2,1,0:T(8,128)S(1)}, f32[15,36,132]{2,1,0:T(8,128)S(1)}) fusion(f32[45,38,134]{2,1,0:T(8,128)S(1)} %pad_maximum_fusion), kind=kLoop, calls=%fused_computation.52 | loop fusion | flops 570240 | bytes 2566080 | tf_op jit(solution)/shard_map/mul | solution.py:46
  18.5 1.4 %fusion.14 = f32[2,15,36,132]{3,2,1,0:T(8,128)S(1)} fusion(f32[2,15,38,134]{3,2,1,0:T(8,128)S(1)} %bitcast.39, f32[15,36,132]{2,1,0:T(8,128)S(1)} %get-tuple-element.16, f32[15,36,132]{2,1,0:T(8,128)S(1)} %get-tuple-element.17, f32[15,36,132]{2,1,0:T(8,128)S(1)} %get-tuple-element.18, f32[15,36,132]{2,1,0:T(8,128)S(1)} %get-tuple-element.15, ...), kind=kLoop, calls=%fused_computation.23 | loop fusion | flops 1853280 | bytes 4561956 | tf_op jit(solution)/shard_map/jit(_where)/select_n | solution.py:56
  20.0 0.9 %fusion.29 = (f32[15,34,130]{2,1,0:T(8,128)S(1)}, f32[15,34,130]{2,1,0:T(8,128)S(1)}, f32[15,34,130]{2,1,0:T(8,128)S(1)}, f32[15,34,130]{2,1,0:T(8,128)S(1)}) fusion(f32[45,38,134]{2,1,0:T(8,128)S(1)} %pad_maximum_fusion, f32[45,38,3]{2,1,0:T(8,128)S(1)} %copy.68, f32[45,3,128]{2,1,0:T(4,128)S(1)} %collective-permute-done.1, ...), kind=kLoop, calls=%fused_computation.44 | loop fusion | flops 1060800 | bytes 2772960 | tf_op jit(solution)/shard_map/mul | solution.py:46
  20.8 1.4 %fusion.5 = f32[2,15,34,130]{3,2,1,0:T(8,128)S(1)} fusion(f32[2,15,36,132]{3,2,1,0:T(8,128)S(1)} %fusion.14, f32[15,34,130]{2,1,0:T(8,128)S(1)} %get-tuple-element.13, f32[15,34,130]{2,1,0:T(8,128)S(1)} %get-tuple-element.14, f32[15,34,130]{2,1,0:T(8,128)S(1)} %get-tuple-element.12, f32[15,34,130]{2,1,0:T(8,128)S(1)} %get-tuple-element.11, ...), kind=kLoop, calls=%fused_computation.10 | loop fusion | flops 1723800 | bytes 4243234 | tf_op jit(solution)/shard_map/jit(_where)/select_n | solution.py:56
  22.3 0.4 fusion.50
  22.6 0.6 %fusion.38 = f32[2,15,32,128]{3,2,1,0:T(8,128)S(1)} fusion(f32[2,15,34,130]{3,2,1,0:T(8,128)S(1)} %fusion.5, f32[15,32,128]{2,1,0:T(8,128)S(1)} %get-tuple-element.20, f32[15,32,128]{2,1,0:T(8,128)S(1)} %get-tuple-element.19, f32[15,32,128]{2,1,0:T(8,128)S(1)} %get-tuple-element.24, f32[15,32,128]{2,1,0:T(8,128)S(1)} %get-tuple-element.23), kind=kLoop, calls=%fused_computation.57 | loop fusion | flops 1474560 | bytes 3932160 | tf_op jit(solution)/shard_map/add | solution.py:47
  23.3 0.7 %select_reduce_fusion = bf16[30,1024]{1,0:T(8,128)(2,1)S(1)} fusion(pred[32,1024]{1,0:T(8,128)(4,1)S(1)} %iota_compare_fusion.1, bf16[30,32,128]{2,1,0:T(8,128)(2,1)S(1)} %bitcast_convert_fusion, s32[1024]{0:T(1024)S(1)} %bitcast.52), kind=kOutput, calls=%fused_computation.4 | convolution fusion | flops 253724672 | bytes 344064 | tf_op jit(solution)/shard_map/dot_general | solution.py:133
  24.0 0.7 %broadcast_in_dim.101 = bf16[30,2,4,256]{3,0,2,1:T(8,128)(2,1)} broadcast(bf16[30,4,256]{2,0,1:T(8,128)(2,1)S(1)} %copy.54), dimensions={0,2,3} | broadcast | bytes 184320 | tf_op jit(solution)/shard_map/broadcast_in_dim | solution.py:143
  24.7 6.8 %all-to-all-start = ((bf16[30,8,256]{2,0,1:T(8,128)(2,1)}), bf16[30,8,256]{2,0,1:T(8,128)(2,1)S(1)}, u32[]{:S(2)}, u32[]{:S(2)}) async-start(bf16[30,8,256]{2,0,1:T(8,128)(2,1)} %bitcast.6), calls=%async_computation | async-start | bytes 262144 | tf_op jit(solution)/shard_map/all_to_all | solution.py:158
  31.5 4.0 %slice_bitcast_fusion = (bf16[1024,1024]{1,0:T(8,128)(2,1)S(1)}, bf16[1024,1024]{1,0:T(8,128)(2,1)}) fusion(bf16[1,2,1024,1024]{3,2,1,0:T(8,128)(2,1)} %param.12), kind=kLoop, calls=%fused_computation | loop fusion | bytes 8388608 | tf_op jit(solution)/shard_map/squeeze | solution.py:110
  35.5 3.7 %all-to-all-done = bf16[30,8,256]{2,0,1:T(8,128)(2,1)S(1)} async-done(((bf16[30,8,256]{2,0,1:T(8,128)(2,1)}), bf16[30,8,256]{2,0,1:T(8,128)(2,1)S(1)}, u32[]{:S(2)}, u32[]{:S(2)}) %all-to-all-start) | async-done | bytes 122912 | tf_op jit(solution)/shard_map/all_to_all | solution.py:158
  39.6 1.6 %copy-done = bf16[1024,1024]{1,0:T(8,128)(2,1)S(1)} copy-done((bf16[1024,1024]{1,0:T(8,128)(2,1)S(1)}, bf16[1024,1024]{1,0:T(8,128)(2,1)}, u32[]{:S(2)}) %copy-start) | copy-done | bytes 2097176
  41.2 2.0 %shard_map.73.rows_ref = bf16[512,1024]{1,0:T(8,128)(2,1)S(1)} custom-call(bf16[512,120]{1,0:T(8,128)(2,1)S(1)} %copy.57.rows_ref, bf16[120,1024]{1,0:T(8,128)(2,1)S(1)} %bitcast.38, bf16[1024,1024]{1,0:T(8,128)(2,1)S(1)} %copy-done), custom_call_target="tpu_custom_call" | custom-call | flops 1199570944 | bytes 3514368 | tf_op jit(solution)/shard_map/pallas_call | solution.py:94
  43.2 1.9 %shard_map.74 = bf16[512,120]{1,0:T(8,128)(2,1)S(1)} custom-call(bf16[512,1024]{1,0:T(8,128)(2,1)S(1)} %shard_map.73.rows_ref, bf16[1024,1024]{1,0:T(8,128)(2,1)S(1)} %get-tuple-element.7.refs_0_, bf16[1024,120]{1,0:T(8,128)(2,1)S(1)} %bitcast.37), custom_call_target="tpu_custom_call" | custom-call | flops 1199570944 | bytes 3514368 | tf_op jit(solution)/shard_map/pallas_call | solution.py:94
  45.3 0.7 %reshape.108 = bf16[30,8,256]{2,0,1:T(8,128)(2,1)} reshape(bf16[2,15,2,4,256]{4,1,0,3,2:T(8,128)(2,1)S(1)} %copy.64) | data formatting | bytes 245760 | tf_op jit(solution)/shard_map/reshape | solution.py:170
  46.0 3.4 %all-to-all-start.1 = ((bf16[30,8,256]{2,0,1:T(8,128)(2,1)}), bf16[30,8,256]{2,0,1:T(8,128)(2,1)S(1)}, u32[]{:S(2)}, u32[]{:S(2)}) async-start(bf16[30,8,256]{2,0,1:T(8,128)(2,1)} %reshape.108), calls=%async_computation.1 | async-start | bytes 262144 | tf_op jit(solution)/shard_map/all_to_all | solution.py:172
  49.4 7.4 %all-to-all-done.1 = bf16[30,8,256]{2,0,1:T(8,128)(2,1)S(1)} async-done(((bf16[30,8,256]{2,0,1:T(8,128)(2,1)}), bf16[30,8,256]{2,0,1:T(8,128)(2,1)S(1)}, u32[]{:S(2)}, u32[]{:S(2)}) %all-to-all-start.1) | async-done | bytes 122912 | tf_op jit(solution)/shard_map/all_to_all | solution.py:172
  57.2 1.5 %fusion.21 = f32[30,32,128]{2,1,0:T(8,128)} fusion(f32[30,32,128]{2,1,0:T(8,128)S(1)} %bitcast.45, pred[32,1024]{1,0:T(8,128)(4,1)S(1)} %iota_compare_fusion.1, bf16[30,1024]{1,0:T(8,128)(2,1)S(1)} %bitcast.50, s32[1024]{0:T(1024)S(1)} %bitcast.53), kind=kOutput, calls=%fused_computation.33 | convolution fusion | flops 252895232 | bytes 1081344 | tf_op jit(solution)/shard_map/dot_general | solution.py:183
  (36 shorter events, 1.3 us)
Async XLA Ops:
  0.0 7.0 %copy-start.2 = (f32[2,15,32,128]{3,2,1,0:T(8,128)S(1)}, f32[2,15,32,128]{3,2,1,0:T(8,128)}, u32[]{:S(2)}) copy-start(f32[2,15,32,128]{3,2,1,0:T(8,128)} %param.7) | copy-start | bytes 1474564
  1.1 5.8 %collective-permute-start.1 = (f32[45,3,128]{2,1,0:T(4,128)S(1)}, f32[45,3,128]{2,1,0:T(4,128)S(1)}, u32[]{:S(2)}, u32[]{:S(2)}) collective-permute-start(f32[45,3,128]{2,1,0:T(4,128)S(1)} %get-tuple-element.26), channel_id=1, source_target_pairs={{8,0},{16,8},{24,16},{9,1},{17,9},{25,17},{10,2},{18,10},{26,18},{... | collective-permute-start | bytes 207368 | tf_op jit(solution)/shard_map/ppermute | solution.py:19
  2.4 4.5 %collective-permute-start = (f32[45,3,128]{2,1,0:T(4,128)S(1)}, f32[45,3,128]{2,1,0:T(4,128)S(1)}, u32[]{:S(2)}, u32[]{:S(2)}) collective-permute-start(f32[45,3,128]{2,1,0:T(4,128)S(1)} %get-tuple-element.25), channel_id=1, source_target_pairs={{0,8},{8,16},{16,24},{1,9},{9,17},{17,25},{2,10},{10,18},{18,26},{... | collective-permute-start | bytes 207368 | tf_op jit(solution)/shard_map/ppermute | solution.py:16
  8.3 3.9 %copy-start.4 = (bf16[1,1024,120]{1,2,0:T(8,128)(2,1)S(1)}, bf16[1,1024,120]{1,2,0:T(8,128)(2,1)}, u32[]{:S(2)}) copy-start(bf16[1,1024,120]{1,2,0:T(8,128)(2,1)} %param.13) | copy-start | bytes 737284
  9.3 6.6 %collective-permute-start.2 = (f32[45,38,6]{0,1,2:T(8,128)S(1)}, f32[45,38,6]{0,1,2:T(8,128)S(1)}, u32[]{:S(2)}, u32[]{:S(2)}) collective-permute-start(f32[45,38,6]{0,1,2:T(8,128)S(1)} %pad_maximum_fusion.14), channel_id=1, source_target_pairs={{0,4},{4,0},{1,5},{5,1},{2,6},{6,2},{3,7},{7,3},{8,12},{12,8},{9,1... | collective-permute-start | bytes 123128 | tf_op jit(solution)/shard_map/ppermute | solution.py:27
  12.5 4.3 %copy-start.3 = (f32[15,32,128]{2,1,0:T(8,128)S(1)}, f32[15,32,128]{2,1,0:T(8,128)}, u32[]{:S(2)}) copy-start(f32[15,32,128]{2,1,0:T(8,128)} %param.8) | copy-start | bytes 737284
  24.7 14.5 %all-to-all-start = ((bf16[30,8,256]{2,0,1:T(8,128)(2,1)}), bf16[30,8,256]{2,0,1:T(8,128)(2,1)S(1)}, u32[]{:S(2)}, u32[]{:S(2)}) async-start(bf16[30,8,256]{2,0,1:T(8,128)(2,1)} %bitcast.6), calls=%async_computation | async-start | bytes 262144 | tf_op jit(solution)/shard_map/all_to_all | solution.py:158
  35.5 4.1 %copy-start.1 = (bf16[1,120,1024]{2,1,0:T(8,128)(2,1)S(1)}, bf16[1,120,1024]{2,1,0:T(8,128)(2,1)}, u32[]{:S(2)}) copy-start(bf16[1,120,1024]{2,1,0:T(8,128)(2,1)} %param.11) | copy-start | bytes 737284
  39.6 1.6 %copy-start = (bf16[1024,1024]{1,0:T(8,128)(2,1)S(1)}, bf16[1024,1024]{1,0:T(8,128)(2,1)}, u32[]{:S(2)}) copy-start(bf16[1024,1024]{1,0:T(8,128)(2,1)} %get-tuple-element.8.refs_1_) | copy-start | bytes 6291460
  45.1 4.3 %copy-start.5 = (s32[1,1024,1]{1,2,0:T(1,128)S(1)}, s32[1,1024,1]{1,2,0:T(1,128)}, u32[]{:S(2)}) copy-start(s32[1,1024,1]{1,2,0:T(1,128)} %param.10) | copy-start | bytes 12292
  46.0 10.8 %all-to-all-start.1 = ((bf16[30,8,256]{2,0,1:T(8,128)(2,1)}), bf16[30,8,256]{2,0,1:T(8,128)(2,1)S(1)}, u32[]{:S(2)}, u32[]{:S(2)}) async-start(bf16[30,8,256]{2,0,1:T(8,128)(2,1)} %reshape.108), calls=%async_computation.1 | async-start | bytes 262144 | tf_op jit(solution)/shard_map/all_to_all | solution.py:172

commit v16 on v14

--- a/solution.py
+++ b/solution.py
@@ -74,24 +74,25 @@
     return values
 
 
-def network_kernel(rows_ref, first_ref, middle_ref, last_ref, out_ref):
-    tile = min(rows_ref.shape[0], 512)
-
-    def one_tile(index, carry):
-        rows = pl.ds(pl.multiple_of(index * tile, tile), tile)
-        hidden = jax.nn.gelu(
-            jnp.dot(rows_ref[rows, :], first_ref[...], preferred_element_type=jnp.float32)
+def network_kernel(rows_ref, first_ref, middle_hbm, last_ref, out_ref, middle_ref, hidden_ref, sems):
+    layers = middle_ref.shape[0]
+    copies = [
+        pltpu.make_async_copy(middle_hbm.at[layer_no], middle_ref.at[layer_no], sems.at[layer_no])
+        for layer_no in range(layers)
+    ]
+    for copy in copies:
+        copy.start()
+    hidden_ref[...] = jax.nn.gelu(
+        jnp.dot(rows_ref[...], first_ref[...], preferred_element_type=jnp.float32)
+    ).astype(jnp.bfloat16)
+    for layer_no in range(layers):
+        copies[layer_no].wait()
+        hidden_ref[...] = jax.nn.gelu(
+            jnp.dot(hidden_ref[...], middle_ref[layer_no], preferred_element_type=jnp.float32)
         ).astype(jnp.bfloat16)
-        for layer_no in range(middle_ref.shape[0]):
-            hidden = jax.nn.gelu(
-                jnp.dot(hidden, middle_ref[layer_no], preferred_element_type=jnp.float32)
-            ).astype(jnp.bfloat16)
-        out_ref[rows, :] = jnp.dot(
-            hidden, last_ref[...], preferred_element_type=jnp.float32
-        ).astype(jnp.bfloat16)
-        return carry
-
-    lax.fori_loop(0, rows_ref.shape[0] // tile, one_tile, 0)
+    out_ref[...] = jnp.dot(
+        hidden_ref[...], last_ref[...], preferred_element_type=jnp.float32
+    ).astype(jnp.bfloat16)
 
 
 def network(rows, w_first, w_middle, w_last):
@@ -103,9 +104,14 @@
     return pl.pallas_call(
         network_kernel,
         out_shape=jax.ShapeDtypeStruct((count, w_last.shape[1]), jnp.bfloat16),
-        in_specs=[vmem] * 4,
+        in_specs=[vmem, vmem, pl.BlockSpec(memory_space=pl.ANY), vmem],
         out_specs=vmem,
-        compiler_params=pltpu.CompilerParams(vmem_limit_bytes=48 * 1024 * 1024),
+        scratch_shapes=[
+            pltpu.VMEM(w_middle.shape, w_middle.dtype),
+            pltpu.VMEM((count, hid), jnp.bfloat16),
+            pltpu.SemaphoreType.DMA((w_middle.shape[0],)),
+        ],
+        compiler_params=pltpu.CompilerParams(vmem_limit_bytes=60 * 1024 * 1024),
         cost_estimate=pl.CostEstimate(
             flops=flops,
             transcendentals=(1 + w_middle.shape[0]) * count * hid,

time: 59.1 us -> 62.1 us (1.051)
  Pallas kernels: 3.23 us -> 6.89 us
    pallas_call x1, Pallas kernels: 3.23 us -> 6.89 us  [network(): pl.pallas_call(network_kernel, out_shape=jax.ShapeDtypeStruct((count, w_l...]
    unnamed x17 -> x13, local copies, waits for them, and re-layouts: 3.34 us -> 1.82 us
    pallas_call x1, local copies, waits for them, and re-layouts: 0.11 us -> 1.01 us  [network(): pl.pallas_call(network_kernel, out_shape=jax.ShapeDtypeStruct((count, w_l...]
    all_to_all x1, waiting for transfers between devices: 7.49 us -> 6.83 us  [on_device(): lax.all_to_all(send_buffer, ('lon', 'lev'), split_axis=1, concat_axis=1,...]
    reshape x1, local copies, waits for them, and re-layouts: 0.12 us -> 0.76 us  [on_device(): inputs = received.reshape(2, level_rows, lon_count, lev_count, capacity)....]
  transfers between devices with their start and end apart: 5 -> 5, of which waited for: 3 -> 3; matrix products, arithmetic and copies ran while one was open for 3% -> 4% of each run, Pallas kernels for 0% -> 0%
where the time goes in v16:
time: 62.1 us; the launch traced here: 61.6 us
  waiting for transfers between devices  17.8 us (29%)
  starting transfers between devices  17.5 us (28%)
  other arithmetic  10.3 us (17%)
  Pallas kernels  6.89 us (11%)
  local copies, waits for them, and re-layouts  6.65 us (11%)
  matrix products  2.2 us (4%)
    all_to_all x1, waiting for transfers between devices, on_device(): lax.all_to_all(outgoing, ('lon', 'lev'), split_axis=1, concat_axis=1, til...  7.42 us
    pallas_call x1, Pallas kernels, network(): pl.pallas_call(network_kernel, out_shape=jax.ShapeDtypeStruct((count, w_l...  6.89 us
    all_to_all x1, waiting for transfers between devices, on_device(): lax.all_to_all(send_buffer, ('lon', 'lev'), split_axis=1, concat_axis=1,...  6.83 us
    all_to_all x1, starting transfers between devices, on_device(): lax.all_to_all(send_buffer, ('lon', 'lev'), split_axis=1, concat_axis=1,...  6.79 us
    ppermute x1, waiting for transfers between devices, halo_exchange(): lax.ppermute(jnp.concatenate([right, left], axis=-1), 'lon', [(0, 1), (1,...  3.52 us
    all_to_all x1, starting transfers between devices, on_device(): lax.all_to_all(outgoing, ('lon', 'lev'), split_axis=1, concat_axis=1, til...  3.37 us
    ppermute x1, starting transfers between devices, halo_exchange(): lax.ppermute(cells[..., cells.shape[-2] - width:, :], 'lat', [(i, i + 1)...  3.04 us
    ppermute x1, starting transfers between devices, halo_exchange(): lax.ppermute(jnp.concatenate([right, left], axis=-1), 'lon', [(0, 1), (1,...  3.03 us
  transfers between devices with their start and end apart: 5, of which 3 were waited for; matrix products, arithmetic and copies ran while one was open for 4% of the time, Pallas kernels for 0%

profile of v16, /device:TPU:0, one launch (start us, length us, event | category | flops | bytes accessed | tf_op | source)
XLA Modules:
  0.0 61.6 jit_solution(17548085142493565918)
XLA Ops:
  0.0 1.1 %pad_maximum_fusion.16 = (f32[45,3,128]{2,1,0:T(4,128)S(1)}, f32[45,3,128]{2,1,0:T(4,128)S(1)}) fusion(f32[15,32,128]{2,1,0:T(8,128)} %param.8, f32[30,32,128]{2,1,0:T(8,128)} %bitcast.35), kind=kLoop, calls=%fused_computation.93 | loop fusion | flops 34560 | bytes 875520 | tf_op jit(solution)/shard_map/slice | solution.py:15
  1.1 1.3 %collective-permute-start.1 = (f32[45,3,128]{2,1,0:T(4,128)S(1)}, f32[45,3,128]{2,1,0:T(4,128)S(1)}, u32[]{:S(2)}, u32[]{:S(2)}) collective-permute-start(f32[45,3,128]{2,1,0:T(4,128)S(1)} %get-tuple-element.24), channel_id=1, source_target_pairs={{8,0},{16,8},{24,16},{9,1},{17,9},{25,17},{10,2},{18,10},{26,18},{... | collective-permute-start | bytes 207368 | tf_op jit(solution)/shard_map/ppermute | solution.py:17
  2.4 3.0 %collective-permute-start = (f32[45,3,128]{2,1,0:T(4,128)S(1)}, f32[45,3,128]{2,1,0:T(4,128)S(1)}, u32[]{:S(2)}, u32[]{:S(2)}) collective-permute-start(f32[45,3,128]{2,1,0:T(4,128)S(1)} %get-tuple-element.23), channel_id=1, source_target_pairs={{0,8},{8,16},{16,24},{1,9},{9,17},{17,25},{2,10},{10,18},{18,26},{... | collective-permute-start | bytes 207368 | tf_op jit(solution)/shard_map/ppermute | solution.py:14
  5.5 0.7 %and_select_fusion = (s32[1,1024]{1,0:T(1,128)S(1)}, s32[1,1024]{1,0:T(1,128)S(1)}) fusion(s32[1,1024]{1,0:T(1,128)} %param.9), kind=kLoop, calls=%fused_computation.95 | loop fusion | flops 11264 | bytes 12288 | tf_op jit(solution)/shard_map/jit(remainder)/select_n | solution.py:138
  6.2 0.7 %and_select_fusion.1 = s32[1,1024]{1,0:T(1,128)S(1)} fusion(s32[1,1024]{1,0:T(1,128)S(1)} %get-tuple-element.6, s32[1,1024]{1,0:T(1,128)} %param.9), kind=kLoop, calls=%fused_computation.97 | loop fusion | flops 12288 | bytes 12288 | tf_op jit(solution)/shard_map/jit(floor_divide)/jit(_where)/select_n | solution.py:137
  7.0 1.1 %pad_maximum_fusion.1 = f32[45,38,128]{2,1,0:T(8,128)S(1)} fusion(f32[45,3,128]{2,1,0:T(4,128)S(1)} %collective-permute-done.1, f32[15,32,128]{2,1,0:T(8,128)} %param.8, f32[30,32,128]{2,1,0:T(8,128)S(1)} %bitcast.36, f32[45,3,128]{2,1,0:T(4,128)S(1)} %collective-permute-done), kind=kLoop, calls=%fused_computation.34 | loop fusion | flops 656640 | bytes 1751040 | tf_op jit(solution)/shard_map/concatenate | solution.py:20
  8.0 0.3 fusion.56
  8.3 0.4 copy.51
  8.8 0.4 copy.50
  9.3 3.0 %collective-permute-start.2 = (f32[45,38,6]{0,1,2:T(8,128)S(1)}, f32[45,38,6]{0,1,2:T(8,128)S(1)}, u32[]{:S(2)}, u32[]{:S(2)}) collective-permute-start(f32[45,38,6]{0,1,2:T(8,128)S(1)} %pad_maximum_fusion.14), channel_id=1, source_target_pairs={{0,4},{4,0},{1,5},{5,1},{2,6},{6,2},{3,7},{7,3},{8,12},{12,8},{9,1... | collective-permute-start | bytes 123128 | tf_op jit(solution)/shard_map/ppermute | solution.py:25
  12.3 3.5 %collective-permute-done.2 = f32[45,38,6]{0,1,2:T(8,128)S(1)} collective-permute-done((f32[45,38,6]{0,1,2:T(8,128)S(1)}, f32[45,38,6]{0,1,2:T(8,128)S(1)}, u32[]{:S(2)}, u32[]{:S(2)}) %collective-permute-start.2) | collective-permute-done | bytes 41072 | tf_op jit(solution)/shard_map/ppermute | solution.py:25
  15.8 0.5 copy.68
  16.3 0.5 copy.67
  16.8 1.0 %pad_maximum_fusion = f32[45,38,134]{2,1,0:T(8,128)S(1)} fusion(f32[45,38,3]{2,1,0:T(8,128)S(1)} %copy.68, f32[45,3,128]{2,1,0:T(4,128)S(1)} %collective-permute-done.1, f32[15,32,128]{2,1,0:T(8,128)S(1)} %copy-done.1, f32[30,32,128]{2,1,0:T(8,128)S(1)} %bitcast.37, f32[45,3,128]{2,1,0:T(4,128)S(1)} %collective-permute-done, f32[45,38,3]{2,1,0:T(8,128)S(1)} %copy.67), kind=kLoop, calls=%fused_computation.4 | loop fusion | flops 1145700 | bytes 1833120 | tf_op jit(solution)/shard_map/concatenate | solution.py:30
  17.9 0.7 %fusion.33 = (f32[15,36,132]{2,1,0:T(8,128)S(1)}, f32[15,36,132]{2,1,0:T(8,128)S(1)}, f32[15,36,132]{2,1,0:T(8,128)S(1)}, f32[15,36,132]{2,1,0:T(8,128)S(1)}) fusion(f32[45,38,134]{2,1,0:T(8,128)S(1)} %pad_maximum_fusion), kind=kLoop, calls=%fused_computation.50 | loop fusion | flops 570240 | bytes 2566080 | tf_op jit(solution)/shard_map/mul | solution.py:44
  18.6 1.4 %fusion.14 = f32[2,15,36,132]{3,2,1,0:T(8,128)S(1)} fusion(f32[2,15,38,134]{3,2,1,0:T(8,128)S(1)} %bitcast.34, f32[15,36,132]{2,1,0:T(8,128)S(1)} %get-tuple-element.14, f32[15,36,132]{2,1,0:T(8,128)S(1)} %get-tuple-element.15, f32[15,36,132]{2,1,0:T(8,128)S(1)} %get-tuple-element.16, f32[15,36,132]{2,1,0:T(8,128)S(1)} %get-tuple-element.13, ...), kind=kLoop, calls=%fused_computation.21 | loop fusion | flops 1853280 | bytes 4561956 | tf_op jit(solution)/shard_map/jit(_where)/select_n | solution.py:54
  20.0 0.9 %fusion.29 = (f32[15,34,130]{2,1,0:T(8,128)S(1)}, f32[15,34,130]{2,1,0:T(8,128)S(1)}, f32[15,34,130]{2,1,0:T(8,128)S(1)}, f32[15,34,130]{2,1,0:T(8,128)S(1)}) fusion(f32[45,38,134]{2,1,0:T(8,128)S(1)} %pad_maximum_fusion, f32[45,38,3]{2,1,0:T(8,128)S(1)} %copy.68, f32[45,3,128]{2,1,0:T(4,128)S(1)} %collective-permute-done.1, ...), kind=kLoop, calls=%fused_computation.42 | loop fusion | flops 1060800 | bytes 2772960 | tf_op jit(solution)/shard_map/mul | solution.py:44
  20.9 1.4 %fusion.5 = f32[2,15,34,130]{3,2,1,0:T(8,128)S(1)} fusion(f32[2,15,36,132]{3,2,1,0:T(8,128)S(1)} %fusion.14, f32[15,34,130]{2,1,0:T(8,128)S(1)} %get-tuple-element.11, f32[15,34,130]{2,1,0:T(8,128)S(1)} %get-tuple-element.12, f32[15,34,130]{2,1,0:T(8,128)S(1)} %get-tuple-element.10, f32[15,34,130]{2,1,0:T(8,128)S(1)} %get-tuple-element.9, ...), kind=kLoop, calls=%fused_computation.8 | loop fusion | flops 1723800 | bytes 4243234 | tf_op jit(solution)/shard_map/jit(_where)/select_n | solution.py:54
  22.3 0.4 fusion.50
  22.7 0.6 fusion.38
  23.3 0.7 %select_reduce_fusion = bf16[30,1024]{1,0:T(8,128)(2,1)S(1)} fusion(pred[32,1024]{1,0:T(8,128)(4,1)S(1)} %iota_compare_fusion.1, bf16[30,32,128]{2,1,0:T(8,128)(2,1)S(1)} %bitcast_convert_fusion, s32[1024]{0:T(1024)S(1)} %bitcast.48), kind=kOutput, calls=%fused_computation.2 | convolution fusion | flops 253724672 | bytes 344064 | tf_op jit(solution)/shard_map/dot_general | solution.py:143
  24.1 0.7 %broadcast_in_dim.101 = bf16[30,2,4,256]{3,0,2,1:T(8,128)(2,1)} broadcast(bf16[30,4,256]{2,0,1:T(8,128)(2,1)S(1)} %copy.54), dimensions={0,2,3} | broadcast | bytes 184320 | tf_op jit(solution)/shard_map/broadcast_in_dim | solution.py:153
  24.7 6.8 %all-to-all-start = ((bf16[30,8,256]{2,0,1:T(8,128)(2,1)}), bf16[30,8,256]{2,0,1:T(8,128)(2,1)S(1)}, u32[]{:S(2)}, u32[]{:S(2)}) async-start(bf16[30,8,256]{2,0,1:T(8,128)(2,1)} %bitcast.6), calls=%async_computation | async-start | bytes 262144 | tf_op jit(solution)/shard_map/all_to_all | solution.py:168
  31.5 0.8 %copy.57 = bf16[1,1024,120]{2,1,0:T(8,128)(2,1)} copy(bf16[1,1024,120]{1,2,0:T(8,128)(2,1)S(1)} %copy-done.2) | data formatting | bytes 491520 | tf_op args[6]
  32.4 6.8 %all-to-all-done = bf16[30,8,256]{2,0,1:T(8,128)(2,1)S(1)} async-done(((bf16[30,8,256]{2,0,1:T(8,128)(2,1)}), bf16[30,8,256]{2,0,1:T(8,128)(2,1)S(1)}, u32[]{:S(2)}, u32[]{:S(2)}) %all-to-all-start) | async-done | bytes 122912 | tf_op jit(solution)/shard_map/all_to_all | solution.py:168
  39.5 0.8 %copy.58.rows_ref = bf16[512,120]{1,0:T(8,128)(2,1)} copy(bf16[512,120]{0,1:T(8,128)(2,1)S(1)} %bitcast.43) | data formatting | bytes 245760 | tf_op jit(solution)/shard_map/reshape | solution.py:174
  40.2 6.9 %shard_map.73 = bf16[512,120]{1,0:T(8,128)(2,1)} custom-call(bf16[512,120]{1,0:T(8,128)(2,1)} %copy.58.rows_ref, bf16[120,1024]{1,0:T(8,128)(2,1)} %bitcast.51, bf16[2,1024,1024]{2,1,0:T(8,128)(2,1)} %bitcast.50, bf16[1024,120]{1,0:T(8,128)(2,1)} %bitcast.45), custom_call_target="tpu_custom_call" | custom-call | flops 2399141888 | bytes 4931584 | tf_op jit(solution)/shard_map/pallas_call | solution.py:104
  47.2 1.0 %copy.59 = bf16[512,120]{0,1:T(8,128)(2,1)S(1)} copy(bf16[512,120]{1,0:T(8,128)(2,1)} %shard_map.73) | data formatting | bytes 245760 | tf_op jit(solution)/shard_map/pallas_call | solution.py:104
  48.2 0.7 %reshape.104 = bf16[30,8,256]{2,0,1:T(8,128)(2,1)} reshape(bf16[2,15,2,4,256]{4,1,0,3,2:T(8,128)(2,1)S(1)} %copy.64) | data formatting | bytes 245760 | tf_op jit(solution)/shard_map/reshape | solution.py:180
  48.9 3.4 %all-to-all-start.1 = ((bf16[30,8,256]{2,0,1:T(8,128)(2,1)}), bf16[30,8,256]{2,0,1:T(8,128)(2,1)S(1)}, u32[]{:S(2)}, u32[]{:S(2)}) async-start(bf16[30,8,256]{2,0,1:T(8,128)(2,1)} %reshape.104), calls=%async_computation.1 | async-start | bytes 262144 | tf_op jit(solution)/shard_map/all_to_all | solution.py:182
  52.3 7.4 %all-to-all-done.1 = bf16[30,8,256]{2,0,1:T(8,128)(2,1)S(1)} async-done(((bf16[30,8,256]{2,0,1:T(8,128)(2,1)}), bf16[30,8,256]{2,0,1:T(8,128)(2,1)S(1)}, u32[]{:S(2)}, u32[]{:S(2)}) %all-to-all-start.1) | async-done | bytes 122912 | tf_op jit(solution)/shard_map/all_to_all | solution.py:182
  60.1 1.5 %fusion.21 = f32[30,32,128]{2,1,0:T(8,128)} fusion(f32[30,32,128]{2,1,0:T(8,128)S(1)} %bitcast.40, pred[32,1024]{1,0:T(8,128)(4,1)S(1)} %iota_compare_fusion.1, bf16[30,1024]{1,0:T(8,128)(2,1)S(1)} %bitcast.46, s32[1024]{0:T(1024)S(1)} %bitcast.49), kind=kOutput, calls=%fused_computation.31 | convolution fusion | flops 252895232 | bytes 1081344 | tf_op jit(solution)/shard_map/dot_general | solution.py:193
  (30 shorter events, 0.9 us)
Async XLA Ops:
  0.0 7.0 %copy-start = (f32[2,15,32,128]{3,2,1,0:T(8,128)S(1)}, f32[2,15,32,128]{3,2,1,0:T(8,128)}, u32[]{:S(2)}) copy-start(f32[2,15,32,128]{3,2,1,0:T(8,128)} %param.7) | copy-start | bytes 1474564
  1.1 5.8 %collective-permute-start.1 = (f32[45,3,128]{2,1,0:T(4,128)S(1)}, f32[45,3,128]{2,1,0:T(4,128)S(1)}, u32[]{:S(2)}, u32[]{:S(2)}) collective-permute-start(f32[45,3,128]{2,1,0:T(4,128)S(1)} %get-tuple-element.24), channel_id=1, source_target_pairs={{8,0},{16,8},{24,16},{9,1},{17,9},{25,17},{10,2},{18,10},{26,18},{... | collective-permute-start | bytes 207368 | tf_op jit(solution)/shard_map/ppermute | solution.py:17
  2.4 4.5 %collective-permute-start = (f32[45,3,128]{2,1,0:T(4,128)S(1)}, f32[45,3,128]{2,1,0:T(4,128)S(1)}, u32[]{:S(2)}, u32[]{:S(2)}) collective-permute-start(f32[45,3,128]{2,1,0:T(4,128)S(1)} %get-tuple-element.23), channel_id=1, source_target_pairs={{0,8},{8,16},{16,24},{1,9},{9,17},{17,25},{2,10},{10,18},{18,26},{... | collective-permute-start | bytes 207368 | tf_op jit(solution)/shard_map/ppermute | solution.py:14
  9.2 7.5 %copy-start.1 = (f32[15,32,128]{2,1,0:T(8,128)S(1)}, f32[15,32,128]{2,1,0:T(8,128)}, u32[]{:S(2)}) copy-start(f32[15,32,128]{2,1,0:T(8,128)} %param.8) | copy-start | bytes 737284
  9.3 6.6 %collective-permute-start.2 = (f32[45,38,6]{0,1,2:T(8,128)S(1)}, f32[45,38,6]{0,1,2:T(8,128)S(1)}, u32[]{:S(2)}, u32[]{:S(2)}) collective-permute-start(f32[45,38,6]{0,1,2:T(8,128)S(1)} %pad_maximum_fusion.14), channel_id=1, source_target_pairs={{0,4},{4,0},{1,5},{5,1},{2,6},{6,2},{3,7},{7,3},{8,12},{12,8},{9,1... | collective-permute-start | bytes 123128 | tf_op jit(solution)/shard_map/ppermute | solution.py:25
  23.3 8.2 %copy-start.2 = (bf16[1,1024,120]{1,2,0:T(8,128)(2,1)S(1)}, bf16[1,1024,120]{1,2,0:T(8,128)(2,1)}, u32[]{:S(2)}) copy-start(bf16[1,1024,120]{1,2,0:T(8,128)(2,1)} %param.13) | copy-start | bytes 737284
  24.7 14.5 %all-to-all-start = ((bf16[30,8,256]{2,0,1:T(8,128)(2,1)}), bf16[30,8,256]{2,0,1:T(8,128)(2,1)S(1)}, u32[]{:S(2)}, u32[]{:S(2)}) async-start(bf16[30,8,256]{2,0,1:T(8,128)(2,1)} %bitcast.6), calls=%async_computation | async-start | bytes 262144 | tf_op jit(solution)/shard_map/all_to_all | solution.py:168
  47.1 5.2 %copy-start.3 = (s32[1,1024,1]{1,2,0:T(1,128)S(1)}, s32[1,1024,1]{1,2,0:T(1,128)}, u32[]{:S(2)}) copy-start(s32[1,1024,1]{1,2,0:T(1,128)} %param.10) | copy-start | bytes 12292
  48.9 10.8 %all-to-all-start.1 = ((bf16[30,8,256]{2,0,1:T(8,128)(2,1)}), bf16[30,8,256]{2,0,1:T(8,128)(2,1)S(1)}, u32[]{:S(2)}, u32[]{:S(2)}) async-start(bf16[30,8,256]{2,0,1:T(8,128)(2,1)} %reshape.104), calls=%async_computation.1 | async-start | bytes 262144 | tf_op jit(solution)/shard_map/all_to_all | solution.py:182

commit v17 on v14

--- a/solution.py
+++ b/solution.py
@@ -86,8 +86,8 @@
             hidden = jax.nn.gelu(
                 jnp.dot(hidden, middle_ref[layer_no], preferred_element_type=jnp.float32)
             ).astype(jnp.bfloat16)
-        out_ref[rows, :] = jnp.dot(
-            hidden, last_ref[...], preferred_element_type=jnp.float32
+        out_ref[:, rows] = lax.dot_general(
+            last_ref[...], hidden, (((1,), (1,)), ((), ())), preferred_element_type=jnp.float32
         ).astype(jnp.bfloat16)
         return carry
 
@@ -102,7 +102,7 @@
     weight_bytes = 2 * (w_first.size + w_middle.size + w_last.size)
     return pl.pallas_call(
         network_kernel,
-        out_shape=jax.ShapeDtypeStruct((count, w_last.shape[1]), jnp.bfloat16),
+        out_shape=jax.ShapeDtypeStruct((w_last.shape[1], count), jnp.bfloat16),
         in_specs=[vmem] * 4,
         out_specs=vmem,
         compiler_params=pltpu.CompilerParams(vmem_limit_bytes=48 * 1024 * 1024),
@@ -111,7 +111,7 @@
             transcendentals=(1 + w_middle.shape[0]) * count * hid,
             bytes_accessed=weight_bytes + 2 * count * (width + w_last.shape[1]),
         ),
-    )(rows, w_first, w_middle, w_last)
+    )(rows, w_first, w_middle, w_last.T)
 
 
 def on_device(fields, diffusivity, cloudy_index, owners, w_in, w_mid, w_out):
@@ -169,8 +169,8 @@
     )
     outcome = network(inputs, w_in[0], w_mid[0], w_out[0])
     outgoing = (
-        outcome.reshape(lon_count, capacity, 2, lev_count, level_rows)
-        .transpose(2, 4, 0, 3, 1)
+        outcome.reshape(2, lev_count, level_rows, lon_count, capacity)
+        .transpose(0, 2, 3, 1, 4)
         .reshape(local_features, group, capacity)
     )
     returned = lax.all_to_all(

time: 59.1 us -> 58.4 us (0.988)
  blocking collectives: 0 us -> 14.4 us
  waiting for transfers between devices: 18.4 us -> 10.9 us
  starting transfers between devices: 17.5 us -> 10.7 us
  local copies, waits for them, and re-layouts: 6.63 us -> 5.76 us
    all_to_all x0 -> x1, blocking collectives: none -> 14.4 us  [on_device(): lax.all_to_all(send_buffer, ('lon', 'lev'), split_axis=1, concat_axis=1,...]
    all_to_all x1 -> x0, waiting for transfers between devices: 7.49 us -> none  [on_device(): lax.all_to_all(send_buffer, ('lon', 'lev'), split_axis=1, concat_axis=1,...]
    all_to_all x1 -> x0, starting transfers between devices: 6.79 us -> none  [on_device(): lax.all_to_all(send_buffer, ('lon', 'lev'), split_axis=1, concat_axis=1,...]
    broadcast_in_dim x3, local copies, waits for them, and re-layouts: 0.71 us -> 0.05 us  [on_device(): jnp.broadcast_to(picked.reshape(local_features, 1, lev_count, per_device)...]
    unnamed x17 -> x16, local copies, waits for them, and re-layouts: 3.34 us -> 3.17 us
  transfers between devices with their start and end apart: 5 -> 4, of which waited for: 3 -> 2; matrix products, arithmetic and copies ran while one was open for 3% -> 3% of each run, Pallas kernels for 0% -> 0%
where the time goes in v17:
time: 58.4 us; the launch traced here: 58 us
  blocking collectives  14.4 us (25%)
  waiting for transfers between devices  10.9 us (19%)
  starting transfers between devices  10.7 us (18%)
  other arithmetic  10.3 us (18%)
  local copies, waits for them, and re-layouts  5.76 us (10%)
  Pallas kernels  3.35 us (6%)
  matrix products  2.2 us (4%)
    all_to_all x1, blocking collectives, on_device(): lax.all_to_all(send_buffer, ('lon', 'lev'), split_axis=1, concat_axis=1,...  14.4 us
    all_to_all x1, waiting for transfers between devices, on_device(): lax.all_to_all(outgoing, ('lon', 'lev'), split_axis=1, concat_axis=1, til...  7.42 us
    ppermute x1, waiting for transfers between devices, halo_exchange(): lax.ppermute(jnp.concatenate([right, left], axis=-1), 'lon', [(0, 1), (1,...  3.52 us
    all_to_all x1, starting transfers between devices, on_device(): lax.all_to_all(outgoing, ('lon', 'lev'), split_axis=1, concat_axis=1, til...  3.37 us
    pallas_call x1, Pallas kernels, network(): pl.pallas_call(network_kernel, out_shape=jax.ShapeDtypeStruct((w_last.sha...  3.35 us
    unnamed x16, local copies, waits for them, and re-layouts  3.17 us
    ppermute x1, starting transfers between devices, halo_exchange(): lax.ppermute(cells[..., cells.shape[-2] - width:, :], 'lat', [(i, i + 1)...  3.04 us
    ppermute x1, starting transfers between devices, halo_exchange(): lax.ppermute(jnp.concatenate([right, left], axis=-1), 'lon', [(0, 1), (1,...  3.03 us
  transfers between devices with their start and end apart: 4, of which 2 were waited for; matrix products, arithmetic and copies ran while one was open for 3% of the time, Pallas kernels for 0%

profile of v17, /device:TPU:0, one launch (start us, length us, event | category | flops | bytes accessed | tf_op | source)
XLA Modules:
  0.0 58.0 jit_solution(4549349668802063232)
XLA Ops:
  0.0 1.1 %pad_maximum_fusion.16 = (f32[45,3,128]{2,1,0:T(4,128)S(1)}, f32[45,3,128]{2,1,0:T(4,128)S(1)}) fusion(f32[15,32,128]{2,1,0:T(8,128)} %param.8, f32[30,32,128]{2,1,0:T(8,128)} %bitcast.38), kind=kLoop, calls=%fused_computation.94 | loop fusion | flops 34560 | bytes 875520 | tf_op jit(solution)/shard_map/slice | solution.py:15
  1.1 1.3 %collective-permute-start.1 = (f32[45,3,128]{2,1,0:T(4,128)S(1)}, f32[45,3,128]{2,1,0:T(4,128)S(1)}, u32[]{:S(2)}, u32[]{:S(2)}) collective-permute-start(f32[45,3,128]{2,1,0:T(4,128)S(1)} %get-tuple-element.24), channel_id=1, source_target_pairs={{8,0},{16,8},{24,16},{9,1},{17,9},{25,17},{10,2},{18,10},{26,18},{... | collective-permute-start | bytes 207368 | tf_op jit(solution)/shard_map/ppermute | solution.py:17
  2.4 3.0 %collective-permute-start = (f32[45,3,128]{2,1,0:T(4,128)S(1)}, f32[45,3,128]{2,1,0:T(4,128)S(1)}, u32[]{:S(2)}, u32[]{:S(2)}) collective-permute-start(f32[45,3,128]{2,1,0:T(4,128)S(1)} %get-tuple-element.23), channel_id=1, source_target_pairs={{0,8},{8,16},{16,24},{1,9},{9,17},{17,25},{2,10},{10,18},{18,26},{... | collective-permute-start | bytes 207368 | tf_op jit(solution)/shard_map/ppermute | solution.py:14
  5.5 0.7 %and_select_fusion = (s32[1,1024]{1,0:T(1,128)S(1)}, s32[1,1024]{1,0:T(1,128)S(1)}) fusion(s32[1,1024]{1,0:T(1,128)} %param.9), kind=kLoop, calls=%fused_computation.96 | loop fusion | flops 11264 | bytes 12288 | tf_op jit(solution)/shard_map/jit(remainder)/select_n | solution.py:132
  6.2 0.7 %and_select_fusion.1 = s32[1,1024]{1,0:T(1,128)S(1)} fusion(s32[1,1024]{1,0:T(1,128)S(1)} %get-tuple-element.6, s32[1,1024]{1,0:T(1,128)} %param.9), kind=kLoop, calls=%fused_computation.98 | loop fusion | flops 12288 | bytes 12288 | tf_op jit(solution)/shard_map/jit(floor_divide)/jit(_where)/select_n | solution.py:131
  7.0 1.1 %pad_maximum_fusion.1 = f32[45,38,128]{2,1,0:T(8,128)S(1)} fusion(f32[45,3,128]{2,1,0:T(4,128)S(1)} %collective-permute-done.1, f32[15,32,128]{2,1,0:T(8,128)} %param.8, f32[30,32,128]{2,1,0:T(8,128)S(1)} %bitcast.39, f32[45,3,128]{2,1,0:T(4,128)S(1)} %collective-permute-done), kind=kLoop, calls=%fused_computation.34 | loop fusion | flops 656640 | bytes 1751040 | tf_op jit(solution)/shard_map/concatenate | solution.py:20
  8.0 0.3 fusion.56
  8.3 0.4 copy.44
  8.8 0.4 copy.43
  9.3 3.0 %collective-permute-start.2 = (f32[45,38,6]{0,1,2:T(8,128)S(1)}, f32[45,38,6]{0,1,2:T(8,128)S(1)}, u32[]{:S(2)}, u32[]{:S(2)}) collective-permute-start(f32[45,38,6]{0,1,2:T(8,128)S(1)} %pad_maximum_fusion.14), channel_id=1, source_target_pairs={{0,4},{4,0},{1,5},{5,1},{2,6},{6,2},{3,7},{7,3},{8,12},{12,8},{9,1... | collective-permute-start | bytes 123128 | tf_op jit(solution)/shard_map/ppermute | solution.py:25
  12.3 3.5 %collective-permute-done.2 = f32[45,38,6]{0,1,2:T(8,128)S(1)} collective-permute-done((f32[45,38,6]{0,1,2:T(8,128)S(1)}, f32[45,38,6]{0,1,2:T(8,128)S(1)}, u32[]{:S(2)}, u32[]{:S(2)}) %collective-permute-start.2) | collective-permute-done | bytes 41072 | tf_op jit(solution)/shard_map/ppermute | solution.py:25
  15.8 0.5 copy.57
  16.3 0.5 copy.56
  16.8 1.0 %pad_maximum_fusion = f32[45,38,134]{2,1,0:T(8,128)S(1)} fusion(f32[45,38,3]{2,1,0:T(8,128)S(1)} %copy.57, f32[45,3,128]{2,1,0:T(4,128)S(1)} %collective-permute-done.1, f32[15,32,128]{2,1,0:T(8,128)S(1)} %copy-done.4, f32[30,32,128]{2,1,0:T(8,128)S(1)} %bitcast.40, f32[45,3,128]{2,1,0:T(4,128)S(1)} %collective-permute-done, f32[45,38,3]{2,1,0:T(8,128)S(1)} %copy.56), kind=kLoop, calls=%fused_computation.4 | loop fusion | flops 1145700 | bytes 1833120 | tf_op jit(solution)/shard_map/concatenate | solution.py:30
  17.8 0.7 %fusion.33 = (f32[15,36,132]{2,1,0:T(8,128)S(1)}, f32[15,36,132]{2,1,0:T(8,128)S(1)}, f32[15,36,132]{2,1,0:T(8,128)S(1)}, f32[15,36,132]{2,1,0:T(8,128)S(1)}) fusion(f32[45,38,134]{2,1,0:T(8,128)S(1)} %pad_maximum_fusion), kind=kLoop, calls=%fused_computation.50 | loop fusion | flops 570240 | bytes 2566080 | tf_op jit(solution)/shard_map/mul | solution.py:44
  18.6 1.4 %fusion.14 = f32[2,15,36,132]{3,2,1,0:T(8,128)S(1)} fusion(f32[2,15,38,134]{3,2,1,0:T(8,128)S(1)} %bitcast.37, f32[15,36,132]{2,1,0:T(8,128)S(1)} %get-tuple-element.14, f32[15,36,132]{2,1,0:T(8,128)S(1)} %get-tuple-element.15, f32[15,36,132]{2,1,0:T(8,128)S(1)} %get-tuple-element.16, f32[15,36,132]{2,1,0:T(8,128)S(1)} %get-tuple-element.13, ...), kind=kLoop, calls=%fused_computation.21 | loop fusion | flops 1853280 | bytes 4561956 | tf_op jit(solution)/shard_map/jit(_where)/select_n | solution.py:54
  20.0 0.9 %fusion.29 = (f32[15,34,130]{2,1,0:T(8,128)S(1)}, f32[15,34,130]{2,1,0:T(8,128)S(1)}, f32[15,34,130]{2,1,0:T(8,128)S(1)}, f32[15,34,130]{2,1,0:T(8,128)S(1)}) fusion(f32[45,38,134]{2,1,0:T(8,128)S(1)} %pad_maximum_fusion, f32[45,38,3]{2,1,0:T(8,128)S(1)} %copy.57, f32[45,3,128]{2,1,0:T(4,128)S(1)} %collective-permute-done.1, ...), kind=kLoop, calls=%fused_computation.42 | loop fusion | flops 1060800 | bytes 2772960 | tf_op jit(solution)/shard_map/mul | solution.py:44
  20.9 1.4 %fusion.5 = f32[2,15,34,130]{3,2,1,0:T(8,128)S(1)} fusion(f32[2,15,36,132]{3,2,1,0:T(8,128)S(1)} %fusion.14, f32[15,34,130]{2,1,0:T(8,128)S(1)} %get-tuple-element.11, f32[15,34,130]{2,1,0:T(8,128)S(1)} %get-tuple-element.12, f32[15,34,130]{2,1,0:T(8,128)S(1)} %get-tuple-element.10, f32[15,34,130]{2,1,0:T(8,128)S(1)} %get-tuple-element.9, ...), kind=kLoop, calls=%fused_computation.8 | loop fusion | flops 1723800 | bytes 4243234 | tf_op jit(solution)/shard_map/jit(_where)/select_n | solution.py:54
  22.3 0.4 fusion.50
  22.7 0.6 %fusion.38 = f32[2,15,32,128]{3,2,1,0:T(8,128)S(1)} fusion(f32[2,15,34,130]{3,2,1,0:T(8,128)S(1)} %fusion.5, f32[15,32,128]{2,1,0:T(8,128)S(1)} %get-tuple-element.18, f32[15,32,128]{2,1,0:T(8,128)S(1)} %get-tuple-element.17, f32[15,32,128]{2,1,0:T(8,128)S(1)} %get-tuple-element.22, f32[15,32,128]{2,1,0:T(8,128)S(1)} %get-tuple-element.21), kind=kLoop, calls=%fused_computation.55 | loop fusion | flops 1474560 | bytes 3932160 | tf_op jit(solution)/shard_map/add | solution.py:45
  23.3 0.7 %select_reduce_fusion = bf16[30,1024]{1,0:T(8,128)(2,1)S(1)} fusion(pred[32,1024]{1,0:T(8,128)(4,1)S(1)} %iota_compare_fusion.1, bf16[30,32,128]{2,1,0:T(8,128)(2,1)S(1)} %bitcast_convert_fusion, s32[1024]{0:T(1024)S(1)} %bitcast.51), kind=kOutput, calls=%fused_computation.2 | convolution fusion | flops 253724672 | bytes 344064 | tf_op jit(solution)/shard_map/dot_general | solution.py:137
  24.1 14.4 %all_to_all.10 = bf16[30,8,256]{2,0,1:T(8,128)(2,1)S(1)} all-to-all(bf16[30,8,256]{2,0,1:T(8,128)(2,1)S(1)} %bitcast.44), channel_id=1, replica_groups=mesh['lat'=4,'lon'=2,'lev'=4] {'lon','lev'}, dimensions={1} | all-to-all | bytes 245760 | tf_op jit(solution)/shard_map/all_to_all | solution.py:162
  38.5 0.1 copy.62
  38.6 0.1 copy.49
  38.8 0.1 copy.50.rows_ref
  38.9 2.2 %copy-done = bf16[1,2,1024,1024]{3,2,1,0:T(8,128)(2,1)S(1)} copy-done((bf16[1,2,1024,1024]{3,2,1,0:T(8,128)(2,1)S(1)}, bf16[1,2,1024,1024]{3,2,1,0:T(8,128)(2,1)}, u32[]{:S(2)}) %copy-start) | copy-done | bytes 4194328
  41.1 3.3 %shard_map.73 = bf16[120,512]{1,0:T(8,128)(2,1)S(1)} custom-call(bf16[512,120]{1,0:T(8,128)(2,1)S(1)} %copy.50.rows_ref, bf16[120,1024]{1,0:T(8,128)(2,1)S(1)} %bitcast.35, bf16[2,1024,1024]{2,1,0:T(8,128)(2,1)S(1)} %bitcast.34, bf16[120,1024]{1,0:T(8,128)(2,1)S(1)} %bitcast.36), custom_call_target="tpu_custom_call" | custom-call | flops 2399141888 | bytes 4931584 | tf_op jit(solution)/shard_map/pallas_call | solution.py:103
  44.6 0.7 %copy.52 = bf16[30,8,256]{2,0,1:T(8,128)(2,1)} copy(bf16[30,8,256]{2,1,0:T(8,128)(2,1)S(1)} %reshape.99) | data formatting | bytes 245760 | tf_op jit(solution)/shard_map/reshape | solution.py:174
  45.3 3.4 %all-to-all-start.1 = ((bf16[30,8,256]{2,0,1:T(8,128)(2,1)}), bf16[30,8,256]{2,0,1:T(8,128)(2,1)S(1)}, u32[]{:S(2)}, u32[]{:S(2)}) async-start(bf16[30,8,256]{2,0,1:T(8,128)(2,1)} %copy.52), calls=%async_computation.1 | async-start | bytes 262144 | tf_op jit(solution)/shard_map/all_to_all | solution.py:176
  48.7 7.4 %all-to-all-done.1 = bf16[30,8,256]{2,0,1:T(8,128)(2,1)S(1)} async-done(((bf16[30,8,256]{2,0,1:T(8,128)(2,1)}), bf16[30,8,256]{2,0,1:T(8,128)(2,1)S(1)}, u32[]{:S(2)}, u32[]{:S(2)}) %all-to-all-start.1) | async-done | bytes 122912 | tf_op jit(solution)/shard_map/all_to_all | solution.py:176
  56.3 0.2 broadcast_select_fusion
  56.5 1.5 %fusion.21 = f32[30,32,128]{2,1,0:T(8,128)} fusion(f32[30,32,128]{2,1,0:T(8,128)S(1)} %bitcast.43, pred[32,1024]{1,0:T(8,128)(4,1)S(1)} %iota_compare_fusion.1, bf16[30,1024]{1,0:T(8,128)(2,1)S(1)} %bitcast.49, s32[1024]{0:T(1024)S(1)} %bitcast.52), kind=kOutput, calls=%fused_computation.31 | convolution fusion | flops 252895232 | bytes 1081344 | tf_op jit(solution)/shard_map/dot_general | solution.py:187
  (32 shorter events, 0.6 us)
Async XLA Ops:
  0.0 7.0 %copy-start.3 = (f32[2,15,32,128]{3,2,1,0:T(8,128)S(1)}, f32[2,15,32,128]{3,2,1,0:T(8,128)}, u32[]{:S(2)}) copy-start(f32[2,15,32,128]{3,2,1,0:T(8,128)} %param.7) | copy-start | bytes 1474564
  1.1 5.8 %collective-permute-start.1 = (f32[45,3,128]{2,1,0:T(4,128)S(1)}, f32[45,3,128]{2,1,0:T(4,128)S(1)}, u32[]{:S(2)}, u32[]{:S(2)}) collective-permute-start(f32[45,3,128]{2,1,0:T(4,128)S(1)} %get-tuple-element.24), channel_id=1, source_target_pairs={{8,0},{16,8},{24,16},{9,1},{17,9},{25,17},{10,2},{18,10},{26,18},{... | collective-permute-start | bytes 207368 | tf_op jit(solution)/shard_map/ppermute | solution.py:17
  2.4 4.5 %collective-permute-start = (f32[45,3,128]{2,1,0:T(4,128)S(1)}, f32[45,3,128]{2,1,0:T(4,128)S(1)}, u32[]{:S(2)}, u32[]{:S(2)}) collective-permute-start(f32[45,3,128]{2,1,0:T(4,128)S(1)} %get-tuple-element.23), channel_id=1, source_target_pairs={{0,8},{8,16},{16,24},{1,9},{9,17},{17,25},{2,10},{10,18},{18,26},{... | collective-permute-start | bytes 207368 | tf_op jit(solution)/shard_map/ppermute | solution.py:14
  9.2 7.5 %copy-start.4 = (f32[15,32,128]{2,1,0:T(8,128)S(1)}, f32[15,32,128]{2,1,0:T(8,128)}, u32[]{:S(2)}) copy-start(f32[15,32,128]{2,1,0:T(8,128)} %param.8) | copy-start | bytes 737284
  9.3 6.6 %collective-permute-start.2 = (f32[45,38,6]{0,1,2:T(8,128)S(1)}, f32[45,38,6]{0,1,2:T(8,128)S(1)}, u32[]{:S(2)}, u32[]{:S(2)}) collective-permute-start(f32[45,38,6]{0,1,2:T(8,128)S(1)} %pad_maximum_fusion.14), channel_id=1, source_target_pairs={{0,4},{4,0},{1,5},{5,1},{2,6},{6,2},{3,7},{7,3},{8,12},{12,8},{9,1... | collective-permute-start | bytes 123128 | tf_op jit(solution)/shard_map/ppermute | solution.py:25
  24.0 14.9 %copy-start.1 = (bf16[1,120,1024]{2,1,0:T(8,128)(2,1)S(1)}, bf16[1,120,1024]{2,1,0:T(8,128)(2,1)}, u32[]{:S(2)}) copy-start(bf16[1,120,1024]{2,1,0:T(8,128)(2,1)} %param.11) | copy-start | bytes 737284
  24.0 14.9 %copy-start.2 = (bf16[1,1024,120]{1,2,0:T(8,128)(2,1)S(1)}, bf16[1,1024,120]{1,2,0:T(8,128)(2,1)}, u32[]{:S(2)}) copy-start(bf16[1,1024,120]{1,2,0:T(8,128)(2,1)} %param.13) | copy-start | bytes 737284
  38.9 2.2 %copy-start = (bf16[1,2,1024,1024]{3,2,1,0:T(8,128)(2,1)S(1)}, bf16[1,2,1024,1024]{3,2,1,0:T(8,128)(2,1)}, u32[]{:S(2)}) copy-start(bf16[1,2,1024,1024]{3,2,1,0:T(8,128)(2,1)} %param.12) | copy-start | bytes 12582916
  44.5 4.2 %copy-start.5 = (s32[1,1024,1]{1,2,0:T(1,128)S(1)}, s32[1,1024,1]{1,2,0:T(1,128)}, u32[]{:S(2)}) copy-start(s32[1,1024,1]{1,2,0:T(1,128)} %param.10) | copy-start | bytes 12292
  45.3 10.8 %all-to-all-start.1 = ((bf16[30,8,256]{2,0,1:T(8,128)(2,1)}), bf16[30,8,256]{2,0,1:T(8,128)(2,1)S(1)}, u32[]{:S(2)}, u32[]{:S(2)}) async-start(bf16[30,8,256]{2,0,1:T(8,128)(2,1)} %copy.52), calls=%async_computation.1 | async-start | bytes 262144 | tf_op jit(solution)/shard_map/all_to_all | solution.py:176

commit v18 on v17

--- a/solution.py
+++ b/solution.py
@@ -167,22 +167,34 @@
         .transpose(2, 4, 0, 3, 1)
         .reshape(lon_count * capacity, feature_count)
     )
-    outcome = network(inputs, w_in[0], w_mid[0], w_out[0])
+    padded_features = 8 * ((local_features + 7) // 8)
+    last_layer = jnp.pad(
+        w_out[0]
+        .reshape(w_out.shape[1], 2, lev_count, level_rows)
+        .transpose(0, 2, 1, 3)
+        .reshape(w_out.shape[1], lev_count, local_features),
+        ((0, 0), (0, 0), (0, padded_features - local_features)),
+    ).reshape(w_out.shape[1], lev_count * padded_features)
+    outcome = network(inputs, w_in[0], w_mid[0], last_layer)
     outgoing = (
-        outcome.reshape(2, lev_count, level_rows, lon_count, capacity)
-        .transpose(0, 2, 3, 1, 4)
-        .reshape(local_features, group, capacity)
+        outcome.reshape(lev_count, padded_features, lon_count, capacity)
+        .transpose(2, 0, 1, 3)
+        .reshape(group, padded_features, capacity)
     )
     returned = lax.all_to_all(
-        outgoing, ("lon", "lev"), split_axis=1, concat_axis=1, tiled=True
-    )
+        outgoing, ("lon", "lev"), split_axis=0, concat_axis=0, tiled=True
+    )[:, :local_features]
     if whole_slices:
-        returned = returned.reshape(local_features, lon_count, cloudy)
-        tendency = returned[:, 0]
+        returned = (
+            returned.reshape(lon_count, lev_count, local_features, capacity)
+            .transpose(0, 2, 1, 3)
+            .reshape(lon_count, local_features, cloudy)
+        )
+        tendency = returned[0]
         for regime in range(1, lon_count):
-            tendency = jnp.where(routes[None, :] == regime, returned[:, regime], tendency)
+            tendency = jnp.where(routes[None, :] == regime, returned[regime], tendency)
     else:
-        tendency = returned.reshape(local_features, group * capacity)[:, slot_index]
+        tendency = returned.transpose(1, 0, 2).reshape(local_features, group * capacity)[:, slot_index]
     spread_rows = jnp.where(row_match[None], tendency[:, None, :], jnp.zeros_like(tendency)[:, None, :])
     spread = lax.dot_general(
         spread_rows.reshape(local_features * lat_rows, cloudy),

time: 58.4 us -> 59 us (1.010)
  blocking collectives: 14.4 us -> 0 us
  waiting for transfers between devices: 10.9 us -> 18.2 us
  starting transfers between devices: 10.7 us -> 17.5 us
  local copies, waits for them, and re-layouts: 5.76 us -> 6.78 us
    all_to_all x1 -> x0, blocking collectives: 14.4 us -> none  [on_device(): lax.all_to_all(send_buffer, ('lon', 'lev'), split_axis=1, concat_axis=1,...]
    all_to_all x1 -> x2, waiting for transfers between devices: 7.42 us -> 14.7 us  [the longest x1 7.42 us: on_device(): lax.all_to_all(outgoing, ('lon', 'lev'), split_axis=0, concat_axis=0, til...]
    all_to_all x1 -> x2, starting transfers between devices: 3.37 us -> 10.2 us  [the longest x1 6.79 us: on_device(): lax.all_to_all(send_buffer, ('lon', 'lev'), split_axis=1, concat_axis=1,...]
    broadcast_in_dim x3, local copies, waits for them, and re-layouts: 0.05 us -> 0.71 us  [on_device(): jnp.broadcast_to(picked.reshape(local_features, 1, lev_count, per_device)...]
    unnamed x16 -> x21, local copies, waits for them, and re-layouts: 3.17 us -> 3.34 us
  transfers between devices with their start and end apart: 4 -> 5, of which waited for: 2 -> 3; matrix products, arithmetic and copies ran while one was open for 3% -> 3% of each run, Pallas kernels for 0% -> 0%
where the time goes in v18:
time: 59 us; the launch traced here: 58.5 us
  waiting for transfers between devices  18.2 us (31%)
  starting transfers between devices  17.5 us (30%)
  other arithmetic  10.1 us (17%)
  local copies, waits for them, and re-layouts  6.78 us (11%)
  Pallas kernels  3.35 us (6%)
  matrix products  2.19 us (4%)
    all_to_all x1, waiting for transfers between devices, on_device(): lax.all_to_all(outgoing, ('lon', 'lev'), split_axis=0, concat_axis=0, til...  7.42 us
    all_to_all x1, waiting for transfers between devices, on_device(): lax.all_to_all(send_buffer, ('lon', 'lev'), split_axis=1, concat_axis=1,...  7.24 us
    all_to_all x1, starting transfers between devices, on_device(): lax.all_to_all(send_buffer, ('lon', 'lev'), split_axis=1, concat_axis=1,...  6.79 us
    ppermute x1, waiting for transfers between devices, halo_exchange(): lax.ppermute(jnp.concatenate([right, left], axis=-1), 'lon', [(0, 1), (1,...  3.52 us
    all_to_all x1, starting transfers between devices, on_device(): lax.all_to_all(outgoing, ('lon', 'lev'), split_axis=0, concat_axis=0, til...  3.37 us
    pallas_call x1, Pallas kernels, network(): pl.pallas_call(network_kernel, out_shape=jax.ShapeDtypeStruct((w_last.sha...  3.35 us
    unnamed x21, local copies, waits for them, and re-layouts  3.34 us
    ppermute x1, starting transfers between devices, halo_exchange(): lax.ppermute(cells[..., cells.shape[-2] - width:, :], 'lat', [(i, i + 1)...  3.04 us
  transfers between devices with their start and end apart: 5, of which 3 were waited for; matrix products, arithmetic and copies ran while one was open for 3% of the time, Pallas kernels for 0%

profile of v18, /device:TPU:0, one launch (start us, length us, event | category | flops | bytes accessed | tf_op | source)
XLA Modules:
  0.0 58.5 jit_solution(5490249438947849932)
XLA Ops:
  0.0 1.1 %pad_maximum_fusion.16 = (f32[45,3,128]{2,1,0:T(4,128)S(1)}, f32[45,3,128]{2,1,0:T(4,128)S(1)}) fusion(f32[15,32,128]{2,1,0:T(8,128)} %param.8, f32[30,32,128]{2,1,0:T(8,128)} %bitcast.56), kind=kLoop, calls=%fused_computation.93 | loop fusion | flops 34560 | bytes 875520 | tf_op jit(solution)/shard_map/slice | solution.py:15
  1.1 1.3 %collective-permute-start.1 = (f32[45,3,128]{2,1,0:T(4,128)S(1)}, f32[45,3,128]{2,1,0:T(4,128)S(1)}, u32[]{:S(2)}, u32[]{:S(2)}) collective-permute-start(f32[45,3,128]{2,1,0:T(4,128)S(1)} %get-tuple-element.24), channel_id=1, source_target_pairs={{8,0},{16,8},{24,16},{9,1},{17,9},{25,17},{10,2},{18,10},{26,18},{... | collective-permute-start | bytes 207368 | tf_op jit(solution)/shard_map/ppermute | solution.py:17
  2.4 3.0 %collective-permute-start = (f32[45,3,128]{2,1,0:T(4,128)S(1)}, f32[45,3,128]{2,1,0:T(4,128)S(1)}, u32[]{:S(2)}, u32[]{:S(2)}) collective-permute-start(f32[45,3,128]{2,1,0:T(4,128)S(1)} %get-tuple-element.23), channel_id=1, source_target_pairs={{0,8},{8,16},{16,24},{1,9},{9,17},{17,25},{2,10},{10,18},{18,26},{... | collective-permute-start | bytes 207368 | tf_op jit(solution)/shard_map/ppermute | solution.py:14
  5.5 0.7 %and_select_fusion = (s32[1,1024]{1,0:T(1,128)S(1)}, s32[1,1024]{1,0:T(1,128)S(1)}) fusion(s32[1,1024]{1,0:T(1,128)} %param.9), kind=kLoop, calls=%fused_computation.97 | loop fusion | flops 11264 | bytes 12288 | tf_op jit(solution)/shard_map/jit(remainder)/select_n | solution.py:132
  6.2 0.7 %and_select_fusion.1 = s32[1,1024]{1,0:T(1,128)S(1)} fusion(s32[1,1024]{1,0:T(1,128)S(1)} %get-tuple-element.6, s32[1,1024]{1,0:T(1,128)} %param.9), kind=kLoop, calls=%fused_computation.99 | loop fusion | flops 12288 | bytes 12288 | tf_op jit(solution)/shard_map/jit(floor_divide)/jit(_where)/select_n | solution.py:131
  7.0 1.1 %pad_maximum_fusion.1 = f32[45,38,128]{2,1,0:T(8,128)S(1)} fusion(f32[45,3,128]{2,1,0:T(4,128)S(1)} %collective-permute-done.1, f32[15,32,128]{2,1,0:T(8,128)} %param.8, f32[30,32,128]{2,1,0:T(8,128)S(1)} %bitcast.57, f32[45,3,128]{2,1,0:T(4,128)S(1)} %collective-permute-done), kind=kLoop, calls=%fused_computation.34 | loop fusion | flops 656640 | bytes 1751040 | tf_op jit(solution)/shard_map/concatenate | solution.py:20
  8.0 0.3 fusion.56
  8.3 0.4 copy.46
  8.8 0.4 copy.45
  9.3 3.0 %collective-permute-start.2 = (f32[45,38,6]{0,1,2:T(8,128)S(1)}, f32[45,38,6]{0,1,2:T(8,128)S(1)}, u32[]{:S(2)}, u32[]{:S(2)}) collective-permute-start(f32[45,38,6]{0,1,2:T(8,128)S(1)} %pad_maximum_fusion.14), channel_id=1, source_target_pairs={{0,4},{4,0},{1,5},{5,1},{2,6},{6,2},{3,7},{7,3},{8,12},{12,8},{9,1... | collective-permute-start | bytes 123128 | tf_op jit(solution)/shard_map/ppermute | solution.py:25
  12.3 3.5 %collective-permute-done.2 = f32[45,38,6]{0,1,2:T(8,128)S(1)} collective-permute-done((f32[45,38,6]{0,1,2:T(8,128)S(1)}, f32[45,38,6]{0,1,2:T(8,128)S(1)}, u32[]{:S(2)}, u32[]{:S(2)}) %collective-permute-start.2) | collective-permute-done | bytes 41072 | tf_op jit(solution)/shard_map/ppermute | solution.py:25
  15.8 0.5 copy.60
  16.3 0.5 copy.59
  16.8 1.0 %pad_maximum_fusion = f32[45,38,134]{2,1,0:T(8,128)S(1)} fusion(f32[45,38,3]{2,1,0:T(8,128)S(1)} %copy.60, f32[45,3,128]{2,1,0:T(4,128)S(1)} %collective-permute-done.1, f32[15,32,128]{2,1,0:T(8,128)S(1)} %copy-done.3, f32[30,32,128]{2,1,0:T(8,128)S(1)} %bitcast.58, f32[45,3,128]{2,1,0:T(4,128)S(1)} %collective-permute-done, f32[45,38,3]{2,1,0:T(8,128)S(1)} %copy.59), kind=kLoop, calls=%fused_computation.4 | loop fusion | flops 1145700 | bytes 1833120 | tf_op jit(solution)/shard_map/concatenate | solution.py:30
  17.8 0.7 %fusion.33 = (f32[15,36,132]{2,1,0:T(8,128)S(1)}, f32[15,36,132]{2,1,0:T(8,128)S(1)}, f32[15,36,132]{2,1,0:T(8,128)S(1)}, f32[15,36,132]{2,1,0:T(8,128)S(1)}) fusion(f32[45,38,134]{2,1,0:T(8,128)S(1)} %pad_maximum_fusion), kind=kLoop, calls=%fused_computation.50 | loop fusion | flops 570240 | bytes 2566080 | tf_op jit(solution)/shard_map/mul | solution.py:44
  18.6 1.4 %fusion.14 = f32[2,15,36,132]{3,2,1,0:T(8,128)S(1)} fusion(f32[2,15,38,134]{3,2,1,0:T(8,128)S(1)} %bitcast.55, f32[15,36,132]{2,1,0:T(8,128)S(1)} %get-tuple-element.14, f32[15,36,132]{2,1,0:T(8,128)S(1)} %get-tuple-element.15, f32[15,36,132]{2,1,0:T(8,128)S(1)} %get-tuple-element.16, f32[15,36,132]{2,1,0:T(8,128)S(1)} %get-tuple-element.13, ...), kind=kLoop, calls=%fused_computation.21 | loop fusion | flops 1853280 | bytes 4561956 | tf_op jit(solution)/shard_map/jit(_where)/select_n | solution.py:54
  20.0 0.9 %fusion.29 = (f32[15,34,130]{2,1,0:T(8,128)S(1)}, f32[15,34,130]{2,1,0:T(8,128)S(1)}, f32[15,34,130]{2,1,0:T(8,128)S(1)}, f32[15,34,130]{2,1,0:T(8,128)S(1)}) fusion(f32[45,38,134]{2,1,0:T(8,128)S(1)} %pad_maximum_fusion, f32[45,38,3]{2,1,0:T(8,128)S(1)} %copy.60, f32[45,3,128]{2,1,0:T(4,128)S(1)} %collective-permute-done.1, ...), kind=kLoop, calls=%fused_computation.42 | loop fusion | flops 1060800 | bytes 2772960 | tf_op jit(solution)/shard_map/mul | solution.py:44
  20.9 1.4 %fusion.5 = f32[2,15,34,130]{3,2,1,0:T(8,128)S(1)} fusion(f32[2,15,36,132]{3,2,1,0:T(8,128)S(1)} %fusion.14, f32[15,34,130]{2,1,0:T(8,128)S(1)} %get-tuple-element.11, f32[15,34,130]{2,1,0:T(8,128)S(1)} %get-tuple-element.12, f32[15,34,130]{2,1,0:T(8,128)S(1)} %get-tuple-element.10, f32[15,34,130]{2,1,0:T(8,128)S(1)} %get-tuple-element.9, ...), kind=kLoop, calls=%fused_computation.8 | loop fusion | flops 1723800 | bytes 4243234 | tf_op jit(solution)/shard_map/jit(_where)/select_n | solution.py:54
  22.3 0.4 fusion.50
  22.7 0.6 %fusion.38 = f32[2,15,32,128]{3,2,1,0:T(8,128)S(1)} fusion(f32[2,15,34,130]{3,2,1,0:T(8,128)S(1)} %fusion.5, f32[15,32,128]{2,1,0:T(8,128)S(1)} %get-tuple-element.18, f32[15,32,128]{2,1,0:T(8,128)S(1)} %get-tuple-element.17, f32[15,32,128]{2,1,0:T(8,128)S(1)} %get-tuple-element.22, f32[15,32,128]{2,1,0:T(8,128)S(1)} %get-tuple-element.21), kind=kLoop, calls=%fused_computation.55 | loop fusion | flops 1474560 | bytes 3932160 | tf_op jit(solution)/shard_map/add | solution.py:45
  23.3 0.7 %select_reduce_fusion = bf16[30,1024]{1,0:T(8,128)(2,1)S(1)} fusion(pred[32,1024]{1,0:T(8,128)(4,1)S(1)} %iota_compare_fusion.1, bf16[30,32,128]{2,1,0:T(8,128)(2,1)S(1)} %bitcast_convert_fusion, s32[1024]{0:T(1024)S(1)} %bitcast.74), kind=kOutput, calls=%fused_computation.2 | convolution fusion | flops 253724672 | bytes 344064 | tf_op jit(solution)/shard_map/dot_general | solution.py:137
  24.1 0.7 %broadcast_in_dim.99 = bf16[30,2,4,256]{3,0,2,1:T(8,128)(2,1)} broadcast(bf16[30,4,256]{2,0,1:T(8,128)(2,1)S(1)} %copy.49), dimensions={0,2,3} | broadcast | bytes 184320 | tf_op jit(solution)/shard_map/broadcast_in_dim | solution.py:147
  24.8 6.8 %all-to-all-start = ((bf16[30,8,256]{2,0,1:T(8,128)(2,1)}), bf16[30,8,256]{2,0,1:T(8,128)(2,1)S(1)}, u32[]{:S(2)}, u32[]{:S(2)}) async-start(bf16[30,8,256]{2,0,1:T(8,128)(2,1)} %bitcast.6), calls=%async_computation | async-start | bytes 262144 | tf_op jit(solution)/shard_map/all_to_all | solution.py:162
  31.6 0.2 copy.52
  32.0 7.2 %all-to-all-done = bf16[30,8,256]{2,0,1:T(8,128)(2,1)S(1)} async-done(((bf16[30,8,256]{2,0,1:T(8,128)(2,1)}), bf16[30,8,256]{2,0,1:T(8,128)(2,1)S(1)}, u32[]{:S(2)}, u32[]{:S(2)}) %all-to-all-start) | async-done | bytes 122912 | tf_op jit(solution)/shard_map/all_to_all | solution.py:162
  39.5 0.1 copy.54.rows_ref
  39.6 2.2 %copy-done = bf16[1,2,1024,1024]{3,2,1,0:T(8,128)(2,1)S(1)} copy-done((bf16[1,2,1024,1024]{3,2,1,0:T(8,128)(2,1)S(1)}, bf16[1,2,1024,1024]{3,2,1,0:T(8,128)(2,1)}, u32[]{:S(2)}) %copy-start) | copy-done | bytes 4194328
  41.8 3.3 %shard_map.73 = bf16[128,512]{1,0:T(8,128)(2,1)S(1)} custom-call(bf16[512,120]{1,0:T(8,128)(2,1)S(1)} %copy.54.rows_ref, bf16[120,1024]{1,0:T(8,128)(2,1)S(1)} %bitcast.54, bf16[2,1024,1024]{2,1,0:T(8,128)(2,1)S(1)} %bitcast.53, bf16[128,1024]{1,0:T(8,128)(2,1)S(1)} %bitcast.52), custom_call_target="tpu_custom_call" | custom-call | flops 2407530496 | bytes 4956160 | tf_op jit(solution)/shard_map/pallas_call | solution.py:103
  45.2 0.7 %copy.55 = bf16[4,32,2,256]{3,1,0,2:T(8,128)(2,1)} copy(bf16[4,32,2,256]{3,2,1,0:T(2,128)(2,1)S(1)} %reshape.125) | data formatting | bytes 262144 | tf_op jit(solution)/shard_map/reshape | solution.py:180
  45.9 3.4 %all-to-all-start.1 = ((bf16[8,32,256]{2,1,0:T(8,128)(2,1)}), bf16[8,32,256]{2,1,0:T(8,128)(2,1)S(1)}, u32[]{:S(2)}, u32[]{:S(2)}) async-start(bf16[8,32,256]{2,1,0:T(8,128)(2,1)} %bitcast.15), calls=%async_computation.1 | async-start | bytes 262144 | tf_op jit(solution)/shard_map/all_to_all | solution.py:184
  49.3 7.4 %all-to-all-done.1 = bf16[8,32,256]{2,1,0:T(8,128)(2,1)S(1)} async-done(((bf16[8,32,256]{2,1,0:T(8,128)(2,1)}), bf16[8,32,256]{2,1,0:T(8,128)(2,1)S(1)}, u32[]{:S(2)}, u32[]{:S(2)}) %all-to-all-start.1) | async-done | bytes 131104 | tf_op jit(solution)/shard_map/all_to_all | solution.py:184
  57.0 1.5 %fusion.21 = f32[30,32,128]{2,1,0:T(8,128)} fusion(f32[30,32,128]{2,1,0:T(8,128)S(1)} %bitcast.61, pred[32,1024]{1,0:T(8,128)(4,1)S(1)} %iota_compare_fusion.1, bf16[30,1024]{1,0:T(8,128)(2,1)S(1)} %broadcast_select_fusion, s32[1024]{0:T(1024)S(1)} %bitcast.75), kind=kOutput, calls=%fused_computation.31 | convolution fusion | flops 252895232 | bytes 1081344 | tf_op jit(solution)/shard_map/dot_general | solution.py:199
  (38 shorter events, 1.0 us)
Async XLA Ops:
  0.0 7.0 %copy-start.2 = (f32[2,15,32,128]{3,2,1,0:T(8,128)S(1)}, f32[2,15,32,128]{3,2,1,0:T(8,128)}, u32[]{:S(2)}) copy-start(f32[2,15,32,128]{3,2,1,0:T(8,128)} %param.7) | copy-start | bytes 1474564
  1.1 5.8 %collective-permute-start.1 = (f32[45,3,128]{2,1,0:T(4,128)S(1)}, f32[45,3,128]{2,1,0:T(4,128)S(1)}, u32[]{:S(2)}, u32[]{:S(2)}) collective-permute-start(f32[45,3,128]{2,1,0:T(4,128)S(1)} %get-tuple-element.24), channel_id=1, source_target_pairs={{8,0},{16,8},{24,16},{9,1},{17,9},{25,17},{10,2},{18,10},{26,18},{... | collective-permute-start | bytes 207368 | tf_op jit(solution)/shard_map/ppermute | solution.py:17
  2.4 4.5 %collective-permute-start = (f32[45,3,128]{2,1,0:T(4,128)S(1)}, f32[45,3,128]{2,1,0:T(4,128)S(1)}, u32[]{:S(2)}, u32[]{:S(2)}) collective-permute-start(f32[45,3,128]{2,1,0:T(4,128)S(1)} %get-tuple-element.23), channel_id=1, source_target_pairs={{0,8},{8,16},{16,24},{1,9},{9,17},{17,25},{2,10},{10,18},{18,26},{... | collective-permute-start | bytes 207368 | tf_op jit(solution)/shard_map/ppermute | solution.py:14
  9.2 7.5 %copy-start.3 = (f32[15,32,128]{2,1,0:T(8,128)S(1)}, f32[15,32,128]{2,1,0:T(8,128)}, u32[]{:S(2)}) copy-start(f32[15,32,128]{2,1,0:T(8,128)} %param.8) | copy-start | bytes 737284
  9.3 6.6 %collective-permute-start.2 = (f32[45,38,6]{0,1,2:T(8,128)S(1)}, f32[45,38,6]{0,1,2:T(8,128)S(1)}, u32[]{:S(2)}, u32[]{:S(2)}) collective-permute-start(f32[45,38,6]{0,1,2:T(8,128)S(1)} %pad_maximum_fusion.14), channel_id=1, source_target_pairs={{0,4},{4,0},{1,5},{5,1},{2,6},{6,2},{3,7},{7,3},{8,12},{12,8},{9,1... | collective-permute-start | bytes 123128 | tf_op jit(solution)/shard_map/ppermute | solution.py:25
  23.3 8.2 %copy-start.4 = (bf16[1,1024,120]{1,2,0:T(8,128)(2,1)S(1)}, bf16[1,1024,120]{1,2,0:T(8,128)(2,1)}, u32[]{:S(2)}) copy-start(bf16[1,1024,120]{1,2,0:T(8,128)(2,1)} %param.13) | copy-start | bytes 737284
  24.8 14.5 %all-to-all-start = ((bf16[30,8,256]{2,0,1:T(8,128)(2,1)}), bf16[30,8,256]{2,0,1:T(8,128)(2,1)S(1)}, u32[]{:S(2)}, u32[]{:S(2)}) async-start(bf16[30,8,256]{2,0,1:T(8,128)(2,1)} %bitcast.6), calls=%async_computation | async-start | bytes 262144 | tf_op jit(solution)/shard_map/all_to_all | solution.py:162
  31.9 7.8 %copy-start.1 = (bf16[1,120,1024]{2,1,0:T(8,128)(2,1)S(1)}, bf16[1,120,1024]{2,1,0:T(8,128)(2,1)}, u32[]{:S(2)}) copy-start(bf16[1,120,1024]{2,1,0:T(8,128)(2,1)} %param.11) | copy-start | bytes 737284
  39.6 2.2 %copy-start = (bf16[1,2,1024,1024]{3,2,1,0:T(8,128)(2,1)S(1)}, bf16[1,2,1024,1024]{3,2,1,0:T(8,128)(2,1)}, u32[]{:S(2)}) copy-start(bf16[1,2,1024,1024]{3,2,1,0:T(8,128)(2,1)} %param.12) | copy-start | bytes 12582916
  41.8 7.4 %copy-start.5 = (s32[1,1024,1]{1,2,0:T(1,128)S(1)}, s32[1,1024,1]{1,2,0:T(1,128)}, u32[]{:S(2)}) copy-start(s32[1,1024,1]{1,2,0:T(1,128)} %param.10) | copy-start | bytes 12292
  45.9 10.8 %all-to-all-start.1 = ((bf16[8,32,256]{2,1,0:T(8,128)(2,1)}), bf16[8,32,256]{2,1,0:T(8,128)(2,1)S(1)}, u32[]{:S(2)}, u32[]{:S(2)}) async-start(bf16[8,32,256]{2,1,0:T(8,128)(2,1)} %bitcast.15), calls=%async_computation.1 | async-start | bytes 262144 | tf_op jit(solution)/shard_map/all_to_all | solution.py:184

commit v19 on v18

--- a/solution.py
+++ b/solution.py
@@ -86,15 +86,25 @@
             hidden = jax.nn.gelu(
                 jnp.dot(hidden, middle_ref[layer_no], preferred_element_type=jnp.float32)
             ).astype(jnp.bfloat16)
-        out_ref[:, rows] = lax.dot_general(
+        result = lax.dot_general(
             last_ref[...], hidden, (((1,), (1,)), ((), ())), preferred_element_type=jnp.float32
         ).astype(jnp.bfloat16)
+        if len(out_ref.shape) == 2:
+            out_ref[:, rows] = result
+        else:
+            pieces, depth, width = out_ref.shape
+            slices = result.shape[0] // depth
+            for block in range(tile // width):
+                for part in range(slices):
+                    out_ref[block * slices + part] = result[
+                        part * depth : (part + 1) * depth, block * width : (block + 1) * width
+                    ]
         return carry
 
     lax.fori_loop(0, rows_ref.shape[0] // tile, one_tile, 0)
 
 
-def network(rows, w_first, w_middle, w_last):
+def network(rows, w_first, w_middle, w_last, blocks=None):
     count, width = rows.shape
     hid = w_first.shape[1]
     vmem = pl.BlockSpec(memory_space=pltpu.VMEM)
@@ -102,7 +112,7 @@
     weight_bytes = 2 * (w_first.size + w_middle.size + w_last.size)
     return pl.pallas_call(
         network_kernel,
-        out_shape=jax.ShapeDtypeStruct((w_last.shape[1], count), jnp.bfloat16),
+        out_shape=jax.ShapeDtypeStruct(blocks or (w_last.shape[1], count), jnp.bfloat16),
         in_specs=[vmem] * 4,
         out_specs=vmem,
         compiler_params=pltpu.CompilerParams(vmem_limit_bytes=48 * 1024 * 1024),
@@ -175,12 +185,17 @@
         .reshape(w_out.shape[1], lev_count, local_features),
         ((0, 0), (0, 0), (0, padded_features - local_features)),
     ).reshape(w_out.shape[1], lev_count * padded_features)
-    outcome = network(inputs, w_in[0], w_mid[0], last_layer)
-    outgoing = (
-        outcome.reshape(lev_count, padded_features, lon_count, capacity)
-        .transpose(2, 0, 1, 3)
-        .reshape(group, padded_features, capacity)
-    )
+    if lon_count * capacity <= 512 and capacity % 128 == 0:
+        outgoing = network(
+            inputs, w_in[0], w_mid[0], last_layer, (group, padded_features, capacity)
+        )
+    else:
+        outgoing = (
+            network(inputs, w_in[0], w_mid[0], last_layer)
+            .reshape(lev_count, padded_features, lon_count, capacity)
+            .transpose(2, 0, 1, 3)
+            .reshape(group, padded_features, capacity)
+        )
     returned = lax.all_to_all(
         outgoing, ("lon", "lev"), split_axis=0, concat_axis=0, tiled=True
     )[:, :local_features]

time: 59 us -> 58.9 us (level)
  local copies, waits for them, and re-layouts: 6.78 us -> 6.07 us
  Pallas kernels: 3.35 us -> 4 us
    reshape x2 -> x0, local copies, waits for them, and re-layouts: 0.71 us -> none  [on_device(): outcome.reshape(lev_count, padded_features, lon_count, capacity)]
    pallas_call x1, Pallas kernels: 3.35 us -> 4 us  [network(): pl.pallas_call(network_kernel, out_shape=jax.ShapeDtypeStruct(blocks or (...]
where the time goes in v19:
time: 58.9 us; the launch traced here: 58.4 us
  waiting for transfers between devices  18.2 us (31%)
  starting transfers between devices  17.5 us (30%)
  other arithmetic  10.1 us (17%)
  local copies, waits for them, and re-layouts  6.07 us (10%)
  Pallas kernels  4 us (7%)
  matrix products  2.19 us (4%)
    all_to_all x1, waiting for transfers between devices, on_device(): lax.all_to_all(outgoing, ('lon', 'lev'), split_axis=0, concat_axis=0, til...  7.42 us
    all_to_all x1, waiting for transfers between devices, on_device(): lax.all_to_all(send_buffer, ('lon', 'lev'), split_axis=1, concat_axis=1,...  7.24 us
    all_to_all x1, starting transfers between devices, on_device(): lax.all_to_all(send_buffer, ('lon', 'lev'), split_axis=1, concat_axis=1,...  6.79 us
    pallas_call x1, Pallas kernels, network(): pl.pallas_call(network_kernel, out_shape=jax.ShapeDtypeStruct(blocks or (...  4 us
    ppermute x1, waiting for transfers between devices, halo_exchange(): lax.ppermute(jnp.concatenate([right, left], axis=-1), 'lon', [(0, 1), (1,...  3.52 us
    all_to_all x1, starting transfers between devices, on_device(): lax.all_to_all(outgoing, ('lon', 'lev'), split_axis=0, concat_axis=0, til...  3.37 us
    unnamed x21, local copies, waits for them, and re-layouts  3.34 us
    ppermute x1, starting transfers between devices, halo_exchange(): lax.ppermute(cells[..., cells.shape[-2] - width:, :], 'lat', [(i, i + 1)...  3.04 us
  transfers between devices with their start and end apart: 5, of which 3 were waited for; matrix products, arithmetic and copies ran while one was open for 3% of the time, Pallas kernels for 0%

profile of v19, /device:TPU:0, one launch (start us, length us, event | category | flops | bytes accessed | tf_op | source)
XLA Modules:
  0.0 58.4 jit_solution(6931267811799519044)
XLA Ops:
  0.0 1.1 %pad_maximum_fusion.16 = (f32[45,3,128]{2,1,0:T(4,128)S(1)}, f32[45,3,128]{2,1,0:T(4,128)S(1)}) fusion(f32[15,32,128]{2,1,0:T(8,128)} %param.8, f32[30,32,128]{2,1,0:T(8,128)} %bitcast.51), kind=kLoop, calls=%fused_computation.93 | loop fusion | flops 34560 | bytes 875520 | tf_op jit(solution)/shard_map/slice | solution.py:15
  1.1 1.3 %collective-permute-start.1 = (f32[45,3,128]{2,1,0:T(4,128)S(1)}, f32[45,3,128]{2,1,0:T(4,128)S(1)}, u32[]{:S(2)}, u32[]{:S(2)}) collective-permute-start(f32[45,3,128]{2,1,0:T(4,128)S(1)} %get-tuple-element.24), channel_id=1, source_target_pairs={{8,0},{16,8},{24,16},{9,1},{17,9},{25,17},{10,2},{18,10},{26,18},{... | collective-permute-start | bytes 207368 | tf_op jit(solution)/shard_map/ppermute | solution.py:17
  2.4 3.0 %collective-permute-start = (f32[45,3,128]{2,1,0:T(4,128)S(1)}, f32[45,3,128]{2,1,0:T(4,128)S(1)}, u32[]{:S(2)}, u32[]{:S(2)}) collective-permute-start(f32[45,3,128]{2,1,0:T(4,128)S(1)} %get-tuple-element.23), channel_id=1, source_target_pairs={{0,8},{8,16},{16,24},{1,9},{9,17},{17,25},{2,10},{10,18},{18,26},{... | collective-permute-start | bytes 207368 | tf_op jit(solution)/shard_map/ppermute | solution.py:14
  5.5 0.7 %and_select_fusion = (s32[1,1024]{1,0:T(1,128)S(1)}, s32[1,1024]{1,0:T(1,128)S(1)}) fusion(s32[1,1024]{1,0:T(1,128)} %param.9), kind=kLoop, calls=%fused_computation.97 | loop fusion | flops 11264 | bytes 12288 | tf_op jit(solution)/shard_map/jit(remainder)/select_n | solution.py:142
  6.2 0.7 %and_select_fusion.1 = s32[1,1024]{1,0:T(1,128)S(1)} fusion(s32[1,1024]{1,0:T(1,128)S(1)} %get-tuple-element.6, s32[1,1024]{1,0:T(1,128)} %param.9), kind=kLoop, calls=%fused_computation.99 | loop fusion | flops 12288 | bytes 12288 | tf_op jit(solution)/shard_map/jit(floor_divide)/jit(_where)/select_n | solution.py:141
  7.0 1.1 %pad_maximum_fusion.1 = f32[45,38,128]{2,1,0:T(8,128)S(1)} fusion(f32[45,3,128]{2,1,0:T(4,128)S(1)} %collective-permute-done.1, f32[15,32,128]{2,1,0:T(8,128)} %param.8, f32[30,32,128]{2,1,0:T(8,128)S(1)} %bitcast.52, f32[45,3,128]{2,1,0:T(4,128)S(1)} %collective-permute-done), kind=kLoop, calls=%fused_computation.34 | loop fusion | flops 656640 | bytes 1751040 | tf_op jit(solution)/shard_map/concatenate | solution.py:20
  8.0 0.3 fusion.56
  8.3 0.4 copy.44
  8.8 0.4 copy.43
  9.3 3.0 %collective-permute-start.2 = (f32[45,38,6]{0,1,2:T(8,128)S(1)}, f32[45,38,6]{0,1,2:T(8,128)S(1)}, u32[]{:S(2)}, u32[]{:S(2)}) collective-permute-start(f32[45,38,6]{0,1,2:T(8,128)S(1)} %pad_maximum_fusion.14), channel_id=1, source_target_pairs={{0,4},{4,0},{1,5},{5,1},{2,6},{6,2},{3,7},{7,3},{8,12},{12,8},{9,1... | collective-permute-start | bytes 123128 | tf_op jit(solution)/shard_map/ppermute | solution.py:25
  12.3 3.5 %collective-permute-done.2 = f32[45,38,6]{0,1,2:T(8,128)S(1)} collective-permute-done((f32[45,38,6]{0,1,2:T(8,128)S(1)}, f32[45,38,6]{0,1,2:T(8,128)S(1)}, u32[]{:S(2)}, u32[]{:S(2)}) %collective-permute-start.2) | collective-permute-done | bytes 41072 | tf_op jit(solution)/shard_map/ppermute | solution.py:25
  15.8 0.5 copy.56
  16.3 0.5 copy.55
  16.8 1.0 %pad_maximum_fusion = f32[45,38,134]{2,1,0:T(8,128)S(1)} fusion(f32[45,38,3]{2,1,0:T(8,128)S(1)} %copy.56, f32[45,3,128]{2,1,0:T(4,128)S(1)} %collective-permute-done.1, f32[15,32,128]{2,1,0:T(8,128)S(1)} %copy-done.3, f32[30,32,128]{2,1,0:T(8,128)S(1)} %bitcast.53, f32[45,3,128]{2,1,0:T(4,128)S(1)} %collective-permute-done, f32[45,38,3]{2,1,0:T(8,128)S(1)} %copy.55), kind=kLoop, calls=%fused_computation.4 | loop fusion | flops 1145700 | bytes 1833120 | tf_op jit(solution)/shard_map/concatenate | solution.py:30
  17.8 0.7 %fusion.33 = (f32[15,36,132]{2,1,0:T(8,128)S(1)}, f32[15,36,132]{2,1,0:T(8,128)S(1)}, f32[15,36,132]{2,1,0:T(8,128)S(1)}, f32[15,36,132]{2,1,0:T(8,128)S(1)}) fusion(f32[45,38,134]{2,1,0:T(8,128)S(1)} %pad_maximum_fusion), kind=kLoop, calls=%fused_computation.50 | loop fusion | flops 570240 | bytes 2566080 | tf_op jit(solution)/shard_map/mul | solution.py:44
  18.6 1.4 %fusion.14 = f32[2,15,36,132]{3,2,1,0:T(8,128)S(1)} fusion(f32[2,15,38,134]{3,2,1,0:T(8,128)S(1)} %bitcast.50, f32[15,36,132]{2,1,0:T(8,128)S(1)} %get-tuple-element.14, f32[15,36,132]{2,1,0:T(8,128)S(1)} %get-tuple-element.15, f32[15,36,132]{2,1,0:T(8,128)S(1)} %get-tuple-element.16, f32[15,36,132]{2,1,0:T(8,128)S(1)} %get-tuple-element.13, ...), kind=kLoop, calls=%fused_computation.21 | loop fusion | flops 1853280 | bytes 4561956 | tf_op jit(solution)/shard_map/jit(_where)/select_n | solution.py:54
  20.0 0.9 %fusion.29 = (f32[15,34,130]{2,1,0:T(8,128)S(1)}, f32[15,34,130]{2,1,0:T(8,128)S(1)}, f32[15,34,130]{2,1,0:T(8,128)S(1)}, f32[15,34,130]{2,1,0:T(8,128)S(1)}) fusion(f32[45,38,134]{2,1,0:T(8,128)S(1)} %pad_maximum_fusion, f32[45,38,3]{2,1,0:T(8,128)S(1)} %copy.56, f32[45,3,128]{2,1,0:T(4,128)S(1)} %collective-permute-done.1, ...), kind=kLoop, calls=%fused_computation.42 | loop fusion | flops 1060800 | bytes 2772960 | tf_op jit(solution)/shard_map/mul | solution.py:44
  20.9 1.4 %fusion.5 = f32[2,15,34,130]{3,2,1,0:T(8,128)S(1)} fusion(f32[2,15,36,132]{3,2,1,0:T(8,128)S(1)} %fusion.14, f32[15,34,130]{2,1,0:T(8,128)S(1)} %get-tuple-element.11, f32[15,34,130]{2,1,0:T(8,128)S(1)} %get-tuple-element.12, f32[15,34,130]{2,1,0:T(8,128)S(1)} %get-tuple-element.10, f32[15,34,130]{2,1,0:T(8,128)S(1)} %get-tuple-element.9, ...), kind=kLoop, calls=%fused_computation.8 | loop fusion | flops 1723800 | bytes 4243234 | tf_op jit(solution)/shard_map/jit(_where)/select_n | solution.py:54
  22.3 0.4 fusion.50
  22.7 0.6 %fusion.38 = f32[2,15,32,128]{3,2,1,0:T(8,128)S(1)} fusion(f32[2,15,34,130]{3,2,1,0:T(8,128)S(1)} %fusion.5, f32[15,32,128]{2,1,0:T(8,128)S(1)} %get-tuple-element.18, f32[15,32,128]{2,1,0:T(8,128)S(1)} %get-tuple-element.17, f32[15,32,128]{2,1,0:T(8,128)S(1)} %get-tuple-element.22, f32[15,32,128]{2,1,0:T(8,128)S(1)} %get-tuple-element.21), kind=kLoop, calls=%fused_computation.55 | loop fusion | flops 1474560 | bytes 3932160 | tf_op jit(solution)/shard_map/add | solution.py:45
  23.3 0.7 %select_reduce_fusion = bf16[30,1024]{1,0:T(8,128)(2,1)S(1)} fusion(pred[32,1024]{1,0:T(8,128)(4,1)S(1)} %iota_compare_fusion.1, bf16[30,32,128]{2,1,0:T(8,128)(2,1)S(1)} %bitcast_convert_fusion, s32[1024]{0:T(1024)S(1)} %bitcast.69), kind=kOutput, calls=%fused_computation.2 | convolution fusion | flops 253724672 | bytes 344064 | tf_op jit(solution)/shard_map/dot_general | solution.py:147
  24.1 0.7 %broadcast_in_dim.99 = bf16[30,2,4,256]{3,0,2,1:T(8,128)(2,1)} broadcast(bf16[30,4,256]{2,0,1:T(8,128)(2,1)S(1)} %copy.47), dimensions={0,2,3} | broadcast | bytes 184320 | tf_op jit(solution)/shard_map/broadcast_in_dim | solution.py:157
  24.8 6.8 %all-to-all-start = ((bf16[30,8,256]{2,0,1:T(8,128)(2,1)}), bf16[30,8,256]{2,0,1:T(8,128)(2,1)S(1)}, u32[]{:S(2)}, u32[]{:S(2)}) async-start(bf16[30,8,256]{2,0,1:T(8,128)(2,1)} %bitcast.6), calls=%async_computation | async-start | bytes 262144 | tf_op jit(solution)/shard_map/all_to_all | solution.py:172
  31.6 0.2 copy.50
  32.0 7.2 %all-to-all-done = bf16[30,8,256]{2,0,1:T(8,128)(2,1)S(1)} async-done(((bf16[30,8,256]{2,0,1:T(8,128)(2,1)}), bf16[30,8,256]{2,0,1:T(8,128)(2,1)S(1)}, u32[]{:S(2)}, u32[]{:S(2)}) %all-to-all-start) | async-done | bytes 122912 | tf_op jit(solution)/shard_map/all_to_all | solution.py:172
  39.3 0.1 copy.63
  39.5 0.1 copy.52.rows_ref
  39.6 2.2 %copy-done = bf16[1,2,1024,1024]{3,2,1,0:T(8,128)(2,1)S(1)} copy-done((bf16[1,2,1024,1024]{3,2,1,0:T(8,128)(2,1)S(1)}, bf16[1,2,1024,1024]{3,2,1,0:T(8,128)(2,1)}, u32[]{:S(2)}) %copy-start) | copy-done | bytes 4194328
  41.8 4.0 %shard_map.73 = bf16[8,32,256]{2,1,0:T(8,128)(2,1)} custom-call(bf16[512,120]{1,0:T(8,128)(2,1)S(1)} %copy.52.rows_ref, bf16[120,1024]{1,0:T(8,128)(2,1)S(1)} %bitcast.49, bf16[2,1024,1024]{2,1,0:T(8,128)(2,1)S(1)} %bitcast.48, bf16[128,1024]{1,0:T(8,128)(2,1)S(1)} %bitcast.47), custom_call_target="tpu_custom_call" | custom-call | flops 2407530496 | bytes 4956160 | tf_op jit(solution)/shard_map/pallas_call | solution.py:113
  45.8 3.4 %all-to-all-start.1 = ((bf16[8,32,256]{2,1,0:T(8,128)(2,1)}), bf16[8,32,256]{2,1,0:T(8,128)(2,1)S(1)}, u32[]{:S(2)}, u32[]{:S(2)}) async-start(bf16[8,32,256]{2,1,0:T(8,128)(2,1)} %shard_map.73), calls=%async_computation.1 | async-start | bytes 262144 | tf_op jit(solution)/shard_map/all_to_all | solution.py:199
  49.2 7.4 %all-to-all-done.1 = bf16[8,32,256]{2,1,0:T(8,128)(2,1)S(1)} async-done(((bf16[8,32,256]{2,1,0:T(8,128)(2,1)}), bf16[8,32,256]{2,1,0:T(8,128)(2,1)S(1)}, u32[]{:S(2)}, u32[]{:S(2)}) %all-to-all-start.1) | async-done | bytes 131104 | tf_op jit(solution)/shard_map/all_to_all | solution.py:199
  56.9 1.5 %fusion.21 = f32[30,32,128]{2,1,0:T(8,128)} fusion(f32[30,32,128]{2,1,0:T(8,128)S(1)} %bitcast.56, pred[32,1024]{1,0:T(8,128)(4,1)S(1)} %iota_compare_fusion.1, bf16[30,1024]{1,0:T(8,128)(2,1)S(1)} %broadcast_select_fusion, s32[1024]{0:T(1024)S(1)} %bitcast.70), kind=kOutput, calls=%fused_computation.31 | convolution fusion | flops 252895232 | bytes 1081344 | tf_op jit(solution)/shard_map/dot_general | solution.py:214
  (36 shorter events, 0.8 us)
Async XLA Ops:
  0.0 7.0 %copy-start.2 = (f32[2,15,32,128]{3,2,1,0:T(8,128)S(1)}, f32[2,15,32,128]{3,2,1,0:T(8,128)}, u32[]{:S(2)}) copy-start(f32[2,15,32,128]{3,2,1,0:T(8,128)} %param.7) | copy-start | bytes 1474564
  1.1 5.8 %collective-permute-start.1 = (f32[45,3,128]{2,1,0:T(4,128)S(1)}, f32[45,3,128]{2,1,0:T(4,128)S(1)}, u32[]{:S(2)}, u32[]{:S(2)}) collective-permute-start(f32[45,3,128]{2,1,0:T(4,128)S(1)} %get-tuple-element.24), channel_id=1, source_target_pairs={{8,0},{16,8},{24,16},{9,1},{17,9},{25,17},{10,2},{18,10},{26,18},{... | collective-permute-start | bytes 207368 | tf_op jit(solution)/shard_map/ppermute | solution.py:17
  2.4 4.5 %collective-permute-start = (f32[45,3,128]{2,1,0:T(4,128)S(1)}, f32[45,3,128]{2,1,0:T(4,128)S(1)}, u32[]{:S(2)}, u32[]{:S(2)}) collective-permute-start(f32[45,3,128]{2,1,0:T(4,128)S(1)} %get-tuple-element.23), channel_id=1, source_target_pairs={{0,8},{8,16},{16,24},{1,9},{9,17},{17,25},{2,10},{10,18},{18,26},{... | collective-permute-start | bytes 207368 | tf_op jit(solution)/shard_map/ppermute | solution.py:14
  9.2 7.5 %copy-start.3 = (f32[15,32,128]{2,1,0:T(8,128)S(1)}, f32[15,32,128]{2,1,0:T(8,128)}, u32[]{:S(2)}) copy-start(f32[15,32,128]{2,1,0:T(8,128)} %param.8) | copy-start | bytes 737284
  9.3 6.6 %collective-permute-start.2 = (f32[45,38,6]{0,1,2:T(8,128)S(1)}, f32[45,38,6]{0,1,2:T(8,128)S(1)}, u32[]{:S(2)}, u32[]{:S(2)}) collective-permute-start(f32[45,38,6]{0,1,2:T(8,128)S(1)} %pad_maximum_fusion.14), channel_id=1, source_target_pairs={{0,4},{4,0},{1,5},{5,1},{2,6},{6,2},{3,7},{7,3},{8,12},{12,8},{9,1... | collective-permute-start | bytes 123128 | tf_op jit(solution)/shard_map/ppermute | solution.py:25
  23.3 8.2 %copy-start.4 = (bf16[1,1024,120]{1,2,0:T(8,128)(2,1)S(1)}, bf16[1,1024,120]{1,2,0:T(8,128)(2,1)}, u32[]{:S(2)}) copy-start(bf16[1,1024,120]{1,2,0:T(8,128)(2,1)} %param.13) | copy-start | bytes 737284
  24.8 14.5 %all-to-all-start = ((bf16[30,8,256]{2,0,1:T(8,128)(2,1)}), bf16[30,8,256]{2,0,1:T(8,128)(2,1)S(1)}, u32[]{:S(2)}, u32[]{:S(2)}) async-start(bf16[30,8,256]{2,0,1:T(8,128)(2,1)} %bitcast.6), calls=%async_computation | async-start | bytes 262144 | tf_op jit(solution)/shard_map/all_to_all | solution.py:172
  31.9 7.8 %copy-start.1 = (bf16[1,120,1024]{2,1,0:T(8,128)(2,1)S(1)}, bf16[1,120,1024]{2,1,0:T(8,128)(2,1)}, u32[]{:S(2)}) copy-start(bf16[1,120,1024]{2,1,0:T(8,128)(2,1)} %param.11) | copy-start | bytes 737284
  39.6 2.2 %copy-start = (bf16[1,2,1024,1024]{3,2,1,0:T(8,128)(2,1)S(1)}, bf16[1,2,1024,1024]{3,2,1,0:T(8,128)(2,1)}, u32[]{:S(2)}) copy-start(bf16[1,2,1024,1024]{3,2,1,0:T(8,128)(2,1)} %param.12) | copy-start | bytes 12582916
  41.8 7.4 %copy-start.5 = (s32[1,1024,1]{1,2,0:T(1,128)S(1)}, s32[1,1024,1]{1,2,0:T(1,128)}, u32[]{:S(2)}) copy-start(s32[1,1024,1]{1,2,0:T(1,128)} %param.10) | copy-start | bytes 12292
  45.8 10.8 %all-to-all-start.1 = ((bf16[8,32,256]{2,1,0:T(8,128)(2,1)}), bf16[8,32,256]{2,1,0:T(8,128)(2,1)S(1)}, u32[]{:S(2)}, u32[]{:S(2)}) async-start(bf16[8,32,256]{2,1,0:T(8,128)(2,1)} %shard_map.73), calls=%async_computation.1 | async-start | bytes 262144 | tf_op jit(solution)/shard_map/all_to_all | solution.py:199

commit v20 on v17

--- a/solution.py
+++ b/solution.py
@@ -144,9 +144,14 @@
     group = lon_count * lev_count
     whole_slices = capacity == per_device
     if whole_slices:
-        send_buffer = jnp.broadcast_to(
-            picked.reshape(local_features, 1, lev_count, per_device),
-            (local_features, lon_count, lev_count, per_device),
+        doubled = jnp.dot(
+            planes.astype(jnp.bfloat16).reshape(local_features * lat_rows, lon_cols),
+            jnp.concatenate([col_picker] * lon_count, axis=1),
+            preferred_element_type=jnp.bfloat16,
+        ).reshape(local_features, lat_rows, lon_count * cloudy)
+        doubled_match = jnp.concatenate([row_match] * lon_count, axis=1)
+        send_buffer = jnp.sum(
+            jnp.where(doubled_match[None], doubled, jnp.zeros_like(doubled)), axis=1
         ).reshape(local_features, group, capacity)
     else:
         pieces = routes.reshape(lev_count, per_device)

time: 58.4 us -> 58.2 us (level)
  other arithmetic: 10.3 us -> 9.48 us
    concatenate x1, other arithmetic: 1.08 us -> 0.13 us  [halo_exchange(): cells = jnp.concatenate([from_above, cells, from_below], axis=-2)]
    unnamed x16 -> x17, local copies, waits for them, and re-layouts: 3.17 us -> 3.2 us
where the time goes in v20:
time: 58.2 us; the launch traced here: 57.8 us
  blocking collectives  14.4 us (25%)
  waiting for transfers between devices  11 us (19%)
  starting transfers between devices  10.7 us (18%)
  other arithmetic  9.48 us (16%)
  local copies, waits for them, and re-layouts  5.77 us (10%)
  Pallas kernels  3.35 us (6%)
  matrix products  2.72 us (5%)
    all_to_all x1, blocking collectives, on_device(): lax.all_to_all(send_buffer, ('lon', 'lev'), split_axis=1, concat_axis=1,...  14.4 us
    all_to_all x1, waiting for transfers between devices, on_device(): lax.all_to_all(outgoing, ('lon', 'lev'), split_axis=1, concat_axis=1, til...  7.42 us
    ppermute x1, waiting for transfers between devices, halo_exchange(): lax.ppermute(jnp.concatenate([right, left], axis=-1), 'lon', [(0, 1), (1,...  3.58 us
    all_to_all x1, starting transfers between devices, on_device(): lax.all_to_all(outgoing, ('lon', 'lev'), split_axis=1, concat_axis=1, til...  3.37 us
    pallas_call x1, Pallas kernels, network(): pl.pallas_call(network_kernel, out_shape=jax.ShapeDtypeStruct((w_last.sha...  3.35 us
    unnamed x17, local copies, waits for them, and re-layouts  3.2 us
    ppermute x1, starting transfers between devices, halo_exchange(): lax.ppermute(cells[..., cells.shape[-2] - width:, :], 'lat', [(i, i + 1)...  3.04 us
    ppermute x1, starting transfers between devices, halo_exchange(): lax.ppermute(jnp.concatenate([right, left], axis=-1), 'lon', [(0, 1), (1,...  3.03 us
  transfers between devices with their start and end apart: 4, of which 2 were waited for; matrix products, arithmetic and copies ran while one was open for 3% of the time, Pallas kernels for 0%

profile of v20, /device:TPU:0, one launch (start us, length us, event | category | flops | bytes accessed | tf_op | source)
XLA Modules:
  0.0 57.8 jit_solution(18174486688962580413)
XLA Ops:
  0.0 1.1 %pad_maximum_fusion.16 = (f32[45,3,128]{2,1,0:T(4,128)S(1)}, f32[45,3,128]{2,1,0:T(4,128)S(1)}) fusion(f32[15,32,128]{2,1,0:T(8,128)} %param.8, f32[30,32,128]{2,1,0:T(8,128)} %bitcast.42), kind=kLoop, calls=%fused_computation.96 | loop fusion | flops 34560 | bytes 875520 | tf_op jit(solution)/shard_map/slice | solution.py:15
  1.1 1.3 %collective-permute-start.1 = (f32[45,3,128]{2,1,0:T(4,128)S(1)}, f32[45,3,128]{2,1,0:T(4,128)S(1)}, u32[]{:S(2)}, u32[]{:S(2)}) collective-permute-start(f32[45,3,128]{2,1,0:T(4,128)S(1)} %get-tuple-element.24), channel_id=1, source_target_pairs={{8,0},{16,8},{24,16},{9,1},{17,9},{25,17},{10,2},{18,10},{26,18},{... | collective-permute-start | bytes 207368 | tf_op jit(solution)/shard_map/ppermute | solution.py:17
  2.4 3.0 %collective-permute-start = (f32[45,3,128]{2,1,0:T(4,128)S(1)}, f32[45,3,128]{2,1,0:T(4,128)S(1)}, u32[]{:S(2)}, u32[]{:S(2)}) collective-permute-start(f32[45,3,128]{2,1,0:T(4,128)S(1)} %get-tuple-element.23), channel_id=1, source_target_pairs={{0,8},{8,16},{16,24},{1,9},{9,17},{17,25},{2,10},{10,18},{18,26},{... | collective-permute-start | bytes 207368 | tf_op jit(solution)/shard_map/ppermute | solution.py:14
  5.5 0.7 %and_select_fusion = (s32[1,1024]{1,0:T(1,128)S(1)}, s32[1,1024]{1,0:T(1,128)S(1)}) fusion(s32[1,1024]{1,0:T(1,128)} %param.9), kind=kLoop, calls=%fused_computation.98 | loop fusion | flops 11264 | bytes 12288 | tf_op jit(solution)/shard_map/jit(remainder)/select_n | solution.py:132
  6.2 0.7 %and_select_fusion.1 = s32[1,1024]{1,0:T(1,128)S(1)} fusion(s32[1,1024]{1,0:T(1,128)S(1)} %get-tuple-element.6, s32[1,1024]{1,0:T(1,128)} %param.9), kind=kLoop, calls=%fused_computation.100 | loop fusion | flops 12288 | bytes 12288 | tf_op jit(solution)/shard_map/jit(floor_divide)/jit(_where)/select_n | solution.py:131
  7.1 0.1 pad_maximum_fusion.1
  7.2 0.3 fusion.55
  7.5 0.4 copy.44
  8.0 0.4 copy.43
  8.4 3.0 %collective-permute-start.2 = (f32[45,38,6]{0,1,2:T(8,128)S(1)}, f32[45,38,6]{0,1,2:T(8,128)S(1)}, u32[]{:S(2)}, u32[]{:S(2)}) collective-permute-start(f32[45,38,6]{0,1,2:T(8,128)S(1)} %pad_maximum_fusion.14), channel_id=1, source_target_pairs={{0,4},{4,0},{1,5},{5,1},{2,6},{6,2},{3,7},{7,3},{8,12},{12,8},{9,1... | collective-permute-start | bytes 123128 | tf_op jit(solution)/shard_map/ppermute | solution.py:25
  11.5 3.6 %collective-permute-done.2 = f32[45,38,6]{0,1,2:T(8,128)S(1)} collective-permute-done((f32[45,38,6]{0,1,2:T(8,128)S(1)}, f32[45,38,6]{0,1,2:T(8,128)S(1)}, u32[]{:S(2)}, u32[]{:S(2)}) %collective-permute-start.2) | collective-permute-done | bytes 41072 | tf_op jit(solution)/shard_map/ppermute | solution.py:25
  15.1 0.5 copy.57
  15.5 0.5 copy.56
  16.0 1.0 %pad_maximum_fusion = f32[45,38,134]{2,1,0:T(8,128)S(1)} fusion(f32[45,38,3]{2,1,0:T(8,128)S(1)} %copy.57, f32[45,3,128]{2,1,0:T(4,128)S(1)} %collective-permute-done.1, f32[15,32,128]{2,1,0:T(8,128)S(1)} %copy-done.4, f32[30,32,128]{2,1,0:T(8,128)S(1)} %bitcast.44, f32[45,3,128]{2,1,0:T(4,128)S(1)} %collective-permute-done, f32[45,38,3]{2,1,0:T(8,128)S(1)} %copy.56), kind=kLoop, calls=%fused_computation.4 | loop fusion | flops 1145700 | bytes 1833120 | tf_op jit(solution)/shard_map/concatenate | solution.py:30
  17.1 0.7 %fusion.35 = (f32[15,36,132]{2,1,0:T(8,128)S(1)}, f32[15,36,132]{2,1,0:T(8,128)S(1)}, f32[15,36,132]{2,1,0:T(8,128)S(1)}, f32[15,36,132]{2,1,0:T(8,128)S(1)}) fusion(f32[45,38,134]{2,1,0:T(8,128)S(1)} %pad_maximum_fusion), kind=kLoop, calls=%fused_computation.53 | loop fusion | flops 570240 | bytes 2566080 | tf_op jit(solution)/shard_map/mul | solution.py:44
  17.8 1.4 %fusion.14 = f32[2,15,36,132]{3,2,1,0:T(8,128)S(1)} fusion(f32[2,15,38,134]{3,2,1,0:T(8,128)S(1)} %bitcast.41, f32[15,36,132]{2,1,0:T(8,128)S(1)} %get-tuple-element.14, f32[15,36,132]{2,1,0:T(8,128)S(1)} %get-tuple-element.15, f32[15,36,132]{2,1,0:T(8,128)S(1)} %get-tuple-element.16, f32[15,36,132]{2,1,0:T(8,128)S(1)} %get-tuple-element.13, ...), kind=kLoop, calls=%fused_computation.21 | loop fusion | flops 1853280 | bytes 4561956 | tf_op jit(solution)/shard_map/jit(_where)/select_n | solution.py:54
  19.2 0.9 %fusion.31 = (f32[15,34,130]{2,1,0:T(8,128)S(1)}, f32[15,34,130]{2,1,0:T(8,128)S(1)}, f32[15,34,130]{2,1,0:T(8,128)S(1)}, f32[15,34,130]{2,1,0:T(8,128)S(1)}) fusion(f32[45,38,134]{2,1,0:T(8,128)S(1)} %pad_maximum_fusion, f32[45,38,3]{2,1,0:T(8,128)S(1)} %copy.57, f32[45,3,128]{2,1,0:T(4,128)S(1)} %collective-permute-done.1, ...), kind=kLoop, calls=%fused_computation.45 | loop fusion | flops 1060800 | bytes 2772960 | tf_op jit(solution)/shard_map/mul | solution.py:44
  20.1 1.4 %fusion.5 = f32[2,15,34,130]{3,2,1,0:T(8,128)S(1)} fusion(f32[2,15,36,132]{3,2,1,0:T(8,128)S(1)} %fusion.14, f32[15,34,130]{2,1,0:T(8,128)S(1)} %get-tuple-element.11, f32[15,34,130]{2,1,0:T(8,128)S(1)} %get-tuple-element.12, f32[15,34,130]{2,1,0:T(8,128)S(1)} %get-tuple-element.10, f32[15,34,130]{2,1,0:T(8,128)S(1)} %get-tuple-element.9, ...), kind=kLoop, calls=%fused_computation.8 | loop fusion | flops 1723800 | bytes 4243234 | tf_op jit(solution)/shard_map/jit(_where)/select_n | solution.py:54
  21.5 0.4 fusion.48
  21.9 0.6 %fusion.38 = f32[2,15,32,128]{3,2,1,0:T(8,128)S(1)} fusion(f32[2,15,34,130]{3,2,1,0:T(8,128)S(1)} %fusion.5, f32[15,32,128]{2,1,0:T(8,128)S(1)} %get-tuple-element.18, f32[15,32,128]{2,1,0:T(8,128)S(1)} %get-tuple-element.17, f32[15,32,128]{2,1,0:T(8,128)S(1)} %get-tuple-element.22, f32[15,32,128]{2,1,0:T(8,128)S(1)} %get-tuple-element.21), kind=kLoop, calls=%fused_computation.58 | loop fusion | flops 1474560 | bytes 3932160 | tf_op jit(solution)/shard_map/add | solution.py:45
  22.6 1.2 %select_reduce_fusion = bf16[30,2048]{1,0:T(8,128)(2,1)S(1)} fusion(pred[32,2048]{1,0:T(8,128)(4,1)S(1)} %pad_add_fusion, bf16[30,32,128]{2,1,0:T(8,128)(2,1)S(1)} %bitcast_convert_fusion, pred[128,1024]{1,0:T(32,128)(4,1)S(1)} %iota_compare_fusion), kind=kOutput, calls=%fused_computation | convolution fusion | flops 507449344 | bytes 565248 | tf_op jit(solution)/shard_map/dot_general | solution.py:147
  23.9 14.4 %all_to_all.10 = bf16[30,8,256]{2,0,1:T(8,128)(2,1)S(1)} all-to-all(bf16[30,8,256]{2,0,1:T(8,128)(2,1)S(1)} %copy.47), channel_id=1, replica_groups=mesh['lat'=4,'lon'=2,'lev'=4] {'lon','lev'}, dimensions={1} | all-to-all | bytes 245760 | tf_op jit(solution)/shard_map/all_to_all | solution.py:167
  38.3 0.1 copy.63
  38.4 0.1 copy.49
  38.5 0.1 copy.50.rows_ref
  38.7 2.2 %copy-done = bf16[1,2,1024,1024]{3,2,1,0:T(8,128)(2,1)S(1)} copy-done((bf16[1,2,1024,1024]{3,2,1,0:T(8,128)(2,1)S(1)}, bf16[1,2,1024,1024]{3,2,1,0:T(8,128)(2,1)}, u32[]{:S(2)}) %copy-start) | copy-done | bytes 4194328
  40.9 3.3 %shard_map.73 = bf16[120,512]{1,0:T(8,128)(2,1)S(1)} custom-call(bf16[512,120]{1,0:T(8,128)(2,1)S(1)} %copy.50.rows_ref, bf16[120,1024]{1,0:T(8,128)(2,1)S(1)} %bitcast.39, bf16[2,1024,1024]{2,1,0:T(8,128)(2,1)S(1)} %bitcast.38, bf16[120,1024]{1,0:T(8,128)(2,1)S(1)} %bitcast.40), custom_call_target="tpu_custom_call" | custom-call | flops 2399141888 | bytes 4931584 | tf_op jit(solution)/shard_map/pallas_call | solution.py:103
  44.4 0.7 %copy.52 = bf16[30,8,256]{2,0,1:T(8,128)(2,1)} copy(bf16[30,8,256]{2,1,0:T(8,128)(2,1)S(1)} %reshape.98) | data formatting | bytes 245760 | tf_op jit(solution)/shard_map/reshape | solution.py:179
  45.1 3.4 %all-to-all-start.1 = ((bf16[30,8,256]{2,0,1:T(8,128)(2,1)}), bf16[30,8,256]{2,0,1:T(8,128)(2,1)S(1)}, u32[]{:S(2)}, u32[]{:S(2)}) async-start(bf16[30,8,256]{2,0,1:T(8,128)(2,1)} %copy.52), calls=%async_computation.1 | async-start | bytes 262144 | tf_op jit(solution)/shard_map/all_to_all | solution.py:181
  48.5 7.4 %all-to-all-done.1 = bf16[30,8,256]{2,0,1:T(8,128)(2,1)S(1)} async-done(((bf16[30,8,256]{2,0,1:T(8,128)(2,1)}), bf16[30,8,256]{2,0,1:T(8,128)(2,1)S(1)}, u32[]{:S(2)}, u32[]{:S(2)}) %all-to-all-start.1) | async-done | bytes 122912 | tf_op jit(solution)/shard_map/all_to_all | solution.py:181
  56.0 0.2 broadcast_select_fusion
  56.3 1.5 %fusion.21 = f32[30,32,128]{2,1,0:T(8,128)} fusion(f32[30,32,128]{2,1,0:T(8,128)S(1)} %bitcast.47, pred[32,1024]{1,0:T(8,128)(4,1)S(1)} %iota_compare_fusion.1, bf16[30,1024]{1,0:T(8,128)(2,1)S(1)} %bitcast.54, s32[1024]{0:T(1024)S(1)} %bitcast.56), kind=kOutput, calls=%fused_computation.31 | convolution fusion | flops 252895232 | bytes 1081344 | tf_op jit(solution)/shard_map/dot_general | solution.py:192
  (34 shorter events, 0.7 us)
Async XLA Ops:
  0.0 7.1 %copy-start.4 = (f32[15,32,128]{2,1,0:T(8,128)S(1)}, f32[15,32,128]{2,1,0:T(8,128)}, u32[]{:S(2)}) copy-start(f32[15,32,128]{2,1,0:T(8,128)} %param.8) | copy-start | bytes 737284
  0.0 7.1 %copy-start.3 = (f32[2,15,32,128]{3,2,1,0:T(8,128)S(1)}, f32[2,15,32,128]{3,2,1,0:T(8,128)}, u32[]{:S(2)}) copy-start(f32[2,15,32,128]{3,2,1,0:T(8,128)} %param.7) | copy-start | bytes 1474564
  1.1 5.9 %collective-permute-start.1 = (f32[45,3,128]{2,1,0:T(4,128)S(1)}, f32[45,3,128]{2,1,0:T(4,128)S(1)}, u32[]{:S(2)}, u32[]{:S(2)}) collective-permute-start(f32[45,3,128]{2,1,0:T(4,128)S(1)} %get-tuple-element.24), channel_id=1, source_target_pairs={{8,0},{16,8},{24,16},{9,1},{17,9},{25,17},{10,2},{18,10},{26,18},{... | collective-permute-start | bytes 207368 | tf_op jit(solution)/shard_map/ppermute | solution.py:17
  2.4 4.6 %collective-permute-start = (f32[45,3,128]{2,1,0:T(4,128)S(1)}, f32[45,3,128]{2,1,0:T(4,128)S(1)}, u32[]{:S(2)}, u32[]{:S(2)}) collective-permute-start(f32[45,3,128]{2,1,0:T(4,128)S(1)} %get-tuple-element.23), channel_id=1, source_target_pairs={{0,8},{8,16},{16,24},{1,9},{9,17},{17,25},{2,10},{10,18},{18,26},{... | collective-permute-start | bytes 207368 | tf_op jit(solution)/shard_map/ppermute | solution.py:14
  8.4 6.6 %collective-permute-start.2 = (f32[45,38,6]{0,1,2:T(8,128)S(1)}, f32[45,38,6]{0,1,2:T(8,128)S(1)}, u32[]{:S(2)}, u32[]{:S(2)}) collective-permute-start(f32[45,38,6]{0,1,2:T(8,128)S(1)} %pad_maximum_fusion.14), channel_id=1, source_target_pairs={{0,4},{4,0},{1,5},{5,1},{2,6},{6,2},{3,7},{7,3},{8,12},{12,8},{9,1... | collective-permute-start | bytes 123128 | tf_op jit(solution)/shard_map/ppermute | solution.py:25
  23.8 14.9 %copy-start.1 = (bf16[1,120,1024]{2,1,0:T(8,128)(2,1)S(1)}, bf16[1,120,1024]{2,1,0:T(8,128)(2,1)}, u32[]{:S(2)}) copy-start(bf16[1,120,1024]{2,1,0:T(8,128)(2,1)} %param.11) | copy-start | bytes 737284
  23.8 14.9 %copy-start.2 = (bf16[1,1024,120]{1,2,0:T(8,128)(2,1)S(1)}, bf16[1,1024,120]{1,2,0:T(8,128)(2,1)}, u32[]{:S(2)}) copy-start(bf16[1,1024,120]{1,2,0:T(8,128)(2,1)} %param.13) | copy-start | bytes 737284
  38.7 2.2 %copy-start = (bf16[1,2,1024,1024]{3,2,1,0:T(8,128)(2,1)S(1)}, bf16[1,2,1024,1024]{3,2,1,0:T(8,128)(2,1)}, u32[]{:S(2)}) copy-start(bf16[1,2,1024,1024]{3,2,1,0:T(8,128)(2,1)} %param.12) | copy-start | bytes 12582916
  44.2 4.2 %copy-start.5 = (s32[1,1024,1]{1,2,0:T(1,128)S(1)}, s32[1,1024,1]{1,2,0:T(1,128)}, u32[]{:S(2)}) copy-start(s32[1,1024,1]{1,2,0:T(1,128)} %param.10) | copy-start | bytes 12292
  45.1 10.8 %all-to-all-start.1 = ((bf16[30,8,256]{2,0,1:T(8,128)(2,1)}), bf16[30,8,256]{2,0,1:T(8,128)(2,1)S(1)}, u32[]{:S(2)}, u32[]{:S(2)}) async-start(bf16[30,8,256]{2,0,1:T(8,128)(2,1)} %copy.52), calls=%async_computation.1 | async-start | bytes 262144 | tf_op jit(solution)/shard_map/all_to_all | solution.py:181

commit v21 on v20

--- a/solution.py
+++ b/solution.py
@@ -75,12 +75,15 @@
 
 
 def network_kernel(rows_ref, first_ref, middle_ref, last_ref, out_ref):
-    tile = min(rows_ref.shape[0], 512)
+    tile = min(rows_ref.shape[1], 512)
 
     def one_tile(index, carry):
         rows = pl.ds(pl.multiple_of(index * tile, tile), tile)
         hidden = jax.nn.gelu(
-            jnp.dot(rows_ref[rows, :], first_ref[...], preferred_element_type=jnp.float32)
+            lax.dot_general(
+                rows_ref[:, rows], first_ref[...], (((0,), (0,)), ((), ())),
+                preferred_element_type=jnp.float32,
+            )
         ).astype(jnp.bfloat16)
         for layer_no in range(middle_ref.shape[0]):
             hidden = jax.nn.gelu(
@@ -91,11 +94,11 @@
         ).astype(jnp.bfloat16)
         return carry
 
-    lax.fori_loop(0, rows_ref.shape[0] // tile, one_tile, 0)
+    lax.fori_loop(0, rows_ref.shape[1] // tile, one_tile, 0)
 
 
 def network(rows, w_first, w_middle, w_last):
-    count, width = rows.shape
+    width, count = rows.shape
     hid = w_first.shape[1]
     vmem = pl.BlockSpec(memory_space=pltpu.VMEM)
     flops = 2 * count * (width * hid + w_middle.shape[0] * hid * hid + hid * w_last.shape[1])
@@ -168,11 +171,17 @@
         send_buffer, ("lon", "lev"), split_axis=1, concat_axis=1, tiled=True
     )
     inputs = (
-        received.reshape(2, level_rows, lon_count, lev_count, capacity)
-        .transpose(2, 4, 0, 3, 1)
-        .reshape(lon_count * capacity, feature_count)
-    )
-    outcome = network(inputs, w_in[0], w_mid[0], w_out[0])
+        received.reshape(local_features, lon_count, lev_count, capacity)
+        .transpose(2, 0, 1, 3)
+        .reshape(feature_count, lon_count * capacity)
+    )
+    first_layer = (
+        w_in[0]
+        .reshape(2, lev_count, level_rows, w_in.shape[2])
+        .transpose(1, 0, 2, 3)
+        .reshape(feature_count, w_in.shape[2])
+    )
+    outcome = network(inputs, first_layer, w_mid[0], w_out[0])
     outgoing = (
         outcome.reshape(2, lev_count, level_rows, lon_count, capacity)
         .transpose(0, 2, 3, 1, 4)

time: 58.2 us -> 59 us (1.014)
  blocking collectives: 14.4 us -> 0 us
  waiting for transfers between devices: 11 us -> 18.5 us
  starting transfers between devices: 10.7 us -> 17.6 us
  local copies, waits for them, and re-layouts: 5.77 us -> 6.47 us
    all_to_all x1 -> x0, blocking collectives: 14.4 us -> none  [on_device(): lax.all_to_all(send_buffer, ('lon', 'lev'), split_axis=1, concat_axis=1,...]
    all_to_all x0 -> x1, waiting for transfers between devices: none -> 7.45 us  [on_device(): lax.all_to_all(send_buffer, ('lon', 'lev'), split_axis=1, concat_axis=1,...]
    all_to_all x0 -> x1, starting transfers between devices: none -> 6.91 us  [on_device(): lax.all_to_all(send_buffer, ('lon', 'lev'), split_axis=1, concat_axis=1,...]
    reshape x2, local copies, waits for them, and re-layouts: 0.04 us -> 0.69 us  [on_device(): send_buffer = jnp.sum(jnp.where(doubled_match[None], doubled, jnp.zeros_l...]
  transfers between devices with their start and end apart: 4 -> 5, of which waited for: 2 -> 3; matrix products, arithmetic and copies ran while one was open for 3% -> 3% of each run, Pallas kernels for 0% -> 0%
where the time goes in v21:
time: 59 us; the launch traced here: 58.5 us
  waiting for transfers between devices  18.5 us (31%)
  starting transfers between devices  17.6 us (30%)
  other arithmetic  9.48 us (16%)
  local copies, waits for them, and re-layouts  6.47 us (11%)
  Pallas kernels  3.43 us (6%)
  matrix products  2.71 us (5%)
    all_to_all x1, waiting for transfers between devices, on_device(): lax.all_to_all(send_buffer, ('lon', 'lev'), split_axis=1, concat_axis=1,...  7.45 us
    all_to_all x1, waiting for transfers between devices, on_device(): lax.all_to_all(outgoing, ('lon', 'lev'), split_axis=1, concat_axis=1, til...  7.42 us
    all_to_all x1, starting transfers between devices, on_device(): lax.all_to_all(send_buffer, ('lon', 'lev'), split_axis=1, concat_axis=1,...  6.91 us
    ppermute x1, waiting for transfers between devices, halo_exchange(): lax.ppermute(jnp.concatenate([right, left], axis=-1), 'lon', [(0, 1), (1,...  3.58 us
    pallas_call x1, Pallas kernels, network(): pl.pallas_call(network_kernel, out_shape=jax.ShapeDtypeStruct((w_last.sha...  3.43 us
    all_to_all x1, starting transfers between devices, on_device(): lax.all_to_all(outgoing, ('lon', 'lev'), split_axis=1, concat_axis=1, til...  3.37 us
    unnamed x17, local copies, waits for them, and re-layouts  3.19 us
    ppermute x1, starting transfers between devices, halo_exchange(): lax.ppermute(cells[..., cells.shape[-2] - width:, :], 'lat', [(i, i + 1)...  3.04 us
  transfers between devices with their start and end apart: 5, of which 3 were waited for; matrix products, arithmetic and copies ran while one was open for 3% of the time, Pallas kernels for 0%

profile of v21, /device:TPU:0, one launch (start us, length us, event | category | flops | bytes accessed | tf_op | source)
XLA Modules:
  0.0 58.5 jit_solution(15345311749622392618)
XLA Ops:
  0.0 1.1 %pad_maximum_fusion.16 = (f32[45,3,128]{2,1,0:T(4,128)S(1)}, f32[45,3,128]{2,1,0:T(4,128)S(1)}) fusion(f32[15,32,128]{2,1,0:T(8,128)} %param.8, f32[30,32,128]{2,1,0:T(8,128)} %bitcast.39), kind=kLoop, calls=%fused_computation.96 | loop fusion | flops 34560 | bytes 875520 | tf_op jit(solution)/shard_map/slice | solution.py:15
  1.1 1.3 %collective-permute-start.1 = (f32[45,3,128]{2,1,0:T(4,128)S(1)}, f32[45,3,128]{2,1,0:T(4,128)S(1)}, u32[]{:S(2)}, u32[]{:S(2)}) collective-permute-start(f32[45,3,128]{2,1,0:T(4,128)S(1)} %get-tuple-element.24), channel_id=1, source_target_pairs={{8,0},{16,8},{24,16},{9,1},{17,9},{25,17},{10,2},{18,10},{26,18},{... | collective-permute-start | bytes 207368 | tf_op jit(solution)/shard_map/ppermute | solution.py:17
  2.4 3.0 %collective-permute-start = (f32[45,3,128]{2,1,0:T(4,128)S(1)}, f32[45,3,128]{2,1,0:T(4,128)S(1)}, u32[]{:S(2)}, u32[]{:S(2)}) collective-permute-start(f32[45,3,128]{2,1,0:T(4,128)S(1)} %get-tuple-element.23), channel_id=1, source_target_pairs={{0,8},{8,16},{16,24},{1,9},{9,17},{17,25},{2,10},{10,18},{18,26},{... | collective-permute-start | bytes 207368 | tf_op jit(solution)/shard_map/ppermute | solution.py:14
  5.5 0.7 %and_select_fusion = (s32[1,1024]{1,0:T(1,128)S(1)}, s32[1,1024]{1,0:T(1,128)S(1)}) fusion(s32[1,1024]{1,0:T(1,128)} %param.9), kind=kLoop, calls=%fused_computation.98 | loop fusion | flops 11264 | bytes 12288 | tf_op jit(solution)/shard_map/jit(remainder)/select_n | solution.py:135
  6.2 0.7 %and_select_fusion.1 = s32[1,1024]{1,0:T(1,128)S(1)} fusion(s32[1,1024]{1,0:T(1,128)S(1)} %get-tuple-element.6, s32[1,1024]{1,0:T(1,128)} %param.9), kind=kLoop, calls=%fused_computation.100 | loop fusion | flops 12288 | bytes 12288 | tf_op jit(solution)/shard_map/jit(floor_divide)/jit(_where)/select_n | solution.py:134
  7.1 0.1 pad_maximum_fusion.1
  7.2 0.3 fusion.55
  7.5 0.4 copy.45
  8.0 0.4 copy.44
  8.4 3.0 %collective-permute-start.2 = (f32[45,38,6]{0,1,2:T(8,128)S(1)}, f32[45,38,6]{0,1,2:T(8,128)S(1)}, u32[]{:S(2)}, u32[]{:S(2)}) collective-permute-start(f32[45,38,6]{0,1,2:T(8,128)S(1)} %pad_maximum_fusion.14), channel_id=1, source_target_pairs={{0,4},{4,0},{1,5},{5,1},{2,6},{6,2},{3,7},{7,3},{8,12},{12,8},{9,1... | collective-permute-start | bytes 123128 | tf_op jit(solution)/shard_map/ppermute | solution.py:25
  11.5 3.6 %collective-permute-done.2 = f32[45,38,6]{0,1,2:T(8,128)S(1)} collective-permute-done((f32[45,38,6]{0,1,2:T(8,128)S(1)}, f32[45,38,6]{0,1,2:T(8,128)S(1)}, u32[]{:S(2)}, u32[]{:S(2)}) %collective-permute-start.2) | collective-permute-done | bytes 41072 | tf_op jit(solution)/shard_map/ppermute | solution.py:25
  15.1 0.5 copy.58
  15.5 0.5 copy.57
  16.0 1.0 %pad_maximum_fusion = f32[45,38,134]{2,1,0:T(8,128)S(1)} fusion(f32[45,38,3]{2,1,0:T(8,128)S(1)} %copy.58, f32[45,3,128]{2,1,0:T(4,128)S(1)} %collective-permute-done.1, f32[15,32,128]{2,1,0:T(8,128)S(1)} %copy-done.3, f32[30,32,128]{2,1,0:T(8,128)S(1)} %bitcast.41, f32[45,3,128]{2,1,0:T(4,128)S(1)} %collective-permute-done, f32[45,38,3]{2,1,0:T(8,128)S(1)} %copy.57), kind=kLoop, calls=%fused_computation.4 | loop fusion | flops 1145700 | bytes 1833120 | tf_op jit(solution)/shard_map/concatenate | solution.py:30
  17.1 0.7 %fusion.35 = (f32[15,36,132]{2,1,0:T(8,128)S(1)}, f32[15,36,132]{2,1,0:T(8,128)S(1)}, f32[15,36,132]{2,1,0:T(8,128)S(1)}, f32[15,36,132]{2,1,0:T(8,128)S(1)}) fusion(f32[45,38,134]{2,1,0:T(8,128)S(1)} %pad_maximum_fusion), kind=kLoop, calls=%fused_computation.53 | loop fusion | flops 570240 | bytes 2566080 | tf_op jit(solution)/shard_map/mul | solution.py:44
  17.8 1.4 %fusion.14 = f32[2,15,36,132]{3,2,1,0:T(8,128)S(1)} fusion(f32[2,15,38,134]{3,2,1,0:T(8,128)S(1)} %bitcast.38, f32[15,36,132]{2,1,0:T(8,128)S(1)} %get-tuple-element.14, f32[15,36,132]{2,1,0:T(8,128)S(1)} %get-tuple-element.15, f32[15,36,132]{2,1,0:T(8,128)S(1)} %get-tuple-element.16, f32[15,36,132]{2,1,0:T(8,128)S(1)} %get-tuple-element.13, ...), kind=kLoop, calls=%fused_computation.21 | loop fusion | flops 1853280 | bytes 4561956 | tf_op jit(solution)/shard_map/jit(_where)/select_n | solution.py:54
  19.2 0.9 %fusion.31 = (f32[15,34,130]{2,1,0:T(8,128)S(1)}, f32[15,34,130]{2,1,0:T(8,128)S(1)}, f32[15,34,130]{2,1,0:T(8,128)S(1)}, f32[15,34,130]{2,1,0:T(8,128)S(1)}) fusion(f32[45,38,134]{2,1,0:T(8,128)S(1)} %pad_maximum_fusion, f32[45,38,3]{2,1,0:T(8,128)S(1)} %copy.58, f32[45,3,128]{2,1,0:T(4,128)S(1)} %collective-permute-done.1, ...), kind=kLoop, calls=%fused_computation.45 | loop fusion | flops 1060800 | bytes 2772960 | tf_op jit(solution)/shard_map/mul | solution.py:44
  20.1 1.4 %fusion.5 = f32[2,15,34,130]{3,2,1,0:T(8,128)S(1)} fusion(f32[2,15,36,132]{3,2,1,0:T(8,128)S(1)} %fusion.14, f32[15,34,130]{2,1,0:T(8,128)S(1)} %get-tuple-element.11, f32[15,34,130]{2,1,0:T(8,128)S(1)} %get-tuple-element.12, f32[15,34,130]{2,1,0:T(8,128)S(1)} %get-tuple-element.10, f32[15,34,130]{2,1,0:T(8,128)S(1)} %get-tuple-element.9, ...), kind=kLoop, calls=%fused_computation.8 | loop fusion | flops 1723800 | bytes 4243234 | tf_op jit(solution)/shard_map/jit(_where)/select_n | solution.py:54
  21.5 0.4 fusion.48
  21.9 0.6 %fusion.38 = f32[2,15,32,128]{3,2,1,0:T(8,128)S(1)} fusion(f32[2,15,34,130]{3,2,1,0:T(8,128)S(1)} %fusion.5, f32[15,32,128]{2,1,0:T(8,128)S(1)} %get-tuple-element.18, f32[15,32,128]{2,1,0:T(8,128)S(1)} %get-tuple-element.17, f32[15,32,128]{2,1,0:T(8,128)S(1)} %get-tuple-element.22, f32[15,32,128]{2,1,0:T(8,128)S(1)} %get-tuple-element.21), kind=kLoop, calls=%fused_computation.58 | loop fusion | flops 1474560 | bytes 3932160 | tf_op jit(solution)/shard_map/add | solution.py:45
  22.6 1.2 %select_reduce_fusion = bf16[30,2048]{1,0:T(8,128)(2,1)S(1)} fusion(pred[32,2048]{1,0:T(8,128)(4,1)S(1)} %pad_add_fusion, bf16[30,32,128]{2,1,0:T(8,128)(2,1)S(1)} %bitcast_convert_fusion, pred[128,1024]{1,0:T(32,128)(4,1)S(1)} %iota_compare_fusion), kind=kOutput, calls=%fused_computation | convolution fusion | flops 507449344 | bytes 565248 | tf_op jit(solution)/shard_map/dot_general | solution.py:150
  23.8 0.7 %copy.48 = bf16[30,8,256]{2,0,1:T(8,128)(2,1)} copy(bf16[30,8,256]{2,1,0:T(8,128)(2,1)S(1)} %slice.212) | data formatting | bytes 245760 | tf_op jit(solution)/shard_map/reshape | solution.py:158
  24.5 6.9 %all-to-all-start = ((bf16[30,8,256]{2,0,1:T(8,128)(2,1)}), bf16[30,8,256]{2,0,1:T(8,128)(2,1)S(1)}, u32[]{:S(2)}, u32[]{:S(2)}) async-start(bf16[30,8,256]{2,0,1:T(8,128)(2,1)} %copy.48), calls=%async_computation | async-start | bytes 262144 | tf_op jit(solution)/shard_map/all_to_all | solution.py:170
  31.7 7.4 %all-to-all-done = bf16[30,8,256]{2,0,1:T(8,128)(2,1)S(1)} async-done(((bf16[30,8,256]{2,0,1:T(8,128)(2,1)}), bf16[30,8,256]{2,0,1:T(8,128)(2,1)S(1)}, u32[]{:S(2)}, u32[]{:S(2)}) %all-to-all-start) | async-done | bytes 122912 | tf_op jit(solution)/shard_map/all_to_all | solution.py:170
  39.1 0.1 copy.64
  39.4 2.2 %copy-done = bf16[1,2,1024,1024]{3,2,1,0:T(8,128)(2,1)S(1)} copy-done((bf16[1,2,1024,1024]{3,2,1,0:T(8,128)(2,1)S(1)}, bf16[1,2,1024,1024]{3,2,1,0:T(8,128)(2,1)}, u32[]{:S(2)}) %copy-start) | copy-done | bytes 4194328
  41.5 3.4 %shard_map.73 = bf16[120,512]{1,0:T(8,128)(2,1)S(1)} custom-call(bf16[120,512]{1,0:T(8,128)(2,1)S(1)} %bitcast.35, bf16[120,1024]{1,0:T(8,128)(2,1)S(1)} %reshape.100.first_ref, bf16[2,1024,1024]{2,1,0:T(8,128)(2,1)S(1)} %bitcast.36, bf16[120,1024]{1,0:T(8,128)(2,1)S(1)} %bitcast.37), custom_call_target="tpu_custom_call" | custom-call | flops 2399141888 | bytes 4931584 | tf_op jit(solution)/shard_map/pallas_call | solution.py:106
  45.1 0.7 %copy.53 = bf16[30,8,256]{2,0,1:T(8,128)(2,1)} copy(bf16[30,8,256]{2,1,0:T(8,128)(2,1)S(1)} %reshape.102) | data formatting | bytes 245760 | tf_op jit(solution)/shard_map/reshape | solution.py:188
  45.8 3.4 %all-to-all-start.1 = ((bf16[30,8,256]{2,0,1:T(8,128)(2,1)}), bf16[30,8,256]{2,0,1:T(8,128)(2,1)S(1)}, u32[]{:S(2)}, u32[]{:S(2)}) async-start(bf16[30,8,256]{2,0,1:T(8,128)(2,1)} %copy.53), calls=%async_computation.1 | async-start | bytes 262144 | tf_op jit(solution)/shard_map/all_to_all | solution.py:190
  49.2 7.4 %all-to-all-done.1 = bf16[30,8,256]{2,0,1:T(8,128)(2,1)S(1)} async-done(((bf16[30,8,256]{2,0,1:T(8,128)(2,1)}), bf16[30,8,256]{2,0,1:T(8,128)(2,1)S(1)}, u32[]{:S(2)}, u32[]{:S(2)}) %all-to-all-start.1) | async-done | bytes 122912 | tf_op jit(solution)/shard_map/all_to_all | solution.py:190
  56.8 0.2 broadcast_select_fusion
  57.0 1.5 %fusion.21 = f32[30,32,128]{2,1,0:T(8,128)} fusion(f32[30,32,128]{2,1,0:T(8,128)S(1)} %bitcast.44, pred[32,1024]{1,0:T(8,128)(4,1)S(1)} %iota_compare_fusion.1, bf16[30,1024]{1,0:T(8,128)(2,1)S(1)} %bitcast.52, s32[1024]{0:T(1024)S(1)} %bitcast.54), kind=kOutput, calls=%fused_computation.31 | convolution fusion | flops 252895232 | bytes 1081344 | tf_op jit(solution)/shard_map/dot_general | solution.py:201
  (36 shorter events, 1.0 us)
Async XLA Ops:
  0.0 7.1 %copy-start.3 = (f32[15,32,128]{2,1,0:T(8,128)S(1)}, f32[15,32,128]{2,1,0:T(8,128)}, u32[]{:S(2)}) copy-start(f32[15,32,128]{2,1,0:T(8,128)} %param.8) | copy-start | bytes 737284
  0.0 7.1 %copy-start.2 = (f32[2,15,32,128]{3,2,1,0:T(8,128)S(1)}, f32[2,15,32,128]{3,2,1,0:T(8,128)}, u32[]{:S(2)}) copy-start(f32[2,15,32,128]{3,2,1,0:T(8,128)} %param.7) | copy-start | bytes 1474564
  1.1 5.9 %collective-permute-start.1 = (f32[45,3,128]{2,1,0:T(4,128)S(1)}, f32[45,3,128]{2,1,0:T(4,128)S(1)}, u32[]{:S(2)}, u32[]{:S(2)}) collective-permute-start(f32[45,3,128]{2,1,0:T(4,128)S(1)} %get-tuple-element.24), channel_id=1, source_target_pairs={{8,0},{16,8},{24,16},{9,1},{17,9},{25,17},{10,2},{18,10},{26,18},{... | collective-permute-start | bytes 207368 | tf_op jit(solution)/shard_map/ppermute | solution.py:17
  2.4 4.6 %collective-permute-start = (f32[45,3,128]{2,1,0:T(4,128)S(1)}, f32[45,3,128]{2,1,0:T(4,128)S(1)}, u32[]{:S(2)}, u32[]{:S(2)}) collective-permute-start(f32[45,3,128]{2,1,0:T(4,128)S(1)} %get-tuple-element.23), channel_id=1, source_target_pairs={{0,8},{8,16},{16,24},{1,9},{9,17},{17,25},{2,10},{10,18},{18,26},{... | collective-permute-start | bytes 207368 | tf_op jit(solution)/shard_map/ppermute | solution.py:14
  8.4 6.6 %collective-permute-start.2 = (f32[45,38,6]{0,1,2:T(8,128)S(1)}, f32[45,38,6]{0,1,2:T(8,128)S(1)}, u32[]{:S(2)}, u32[]{:S(2)}) collective-permute-start(f32[45,38,6]{0,1,2:T(8,128)S(1)} %pad_maximum_fusion.14), channel_id=1, source_target_pairs={{0,4},{4,0},{1,5},{5,1},{2,6},{6,2},{3,7},{7,3},{8,12},{12,8},{9,1... | collective-permute-start | bytes 123128 | tf_op jit(solution)/shard_map/ppermute | solution.py:25
  22.6 8.9 %copy-start.4 = (bf16[1,120,1024]{2,1,0:T(8,128)(2,1)S(1)}, bf16[1,120,1024]{2,1,0:T(8,128)(2,1)}, u32[]{:S(2)}) copy-start(bf16[1,120,1024]{2,1,0:T(8,128)(2,1)} %param.11) | copy-start | bytes 737284
  24.5 14.8 %copy-start.1 = (bf16[1,1024,120]{1,2,0:T(8,128)(2,1)S(1)}, bf16[1,1024,120]{1,2,0:T(8,128)(2,1)}, u32[]{:S(2)}) copy-start(bf16[1,1024,120]{1,2,0:T(8,128)(2,1)} %param.13) | copy-start | bytes 737284
  24.5 14.6 %all-to-all-start = ((bf16[30,8,256]{2,0,1:T(8,128)(2,1)}), bf16[30,8,256]{2,0,1:T(8,128)(2,1)S(1)}, u32[]{:S(2)}, u32[]{:S(2)}) async-start(bf16[30,8,256]{2,0,1:T(8,128)(2,1)} %copy.48), calls=%async_computation | async-start | bytes 262144 | tf_op jit(solution)/shard_map/all_to_all | solution.py:170
  39.4 2.2 %copy-start = (bf16[1,2,1024,1024]{3,2,1,0:T(8,128)(2,1)S(1)}, bf16[1,2,1024,1024]{3,2,1,0:T(8,128)(2,1)}, u32[]{:S(2)}) copy-start(bf16[1,2,1024,1024]{3,2,1,0:T(8,128)(2,1)} %param.12) | copy-start | bytes 12582916
  45.0 4.2 %copy-start.5 = (s32[1,1024,1]{1,2,0:T(1,128)S(1)}, s32[1,1024,1]{1,2,0:T(1,128)}, u32[]{:S(2)}) copy-start(s32[1,1024,1]{1,2,0:T(1,128)} %param.10) | copy-start | bytes 12292
  45.8 10.8 %all-to-all-start.1 = ((bf16[30,8,256]{2,0,1:T(8,128)(2,1)}), bf16[30,8,256]{2,0,1:T(8,128)(2,1)S(1)}, u32[]{:S(2)}, u32[]{:S(2)}) async-start(bf16[30,8,256]{2,0,1:T(8,128)(2,1)} %copy.53), calls=%async_computation.1 | async-start | bytes 262144 | tf_op jit(solution)/shard_map/all_to_all | solution.py:190
